TPU v7x, 128 devices: a whole 4x4x4 slice. The times are simulated.
128 devices in a mesh: segment: 8 (over x, core), blk: 16 (over y, z).
Axes of the slice: x: 4, y: 4, z: 4, core: 2. Of those that a mesh axis runs over, the one named last changes fastest.
Arguments:
- fresh: bfloat16 [256, 4096], replicated, may hold values from -6 to 6
- previous: bfloat16 [8, 256, 4096], P('segment'), may hold values from -6 to 6
- span_index: int32 [8], P('segment'), may hold values from 0 to 7
- cache_counts: int32 [8, 16], P('segment'), may hold values from 1 to 2048, 16384 in all within a row
- norm_gain: float32 [8, 4096], P('segment'), may hold values from 0.1 to 1.9
- w_query: bfloat16 [8, 4096, 4096], P('segment', None, 'blk'), may hold values from -0.375 to 0.375
- w_keyval: bfloat16 [8, 4096, 2048], P('segment', None, 'blk'), may hold values from -0.09375 to 0.09375
- w_out: bfloat16 [8, 4096, 4096], P('segment', 'blk'), may hold values from -0.09375 to 0.09375
- cache_keys: bfloat16 [8, 32768, 1024], P('segment', 'blk'), may hold values from -220 to 220
- cache_values: bfloat16 [8, 32768, 1024], P('segment', 'blk'), may hold values from -6 to 6
Outputs:
- mixed: bfloat16 [8, 256, 4096], P('segment')
Inputs may be any that keep to these rules, and one draw needn't show every extreme that they name: Each row of cache_counts sums to 16384 and its largest entry is 2048.
All inputs are finite; a program needn't handle non-finite values.
Results may differ from a plain program's by a relative error of at most 0.012.
Values may be sent and summed in bfloat16 or wider, within the bound.
No kernel may reach another device: no remote copies, remote signals or barrier semaphores. Data moves between devices by JAX's collectives and lax.ppermute only.
A program may use at most 128 MiB of HBM per device.

v0:
```python
import jax
import jax.numpy as jnp
from jax import lax
from jax.sharding import PartitionSpec as P

KVH = 8
HD = 128


ROPE_BASE = 500000.0
EPSILON = 1e-05


def passed_along(block, axis, distance):
    devices = range(lax.axis_size(axis))
    route = [(i - distance, i) for i in devices if i - distance in devices]
    return lax.ppermute(block, axis, route)


def swapped(block, axis, distance):
    count = lax.axis_size(axis)
    route = []
    for low in range(count):
        high = low | 1 << distance
        if high != low and high < count:
            route += [(low, high), (high, low)]
    return lax.ppermute(block, axis, route)


def rotate(projected, first_span):
    length = projected.shape[0]
    half_width = projected.shape[-1] // 2
    positions = (first_span * length + jnp.arange(length, dtype=jnp.int32)).astype(jnp.float32)
    inverse = ROPE_BASE ** (
        -(jnp.arange(half_width, dtype=jnp.float32) * 2.0) / projected.shape[-1]
    )
    angles = positions[:, None] * inverse[None, :]
    cosine = jnp.cos(angles)[:, None, :]
    sine_table = jnp.sin(angles)[:, None, :]
    left_part = projected[..., :half_width]
    right_part = projected[..., half_width:]
    return jnp.concatenate(
        [
            left_part * cosine - right_part * sine_table,
            right_part * cosine + left_part * sine_table,
        ],
        axis=-1,
    )


def attend_rows(query_rows, key_rows, value_rows, allowed):
    scores = lax.dot_general(
        query_rows, key_rows, (((1,), (1,)), ((), ())), preferred_element_type=jnp.float32
    ) * query_rows.shape[-1] ** (-0.5)
    scores = jnp.where(allowed, scores, -jnp.inf)
    highest = jnp.max(scores, axis=-1, keepdims=True)
    weights = jnp.exp(scores - highest)
    totals = jnp.sum(weights, axis=-1, keepdims=True)
    partial_out = (
        jnp.dot(weights.astype(jnp.bfloat16), value_rows, preferred_element_type=jnp.float32)
        / totals
    ).astype(jnp.bfloat16)
    return (partial_out, (highest + jnp.log(totals))[:, 0])


def shards(
    fresh,
    previous,
    span_index,
    cache_counts,
    norm_gain,
    w_query,
    w_keyval,
    w_out,
    cache_keys,
    cache_values,
):
    blocks = lax.axis_size("blk")
    position = lax.axis_index("blk")
    span_rows = fresh.shape[0]
    arrived = passed_along(previous[0], "segment", 1)
    current = jnp.where(lax.axis_index("segment") == 0, fresh, arrived)
    widened = current.astype(jnp.float32)
    normed = (
        widened
        * lax.rsqrt(jnp.mean(widened * widened, axis=-1, keepdims=True) + EPSILON)
        * norm_gain[0]
    ).astype(jnp.bfloat16)
    first_span = span_index[0]
    heads_here = w_query.shape[2] // HD
    ratio = blocks // KVH
    queries = jnp.dot(normed, w_query[0], preferred_element_type=jnp.float32).reshape(
        span_rows, heads_here, HD
    )
    queries = rotate(queries, first_span).astype(jnp.bfloat16).reshape(span_rows, heads_here * HD)
    projected = jnp.dot(normed, w_keyval[0], preferred_element_type=jnp.float32)
    odd_member = position % 2 == 1
    as_key = rotate(projected[:, None, :], first_span)[:, 0, :].astype(jnp.bfloat16)
    mine = jnp.where(odd_member, projected.astype(jnp.bfloat16), as_key)
    partner = swapped(mine, "blk", 0)
    own_keys = jnp.where(odd_member, partner, mine)
    own_values = jnp.where(odd_member, mine, partner)
    query_rows = queries.reshape(span_rows * heads_here, HD)
    row_tokens = jnp.arange(span_rows * heads_here, dtype=jnp.int32) // heads_here
    causal = row_tokens[:, None] >= jnp.arange(span_rows, dtype=jnp.int32)[None, :]
    own_out, own_log = attend_rows(query_rows, own_keys, own_values, causal)
    own_out = own_out.reshape(span_rows, heads_here * HD)
    own_log = own_log.reshape(span_rows, heads_here).T
    cache_rows = cache_keys.shape[1]
    offsets = jnp.arange(cache_rows, dtype=jnp.int32)
    every_query = lax.all_gather(queries, "blk", axis=0, tiled=True)
    live = cache_counts[0, position]

    def holder(source):
        query_block = lax.dynamic_slice_in_dim(
            every_query, source * span_rows, span_rows, 0
        ).reshape(span_rows * heads_here, HD)
        head_start = source // ratio * HD
        key_rows = lax.dynamic_slice_in_dim(cache_keys[0], head_start, HD, 1)
        value_rows = lax.dynamic_slice_in_dim(cache_values[0], head_start, HD, 1)
        partial_out, log_totals = attend_rows(
            query_block, key_rows, value_rows, (offsets < live)[None, :]
        )
        return (
            partial_out.reshape(span_rows, heads_here * HD),
            log_totals.reshape(span_rows, heads_here).T,
        )

    held_outs, held_logs = lax.map(holder, jnp.arange(blocks, dtype=jnp.int32))
    shard_outs = lax.all_to_all(held_outs, "blk", split_axis=0, concat_axis=0, tiled=True)
    shard_logs = lax.all_to_all(held_logs, "blk", split_axis=0, concat_axis=0, tiled=True)
    all_outs = (
        jnp.concatenate([own_out[None], shard_outs], axis=0)
        .astype(jnp.float32)
        .reshape(blocks + 1, span_rows, heads_here, HD)
    )
    all_logs = jnp.concatenate([own_log[None], shard_logs], axis=0).transpose(0, 2, 1)
    ceiling = jnp.max(all_logs, axis=0)
    factors = jnp.exp(all_logs - ceiling)
    attended = (
        jnp.sum(factors[..., None] * all_outs, axis=0) / jnp.sum(factors, axis=0)[..., None]
    ).astype(jnp.bfloat16)
    attended = attended.reshape(span_rows, heads_here * HD)
    head_terms = lax.optimization_barrier(
        jnp.dot(attended, w_out[0], preferred_element_type=jnp.float32).astype(jnp.bfloat16)
    ).astype(jnp.float32)
    summed = lax.psum(head_terms.astype(jnp.bfloat16), "blk").astype(jnp.float32)
    mixed = (widened + summed).astype(jnp.bfloat16)
    return mixed[None]


def solution(mesh):
    placed = (
        P(),
        P("segment", None, None),
        P("segment"),
        P("segment", None),
        P("segment", None),
        P("segment", None, "blk"),
        P("segment", None, "blk"),
        P("segment", "blk", None),
        P("segment", "blk", None),
        P("segment", "blk", None),
    )
    return jax.shard_map(
        shards, mesh=mesh, in_specs=placed, out_specs=P("segment", None, None), check_vma=False
    )
```

profile of v0, /device:TPU:2, one launch (start us, length us, event | category | flops | bytes accessed | tf_op | source)
XLA Modules:
  0.0 425.7 jit_solution(5192613194957220926)
XLA Ops:
  6.5 2.0 collective-permute-start
  8.6 4.1 copy.33
  13.7 20.6 %collective-permute-done = bf16[256,4096]{1,0:T(8,128)(2,1)} collective-permute-done((bf16[256,4096]{1,0:T(8,128)(2,1)}, bf16[256,4096]{1,0:T(8,128)(2,1)}, u32[]{:S(2)}, u32[]{:S(2)}) %collective-permute-start) | collective-permute-done | bytes 2097184 | tf_op jit(solution)/shard_map/ppermute | solution.py:17
  34.3 2.5 fusion.23
  39.7 47.2 %all-gather.2.cloned.1.call-done = bf16[4096,256]{1,0:T(8,128)(2,1)} async-done(((bf16[256,256]{1,0:T(8,128)(2,1)}), bf16[4096,256]{1,0:T(8,128)(2,1)}) %all-gather.2.cloned.1.call-update) | async-done | bytes 2097168 | tf_op jit(solution)/shard_map/all_gather | solution.py:111
  86.9 177.8 %while.15 = (s32[]{:T(128)}, bf16[16,256,256]{2,1,0:T(8,128)(2,1)}, f32[16,2,256]{2,1,0:T(2,128)S(1)}, s32[]{:T(128)}, s32[16]{0:T(128)S(1)}, /*index=5*/bf16[40...) while((s32[]{:T(128)}, bf16[16,256,256]{2,1,0:T(8,128)(2,1)}, ...), condition=%wide.region_6.7_spmd.clone, body=%wide.region_3.6_spmd.clone.sunk | while | flops 548537856 | bytes 14979499 | solution.py:129
  92.2 1.9 fusion.77
  95.0 2.0 fusion.79
  103.3 1.9 fusion.77
  106.1 2.0 fusion.79
  114.4 1.9 fusion.77
  117.2 2.0 fusion.79
  125.5 1.9 fusion.77
  128.3 2.0 fusion.79
  136.6 1.9 fusion.77
  139.4 2.0 fusion.79
  147.7 1.9 fusion.77
  150.5 2.0 fusion.79
  158.9 1.9 fusion.77
  161.7 2.0 fusion.79
  170.0 1.9 fusion.77
  172.8 2.0 fusion.79
  181.1 1.9 fusion.77
  183.9 2.0 fusion.79
  192.2 1.9 fusion.77
  195.0 2.0 fusion.79
  203.3 1.9 fusion.77
  206.1 2.0 fusion.79
  214.4 1.9 fusion.77
  217.2 2.0 fusion.79
  225.5 1.9 fusion.77
  228.3 2.0 fusion.79
  236.7 1.9 fusion.77
  239.5 2.0 fusion.79
  247.8 1.9 fusion.77
  250.6 2.0 fusion.79
  258.9 1.9 fusion.77
  261.7 2.0 fusion.79
  264.7 12.4 %all_to_all.10 = f32[16,2,256]{2,1,0:T(2,128)S(1)} all-to-all(f32[16,2,256]{2,1,0:T(2,128)S(1)} %get-tuple-element.120), channel_id=1, replica_groups=mesh['segment'=8,'blk'=16] {'blk'}, dimensions={0} | all-to-all | bytes 65536 | tf_op jit(solution)/shard_map/all_to_all | solution.py:131
  277.1 4.4 %all-to-all-start.1 = ((bf16[16,256,256]{2,1,0:T(8,128)(2,1)}), bf16[16,256,256]{2,1,0:T(8,128)(2,1)}, u32[]{:S(2)}, u32[]{:S(2)}) async-start(bf16[16,256,256]{2,1,0:T(8,128)(2,1)} %get-tuple-element.121), calls=%async_computation.1 | async-start | bytes 4194304 | tf_op jit(solution)/shard_map/all_to_all | solution.py:130
  281.5 2.8 fusion.33
  286.8 18.0 %collective-permute-done.1 = bf16[256,128]{0,1:T(8,128)(2,1)S(1)} collective-permute-done((bf16[256,128]{0,1:T(8,128)(2,1)S(1)}, bf16[256,128]{0,1:T(8,128)(2,1)S(1)}, u32[]{:S(2)}, u32[]{:S(2)}) %collective-permute-start.1) | collective-permute-done | bytes 65568 | tf_op jit(solution)/shard_map/ppermute | solution.py:27
  305.9 2.1 copy.31
  309.3 4.0 concatenate.34
  313.3 7.7 %multiply_reduce_fusion = f32[256,2,128]{2,1,0:T(2,128)S(1)} fusion(bf16[16,256,2,128]{3,2,1,0:T(2,128)(2,1)} %concatenate.34, bf16[1,256,2,128]{3,2,1,0:T(2,128)(2,1)S(1)} %bitcast.73, f32[17,256,2]{2,1,0:T(8,128)} %copy.31), kind=kLoop, calls=%fused_computation.28 | loop fusion | flops 4390912 | bytes 2525184 | tf_op jit(solution)/shard_map/reduce_sum | solution.py:141
  321.4 2.0 convolution_convert_fusion
  323.4 91.1 %all-reduce.2.cloned.1.call-done = bf16[256,4096]{1,0:T(8,128)(2,1)} async-done(((bf16[256,4096]{1,0:T(8,128)(2,1)}), bf16[256,4096]{1,0:T(8,128)(2,1)}) %all-reduce.2.cloned.1.call-update) | async-done | bytes 2097168 | tf_op jit(solution)/shard_map/psum | solution.py:147
  414.5 4.3 %fusion.27 = bf16[1,256,4096]{2,1,0:T(8,128)(2,1)} fusion(bf16[256,4096]{1,0:T(8,128)(2,1)} %all-reduce.2.cloned.1.call-done, bf16[256,4096]{1,0:T(8,128)(2,1)} %copy-done.1), kind=kLoop, calls=%fused_computation.33 | loop fusion | flops 4194304 | bytes 6291456 | tf_op jit(solution)/shard_map/broadcast_in_dim | solution.py:149
  (219 shorter events, 73.5 us)
Async XLA Ops:
  6.5 314.8 %copy-start = (bf16[1,256,4096]{2,1,0:T(8,128)(2,1)S(1)}, bf16[1,256,4096]{2,1,0:T(8,128)(2,1)}, u32[]{:S(2)}) copy-start(bf16[1,256,4096]{2,1,0:T(8,128)(2,1)} %param.19) | copy-start | bytes 6291460
  6.5 80.3 %all-gather.2.cloned.1.call-start = ((), (), s32[]{:S(2)}) async-start(), calls=%async_computation.2 | async-start | bytes 2228224 | tf_op jit(solution)/shard_map/all_gather | solution.py:111
  6.5 27.8 %collective-permute-start = (bf16[256,4096]{1,0:T(8,128)(2,1)}, bf16[256,4096]{1,0:T(8,128)(2,1)}, u32[]{:S(2)}, u32[]{:S(2)}) collective-permute-start(bf16[256,4096]{1,0:T(8,128)(2,1)} %bitcast.76), channel_id=1, source_target_pairs={{0,16},{16,32},{32,48},{48,64},{64,80},{80,96},{96,112},{1,17},{17... | collective-permute-start | bytes 6291464 | tf_op jit(solution)/shard_map/ppermute | solution.py:17
  13.7 23.2 %copy-start.2 = (bf16[256,4096]{1,0:T(8,128)(2,1)S(1)}, bf16[256,4096]{1,0:T(8,128)(2,1)}, u32[]{:S(2)}) copy-start(bf16[256,4096]{1,0:T(8,128)(2,1)} %copy.33) | copy-start | bytes 6291460
  13.7 23.2 %copy-start.3 = (f32[1,4096]{1,0:T(1,128)S(1)}, f32[1,4096]{1,0:T(1,128)}, u32[]{:S(2)}) copy-start(f32[1,4096]{1,0:T(1,128)} %param.16) | copy-start | bytes 49156
  36.9 1.3 copy-start.1
  36.9 2.1 copy-start.4
  277.1 32.3 %all-to-all-start.1 = ((bf16[16,256,256]{2,1,0:T(8,128)(2,1)}), bf16[16,256,256]{2,1,0:T(8,128)(2,1)}, u32[]{:S(2)}, u32[]{:S(2)}) async-start(bf16[16,256,256]{2,1,0:T(8,128)(2,1)} %get-tuple-element.121), calls=%async_computation.1 | async-start | bytes 4194304 | tf_op jit(solution)/shard_map/all_to_all | solution.py:130
  281.5 133.0 %all-reduce.2.cloned.1.call-start = ((), (), s32[]{:S(2)}) async-start(), calls=%async_computation.3 | async-start | bytes 4194304 | tf_op jit(solution)/shard_map/psum | solution.py:147
  284.7 20.1 %collective-permute-start.1 = (bf16[256,128]{0,1:T(8,128)(2,1)S(1)}, bf16[256,128]{0,1:T(8,128)(2,1)S(1)}, u32[]{:S(2)}, u32[]{:S(2)}) collective-permute-start(bf16[256,128]{0,1:T(8,128)(2,1)S(1)} %fusion.54), channel_id=1, source_target_pairs={{0,1},{1,0},{2,3},{3,2},{4,5},{5,4},{6,7},{7,6},{8,9},{9,8},{10,11... | collective-permute-start | bytes 196616 | tf_op jit(solution)/shard_map/ppermute | solution.py:27
Sparse Core Ops, SparseCore 0:
  39.2 47.6 all-gather.1
  323.5 90.9 all-reduce.1
where the time goes:
time: 429 us; the launch traced here: 426 us
  waiting for transfers between devices  178 us (41%)
  matrix products  68.5 us (16%)
  local copies, waits for them, and re-layouts  52.7 us (12%)
  loops' own time  50.4 us (12%)
  other arithmetic  41 us (10%)
  between operations  14.3 us (3%)
  blocking collectives  12.4 us (3%)
  starting transfers between devices  8.33 us (2%)
    psum x1, waiting for transfers between devices, shards(): lax.psum(head_terms.astype(jnp.bfloat16), 'blk').astype(jnp.float32)  91.1 us
    another operation x1, loops' own time, shards(): held_outs, held_logs = lax.map(holder, jnp.arange(blocks, dtype=jnp.int32))  50.4 us
    all_gather x1, waiting for transfers between devices, shards(): every_query = lax.all_gather(queries, 'blk', axis=0, tiled=True)  47.2 us
    dot_general x17, matrix products, attend_rows(): jnp.dot(weights.astype(jnp.bfloat16), value_rows, preferred_element_type=...  32.6 us
    dot_general x17, matrix products, attend_rows(): lax.dot_general(query_rows, key_rows, (((1,), (1,)), ((), ())), preferred...  30.1 us
    ppermute x1, waiting for transfers between devices, passed_along(): return lax.ppermute(block, axis, route)  20.6 us
    ppermute x1, waiting for transfers between devices, swapped(): return lax.ppermute(block, axis, route)  18 us
    reduce_sum x17, other arithmetic, attend_rows(): totals = jnp.sum(weights, axis=-1, keepdims=True)  15.2 us
  transfers between devices with their start and end apart: 5, of which 5 were waited for; matrix products, arithmetic and copies ran while one was open for 3% of the time, Pallas kernels for 0%

commit v1 on v0

--- a/solution.py
+++ b/solution.py
@@ -2,6 +2,8 @@
 import jax.numpy as jnp
 from jax import lax
 from jax.sharding import PartitionSpec as P
+from jax.experimental import pallas as pl
+from jax.experimental.pallas import tpu as pltpu
 
 KVH = 8
 HD = 128
@@ -61,6 +63,55 @@
         / totals
     ).astype(jnp.bfloat16)
     return (partial_out, (highest + jnp.log(totals))[:, 0])
+
+
+def cache_kernel(live_ref, q_ref, k_ref, v_ref, out_ref, log_ref):
+    live = live_ref[0]
+    keys = k_ref[...]
+    values = v_ref[...]
+    visible = lax.broadcasted_iota(jnp.int32, (1, keys.shape[0]), 1) < live
+    for src in range(q_ref.shape[0]):
+        for h in range(q_ref.shape[2] // HD):
+            q = q_ref[src, :, h * HD:(h + 1) * HD]
+            scores = lax.dot_general(
+                q, keys, (((1,), (1,)), ((), ())), preferred_element_type=jnp.float32
+            ) * HD ** (-0.5)
+            scores = jnp.where(visible, scores, -jnp.inf)
+            highest = jnp.max(scores, axis=-1, keepdims=True)
+            weights = jnp.exp(scores - highest)
+            totals = jnp.sum(weights, axis=-1, keepdims=True)
+            part = jnp.dot(weights.astype(jnp.bfloat16), values, preferred_element_type=jnp.float32)
+            out_ref[src, :, h * HD:(h + 1) * HD] = (part / totals).astype(out_ref.dtype)
+            log_ref[src, :, h:h + 1] = highest + jnp.log(totals)
+
+
+def cache_attention(live, every_query, cached_keys, cached_values):
+    sources, span_rows, width = every_query.shape
+    heads_here = width // HD
+    kv_heads = cached_keys.shape[1] // HD
+    per_head = sources // kv_heads
+    rows = cached_keys.shape[0]
+    grid_spec = pltpu.PrefetchScalarGridSpec(
+        num_scalar_prefetch=1,
+        grid=(kv_heads,),
+        in_specs=[
+            pl.BlockSpec((per_head, span_rows, width), lambda g, live: (g, 0, 0)),
+            pl.BlockSpec((rows, HD), lambda g, live: (0, g)),
+            pl.BlockSpec((rows, HD), lambda g, live: (0, g)),
+        ],
+        out_specs=[
+            pl.BlockSpec((per_head, span_rows, width), lambda g, live: (g, 0, 0)),
+            pl.BlockSpec((per_head, span_rows, heads_here), lambda g, live: (g, 0, 0)),
+        ],
+    )
+    return pl.pallas_call(
+        cache_kernel,
+        grid_spec=grid_spec,
+        out_shape=[
+            jax.ShapeDtypeStruct((sources, span_rows, width), jnp.bfloat16),
+            jax.ShapeDtypeStruct((sources, span_rows, heads_here), jnp.float32),
+        ],
+    )(live, every_query, cached_keys, cached_values)
 
 
 def shards(
@@ -105,28 +156,12 @@
     causal = row_tokens[:, None] >= jnp.arange(span_rows, dtype=jnp.int32)[None, :]
     own_out, own_log = attend_rows(query_rows, own_keys, own_values, causal)
     own_out = own_out.reshape(span_rows, heads_here * HD)
-    own_log = own_log.reshape(span_rows, heads_here).T
-    cache_rows = cache_keys.shape[1]
-    offsets = jnp.arange(cache_rows, dtype=jnp.int32)
-    every_query = lax.all_gather(queries, "blk", axis=0, tiled=True)
-    live = cache_counts[0, position]
-
-    def holder(source):
-        query_block = lax.dynamic_slice_in_dim(
-            every_query, source * span_rows, span_rows, 0
-        ).reshape(span_rows * heads_here, HD)
-        head_start = source // ratio * HD
-        key_rows = lax.dynamic_slice_in_dim(cache_keys[0], head_start, HD, 1)
-        value_rows = lax.dynamic_slice_in_dim(cache_values[0], head_start, HD, 1)
-        partial_out, log_totals = attend_rows(
-            query_block, key_rows, value_rows, (offsets < live)[None, :]
-        )
-        return (
-            partial_out.reshape(span_rows, heads_here * HD),
-            log_totals.reshape(span_rows, heads_here).T,
-        )
-
-    held_outs, held_logs = lax.map(holder, jnp.arange(blocks, dtype=jnp.int32))
+    own_log = own_log.reshape(span_rows, heads_here)
+    every_query = lax.all_to_all(
+        jnp.broadcast_to(queries[None], (blocks,) + queries.shape), "blk", 0, 0, tiled=True
+    ).reshape(blocks, span_rows, heads_here * HD)
+    live = cache_counts[0, position].reshape(1)
+    held_outs, held_logs = cache_attention(live, every_query, cache_keys[0], cache_values[0])
     shard_outs = lax.all_to_all(held_outs, "blk", split_axis=0, concat_axis=0, tiled=True)
     shard_logs = lax.all_to_all(held_logs, "blk", split_axis=0, concat_axis=0, tiled=True)
     all_outs = (
@@ -134,18 +169,23 @@
         .astype(jnp.float32)
         .reshape(blocks + 1, span_rows, heads_here, HD)
     )
-    all_logs = jnp.concatenate([own_log[None], shard_logs], axis=0).transpose(0, 2, 1)
+    all_logs = jnp.concatenate([own_log[None], shard_logs], axis=0)
     ceiling = jnp.max(all_logs, axis=0)
     factors = jnp.exp(all_logs - ceiling)
     attended = (
         jnp.sum(factors[..., None] * all_outs, axis=0) / jnp.sum(factors, axis=0)[..., None]
     ).astype(jnp.bfloat16)
     attended = attended.reshape(span_rows, heads_here * HD)
-    head_terms = lax.optimization_barrier(
-        jnp.dot(attended, w_out[0], preferred_element_type=jnp.float32).astype(jnp.bfloat16)
-    ).astype(jnp.float32)
-    summed = lax.psum(head_terms.astype(jnp.bfloat16), "blk").astype(jnp.float32)
-    mixed = (widened + summed).astype(jnp.bfloat16)
+    head_terms = jnp.dot(attended, w_out[0], preferred_element_type=jnp.float32).astype(jnp.bfloat16)
+    chunk = span_rows // blocks
+    gathered_terms = lax.all_to_all(
+        head_terms.reshape(blocks, chunk, -1), "blk", 0, 0, tiled=True
+    )
+    own_rows = lax.dynamic_slice_in_dim(widened, position * chunk, chunk, 0)
+    mixed_rows = (own_rows + jnp.sum(gathered_terms.astype(jnp.float32), axis=0)).astype(jnp.bfloat16)
+    mixed = lax.all_to_all(
+        jnp.broadcast_to(mixed_rows[None], (blocks,) + mixed_rows.shape), "blk", 0, 0, tiled=True
+    ).reshape(span_rows, -1)
     return mixed[None]
 
 

time: 429 us -> 233 us (0.54)
  waiting for transfers between devices: 178 us -> 95.3 us
  matrix products: 68.5 us -> 6.45 us
  loops' own time: 50.4 us -> 0 us
  local copies, waits for them, and re-layouts: 52.7 us -> 18.8 us
  Pallas kernels: 0 us -> 31.7 us
  blocking collectives: 12.4 us -> 41.6 us
  other arithmetic: 41 us -> 16.3 us
  between operations: 14.3 us -> 0.89 us
  starting transfers between devices: 8.33 us -> 21.2 us
    psum x1 -> x0, waiting for transfers between devices: 91.1 us -> none  [shards(): lax.psum(head_terms.astype(jnp.bfloat16), 'blk').astype(jnp.float32)]
    all_to_all x0 -> x2, waiting for transfers between devices: none -> 56.4 us  [the longest x1 28.4 us: shards(): lax.all_to_all(jnp.broadcast_to(queries[None], (blocks,) + queries.shape)...]
    another operation x1 -> x0, loops' own time: 50.4 us -> none  [shards(): held_outs, held_logs = lax.map(holder, jnp.arange(blocks, dtype=jnp.int32))]
    all_gather x1 -> x0, waiting for transfers between devices: 47.2 us -> none  [shards(): every_query = lax.all_gather(queries, 'blk', axis=0, tiled=True)]
    dot_general x17 -> x1, matrix products: 32.6 us -> 0.3 us  [attend_rows(): jnp.dot(weights.astype(jnp.bfloat16), value_rows, preferred_element_type=...]
    pallas_call x0 -> x1, Pallas kernels: none -> 31.7 us  [cache_attention(): pl.pallas_call(cache_kernel, grid_spec=grid_spec, out_shape=[jax.ShapeDty...]
    all_to_all x0 -> x1, blocking collectives: none -> 30.2 us  [shards(): lax.all_to_all(jnp.broadcast_to(mixed_rows[None], (blocks,) + mixed_rows....]
    dot_general x17 -> x1, matrix products: 30.1 us -> 0.33 us  [attend_rows(): lax.dot_general(query_rows, key_rows, (((1,), (1,)), ((), ())), preferred...]
  transfers between devices with their start and end apart: 5 -> 5, of which waited for: 5 -> 4; matrix products, arithmetic and copies ran while one was open for 3% -> 5% of each run, Pallas kernels for 0% -> 0%
where the time goes in v1:
time: 233 us; the launch traced here: 232 us
  waiting for transfers between devices  95.3 us (41%)
  blocking collectives  41.6 us (18%)
  Pallas kernels  31.7 us (14%)
  starting transfers between devices  21.2 us (9%)
  local copies, waits for them, and re-layouts  18.8 us (8%)
  other arithmetic  16.3 us (7%)
  matrix products  6.45 us (3%)
    pallas_call x1, Pallas kernels, cache_attention(): pl.pallas_call(cache_kernel, grid_spec=grid_spec, out_shape=[jax.ShapeDty...  31.7 us
    all_to_all x1, blocking collectives, shards(): lax.all_to_all(jnp.broadcast_to(mixed_rows[None], (blocks,) + mixed_rows....  30.2 us
    all_to_all x1, waiting for transfers between devices, shards(): lax.all_to_all(jnp.broadcast_to(queries[None], (blocks,) + queries.shape)...  28.4 us
    all_to_all x1, waiting for transfers between devices, shards(): lax.all_to_all(head_terms.reshape(blocks, chunk, -1), 'blk', 0, 0, tiled=...  27.9 us
    ppermute x1, waiting for transfers between devices, passed_along(): return lax.ppermute(block, axis, route)  20.7 us
    ppermute x1, waiting for transfers between devices, swapped(): return lax.ppermute(block, axis, route)  18.3 us
    all_to_all x1, blocking collectives, shards(): lax.all_to_all(held_logs, 'blk', split_axis=0, concat_axis=0, tiled=True)  11.3 us
    all_to_all x1, starting transfers between devices, shards(): lax.all_to_all(jnp.broadcast_to(queries[None], (blocks,) + queries.shape)...  8.23 us
  transfers between devices with their start and end apart: 5, of which 4 were waited for; matrix products, arithmetic and copies ran while one was open for 5% of the time, Pallas kernels for 0%

profile of v1, /device:TPU:2, one launch (start us, length us, event | category | flops | bytes accessed | tf_op | source)
XLA Modules:
  0.0 232.2 jit_solution(1369369091477945391)
XLA Ops:
  0.0 2.0 collective-permute-start
  2.7 4.1 %copy.34 = bf16[256,4096]{1,0:T(8,128)(2,1)} copy(bf16[256,4096]{0,1:T(8,128)(2,1)} %bitcast.39) | data formatting | bytes 4194304 | tf_op jit(solution)/shard_map/dot_general | solution.py:143
  6.8 0.3 multiply_cosine_fusion.1
  7.1 20.7 %collective-permute-done = bf16[256,4096]{1,0:T(8,128)(2,1)} collective-permute-done((bf16[256,4096]{1,0:T(8,128)(2,1)}, bf16[256,4096]{1,0:T(8,128)(2,1)}, u32[]{:S(2)}, u32[]{:S(2)}) %collective-permute-start) | collective-permute-done | bytes 2097184 | tf_op jit(solution)/shard_map/ppermute | solution.py:19
  27.8 3.9 %fusion.34 = (f32[256,4096]{1,0:T(8,128)}, bf16[256,4096]{1,0:T(8,128)(2,1)S(1)}) fusion(bf16[256,4096]{1,0:T(8,128)(2,1)} %param.10, bf16[256,4096]{1,0:T(8,128)(2,1)} %collective-permute-done, pred[]{:T(512)S(6)} %eq.8), kind=kLoop, calls=%fused_computation.63 | loop fusion | flops 2097152 | bytes 10485761 | tf_op jit(solution)/shard_map/convert_element_type | solution.py:134
  31.7 0.5 multiply_reduce_fusion.1
  32.2 0.0 copy-done.3
  32.2 1.8 copy-done.2
  34.1 1.0 fusion.1
  35.1 0.0 copy-done.1
  35.1 0.1 copy.28
  35.2 1.5 broadcast_in_dim.11
  36.8 8.2 %all-to-all-start = ((bf16[16,256,256]{2,1,0:T(8,128)(2,1)}), bf16[16,256,256]{2,1,0:T(8,128)(2,1)}, u32[]{:S(2)}, u32[]{:S(2)}) async-start(bf16[16,256,256]{2,1,0:T(8,128)(2,1)} %broadcast_in_dim.11), calls=%async_computation | async-start | bytes 4194304 | tf_op jit(solution)/shard_map/all_to_all | solution.py:160
  45.0 0.0 copy-done.4
  45.0 0.6 constant_dynamic-slice_fusion
  45.7 28.4 %all-to-all-done.q_ref = bf16[16,256,256]{2,1,0:T(8,128)(2,1)} async-done(((bf16[16,256,256]{2,1,0:T(8,128)(2,1)}), bf16[16,256,256]{2,1,0:T(8,128)(2,1)}, u32[]{:S(2)}, u32[]{:S(2)}) %all-to-all-start) | async-done | bytes 2097184 | tf_op jit(solution)/shard_map/all_to_all | solution.py:160
  74.1 31.7 %shard_map.100 = (bf16[16,256,256]{2,1,0:T(8,128)(2,1)}, f32[16,256,2]{2,1,0:T(8,128)}) custom-call(s32[1]{0:T(128)} %bitcast.12.live_ref, bf16[16,256,256]{2,1,0:T(8,128)(2,1)} %all-to-all-done.q_ref, bf16[2048,1024]{1,0:T(8,128)(2,1)} %bitcast.37, bf16[2048,1024]{1,0:T(8,128)(2,1)} %bitcast.38), custom_call_target="tpu_custom_call" | custom-call | tf_op jit(solution)/shard_map/pallas_call | solution.py:107
  105.8 2.2 copy.29
  108.0 11.3 %all_to_all.25 = f32[16,256,2]{1,2,0:T(2,128)S(1)} all-to-all(f32[16,256,2]{1,2,0:T(2,128)S(1)} %copy.29), channel_id=1, replica_groups=mesh['segment'=8,'blk'=16] {'blk'}, dimensions={0} | all-to-all | bytes 65536 | tf_op jit(solution)/shard_map/all_to_all | solution.py:166
  119.3 4.4 %all-to-all-start.2 = ((bf16[16,256,256]{2,1,0:T(8,128)(2,1)}), bf16[16,256,256]{2,1,0:T(8,128)(2,1)}, u32[]{:S(2)}, u32[]{:S(2)}) async-start(bf16[16,256,256]{2,1,0:T(8,128)(2,1)} %get-tuple-element.8), calls=%async_computation.2 | async-start | bytes 4194304 | tf_op jit(solution)/shard_map/all_to_all | solution.py:165
  123.8 2.8 %fusion.5 = f32[256,128]{0,1:T(8,128)S(1)} fusion(bf16[1,4096,128]{2,1,0:T(8,128)(2,1)} %param.16, f32[4096]{0:T(1024)S(1)} %bitcast.49, f32[256]{0:T(256)S(1)} %add_rsqrt_fusion, bf16[256,4096]{1,0:T(8,128)(2,1)} %copy-done.1), kind=kOutput, calls=%fused_computation.13 | convolution fusion | flops 272629760 | bytes 3294208 | tf_op jit(solution)/shard_map/dot_general | solution.py:147
  126.6 0.3 fusion.21
  126.9 2.0 collective-permute-start.1
  128.9 0.1 copy.26
  129.1 0.1 copy.27
  129.2 18.3 %collective-permute-done.1 = bf16[256,128]{0,1:T(8,128)(2,1)S(1)} collective-permute-done((bf16[256,128]{0,1:T(8,128)(2,1)S(1)}, bf16[256,128]{0,1:T(8,128)(2,1)S(1)}, u32[]{:S(2)}, u32[]{:S(2)}) %collective-permute-start.1) | collective-permute-done | bytes 65568 | tf_op jit(solution)/shard_map/ppermute | solution.py:29
  147.4 0.3 fusion.37
  147.8 0.1 fusion.8
  147.9 0.1 add.80
  148.1 0.1 add.78
  148.2 0.1 copy.31
  148.3 0.1 copy.30
  148.4 0.3 fusion.4
  148.8 0.1 copy.33
  148.9 2.1 copy.32
  151.0 0.0 all-to-all-done.2
  151.0 4.0 %concatenate.38 = bf16[16,256,2,128]{3,2,1,0:T(2,128)(2,1)} reshape(bf16[16,256,256]{2,1,0:T(8,128)(2,1)} %all-to-all-done.2) | data formatting | bytes 4194304 | tf_op jit(solution)/shard_map/concatenate | solution.py:168
  154.9 7.7 %multiply_reduce_fusion = f32[256,2,128]{2,1,0:T(2,128)S(1)} fusion(bf16[16,256,2,128]{3,2,1,0:T(2,128)(2,1)} %concatenate.38, bf16[1,256,2,128]{3,2,1,0:T(2,128)(2,1)S(1)} %bitcast.44, f32[17,256,2]{2,1,0:T(8,128)} %copy.32), kind=kLoop, calls=%fused_computation.1 | loop fusion | flops 4390912 | bytes 2525184 | tf_op jit(solution)/shard_map/reduce_sum | solution.py:176
  162.7 0.3 divide_convert_fusion
  163.0 0.0 copy-done
  163.0 2.0 convolution_convert_fusion
  165.1 4.5 %all-to-all-start.3 = ((bf16[16,16,4096]{2,1,0:T(8,128)(2,1)}), bf16[16,16,4096]{2,1,0:T(8,128)(2,1)}, u32[]{:S(2)}, u32[]{:S(2)}) async-start(bf16[16,16,4096]{2,1,0:T(8,128)(2,1)} %bitcast.35), calls=%async_computation.3 | async-start | bytes 4194304 | tf_op jit(solution)/shard_map/all_to_all | solution.py:181
  169.6 27.9 %all-to-all-done.3 = bf16[16,16,4096]{2,1,0:T(8,128)(2,1)} async-done(((bf16[16,16,4096]{2,1,0:T(8,128)(2,1)}), bf16[16,16,4096]{2,1,0:T(8,128)(2,1)}, u32[]{:S(2)}, u32[]{:S(2)}) %all-to-all-start.3) | async-done | bytes 2097184 | tf_op jit(solution)/shard_map/all_to_all | solution.py:181
  197.5 1.9 convert_reduce_fusion
  199.4 1.0 add_convert_fusion
  200.4 0.2 broadcast_in_dim.12
  200.7 30.2 %all_to_all.26 = bf16[16,16,4096]{2,1,0:T(8,128)(2,1)S(1)} all-to-all(bf16[16,16,4096]{2,1,0:T(8,128)(2,1)S(1)} %broadcast_in_dim.12), channel_id=1, replica_groups=mesh['segment'=8,'blk'=16] {'blk'}, dimensions={0} | all-to-all | bytes 4194304 | tf_op jit(solution)/shard_map/all_to_all | solution.py:186
  230.9 1.3 copy.42
  (16 shorter events, 0.2 us)
Async XLA Ops:
  0.0 163.0 %copy-start = (bf16[1,256,4096]{2,1,0:T(8,128)(2,1)S(1)}, bf16[1,256,4096]{2,1,0:T(8,128)(2,1)}, u32[]{:S(2)}) copy-start(bf16[1,256,4096]{2,1,0:T(8,128)(2,1)} %param.17) | copy-start | bytes 6291460
  0.0 27.8 %collective-permute-start = (bf16[256,4096]{1,0:T(8,128)(2,1)}, bf16[256,4096]{1,0:T(8,128)(2,1)}, u32[]{:S(2)}, u32[]{:S(2)}) collective-permute-start(bf16[256,4096]{1,0:T(8,128)(2,1)} %bitcast.47), channel_id=1, source_target_pairs={{0,16},{16,32},{32,48},{48,64},{64,80},{80,96},{96,112},{1,17},{17... | collective-permute-start | bytes 6291464 | tf_op jit(solution)/shard_map/ppermute | solution.py:19
  27.8 4.4 %copy-start.3 = (f32[1,4096]{1,0:T(1,128)S(1)}, f32[1,4096]{1,0:T(1,128)}, u32[]{:S(2)}) copy-start(f32[1,4096]{1,0:T(1,128)} %param.14) | copy-start | bytes 49156
  31.7 3.3 %copy-start.1 = (bf16[256,4096]{1,0:T(8,128)(2,1)}, bf16[256,4096]{1,0:T(8,128)(2,1)S(1)}, u32[]{:S(2)}) copy-start(bf16[256,4096]{1,0:T(8,128)(2,1)S(1)} %get-tuple-element.10) | copy-start | bytes 6291460
  31.7 2.3 %copy-start.2 = (bf16[256,4096]{1,0:T(8,128)(2,1)S(1)}, bf16[256,4096]{1,0:T(8,128)(2,1)}, u32[]{:S(2)}) copy-start(bf16[256,4096]{1,0:T(8,128)(2,1)} %copy.34) | copy-start | bytes 6291460
  36.8 8.2 %copy-start.4 = (s32[1,16]{1,0:T(1,128)S(1)}, s32[1,16]{1,0:T(1,128)}, u32[]{:S(2)}) copy-start(s32[1,16]{1,0:T(1,128)} %param.13) | copy-start | bytes 196
  36.8 37.3 %all-to-all-start = ((bf16[16,256,256]{2,1,0:T(8,128)(2,1)}), bf16[16,256,256]{2,1,0:T(8,128)(2,1)}, u32[]{:S(2)}, u32[]{:S(2)}) async-start(bf16[16,256,256]{2,1,0:T(8,128)(2,1)} %broadcast_in_dim.11), calls=%async_computation | async-start | bytes 4194304 | tf_op jit(solution)/shard_map/all_to_all | solution.py:160
  119.3 31.7 %all-to-all-start.2 = ((bf16[16,256,256]{2,1,0:T(8,128)(2,1)}), bf16[16,256,256]{2,1,0:T(8,128)(2,1)}, u32[]{:S(2)}, u32[]{:S(2)}) async-start(bf16[16,256,256]{2,1,0:T(8,128)(2,1)} %get-tuple-element.8), calls=%async_computation.2 | async-start | bytes 4194304 | tf_op jit(solution)/shard_map/all_to_all | solution.py:165
  126.9 20.5 %collective-permute-start.1 = (bf16[256,128]{0,1:T(8,128)(2,1)S(1)}, bf16[256,128]{0,1:T(8,128)(2,1)S(1)}, u32[]{:S(2)}, u32[]{:S(2)}) collective-permute-start(bf16[256,128]{0,1:T(8,128)(2,1)S(1)} %fusion.24), channel_id=1, source_target_pairs={{0,1},{1,0},{2,3},{3,2},{4,5},{5,4},{6,7},{7,6},{8,9},{9,8},{10,11... | collective-permute-start | bytes 196616 | tf_op jit(solution)/shard_map/ppermute | solution.py:29
  165.1 32.5 %all-to-all-start.3 = ((bf16[16,16,4096]{2,1,0:T(8,128)(2,1)}), bf16[16,16,4096]{2,1,0:T(8,128)(2,1)}, u32[]{:S(2)}, u32[]{:S(2)}) async-start(bf16[16,16,4096]{2,1,0:T(8,128)(2,1)} %bitcast.35), calls=%async_computation.3 | async-start | bytes 4194304 | tf_op jit(solution)/shard_map/all_to_all | solution.py:181

commit v2 on v1

v2 whole, which is shorter than its diff:
```python
import jax
import jax.numpy as jnp
from jax import lax
from jax.sharding import PartitionSpec as P
from jax.experimental import pallas as pl
from jax.experimental.pallas import tpu as pltpu

KVH = 8
HD = 128


ROPE_BASE = 500000.0
EPSILON = 1e-05


def passed_along(block, axis, distance):
    devices = range(lax.axis_size(axis))
    route = [(i - distance, i) for i in devices if i - distance in devices]
    return lax.ppermute(block, axis, route)


def swapped(block, axis, distance):
    count = lax.axis_size(axis)
    route = []
    for low in range(count):
        high = low | 1 << distance
        if high != low and high < count:
            route += [(low, high), (high, low)]
    return lax.ppermute(block, axis, route)


def rotate(projected, first_span):
    length = projected.shape[0]
    half_width = projected.shape[-1] // 2
    positions = (first_span * length + jnp.arange(length, dtype=jnp.int32)).astype(jnp.float32)
    inverse = ROPE_BASE ** (
        -(jnp.arange(half_width, dtype=jnp.float32) * 2.0) / projected.shape[-1]
    )
    angles = positions[:, None] * inverse[None, :]
    cosine = jnp.cos(angles)[:, None, :]
    sine_table = jnp.sin(angles)[:, None, :]
    left_part = projected[..., :half_width]
    right_part = projected[..., half_width:]
    return jnp.concatenate(
        [
            left_part * cosine - right_part * sine_table,
            right_part * cosine + left_part * sine_table,
        ],
        axis=-1,
    )


def attend_rows(query_rows, key_rows, value_rows, allowed):
    scores = lax.dot_general(
        query_rows, key_rows, (((1,), (1,)), ((), ())), preferred_element_type=jnp.float32
    ) * query_rows.shape[-1] ** (-0.5)
    scores = jnp.where(allowed, scores, -jnp.inf)
    highest = jnp.max(scores, axis=-1, keepdims=True)
    weights = jnp.exp(scores - highest)
    totals = jnp.sum(weights, axis=-1, keepdims=True)
    partial_out = (
        jnp.dot(weights.astype(jnp.bfloat16), value_rows, preferred_element_type=jnp.float32)
        / totals
    ).astype(jnp.bfloat16)
    return (partial_out, (highest + jnp.log(totals))[:, 0])


def cache_kernel(live_ref, q_ref, k_ref, v_ref, out_ref):
    live = live_ref[0]
    keys = k_ref[...]
    values = v_ref[...]
    rows = q_ref.shape[1]
    width = out_ref.shape[2]
    visible = lax.broadcasted_iota(jnp.int32, (1, keys.shape[0]), 1) < live
    for src in range(q_ref.shape[0]):
        log_rows = []
        for h in range(q_ref.shape[2] // HD):
            q = q_ref[src, :, h * HD:(h + 1) * HD]
            scores = lax.dot_general(
                q, keys, (((1,), (1,)), ((), ())), preferred_element_type=jnp.float32
            ) * HD ** (-0.5)
            scores = jnp.where(visible, scores, -jnp.inf)
            highest = jnp.max(scores, axis=-1, keepdims=True)
            weights = jnp.exp(scores - highest)
            totals = jnp.sum(weights, axis=-1, keepdims=True)
            part = jnp.dot(weights.astype(jnp.bfloat16), values, preferred_element_type=jnp.float32)
            out_ref[src, :rows, h * HD:(h + 1) * HD] = (part / totals).astype(out_ref.dtype)
            log_col = jnp.broadcast_to(highest + jnp.log(totals), (rows, HD))
            rest = jnp.transpose(log_col)[0:1, :]
            for _ in range(3):
                piece = rest.astype(jnp.bfloat16).astype(jnp.float32)
                log_rows.append(piece)
                rest = rest - piece
        if rows < width:
            log_rows = [jnp.concatenate([r, jnp.zeros((1, width - rows), jnp.float32)], axis=1) for r in log_rows]
        log_rows += [jnp.zeros((1, width), jnp.float32)] * (out_ref.shape[1] - rows - len(log_rows))
        out_ref[src, rows:, :] = jnp.concatenate(log_rows, axis=0).astype(out_ref.dtype)


LOG_ROWS = 8


def cache_attention(live, every_query, cached_keys, cached_values):
    sources, span_rows, width = every_query.shape
    kv_heads = cached_keys.shape[1] // HD
    per_head = sources // kv_heads
    rows = cached_keys.shape[0]
    grid_spec = pltpu.PrefetchScalarGridSpec(
        num_scalar_prefetch=1,
        grid=(kv_heads,),
        in_specs=[
            pl.BlockSpec((per_head, span_rows, width), lambda g, live: (g, 0, 0)),
            pl.BlockSpec((rows, HD), lambda g, live: (0, g)),
            pl.BlockSpec((rows, HD), lambda g, live: (0, g)),
        ],
        out_specs=pl.BlockSpec((per_head, span_rows + LOG_ROWS, width), lambda g, live: (g, 0, 0)),
    )
    return pl.pallas_call(
        cache_kernel,
        grid_spec=grid_spec,
        out_shape=jax.ShapeDtypeStruct((sources, span_rows + LOG_ROWS, width), jnp.bfloat16),
    )(live, every_query, cached_keys, cached_values)


def shards(
    fresh,
    previous,
    span_index,
    cache_counts,
    norm_gain,
    w_query,
    w_keyval,
    w_out,
    cache_keys,
    cache_values,
):
    blocks = lax.axis_size("blk")
    position = lax.axis_index("blk")
    span_rows = fresh.shape[0]
    chunks = 2
    rows = span_rows // chunks
    first_span = span_index[0]
    heads_here = w_query.shape[2] // HD
    odd_member = position % 2 == 1
    live = cache_counts[0, position].reshape(1)
    first_segment = lax.axis_index("segment") == 0
    key_parts, value_parts, results = [], [], []
    for c in range(chunks):
        arrived = passed_along(previous[0, c * rows:(c + 1) * rows], "segment", 1)
        current = jnp.where(first_segment, fresh[c * rows:(c + 1) * rows], arrived)
        widened = current.astype(jnp.float32)
        normed = (
            widened
            * lax.rsqrt(jnp.mean(widened * widened, axis=-1, keepdims=True) + EPSILON)
            * norm_gain[0]
        ).astype(jnp.bfloat16)
        chunk_span = first_span * chunks + c
        queries = jnp.dot(normed, w_query[0], preferred_element_type=jnp.float32).reshape(
            rows, heads_here, HD
        )
        queries = rotate(queries, chunk_span).astype(jnp.bfloat16).reshape(rows, heads_here * HD)
        projected = jnp.dot(normed, w_keyval[0], preferred_element_type=jnp.float32)
        as_key = rotate(projected[:, None, :], chunk_span)[:, 0, :].astype(jnp.bfloat16)
        mine = jnp.where(odd_member, projected.astype(jnp.bfloat16), as_key)
        partner = swapped(mine, "blk", 0)
        key_parts.append(jnp.where(odd_member, partner, mine))
        value_parts.append(jnp.where(odd_member, mine, partner))
        every_query = lax.all_to_all(
            jnp.broadcast_to(queries[None], (blocks,) + queries.shape), "blk", 0, 0, tiled=True
        )
        held = cache_attention(live, every_query, cache_keys[0], cache_values[0])
        arrived_parts = lax.all_to_all(held, "blk", split_axis=0, concat_axis=0, tiled=True)
        shard_outs = arrived_parts[:, :rows].astype(jnp.float32).reshape(blocks, rows, heads_here, HD)
        log_parts = arrived_parts[:, rows:rows + 3 * heads_here, :rows].astype(jnp.float32)
        shard_logs = sum(
            log_parts[:, i::3] for i in (2, 1, 0)
        ).transpose(0, 2, 1)
        own_keys = jnp.concatenate(key_parts, axis=0)
        own_values = jnp.concatenate(value_parts, axis=0)
        query_rows = queries.reshape(rows * heads_here, HD)
        row_tokens = c * rows + jnp.arange(rows * heads_here, dtype=jnp.int32) // heads_here
        causal = row_tokens[:, None] >= jnp.arange(own_keys.shape[0], dtype=jnp.int32)[None, :]
        own_out, own_log = attend_rows(query_rows, own_keys, own_values, causal)
        own_out = own_out.reshape(rows, heads_here * HD)
        own_log = own_log.reshape(rows, heads_here)
        all_outs = (
            jnp.concatenate([own_out[None].astype(jnp.float32).reshape(1, rows, heads_here, HD), shard_outs], axis=0)
        )
        all_logs = jnp.concatenate([own_log[None], shard_logs], axis=0)
        ceiling = jnp.max(all_logs, axis=0)
        factors = jnp.exp(all_logs - ceiling)
        attended = (
            jnp.sum(factors[..., None] * all_outs, axis=0) / jnp.sum(factors, axis=0)[..., None]
        ).astype(jnp.bfloat16)
        attended = attended.reshape(rows, heads_here * HD)
        head_terms = jnp.dot(attended, w_out[0], preferred_element_type=jnp.float32).astype(jnp.bfloat16)
        chunk = rows // blocks
        gathered_terms = lax.all_to_all(
            head_terms.reshape(blocks, chunk, -1), "blk", 0, 0, tiled=True
        )
        own_rows = lax.dynamic_slice_in_dim(widened, position * chunk, chunk, 0)
        mixed_rows = (own_rows + jnp.sum(gathered_terms.astype(jnp.float32), axis=0)).astype(jnp.bfloat16)
        results.append(lax.all_to_all(
            jnp.broadcast_to(mixed_rows[None], (blocks,) + mixed_rows.shape), "blk", 0, 0, tiled=True
        ).reshape(rows, -1))
    return jnp.concatenate(results, axis=0)[None]


def solution(mesh):
    placed = (
        P(),
        P("segment", None, None),
        P("segment"),
        P("segment", None),
        P("segment", None),
        P("segment", None, "blk"),
        P("segment", None, "blk"),
        P("segment", "blk", None),
        P("segment", "blk", None),
        P("segment", "blk", None),
    )
    return jax.shard_map(
        shards, mesh=mesh, in_specs=placed, out_specs=P("segment", None, None), check_vma=False
    )
```

time: 233 us -> 255 us (1.094)
  starting transfers between devices: 21.2 us -> 44.4 us
  blocking collectives: 41.6 us -> 19.3 us
  waiting for transfers between devices: 95.3 us -> 84.2 us
  Pallas kernels: 31.7 us -> 40.3 us
  other arithmetic: 16.3 us -> 24.2 us
  local copies, waits for them, and re-layouts: 18.8 us -> 26.2 us
  matrix products: 6.45 us -> 13.6 us
    all_to_all x1 -> x3, waiting for transfers between devices: 0.01 us -> 24 us  [the longest x1 14.1 us: shards(): lax.all_to_all(jnp.broadcast_to(mixed_rows[None], (blocks,) + mixed_rows....]
    all_to_all x1 -> x2, waiting for transfers between devices: 28.4 us -> 13.5 us  [shards(): lax.all_to_all(jnp.broadcast_to(queries[None], (blocks,) + queries.shape)...]
    all_to_all x1 -> x0, blocking collectives: 11.3 us -> none  [shards(): lax.all_to_all(held_logs, 'blk', split_axis=0, concat_axis=0, tiled=True)]
    all_to_all x1 -> x3, starting transfers between devices: 4.44 us -> 15.4 us  [the longest x2 11.1 us: shards(): lax.all_to_all(held, 'blk', split_axis=0, concat_axis=0, tiled=True)]
    ppermute x1 -> x2, waiting for transfers between devices: 18.3 us -> 7.32 us  [swapped(): return lax.ppermute(block, axis, route)]
    all_to_all x1, blocking collectives: 30.2 us -> 19.3 us  [shards(): lax.all_to_all(jnp.broadcast_to(mixed_rows[None], (blocks,) + mixed_rows....]
    pallas_call x1 -> x2, Pallas kernels: 31.7 us -> 40.3 us  [cache_attention(): pl.pallas_call(cache_kernel, grid_spec=grid_spec, out_shape=jax.ShapeDtyp...]
    all_to_all x1 -> x2, waiting for transfers between devices: 27.9 us -> 22.8 us  [shards(): lax.all_to_all(head_terms.reshape(blocks, chunk, -1), 'blk', 0, 0, tiled=...]
  transfers between devices with their start and end apart: 5 -> 11, of which waited for: 4 -> 8; matrix products, arithmetic and copies ran while one was open for 5% -> 13% of each run, Pallas kernels for 0% -> 16%
where the time goes in v2:
time: 255 us; the launch traced here: 254 us
  waiting for transfers between devices  84.2 us (33%)
  starting transfers between devices  44.4 us (17%)
  Pallas kernels  40.3 us (16%)
  local copies, waits for them, and re-layouts  26.2 us (10%)
  other arithmetic  24.2 us (9%)
  blocking collectives  19.3 us (8%)
  matrix products  13.6 us (5%)
    pallas_call x2, Pallas kernels, cache_attention(): pl.pallas_call(cache_kernel, grid_spec=grid_spec, out_shape=jax.ShapeDtyp...  40.3 us
    all_to_all x2, waiting for transfers between devices, shards(): lax.all_to_all(head_terms.reshape(blocks, chunk, -1), 'blk', 0, 0, tiled=...  22.8 us
    all_to_all x1, blocking collectives, shards(): lax.all_to_all(jnp.broadcast_to(mixed_rows[None], (blocks,) + mixed_rows....  19.3 us
    ppermute x2, waiting for transfers between devices, passed_along(): return lax.ppermute(block, axis, route)  16.5 us
    all_to_all x1, waiting for transfers between devices, shards(): lax.all_to_all(jnp.broadcast_to(mixed_rows[None], (blocks,) + mixed_rows....  14.1 us
    all_to_all x2, waiting for transfers between devices, shards(): lax.all_to_all(jnp.broadcast_to(queries[None], (blocks,) + queries.shape)...  13.5 us
    all_to_all x2, starting transfers between devices, shards(): lax.all_to_all(jnp.broadcast_to(queries[None], (blocks,) + queries.shape)...  11.7 us
    all_to_all x2, starting transfers between devices, shards(): lax.all_to_all(held, 'blk', split_axis=0, concat_axis=0, tiled=True)  11.1 us
  transfers between devices with their start and end apart: 11, of which 8 were waited for; matrix products, arithmetic and copies ran while one was open for 13% of the time, Pallas kernels for 16%

profile of v2, /device:TPU:2, one launch (start us, length us, event | category | flops | bytes accessed | tf_op | source)
XLA Modules:
  0.0 253.5 jit_solution(13515305334868014083)
XLA Ops:
  0.0 2.8 %slice_bitcast_fusion.1 = (bf16[128,4096]{1,0:T(8,128)(2,1)}, bf16[128,4096]{1,0:T(8,128)(2,1)S(1)}) fusion(bf16[1,256,4096]{2,1,0:T(8,128)(2,1)} %param.11), kind=kLoop, calls=%fused_computation.33 | loop fusion | bytes 4194304 | tf_op jit(solution)/shard_map/squeeze | solution.py:149
  2.8 1.9 collective-permute-start
  4.8 3.5 %collective-permute-start.2 = (bf16[128,4096]{1,0:T(8,128)(2,1)S(1)}, bf16[128,4096]{1,0:T(8,128)(2,1)}, u32[]{:S(2)}, u32[]{:S(2)}) collective-permute-start(bf16[128,4096]{1,0:T(8,128)(2,1)S(1)} %get-tuple-element.20), channel_id=1, source_target_pairs={{0,16},{16,32},{32,48},{48,64},{64,80},{80,96},{96,112},{1,17},{17... | collective-permute-start | bytes 3145736 | tf_op jit(solution)/shard_map/ppermute | solution.py:19
  9.0 4.1 %copy.47 = bf16[256,4096]{1,0:T(8,128)(2,1)} copy(bf16[256,4096]{0,1:T(8,128)(2,1)} %bitcast.79) | data formatting | bytes 4194304 | tf_op jit(solution)/shard_map/dot_general | solution.py:158
  14.0 5.3 %collective-permute-done = bf16[128,4096]{1,0:T(8,128)(2,1)} collective-permute-done((bf16[128,4096]{1,0:T(8,128)(2,1)}, bf16[128,4096]{1,0:T(8,128)(2,1)}, u32[]{:S(2)}, u32[]{:S(2)}) %collective-permute-start) | collective-permute-done | bytes 1048608 | tf_op jit(solution)/shard_map/ppermute | solution.py:19
  19.3 11.2 %collective-permute-done.2 = bf16[128,4096]{1,0:T(8,128)(2,1)} collective-permute-done((bf16[128,4096]{1,0:T(8,128)(2,1)S(1)}, bf16[128,4096]{1,0:T(8,128)(2,1)}, u32[]{:S(2)}, u32[]{:S(2)}) %collective-permute-start.2) | collective-permute-done | bytes 1048608 | tf_op jit(solution)/shard_map/ppermute | solution.py:19
  30.5 4.5 %fusion.63 = (f32[128,4096]{1,0:T(8,128)}, bf16[128,4096]{1,0:T(8,128)(2,1)S(1)}, f32[128,4096]{1,0:T(8,128)}, bf16[128,4096]{1,0:T(8,128)(2,1)S(1)}) fusion(bf16[128,4096]{1,0:T(8,128)(2,1)} %collective-permute-done, bf16[256,4096]{1,0:T(8,128)(2,1)} %param.10, pred[]{:T(512)S(6)} %eq.8, bf16[128,4096]{1,0:T(8,128)(2,1)} %collective-permute-done.2), kind=kLoop, calls=%fused_computation.127 | loop fusion | flops 2097152 | bytes 10485761 | tf_op jit(solution)/shard_map/convert_element_type | solution.py:151
  35.6 1.8 copy-done.6
  38.4 1.1 broadcast_in_dim.23
  39.5 8.0 %all-to-all-start = ((bf16[16,128,256]{2,1,0:T(8,128)(2,1)}), bf16[16,128,256]{2,1,0:T(8,128)(2,1)S(1)}, u32[]{:S(2)}, u32[]{:S(2)}) async-start(bf16[16,128,256]{2,1,0:T(8,128)(2,1)} %broadcast_in_dim.23), calls=%async_computation | async-start | bytes 2097152 | tf_op jit(solution)/shard_map/all_to_all | solution.py:168
  47.5 2.7 %fusion.8 = f32[128,2,128]{0,2,1:T(8,128)S(1)} fusion(bf16[2,128,4096]{2,1,0:T(8,128)(2,1)} %bitcast.80, f32[128]{0:T(128)S(1)} %add_rsqrt_fusion, bf16[128,4096]{1,0:T(8,128)(2,1)} %copy-done.3, f32[4096]{0:T(1024)S(1)} %bitcast.95), kind=kOutput, calls=%fused_computation.23 | convolution fusion | flops 270532608 | bytes 3293696 | tf_op jit(solution)/shard_map/dot_general | solution.py:158
  50.4 13.5 %all-to-all-done.q_ref = bf16[16,128,256]{2,1,0:T(8,128)(2,1)S(1)} async-done(((bf16[16,128,256]{2,1,0:T(8,128)(2,1)}), bf16[16,128,256]{2,1,0:T(8,128)(2,1)S(1)}, u32[]{:S(2)}, u32[]{:S(2)}) %all-to-all-start) | async-done | bytes 1048608 | tf_op jit(solution)/shard_map/all_to_all | solution.py:168
  63.9 1.2 broadcast_in_dim.27
  65.3 3.7 %all-to-all-start.4 = ((bf16[16,128,256]{2,1,0:T(8,128)(2,1)}), bf16[16,128,256]{2,1,0:T(8,128)(2,1)S(1)}, u32[]{:S(2)}, u32[]{:S(2)}) async-start(bf16[16,128,256]{2,1,0:T(8,128)(2,1)} %broadcast_in_dim.27), calls=%async_computation.4 | async-start | bytes 2097152 | tf_op jit(solution)/shard_map/all_to_all | solution.py:168
  69.0 2.3 fusion.12
  72.3 1.9 collective-permute-start.1
  74.2 20.2 %shard_map.100 = bf16[16,136,256]{2,1,0:T(8,128)(2,1)} custom-call(s32[1]{0:T(128)} %bitcast.11.live_ref, bf16[16,128,256]{2,1,0:T(8,128)(2,1)} %copy-done.2, bf16[2048,1024]{1,0:T(8,128)(2,1)} %bitcast.74, bf16[2048,1024]{1,0:T(8,128)(2,1)} %bitcast.76), custom_call_target="tpu_custom_call" | custom-call | tf_op jit(solution)/shard_map/pallas_call | solution.py:118
  94.3 1.0 copy-done.1
  95.3 6.5 %all-to-all-start.1 = ((bf16[16,136,256]{2,1,0:T(8,128)(2,1)}), bf16[16,136,256]{2,1,0:T(8,128)(2,1)S(1)}, u32[]{:S(2)}, u32[]{:S(2)}) async-start(bf16[16,136,256]{2,1,0:T(8,128)(2,1)} %shard_map.100), calls=%async_computation.1 | async-start | bytes 2228224 | tf_op jit(solution)/shard_map/all_to_all | solution.py:172
  103.6 2.0 collective-permute-start.3
  105.6 1.4 broadcast_select_fusion.2
  107.3 7.3 %collective-permute-done.3 = bf16[128,128]{0,1:T(8,128)(2,1)S(1)} collective-permute-done((bf16[128,128]{0,1:T(8,128)(2,1)S(1)}, bf16[128,128]{0,1:T(8,128)(2,1)S(1)}, u32[]{:S(2)}, u32[]{:S(2)}) %collective-permute-start.3) | collective-permute-done | bytes 32800 | tf_op jit(solution)/shard_map/ppermute | solution.py:29
  115.3 1.8 fusion.71
  117.1 20.2 %shard_map.101 = bf16[16,136,256]{2,1,0:T(8,128)(2,1)} custom-call(s32[1]{0:T(128)} %bitcast.11.live_ref, bf16[16,128,256]{2,1,0:T(8,128)(2,1)} %copy-done.1, bf16[2048,1024]{1,0:T(8,128)(2,1)} %bitcast.75, bf16[2048,1024]{1,0:T(8,128)(2,1)} %bitcast.77), custom_call_target="tpu_custom_call" | custom-call | tf_op jit(solution)/shard_map/pallas_call | solution.py:118
  137.3 4.6 %all-to-all-start.5 = ((bf16[16,136,256]{2,1,0:T(8,128)(2,1)}), bf16[16,136,256]{2,1,0:T(8,128)(2,1)}, u32[]{:S(2)}, u32[]{:S(2)}) async-start(bf16[16,136,256]{2,1,0:T(8,128)(2,1)} %shard_map.101), calls=%async_computation.5 | async-start | bytes 2228224 | tf_op jit(solution)/shard_map/all_to_all | solution.py:172
  142.2 1.0 fusion.17
  146.4 1.0 fusion.6
  147.4 1.2 fusion.7
  148.7 9.9 %all-to-all-done.5 = bf16[16,136,256]{2,1,0:T(8,128)(2,1)} async-done(((bf16[16,136,256]{2,1,0:T(8,128)(2,1)}), bf16[16,136,256]{2,1,0:T(8,128)(2,1)}, u32[]{:S(2)}, u32[]{:S(2)}) %all-to-all-start.5) | async-done | bytes 1114144 | tf_op jit(solution)/shard_map/all_to_all | solution.py:172
  159.4 1.1 slice.93
  160.5 2.2 reshape.467
  162.9 1.3 slice.99
  164.2 1.1 reshape.470
  165.9 4.0 %multiply_reduce_fusion = f32[128,2,128]{2,1,0:T(2,128)S(1)} fusion(bf16[16,128,2,128]{3,2,1,0:T(2,128)(2,1)} %reshape.470, bf16[1,128,2,128]{3,2,1,0:T(2,128)(2,1)S(1)} %bitcast.91, f32[17,128,2]{2,1,0:T(8,128)S(1)} %copy.45), kind=kLoop, calls=%fused_computation.4 | loop fusion | flops 2195456 | bytes 1262592 | tf_op jit(solution)/shard_map/reduce_sum | solution.py:193
  170.1 1.4 fusion.1
  171.5 4.3 %all-to-all-start.6 = ((bf16[16,8,4096]{2,1,0:T(8,128)(2,1)}), bf16[16,8,4096]{2,1,0:T(8,128)(2,1)}, u32[]{:S(2)}, u32[]{:S(2)}) async-start(bf16[16,8,4096]{2,1,0:T(8,128)(2,1)} %fusion.1), calls=%async_computation.6 | async-start | bytes 2097152 | tf_op jit(solution)/shard_map/all_to_all | solution.py:198
  176.2 4.0 %multiply_reduce_fusion.1 = f32[128,2,128]{2,1,0:T(2,128)S(1)} fusion(bf16[16,128,2,128]{3,2,1,0:T(2,128)(2,1)} %reshape.467, bf16[1,128,2,128]{3,2,1,0:T(2,128)(2,1)S(1)} %bitcast.90, f32[17,128,2]{2,1,0:T(8,128)S(1)} %copy.37), kind=kLoop, calls=%fused_computation.5 | loop fusion | flops 2195456 | bytes 1262592 | tf_op jit(solution)/shard_map/reduce_sum | solution.py:193
  180.4 1.5 fusion
  181.9 9.3 %all-to-all-done.6 = bf16[16,8,4096]{2,1,0:T(8,128)(2,1)} async-done(((bf16[16,8,4096]{2,1,0:T(8,128)(2,1)}), bf16[16,8,4096]{2,1,0:T(8,128)(2,1)}, u32[]{:S(2)}, u32[]{:S(2)}) %all-to-all-start.6) | async-done | bytes 1048608 | tf_op jit(solution)/shard_map/all_to_all | solution.py:198
  191.1 3.7 %all-to-all-start.2 = ((bf16[16,8,4096]{2,1,0:T(8,128)(2,1)}), bf16[16,8,4096]{2,1,0:T(8,128)(2,1)S(1)}, u32[]{:S(2)}, u32[]{:S(2)}) async-start(bf16[16,8,4096]{2,1,0:T(8,128)(2,1)} %fusion), calls=%async_computation.2 | async-start | bytes 2097152 | tf_op jit(solution)/shard_map/all_to_all | solution.py:198
  194.8 1.4 convert_reduce_fusion
  197.1 13.6 %all-to-all-done.2 = bf16[16,8,4096]{2,1,0:T(8,128)(2,1)S(1)} async-done(((bf16[16,8,4096]{2,1,0:T(8,128)(2,1)}), bf16[16,8,4096]{2,1,0:T(8,128)(2,1)S(1)}, u32[]{:S(2)}, u32[]{:S(2)}) %all-to-all-start.2) | async-done | bytes 1048608 | tf_op jit(solution)/shard_map/all_to_all | solution.py:198
  210.7 1.1 broadcast_in_dim.28
  211.8 4.3 %all-to-all-start.7 = ((bf16[16,8,4096]{2,1,0:T(8,128)(2,1)}), bf16[16,8,4096]{2,1,0:T(8,128)(2,1)}, u32[]{:S(2)}, u32[]{:S(2)}) async-start(bf16[16,8,4096]{2,1,0:T(8,128)(2,1)} %broadcast_in_dim.28), calls=%async_computation.7 | async-start | bytes 2097152 | tf_op jit(solution)/shard_map/all_to_all | solution.py:203
  216.3 0.9 add_convert_fusion.1
  217.2 14.1 %all-to-all-done.7 = bf16[16,8,4096]{2,1,0:T(8,128)(2,1)} async-done(((bf16[16,8,4096]{2,1,0:T(8,128)(2,1)}), bf16[16,8,4096]{2,1,0:T(8,128)(2,1)}, u32[]{:S(2)}, u32[]{:S(2)}) %all-to-all-start.7) | async-done | bytes 1048608 | tf_op jit(solution)/shard_map/all_to_all | solution.py:203
  231.4 19.3 %all_to_all.40 = bf16[16,8,4096]{2,1,0:T(8,128)(2,1)S(1)} all-to-all(bf16[16,8,4096]{2,1,0:T(8,128)(2,1)S(1)} %broadcast_in_dim.24), channel_id=1, replica_groups=mesh['segment'=8,'blk'=16] {'blk'}, dimensions={0} | all-to-all | bytes 2097152 | tf_op jit(solution)/shard_map/all_to_all | solution.py:203
  250.8 2.8 %maximum_bitcast_fusion = bf16[1,256,4096]{2,1,0:T(8,128)(2,1)} fusion(bf16[128,4096]{1,0:T(8,128)(2,1)} %bitcast.31, bf16[128,4096]{1,0:T(8,128)(2,1)S(1)} %bitcast.78), kind=kLoop, calls=%fused_computation.6 | loop fusion | flops 4194304 | bytes 4194304 | tf_op jit(solution)/shard_map/broadcast_in_dim | solution.py:206
  (87 shorter events, 13.5 us)
Async XLA Ops:
  0.0 170.1 %copy-start = (bf16[1,256,4096]{2,1,0:T(8,128)(2,1)S(1)}, bf16[1,256,4096]{2,1,0:T(8,128)(2,1)}, u32[]{:S(2)}) copy-start(bf16[1,256,4096]{2,1,0:T(8,128)(2,1)} %param.17) | copy-start | bytes 6291460
  2.8 16.4 %collective-permute-start = (bf16[128,4096]{1,0:T(8,128)(2,1)}, bf16[128,4096]{1,0:T(8,128)(2,1)}, u32[]{:S(2)}, u32[]{:S(2)}) collective-permute-start(bf16[128,4096]{1,0:T(8,128)(2,1)} %get-tuple-element.19), channel_id=1, source_target_pairs={{0,16},{16,32},{32,48},{48,64},{64,80},{80,96},{96,112},{1,17},{17... | collective-permute-start | bytes 3145736 | tf_op jit(solution)/shard_map/ppermute | solution.py:19
  4.8 25.7 %collective-permute-start.2 = (bf16[128,4096]{1,0:T(8,128)(2,1)S(1)}, bf16[128,4096]{1,0:T(8,128)(2,1)}, u32[]{:S(2)}, u32[]{:S(2)}) collective-permute-start(bf16[128,4096]{1,0:T(8,128)(2,1)S(1)} %get-tuple-element.20), channel_id=1, source_target_pairs={{0,16},{16,32},{32,48},{48,64},{64,80},{80,96},{96,112},{1,17},{17... | collective-permute-start | bytes 3145736 | tf_op jit(solution)/shard_map/ppermute | solution.py:19
  8.9 4.1 %copy-start.12 = (s32[1,16]{1,0:T(1,128)S(1)}, s32[1,16]{1,0:T(1,128)}, u32[]{:S(2)}) copy-start(s32[1,16]{1,0:T(1,128)} %param.13) | copy-start | bytes 196
  30.5 5.0 %copy-start.11 = (f32[1,4096]{1,0:T(1,128)S(1)}, f32[1,4096]{1,0:T(1,128)}, u32[]{:S(2)}) copy-start(f32[1,4096]{1,0:T(1,128)} %param.14) | copy-start | bytes 49156
  35.0 3.2 %copy-start.3 = (bf16[128,4096]{1,0:T(8,128)(2,1)}, bf16[128,4096]{1,0:T(8,128)(2,1)S(1)}, u32[]{:S(2)}) copy-start(bf16[128,4096]{1,0:T(8,128)(2,1)S(1)} %get-tuple-element.18) | copy-start | bytes 3145732
  35.0 3.2 %copy-start.5 = (bf16[128,4096]{1,0:T(8,128)(2,1)}, bf16[128,4096]{1,0:T(8,128)(2,1)S(1)}, u32[]{:S(2)}) copy-start(bf16[128,4096]{1,0:T(8,128)(2,1)S(1)} %get-tuple-element.6) | copy-start | bytes 3145732
  35.0 2.3 copy-start.6
  39.5 24.4 %all-to-all-start = ((bf16[16,128,256]{2,1,0:T(8,128)(2,1)}), bf16[16,128,256]{2,1,0:T(8,128)(2,1)S(1)}, u32[]{:S(2)}, u32[]{:S(2)}) async-start(bf16[16,128,256]{2,1,0:T(8,128)(2,1)} %broadcast_in_dim.23), calls=%async_computation | async-start | bytes 2097152 | tf_op jit(solution)/shard_map/all_to_all | solution.py:168
  63.9 1.3 copy-start.2
  65.3 29.0 %all-to-all-start.4 = ((bf16[16,128,256]{2,1,0:T(8,128)(2,1)}), bf16[16,128,256]{2,1,0:T(8,128)(2,1)S(1)}, u32[]{:S(2)}, u32[]{:S(2)}) async-start(bf16[16,128,256]{2,1,0:T(8,128)(2,1)} %broadcast_in_dim.27), calls=%async_computation.4 | async-start | bytes 2097152 | tf_op jit(solution)/shard_map/all_to_all | solution.py:168
  68.9 2.3 copy-start.4
  68.9 2.3 copy-start.10
  72.3 33.4 %collective-permute-start.1 = (bf16[128,128]{0,1:T(8,128)(2,1)S(1)}, bf16[128,128]{0,1:T(8,128)(2,1)}, u32[]{:S(2)}, u32[]{:S(2)}) collective-permute-start(bf16[128,128]{0,1:T(8,128)(2,1)S(1)} %fusion.56), channel_id=1, source_target_pairs={{0,1},{1,0},{2,3},{3,2},{4,5},{5,4},{6,7},{7,6},{8,9},{9,8},{10,11... | collective-permute-start | bytes 98312 | tf_op jit(solution)/shard_map/ppermute | solution.py:29
  94.3 1.0 copy-start.1
  95.3 42.0 %all-to-all-start.1 = ((bf16[16,136,256]{2,1,0:T(8,128)(2,1)}), bf16[16,136,256]{2,1,0:T(8,128)(2,1)S(1)}, u32[]{:S(2)}, u32[]{:S(2)}) async-start(bf16[16,136,256]{2,1,0:T(8,128)(2,1)} %shard_map.100), calls=%async_computation.1 | async-start | bytes 2228224 | tf_op jit(solution)/shard_map/all_to_all | solution.py:172
  103.6 11.0 %collective-permute-start.3 = (bf16[128,128]{0,1:T(8,128)(2,1)S(1)}, bf16[128,128]{0,1:T(8,128)(2,1)S(1)}, u32[]{:S(2)}, u32[]{:S(2)}) collective-permute-start(bf16[128,128]{0,1:T(8,128)(2,1)S(1)} %fusion.57), channel_id=1, source_target_pairs={{0,1},{1,0},{2,3},{3,2},{4,5},{5,4},{6,7},{7,6},{8,9},{9,8},{10,11... | collective-permute-start | bytes 98312 | tf_op jit(solution)/shard_map/ppermute | solution.py:29
  117.1 26.1 %copy-start.7 = (f32[256]{0:T(256)}, f32[256]{0:T(256)S(1)}, u32[]{:S(2)}) copy-start(f32[256]{0:T(256)S(1)} %get-tuple-element.41) | copy-start | bytes 3076
  137.3 21.3 %all-to-all-start.5 = ((bf16[16,136,256]{2,1,0:T(8,128)(2,1)}), bf16[16,136,256]{2,1,0:T(8,128)(2,1)}, u32[]{:S(2)}, u32[]{:S(2)}) async-start(bf16[16,136,256]{2,1,0:T(8,128)(2,1)} %shard_map.101), calls=%async_computation.5 | async-start | bytes 2228224 | tf_op jit(solution)/shard_map/all_to_all | solution.py:172
  143.2 0.6 copy-start.9
  159.4 3.3 %copy-start.8 = (f32[128,2]{0,1:T(2,128)S(1)}, f32[128,2]{0,1:T(2,128)}, u32[]{:S(2)}) copy-start(f32[128,2]{0,1:T(2,128)} %copy.36) | copy-start | bytes 3076
  171.5 19.7 %all-to-all-start.6 = ((bf16[16,8,4096]{2,1,0:T(8,128)(2,1)}), bf16[16,8,4096]{2,1,0:T(8,128)(2,1)}, u32[]{:S(2)}, u32[]{:S(2)}) async-start(bf16[16,8,4096]{2,1,0:T(8,128)(2,1)} %fusion.1), calls=%async_computation.6 | async-start | bytes 2097152 | tf_op jit(solution)/shard_map/all_to_all | solution.py:198
  191.1 19.6 %all-to-all-start.2 = ((bf16[16,8,4096]{2,1,0:T(8,128)(2,1)}), bf16[16,8,4096]{2,1,0:T(8,128)(2,1)S(1)}, u32[]{:S(2)}, u32[]{:S(2)}) async-start(bf16[16,8,4096]{2,1,0:T(8,128)(2,1)} %fusion), calls=%async_computation.2 | async-start | bytes 2097152 | tf_op jit(solution)/shard_map/all_to_all | solution.py:198
  211.8 19.5 %all-to-all-start.7 = ((bf16[16,8,4096]{2,1,0:T(8,128)(2,1)}), bf16[16,8,4096]{2,1,0:T(8,128)(2,1)}, u32[]{:S(2)}, u32[]{:S(2)}) async-start(bf16[16,8,4096]{2,1,0:T(8,128)(2,1)} %broadcast_in_dim.28), calls=%async_computation.7 | async-start | bytes 2097152 | tf_op jit(solution)/shard_map/all_to_all | solution.py:203

commit v3 on v1

--- a/solution.py
+++ b/solution.py
@@ -65,12 +65,15 @@
     return (partial_out, (highest + jnp.log(totals))[:, 0])
 
 
-def cache_kernel(live_ref, q_ref, k_ref, v_ref, out_ref, log_ref):
+def cache_kernel(live_ref, q_ref, k_ref, v_ref, out_ref):
     live = live_ref[0]
     keys = k_ref[...]
     values = v_ref[...]
+    rows = q_ref.shape[1]
+    width = out_ref.shape[2]
     visible = lax.broadcasted_iota(jnp.int32, (1, keys.shape[0]), 1) < live
     for src in range(q_ref.shape[0]):
+        log_rows = []
         for h in range(q_ref.shape[2] // HD):
             q = q_ref[src, :, h * HD:(h + 1) * HD]
             scores = lax.dot_general(
@@ -81,13 +84,24 @@
             weights = jnp.exp(scores - highest)
             totals = jnp.sum(weights, axis=-1, keepdims=True)
             part = jnp.dot(weights.astype(jnp.bfloat16), values, preferred_element_type=jnp.float32)
-            out_ref[src, :, h * HD:(h + 1) * HD] = (part / totals).astype(out_ref.dtype)
-            log_ref[src, :, h:h + 1] = highest + jnp.log(totals)
+            out_ref[src, :rows, h * HD:(h + 1) * HD] = (part / totals).astype(out_ref.dtype)
+            log_col = jnp.broadcast_to(highest + jnp.log(totals), (rows, HD))
+            rest = jnp.transpose(log_col)[0:1, :]
+            for _ in range(3):
+                piece = rest.astype(jnp.bfloat16).astype(jnp.float32)
+                log_rows.append(piece)
+                rest = rest - piece
+        if rows < width:
+            log_rows = [jnp.concatenate([r, jnp.zeros((1, width - rows), jnp.float32)], axis=1) for r in log_rows]
+        log_rows += [jnp.zeros((1, width), jnp.float32)] * (out_ref.shape[1] - rows - len(log_rows))
+        out_ref[src, rows:, :] = jnp.concatenate(log_rows, axis=0).astype(out_ref.dtype)
+
+
+LOG_ROWS = 8
 
 
 def cache_attention(live, every_query, cached_keys, cached_values):
     sources, span_rows, width = every_query.shape
-    heads_here = width // HD
     kv_heads = cached_keys.shape[1] // HD
     per_head = sources // kv_heads
     rows = cached_keys.shape[0]
@@ -99,18 +113,12 @@
             pl.BlockSpec((rows, HD), lambda g, live: (0, g)),
             pl.BlockSpec((rows, HD), lambda g, live: (0, g)),
         ],
-        out_specs=[
-            pl.BlockSpec((per_head, span_rows, width), lambda g, live: (g, 0, 0)),
-            pl.BlockSpec((per_head, span_rows, heads_here), lambda g, live: (g, 0, 0)),
-        ],
+        out_specs=pl.BlockSpec((per_head, span_rows + LOG_ROWS, width), lambda g, live: (g, 0, 0)),
     )
     return pl.pallas_call(
         cache_kernel,
         grid_spec=grid_spec,
-        out_shape=[
-            jax.ShapeDtypeStruct((sources, span_rows, width), jnp.bfloat16),
-            jax.ShapeDtypeStruct((sources, span_rows, heads_here), jnp.float32),
-        ],
+        out_shape=jax.ShapeDtypeStruct((sources, span_rows + LOG_ROWS, width), jnp.bfloat16),
     )(live, every_query, cached_keys, cached_values)
 
 
@@ -129,6 +137,10 @@
     blocks = lax.axis_size("blk")
     position = lax.axis_index("blk")
     span_rows = fresh.shape[0]
+    first_span = span_index[0]
+    heads_here = w_query.shape[2] // HD
+    odd_member = position % 2 == 1
+    live = cache_counts[0, position].reshape(1)
     arrived = passed_along(previous[0], "segment", 1)
     current = jnp.where(lax.axis_index("segment") == 0, fresh, arrived)
     widened = current.astype(jnp.float32)
@@ -137,45 +149,37 @@
         * lax.rsqrt(jnp.mean(widened * widened, axis=-1, keepdims=True) + EPSILON)
         * norm_gain[0]
     ).astype(jnp.bfloat16)
-    first_span = span_index[0]
-    heads_here = w_query.shape[2] // HD
-    ratio = blocks // KVH
     queries = jnp.dot(normed, w_query[0], preferred_element_type=jnp.float32).reshape(
         span_rows, heads_here, HD
     )
     queries = rotate(queries, first_span).astype(jnp.bfloat16).reshape(span_rows, heads_here * HD)
     projected = jnp.dot(normed, w_keyval[0], preferred_element_type=jnp.float32)
-    odd_member = position % 2 == 1
     as_key = rotate(projected[:, None, :], first_span)[:, 0, :].astype(jnp.bfloat16)
     mine = jnp.where(odd_member, projected.astype(jnp.bfloat16), as_key)
     partner = swapped(mine, "blk", 0)
     own_keys = jnp.where(odd_member, partner, mine)
     own_values = jnp.where(odd_member, mine, partner)
+    every_query = lax.all_to_all(
+        jnp.broadcast_to(queries[None], (blocks,) + queries.shape), "blk", 0, 0, tiled=True
+    )
+    held = cache_attention(live, every_query, cache_keys[0], cache_values[0])
+    arrived_parts = lax.all_to_all(held, "blk", split_axis=0, concat_axis=0, tiled=True)
+    log_parts = arrived_parts[:, span_rows:span_rows + 3 * heads_here].astype(jnp.float32)
+    shard_logs = sum(log_parts[:, i::3] for i in (2, 1, 0))
     query_rows = queries.reshape(span_rows * heads_here, HD)
     row_tokens = jnp.arange(span_rows * heads_here, dtype=jnp.int32) // heads_here
     causal = row_tokens[:, None] >= jnp.arange(span_rows, dtype=jnp.int32)[None, :]
     own_out, own_log = attend_rows(query_rows, own_keys, own_values, causal)
     own_out = own_out.reshape(span_rows, heads_here * HD)
-    own_log = own_log.reshape(span_rows, heads_here)
-    every_query = lax.all_to_all(
-        jnp.broadcast_to(queries[None], (blocks,) + queries.shape), "blk", 0, 0, tiled=True
-    ).reshape(blocks, span_rows, heads_here * HD)
-    live = cache_counts[0, position].reshape(1)
-    held_outs, held_logs = cache_attention(live, every_query, cache_keys[0], cache_values[0])
-    shard_outs = lax.all_to_all(held_outs, "blk", split_axis=0, concat_axis=0, tiled=True)
-    shard_logs = lax.all_to_all(held_logs, "blk", split_axis=0, concat_axis=0, tiled=True)
-    all_outs = (
-        jnp.concatenate([own_out[None], shard_outs], axis=0)
-        .astype(jnp.float32)
-        .reshape(blocks + 1, span_rows, heads_here, HD)
-    )
-    all_logs = jnp.concatenate([own_log[None], shard_logs], axis=0)
-    ceiling = jnp.max(all_logs, axis=0)
-    factors = jnp.exp(all_logs - ceiling)
-    attended = (
-        jnp.sum(factors[..., None] * all_outs, axis=0) / jnp.sum(factors, axis=0)[..., None]
-    ).astype(jnp.bfloat16)
-    attended = attended.reshape(span_rows, heads_here * HD)
+    own_log = own_log.reshape(span_rows, heads_here).T
+    ceiling = jnp.maximum(own_log, jnp.max(shard_logs, axis=0))
+    own_factor = jnp.exp(own_log - ceiling)
+    factors = jnp.exp(shard_logs - ceiling)
+    spread = lambda f: jnp.repeat(jnp.swapaxes(f, -1, -2), HD, axis=-1)
+    weighted = spread(own_factor) * own_out.astype(jnp.float32) + jnp.sum(
+        spread(factors) * arrived_parts[:, :span_rows].astype(jnp.float32), axis=0
+    )
+    attended = (weighted / spread(own_factor + jnp.sum(factors, axis=0))).astype(jnp.bfloat16)
     head_terms = jnp.dot(attended, w_out[0], preferred_element_type=jnp.float32).astype(jnp.bfloat16)
     chunk = span_rows // blocks
     gathered_terms = lax.all_to_all(

time: 233 us -> 228 us (0.979)
  blocking collectives: 41.6 us -> 28.9 us
  local copies, waits for them, and re-layouts: 18.8 us -> 27.6 us
  other arithmetic: 16.3 us -> 13.2 us
    all_to_all x1 -> x0, blocking collectives: 11.3 us -> none  [shards(): lax.all_to_all(held_logs, 'blk', split_axis=0, concat_axis=0, tiled=True)]
    broadcast_in_dim x0 -> x1, local copies, waits for them, and re-layouts: none -> 8.32 us  [shards(): spread = lambda f: jnp.repeat(jnp.swapaxes(f, -1, -2), HD, axis=-1)]
    reshape x0 -> x1, local copies, waits for them, and re-layouts: none -> 6.43 us  [shards(): spread = lambda f: jnp.repeat(jnp.swapaxes(f, -1, -2), HD, axis=-1)]
    all_to_all x1, waiting for transfers between devices: 0.01 us -> 5.03 us  [shards(): lax.all_to_all(held, 'blk', split_axis=0, concat_axis=0, tiled=True)]
    reduce_sum x2, other arithmetic: 7.78 us -> 3.43 us  [the longest x1 3.38 us: shards(): jnp.sum(spread(factors) * arrived_parts[:, :span_rows].astype(jnp.float32...]
    concatenate x1 -> x0, local copies, waits for them, and re-layouts: 3.96 us -> none  [shards(): jnp.concatenate([own_out[None], shard_outs], axis=0).astype(jnp.float32)]
  transfers between devices with their start and end apart: 5 -> 5, of which waited for: 4 -> 5; matrix products, arithmetic and copies ran while one was open for 5% -> 4% of each run, Pallas kernels for 0% -> 0%
where the time goes in v3:
time: 228 us; the launch traced here: 227 us
  waiting for transfers between devices  96.8 us (42%)
  Pallas kernels  31.5 us (14%)
  blocking collectives  28.9 us (13%)
  local copies, waits for them, and re-layouts  27.6 us (12%)
  starting transfers between devices  22 us (10%)
  other arithmetic  13.2 us (6%)
  matrix products  6.19 us (3%)
    pallas_call x1, Pallas kernels, cache_attention(): pl.pallas_call(cache_kernel, grid_spec=grid_spec, out_shape=jax.ShapeDtyp...  31.5 us
    all_to_all x1, blocking collectives, shards(): lax.all_to_all(jnp.broadcast_to(mixed_rows[None], (blocks,) + mixed_rows....  28.9 us
    all_to_all x1, waiting for transfers between devices, shards(): lax.all_to_all(jnp.broadcast_to(queries[None], (blocks,) + queries.shape)...  28.5 us
    all_to_all x1, waiting for transfers between devices, shards(): lax.all_to_all(head_terms.reshape(blocks, chunk, -1), 'blk', 0, 0, tiled=...  26.2 us
    ppermute x1, waiting for transfers between devices, passed_along(): return lax.ppermute(block, axis, route)  20.7 us
    ppermute x1, waiting for transfers between devices, swapped(): return lax.ppermute(block, axis, route)  16.4 us
    broadcast_in_dim x1, local copies, waits for them, and re-layouts, shards(): spread = lambda f: jnp.repeat(jnp.swapaxes(f, -1, -2), HD, axis=-1)  8.32 us
    all_to_all x1, starting transfers between devices, shards(): lax.all_to_all(jnp.broadcast_to(queries[None], (blocks,) + queries.shape)...  8.23 us
  transfers between devices with their start and end apart: 5, of which 5 were waited for; matrix products, arithmetic and copies ran while one was open for 4% of the time, Pallas kernels for 0%

profile of v3, /device:TPU:2, one launch (start us, length us, event | category | flops | bytes accessed | tf_op | source)
XLA Modules:
  0.0 227.2 jit_solution(2493526441277988631)
XLA Ops:
  0.0 2.0 collective-permute-start
  2.7 4.1 %copy.32 = bf16[256,4096]{1,0:T(8,128)(2,1)} copy(bf16[256,4096]{0,1:T(8,128)(2,1)} %bitcast.49) | data formatting | bytes 4194304 | tf_op jit(solution)/shard_map/dot_general | solution.py:152
  6.8 0.3 multiply_cosine_fusion.1
  7.1 20.7 %collective-permute-done = bf16[256,4096]{1,0:T(8,128)(2,1)} collective-permute-done((bf16[256,4096]{1,0:T(8,128)(2,1)}, bf16[256,4096]{1,0:T(8,128)(2,1)}, u32[]{:S(2)}, u32[]{:S(2)}) %collective-permute-start) | collective-permute-done | bytes 2097184 | tf_op jit(solution)/shard_map/ppermute | solution.py:19
  27.8 3.9 %fusion.39 = (f32[256,4096]{1,0:T(8,128)}, bf16[256,4096]{1,0:T(8,128)(2,1)S(1)}) fusion(bf16[256,4096]{1,0:T(8,128)(2,1)} %param.10, bf16[256,4096]{1,0:T(8,128)(2,1)} %collective-permute-done, pred[]{:T(512)S(6)} %eq.8), kind=kLoop, calls=%fused_computation.73 | loop fusion | flops 2097152 | bytes 10485761 | tf_op jit(solution)/shard_map/convert_element_type | solution.py:146
  31.7 0.5 multiply_reduce_fusion.1
  32.2 0.0 copy-done.4
  32.3 1.8 copy-done.2
  34.1 1.0 fusion.1
  35.1 0.1 copy.25
  35.2 1.5 broadcast_in_dim.18
  36.8 8.2 %all-to-all-start = ((bf16[16,256,256]{2,1,0:T(8,128)(2,1)}), bf16[16,256,256]{2,1,0:T(8,128)(2,1)}, u32[]{:S(2)}, u32[]{:S(2)}) async-start(bf16[16,256,256]{2,1,0:T(8,128)(2,1)} %broadcast_in_dim.18), calls=%async_computation | async-start | bytes 4194304 | tf_op jit(solution)/shard_map/all_to_all | solution.py:162
  45.0 0.6 constant_dynamic-slice_fusion
  45.6 28.5 %all-to-all-done.q_ref = bf16[16,256,256]{2,1,0:T(8,128)(2,1)} async-done(((bf16[16,256,256]{2,1,0:T(8,128)(2,1)}), bf16[16,256,256]{2,1,0:T(8,128)(2,1)}, u32[]{:S(2)}, u32[]{:S(2)}) %all-to-all-start) | async-done | bytes 2097184 | tf_op jit(solution)/shard_map/all_to_all | solution.py:162
  74.1 31.5 %shard_map.100 = bf16[16,264,256]{2,1,0:T(8,128)(2,1)} custom-call(s32[1]{0:T(128)} %bitcast.12.live_ref, bf16[16,256,256]{2,1,0:T(8,128)(2,1)} %all-to-all-done.q_ref, bf16[2048,1024]{1,0:T(8,128)(2,1)} %bitcast.47, bf16[2048,1024]{1,0:T(8,128)(2,1)} %bitcast.48), custom_call_target="tpu_custom_call" | custom-call | tf_op jit(solution)/shard_map/pallas_call | solution.py:118
  105.6 4.6 %all-to-all-start.1 = ((bf16[16,264,256]{2,1,0:T(8,128)(2,1)}), bf16[16,264,256]{2,1,0:T(8,128)(2,1)}, u32[]{:S(2)}, u32[]{:S(2)}) async-start(bf16[16,264,256]{2,1,0:T(8,128)(2,1)} %shard_map.100), calls=%async_computation.1 | async-start | bytes 4325376 | tf_op jit(solution)/shard_map/all_to_all | solution.py:166
  110.2 2.6 %fusion.5 = f32[256,128]{0,1:T(8,128)S(1)} fusion(bf16[1,4096,128]{2,1,0:T(8,128)(2,1)S(1)} %copy-done.3, f32[4096]{0:T(1024)S(1)} %bitcast.59, f32[256]{0:T(256)S(1)} %add_rsqrt_fusion, bf16[256,4096]{1,0:T(8,128)(2,1)} %copy-done.1), kind=kOutput, calls=%fused_computation.13 | convolution fusion | flops 272629760 | bytes 3294208 | tf_op jit(solution)/shard_map/dot_general | solution.py:156
  112.8 0.3 fusion.24
  113.2 2.0 collective-permute-start.1
  115.2 0.1 copy.23
  115.3 0.1 copy.24
  115.4 16.4 %collective-permute-done.1 = bf16[256,128]{0,1:T(8,128)(2,1)S(1)} collective-permute-done((bf16[256,128]{0,1:T(8,128)(2,1)S(1)}, bf16[256,128]{0,1:T(8,128)(2,1)S(1)}, u32[]{:S(2)}, u32[]{:S(2)}) %collective-permute-start.1) | collective-permute-done | bytes 65568 | tf_op jit(solution)/shard_map/ppermute | solution.py:29
  131.8 0.3 fusion.42
  132.2 0.1 fusion.8
  132.3 0.1 add.85
  132.5 0.1 copy.27
  132.5 0.3 fusion.4
  132.8 5.0 %all-to-all-done.1 = bf16[16,264,256]{2,1,0:T(8,128)(2,1)} async-done(((bf16[16,264,256]{2,1,0:T(8,128)(2,1)}), bf16[16,264,256]{2,1,0:T(8,128)(2,1)}, u32[]{:S(2)}, u32[]{:S(2)}) %all-to-all-start.1) | async-done | bytes 2162720 | tf_op jit(solution)/shard_map/all_to_all | solution.py:166
  137.9 0.8 slice_convert_fusion
  138.7 0.1 slice.34
  138.8 0.1 slice.33
  138.9 0.1 slice.32
  139.2 0.1 copy.31
  139.3 0.1 copy.28
  139.5 2.0 copy.30
  141.4 8.3 %broadcast_in_dim.20 = f32[16,256,2,128]{3,2,1,0:T(2,128)} broadcast(f32[16,256,2]{2,1,0:T(8,128)} %copy.30), dimensions={0,1,2} | broadcast | bytes 4227072 | tf_op jit(solution)/shard_map/broadcast_in_dim | solution.py:178
  149.8 6.4 %reshape.185 = f32[16,256,256]{2,1,0:T(8,128)} reshape(f32[16,256,2,128]{3,2,1,0:T(2,128)} %broadcast_in_dim.20) | data formatting | bytes 8388608 | tf_op jit(solution)/shard_map/reshape | solution.py:178
  156.2 3.4 %multiply_reduce_fusion = f32[256,256]{1,0:T(8,128)S(1)} fusion(f32[16,256,256]{2,1,0:T(8,128)} %reshape.185, bf16[16,264,256]{2,1,0:T(8,128)(2,1)} %all-to-all-done.1), kind=kLoop, calls=%fused_computation.2 | loop fusion | flops 3080192 | bytes 6553600 | tf_op jit(solution)/shard_map/reduce_sum | solution.py:179
  159.6 0.1 reduce_sum.52
  159.7 0.7 fusion.13
  160.5 2.0 convolution_convert_fusion
  162.5 5.1 %all-to-all-start.2 = ((bf16[16,16,4096]{2,1,0:T(8,128)(2,1)}), bf16[16,16,4096]{2,1,0:T(8,128)(2,1)}, u32[]{:S(2)}, u32[]{:S(2)}) async-start(bf16[16,16,4096]{2,1,0:T(8,128)(2,1)} %bitcast.45), calls=%async_computation.2 | async-start | bytes 4194304 | tf_op jit(solution)/shard_map/all_to_all | solution.py:185
  167.6 26.2 %all-to-all-done.2 = bf16[16,16,4096]{2,1,0:T(8,128)(2,1)} async-done(((bf16[16,16,4096]{2,1,0:T(8,128)(2,1)}), bf16[16,16,4096]{2,1,0:T(8,128)(2,1)}, u32[]{:S(2)}, u32[]{:S(2)}) %all-to-all-start.2) | async-done | bytes 2097184 | tf_op jit(solution)/shard_map/all_to_all | solution.py:185
  193.8 1.9 convert_reduce_fusion
  195.8 1.0 add_convert_fusion
  196.7 0.2 broadcast_in_dim.22
  197.0 28.9 %all_to_all.20 = bf16[16,16,4096]{2,1,0:T(8,128)(2,1)S(1)} all-to-all(bf16[16,16,4096]{2,1,0:T(8,128)(2,1)S(1)} %broadcast_in_dim.22), channel_id=1, replica_groups=mesh['segment'=8,'blk'=16] {'blk'}, dimensions={0} | all-to-all | bytes 4194304 | tf_op jit(solution)/shard_map/all_to_all | solution.py:190
  225.9 1.3 copy.40
  (24 shorter events, 0.2 us)
Async XLA Ops:
  0.0 160.4 %copy-start = (bf16[1,256,4096]{2,1,0:T(8,128)(2,1)S(1)}, bf16[1,256,4096]{2,1,0:T(8,128)(2,1)}, u32[]{:S(2)}) copy-start(bf16[1,256,4096]{2,1,0:T(8,128)(2,1)} %param.17) | copy-start | bytes 6291460
  0.0 27.8 %collective-permute-start = (bf16[256,4096]{1,0:T(8,128)(2,1)}, bf16[256,4096]{1,0:T(8,128)(2,1)}, u32[]{:S(2)}, u32[]{:S(2)}) collective-permute-start(bf16[256,4096]{1,0:T(8,128)(2,1)} %bitcast.57), channel_id=1, source_target_pairs={{0,16},{16,32},{32,48},{48,64},{64,80},{80,96},{96,112},{1,17},{17... | collective-permute-start | bytes 6291464 | tf_op jit(solution)/shard_map/ppermute | solution.py:19
  27.8 4.5 %copy-start.4 = (f32[1,4096]{1,0:T(1,128)S(1)}, f32[1,4096]{1,0:T(1,128)}, u32[]{:S(2)}) copy-start(f32[1,4096]{1,0:T(1,128)} %param.14) | copy-start | bytes 49156
  31.7 3.3 %copy-start.1 = (bf16[256,4096]{1,0:T(8,128)(2,1)}, bf16[256,4096]{1,0:T(8,128)(2,1)S(1)}, u32[]{:S(2)}) copy-start(bf16[256,4096]{1,0:T(8,128)(2,1)S(1)} %get-tuple-element.6) | copy-start | bytes 6291460
  31.7 2.3 %copy-start.2 = (bf16[256,4096]{1,0:T(8,128)(2,1)S(1)}, bf16[256,4096]{1,0:T(8,128)(2,1)}, u32[]{:S(2)}) copy-start(bf16[256,4096]{1,0:T(8,128)(2,1)} %copy.32) | copy-start | bytes 6291460
  36.8 8.2 %copy-start.6 = (s32[1,16]{1,0:T(1,128)S(1)}, s32[1,16]{1,0:T(1,128)}, u32[]{:S(2)}) copy-start(s32[1,16]{1,0:T(1,128)} %param.13) | copy-start | bytes 196
  36.8 37.3 %all-to-all-start = ((bf16[16,256,256]{2,1,0:T(8,128)(2,1)}), bf16[16,256,256]{2,1,0:T(8,128)(2,1)}, u32[]{:S(2)}, u32[]{:S(2)}) async-start(bf16[16,256,256]{2,1,0:T(8,128)(2,1)} %broadcast_in_dim.18), calls=%async_computation | async-start | bytes 4194304 | tf_op jit(solution)/shard_map/all_to_all | solution.py:162
  105.6 4.6 %copy-start.3 = (bf16[1,4096,128]{2,1,0:T(8,128)(2,1)S(1)}, bf16[1,4096,128]{2,1,0:T(8,128)(2,1)}, u32[]{:S(2)}) copy-start(bf16[1,4096,128]{2,1,0:T(8,128)(2,1)} %param.16) | copy-start | bytes 3145732
  105.6 4.6 %copy-start.5 = (f32[1,4096]{1,0:T(1,128)S(1)}, f32[1,4096]{1,0:T(1,128)}, u32[]{:S(2)}) copy-start(f32[1,4096]{1,0:T(1,128)} %param.14) | copy-start | bytes 49156
  105.6 32.2 %all-to-all-start.1 = ((bf16[16,264,256]{2,1,0:T(8,128)(2,1)}), bf16[16,264,256]{2,1,0:T(8,128)(2,1)}, u32[]{:S(2)}, u32[]{:S(2)}) async-start(bf16[16,264,256]{2,1,0:T(8,128)(2,1)} %shard_map.100), calls=%async_computation.1 | async-start | bytes 4325376 | tf_op jit(solution)/shard_map/all_to_all | solution.py:166
  113.2 18.7 %collective-permute-start.1 = (bf16[256,128]{0,1:T(8,128)(2,1)S(1)}, bf16[256,128]{0,1:T(8,128)(2,1)S(1)}, u32[]{:S(2)}, u32[]{:S(2)}) collective-permute-start(bf16[256,128]{0,1:T(8,128)(2,1)S(1)} %fusion.27), channel_id=1, source_target_pairs={{0,1},{1,0},{2,3},{3,2},{4,5},{5,4},{6,7},{7,6},{8,9},{9,8},{10,11... | collective-permute-start | bytes 196616 | tf_op jit(solution)/shard_map/ppermute | solution.py:29
  162.5 31.3 %all-to-all-start.2 = ((bf16[16,16,4096]{2,1,0:T(8,128)(2,1)}), bf16[16,16,4096]{2,1,0:T(8,128)(2,1)}, u32[]{:S(2)}, u32[]{:S(2)}) async-start(bf16[16,16,4096]{2,1,0:T(8,128)(2,1)} %bitcast.45), calls=%async_computation.2 | async-start | bytes 4194304 | tf_op jit(solution)/shard_map/all_to_all | solution.py:185

commit v4 on v3

--- a/solution.py
+++ b/solution.py
@@ -122,6 +122,44 @@
     )(live, every_query, cached_keys, cached_values)
 
 
+def combine_kernel(parts_ref, own_out_ref, own_log_ref, out_ref):
+    sources = parts_ref.shape[0]
+    rows = out_ref.shape[0]
+    heads_here = out_ref.shape[1] // HD
+    log_rows = []
+    for b in range(sources):
+        packed = parts_ref[b, rows:rows + LOG_ROWS, :].astype(jnp.float32)
+        for h in range(heads_here):
+            log_rows.append((packed[3 * h + 2:3 * h + 3] + packed[3 * h + 1:3 * h + 2]) + packed[3 * h:3 * h + 1])
+    table_rows = 128 * pl.cdiv(len(log_rows), 128)
+    which = lax.broadcasted_iota(jnp.int32, (table_rows, rows), 0)
+    table = jnp.zeros((table_rows, rows), jnp.float32)
+    for j, row in enumerate(log_rows):
+        table = jnp.where(which == j, jnp.broadcast_to(row, (table_rows, rows)), table)
+    columns = jnp.transpose(table)
+    for h in range(heads_here):
+        own_log = own_log_ref[:, h:h + 1]
+        logs = [columns[:, b * heads_here + h:b * heads_here + h + 1] for b in range(sources)]
+        ceiling = own_log
+        for lg in logs:
+            ceiling = jnp.maximum(ceiling, lg)
+        own_factor = jnp.exp(own_log - ceiling)
+        weighted = own_factor * own_out_ref[:, h * HD:(h + 1) * HD].astype(jnp.float32)
+        total = own_factor
+        for b, lg in enumerate(logs):
+            factor = jnp.exp(lg - ceiling)
+            weighted = weighted + factor * parts_ref[b, :rows, h * HD:(h + 1) * HD].astype(jnp.float32)
+            total = total + factor
+        out_ref[:, h * HD:(h + 1) * HD] = (weighted / total).astype(out_ref.dtype)
+
+
+def combine(arrived_parts, own_out, own_log):
+    return pl.pallas_call(
+        combine_kernel,
+        out_shape=jax.ShapeDtypeStruct(own_out.shape, jnp.bfloat16),
+    )(arrived_parts, own_out, own_log)
+
+
 def shards(
     fresh,
     previous,
@@ -164,22 +202,13 @@
     )
     held = cache_attention(live, every_query, cache_keys[0], cache_values[0])
     arrived_parts = lax.all_to_all(held, "blk", split_axis=0, concat_axis=0, tiled=True)
-    log_parts = arrived_parts[:, span_rows:span_rows + 3 * heads_here].astype(jnp.float32)
-    shard_logs = sum(log_parts[:, i::3] for i in (2, 1, 0))
     query_rows = queries.reshape(span_rows * heads_here, HD)
     row_tokens = jnp.arange(span_rows * heads_here, dtype=jnp.int32) // heads_here
     causal = row_tokens[:, None] >= jnp.arange(span_rows, dtype=jnp.int32)[None, :]
     own_out, own_log = attend_rows(query_rows, own_keys, own_values, causal)
     own_out = own_out.reshape(span_rows, heads_here * HD)
-    own_log = own_log.reshape(span_rows, heads_here).T
-    ceiling = jnp.maximum(own_log, jnp.max(shard_logs, axis=0))
-    own_factor = jnp.exp(own_log - ceiling)
-    factors = jnp.exp(shard_logs - ceiling)
-    spread = lambda f: jnp.repeat(jnp.swapaxes(f, -1, -2), HD, axis=-1)
-    weighted = spread(own_factor) * own_out.astype(jnp.float32) + jnp.sum(
-        spread(factors) * arrived_parts[:, :span_rows].astype(jnp.float32), axis=0
-    )
-    attended = (weighted / spread(own_factor + jnp.sum(factors, axis=0))).astype(jnp.bfloat16)
+    own_log = own_log.reshape(span_rows, heads_here)
+    attended = combine(arrived_parts, own_out, own_log)
     head_terms = jnp.dot(attended, w_out[0], preferred_element_type=jnp.float32).astype(jnp.bfloat16)
     chunk = span_rows // blocks
     gathered_terms = lax.all_to_all(

time: 228 us -> 214 us (0.939)
  local copies, waits for them, and re-layouts: 27.6 us -> 11.5 us
  Pallas kernels: 31.5 us -> 39.7 us
  other arithmetic: 13.2 us -> 8.19 us
    broadcast_in_dim x1 -> x0, local copies, waits for them, and re-layouts: 8.32 us -> none  [shards(): spread = lambda f: jnp.repeat(jnp.swapaxes(f, -1, -2), HD, axis=-1)]
    pallas_call x0 -> x1, Pallas kernels: none -> 8.04 us  [combine(): pl.pallas_call(combine_kernel, out_shape=jax.ShapeDtypeStruct(own_out.sha...]
    reshape x1, local copies, waits for them, and re-layouts: 6.43 us -> 0.7 us  [shards(): own_out = own_out.reshape(span_rows, heads_here * HD)]
    reduce_sum x2 -> x0, other arithmetic: 3.43 us -> none  [the longest x1 3.38 us: shards(): jnp.sum(spread(factors) * arrived_parts[:, :span_rows].astype(jnp.float32...]
  transfers between devices with their start and end apart: 5 -> 5, of which waited for: 5 -> 5; matrix products, arithmetic and copies ran while one was open for 4% -> 5% of each run, Pallas kernels for 0% -> 0%
where the time goes in v4:
time: 214 us
  waiting for transfers between devices  95.6 us (45%)
  Pallas kernels  39.7 us (19%)
  blocking collectives  28.8 us (13%)
  starting transfers between devices  21.9 us (10%)
  local copies, waits for them, and re-layouts  11.5 us (5%)
  other arithmetic  8.19 us (4%)
  matrix products  7.08 us (3%)
    pallas_call x1, Pallas kernels, cache_attention(): pl.pallas_call(cache_kernel, grid_spec=grid_spec, out_shape=jax.ShapeDtyp...  31.7 us
    all_to_all x1, blocking collectives, shards(): lax.all_to_all(jnp.broadcast_to(mixed_rows[None], (blocks,) + mixed_rows....  28.8 us
    all_to_all x1, waiting for transfers between devices, shards(): lax.all_to_all(jnp.broadcast_to(queries[None], (blocks,) + queries.shape)...  28.4 us
    all_to_all x1, waiting for transfers between devices, shards(): lax.all_to_all(head_terms.reshape(blocks, chunk, -1), 'blk', 0, 0, tiled=...  26.3 us
    ppermute x1, waiting for transfers between devices, passed_along(): return lax.ppermute(block, axis, route)  20.7 us
    ppermute x1, waiting for transfers between devices, swapped(): return lax.ppermute(block, axis, route)  16.4 us
    all_to_all x1, starting transfers between devices, shards(): lax.all_to_all(jnp.broadcast_to(queries[None], (blocks,) + queries.shape)...  8.23 us
    pallas_call x1, Pallas kernels, combine(): pl.pallas_call(combine_kernel, out_shape=jax.ShapeDtypeStruct(own_out.sha...  8.04 us
  transfers between devices with their start and end apart: 5, of which 5 were waited for; matrix products, arithmetic and copies ran while one was open for 5% of the time, Pallas kernels for 0%

profile of v4, /device:TPU:2, one launch (start us, length us, event | category | flops | bytes accessed | tf_op | source)
XLA Modules:
  0.0 213.7 jit_solution(1737566682808100389)
XLA Ops:
  0.0 0.0 copy-start
  0.0 2.0 collective-permute-start
  2.7 4.1 %copy.17 = bf16[256,4096]{1,0:T(8,128)(2,1)} copy(bf16[256,4096]{0,1:T(8,128)(2,1)} %bitcast.35) | data formatting | bytes 4194304 | tf_op jit(solution)/shard_map/dot_general | solution.py:190
  6.8 0.3 multiply_cosine_fusion.1
  7.1 20.7 %collective-permute-done = bf16[256,4096]{1,0:T(8,128)(2,1)} collective-permute-done((bf16[256,4096]{1,0:T(8,128)(2,1)}, bf16[256,4096]{1,0:T(8,128)(2,1)}, u32[]{:S(2)}, u32[]{:S(2)}) %collective-permute-start) | collective-permute-done | bytes 2097184 | tf_op jit(solution)/shard_map/ppermute | solution.py:19
  27.8 0.0 copy-start.4
  27.8 3.9 %fusion.31 = (f32[256,4096]{1,0:T(8,128)}, bf16[256,4096]{1,0:T(8,128)(2,1)S(1)}) fusion(bf16[256,4096]{1,0:T(8,128)(2,1)} %param.10, bf16[256,4096]{1,0:T(8,128)(2,1)} %collective-permute-done, pred[]{:T(512)S(6)} %eq.8), kind=kLoop, calls=%fused_computation.57 | loop fusion | flops 2097152 | bytes 10485761 | tf_op jit(solution)/shard_map/convert_element_type | solution.py:184
  31.7 0.0 copy-start.1
  31.7 0.0 copy-start.2
  31.7 0.5 multiply_reduce_fusion
  32.2 0.0 copy-done.4
  32.3 1.8 copy-done.2
  34.1 1.0 fusion.1
  35.1 0.0 copy-done.1
  35.1 0.1 copy.14
  35.2 1.5 broadcast_in_dim.9
  36.8 0.0 copy-start.6
  36.8 8.2 %all-to-all-start = ((bf16[16,256,256]{2,1,0:T(8,128)(2,1)}), bf16[16,256,256]{2,1,0:T(8,128)(2,1)}, u32[]{:S(2)}, u32[]{:S(2)}) async-start(bf16[16,256,256]{2,1,0:T(8,128)(2,1)} %broadcast_in_dim.9), calls=%async_computation | async-start | bytes 4194304 | tf_op jit(solution)/shard_map/all_to_all | solution.py:200
  45.0 0.0 copy-done.6
  45.0 0.7 constant_dynamic-slice_fusion
  45.7 28.4 %all-to-all-done.q_ref = bf16[16,256,256]{2,1,0:T(8,128)(2,1)} async-done(((bf16[16,256,256]{2,1,0:T(8,128)(2,1)}), bf16[16,256,256]{2,1,0:T(8,128)(2,1)}, u32[]{:S(2)}, u32[]{:S(2)}) %all-to-all-start) | async-done | bytes 2097184 | tf_op jit(solution)/shard_map/all_to_all | solution.py:200
  74.1 31.7 %shard_map.100 = bf16[16,264,256]{2,1,0:T(8,128)(2,1)} custom-call(s32[1]{0:T(128)} %bitcast.1.live_ref, bf16[16,256,256]{2,1,0:T(8,128)(2,1)} %all-to-all-done.q_ref, bf16[2048,1024]{1,0:T(8,128)(2,1)} %bitcast.33, bf16[2048,1024]{1,0:T(8,128)(2,1)} %bitcast.34), custom_call_target="tpu_custom_call" | custom-call | tf_op jit(solution)/shard_map/pallas_call | solution.py:118
  105.8 0.0 copy-start.3
  105.8 4.6 %all-to-all-start.1 = ((bf16[16,264,256]{2,1,0:T(8,128)(2,1)}), bf16[16,264,256]{2,1,0:T(8,128)(2,1)}, u32[]{:S(2)}, u32[]{:S(2)}) async-start(bf16[16,264,256]{2,1,0:T(8,128)(2,1)} %shard_map.100), calls=%async_computation.1 | async-start | bytes 4325376 | tf_op jit(solution)/shard_map/all_to_all | solution.py:204
  110.3 0.0 copy-done.3
  110.4 0.0 copy-done.5
  110.4 2.6 %fusion.5 = f32[256,128]{0,1:T(8,128)S(1)} fusion(bf16[1,4096,128]{2,1,0:T(8,128)(2,1)S(1)} %copy-done.3, f32[4096]{0:T(1024)S(1)} %bitcast.43, f32[256]{0:T(256)S(1)} %add_rsqrt_fusion, bf16[256,4096]{1,0:T(8,128)(2,1)} %copy-done.1), kind=kOutput, calls=%fused_computation.12 | convolution fusion | flops 272629760 | bytes 3294208 | tf_op jit(solution)/shard_map/dot_general | solution.py:194
  112.9 0.3 fusion.19
  113.3 2.0 collective-permute-start.1
  115.3 0.1 copy.15
  115.4 0.1 copy.16
  115.5 16.4 %collective-permute-done.1 = bf16[256,128]{0,1:T(8,128)(2,1)S(1)} collective-permute-done((bf16[256,128]{0,1:T(8,128)(2,1)S(1)}, bf16[256,128]{0,1:T(8,128)(2,1)S(1)}, u32[]{:S(2)}, u32[]{:S(2)}) %collective-permute-start.1) | collective-permute-done | bytes 65568 | tf_op jit(solution)/shard_map/ppermute | solution.py:29
  131.9 0.3 fusion.32
  132.3 0.1 fusion.7
  132.4 0.8 add.66.own_log_ref
  133.2 0.3 fusion.4
  133.5 0.7 reshape.158.own_out_ref
  134.2 3.8 %all-to-all-done.1.parts_ref = bf16[16,264,256]{2,1,0:T(8,128)(2,1)} async-done(((bf16[16,264,256]{2,1,0:T(8,128)(2,1)}), bf16[16,264,256]{2,1,0:T(8,128)(2,1)}, u32[]{:S(2)}, u32[]{:S(2)}) %all-to-all-start.1) | async-done | bytes 2162720 | tf_op jit(solution)/shard_map/all_to_all | solution.py:204
  138.0 8.0 %shard_map.101 = bf16[256,256]{1,0:T(8,128)(2,1)} custom-call(bf16[16,264,256]{2,1,0:T(8,128)(2,1)} %all-to-all-done.1.parts_ref, bf16[256,256]{1,0:T(8,128)(2,1)} %reshape.158.own_out_ref, f32[256,2]{1,0:T(8,128)} %add.66.own_log_ref), custom_call_target="tpu_custom_call" | custom-call | tf_op jit(solution)/shard_map/pallas_call | solution.py:157
  146.0 0.0 copy-done
  146.0 2.9 %convolution_convert_fusion = bf16[256,4096]{1,0:T(8,128)(2,1)} fusion(bf16[256,256]{1,0:T(8,128)(2,1)} %shard_map.101, bf16[1,256,4096]{2,1,0:T(8,128)(2,1)S(1)} %copy-done), kind=kOutput, calls=%fused_computation | convolution fusion | flops 537919488 | bytes 4325376 | tf_op jit(solution)/shard_map/dot_general | solution.py:212
  149.0 5.1 %all-to-all-start.2 = ((bf16[16,16,4096]{2,1,0:T(8,128)(2,1)}), bf16[16,16,4096]{2,1,0:T(8,128)(2,1)}, u32[]{:S(2)}, u32[]{:S(2)}) async-start(bf16[16,16,4096]{2,1,0:T(8,128)(2,1)} %bitcast.31), calls=%async_computation.2 | async-start | bytes 4194304 | tf_op jit(solution)/shard_map/all_to_all | solution.py:214
  154.1 26.3 %all-to-all-done.2 = bf16[16,16,4096]{2,1,0:T(8,128)(2,1)} async-done(((bf16[16,16,4096]{2,1,0:T(8,128)(2,1)}), bf16[16,16,4096]{2,1,0:T(8,128)(2,1)}, u32[]{:S(2)}, u32[]{:S(2)}) %all-to-all-start.2) | async-done | bytes 2097184 | tf_op jit(solution)/shard_map/all_to_all | solution.py:214
  180.4 1.9 convert_reduce_fusion
  182.3 1.0 add_convert_fusion
  183.3 0.2 broadcast_in_dim.12
  183.6 28.8 %all_to_all.20 = bf16[16,16,4096]{2,1,0:T(8,128)(2,1)S(1)} all-to-all(bf16[16,16,4096]{2,1,0:T(8,128)(2,1)S(1)} %broadcast_in_dim.12), channel_id=1, replica_groups=mesh['segment'=8,'blk'=16] {'blk'}, dimensions={0} | all-to-all | bytes 4194304 | tf_op jit(solution)/shard_map/all_to_all | solution.py:219
  212.3 1.3 copy.20
  (9 shorter events, 0.1 us)
Async XLA Ops:
  0.0 146.0 %copy-start = (bf16[1,256,4096]{2,1,0:T(8,128)(2,1)S(1)}, bf16[1,256,4096]{2,1,0:T(8,128)(2,1)}, u32[]{:S(2)}) copy-start(bf16[1,256,4096]{2,1,0:T(8,128)(2,1)} %param.17) | copy-start | bytes 6291460
  0.0 27.8 %collective-permute-start = (bf16[256,4096]{1,0:T(8,128)(2,1)}, bf16[256,4096]{1,0:T(8,128)(2,1)}, u32[]{:S(2)}, u32[]{:S(2)}) collective-permute-start(bf16[256,4096]{1,0:T(8,128)(2,1)} %bitcast.41), channel_id=1, source_target_pairs={{0,16},{16,32},{32,48},{48,64},{64,80},{80,96},{96,112},{1,17},{17... | collective-permute-start | bytes 6291464 | tf_op jit(solution)/shard_map/ppermute | solution.py:19
  27.8 4.5 %copy-start.4 = (f32[1,4096]{1,0:T(1,128)S(1)}, f32[1,4096]{1,0:T(1,128)}, u32[]{:S(2)}) copy-start(f32[1,4096]{1,0:T(1,128)} %param.14) | copy-start | bytes 49156
  31.7 3.3 %copy-start.1 = (bf16[256,4096]{1,0:T(8,128)(2,1)}, bf16[256,4096]{1,0:T(8,128)(2,1)S(1)}, u32[]{:S(2)}) copy-start(bf16[256,4096]{1,0:T(8,128)(2,1)S(1)} %get-tuple-element.6) | copy-start | bytes 6291460
  31.7 2.3 %copy-start.2 = (bf16[256,4096]{1,0:T(8,128)(2,1)S(1)}, bf16[256,4096]{1,0:T(8,128)(2,1)}, u32[]{:S(2)}) copy-start(bf16[256,4096]{1,0:T(8,128)(2,1)} %copy.17) | copy-start | bytes 6291460
  36.8 8.2 %copy-start.6 = (s32[1,16]{1,0:T(1,128)S(1)}, s32[1,16]{1,0:T(1,128)}, u32[]{:S(2)}) copy-start(s32[1,16]{1,0:T(1,128)} %param.13) | copy-start | bytes 196
  36.8 37.3 %all-to-all-start = ((bf16[16,256,256]{2,1,0:T(8,128)(2,1)}), bf16[16,256,256]{2,1,0:T(8,128)(2,1)}, u32[]{:S(2)}, u32[]{:S(2)}) async-start(bf16[16,256,256]{2,1,0:T(8,128)(2,1)} %broadcast_in_dim.9), calls=%async_computation | async-start | bytes 4194304 | tf_op jit(solution)/shard_map/all_to_all | solution.py:200
  105.8 4.6 %copy-start.3 = (bf16[1,4096,128]{2,1,0:T(8,128)(2,1)S(1)}, bf16[1,4096,128]{2,1,0:T(8,128)(2,1)}, u32[]{:S(2)}) copy-start(bf16[1,4096,128]{2,1,0:T(8,128)(2,1)} %param.16) | copy-start | bytes 3145732
  105.8 4.6 %copy-start.5 = (f32[1,4096]{1,0:T(1,128)S(1)}, f32[1,4096]{1,0:T(1,128)}, u32[]{:S(2)}) copy-start(f32[1,4096]{1,0:T(1,128)} %param.14) | copy-start | bytes 49156
  105.8 32.2 %all-to-all-start.1 = ((bf16[16,264,256]{2,1,0:T(8,128)(2,1)}), bf16[16,264,256]{2,1,0:T(8,128)(2,1)}, u32[]{:S(2)}, u32[]{:S(2)}) async-start(bf16[16,264,256]{2,1,0:T(8,128)(2,1)} %shard_map.100), calls=%async_computation.1 | async-start | bytes 4325376 | tf_op jit(solution)/shard_map/all_to_all | solution.py:204
  113.3 18.7 %collective-permute-start.1 = (bf16[256,128]{0,1:T(8,128)(2,1)S(1)}, bf16[256,128]{0,1:T(8,128)(2,1)S(1)}, u32[]{:S(2)}, u32[]{:S(2)}) collective-permute-start(bf16[256,128]{0,1:T(8,128)(2,1)S(1)} %fusion.22), channel_id=1, source_target_pairs={{0,1},{1,0},{2,3},{3,2},{4,5},{5,4},{6,7},{7,6},{8,9},{9,8},{10,11... | collective-permute-start | bytes 196616 | tf_op jit(solution)/shard_map/ppermute | solution.py:29
  149.0 31.4 %all-to-all-start.2 = ((bf16[16,16,4096]{2,1,0:T(8,128)(2,1)}), bf16[16,16,4096]{2,1,0:T(8,128)(2,1)}, u32[]{:S(2)}, u32[]{:S(2)}) async-start(bf16[16,16,4096]{2,1,0:T(8,128)(2,1)} %bitcast.31), calls=%async_computation.2 | async-start | bytes 4194304 | tf_op jit(solution)/shard_map/all_to_all | solution.py:214

commit v5 on v4

--- a/solution.py
+++ b/solution.py
@@ -65,38 +65,68 @@
     return (partial_out, (highest + jnp.log(totals))[:, 0])
 
 
-def cache_kernel(live_ref, q_ref, k_ref, v_ref, out_ref):
+def cache_kernel(live_ref, q_ref, k_ref, v_ref, out_ref, score_ref, high_ref, sum_ref, acc_ref):
     live = live_ref[0]
-    keys = k_ref[...]
-    values = v_ref[...]
     rows = q_ref.shape[1]
     width = out_ref.shape[2]
-    visible = lax.broadcasted_iota(jnp.int32, (1, keys.shape[0]), 1) < live
+    pieces, piece = score_ref.shape[0], score_ref.shape[2]
     for src in range(q_ref.shape[0]):
         log_rows = []
         for h in range(q_ref.shape[2] // HD):
             q = q_ref[src, :, h * HD:(h + 1) * HD]
-            scores = lax.dot_general(
-                q, keys, (((1,), (1,)), ((), ())), preferred_element_type=jnp.float32
-            ) * HD ** (-0.5)
-            scores = jnp.where(visible, scores, -jnp.inf)
-            highest = jnp.max(scores, axis=-1, keepdims=True)
-            weights = jnp.exp(scores - highest)
-            totals = jnp.sum(weights, axis=-1, keepdims=True)
-            part = jnp.dot(weights.astype(jnp.bfloat16), values, preferred_element_type=jnp.float32)
-            out_ref[src, :rows, h * HD:(h + 1) * HD] = (part / totals).astype(out_ref.dtype)
+            high_ref[...] = jnp.full(high_ref.shape, -jnp.inf, jnp.float32)
+            sum_ref[...] = jnp.zeros(sum_ref.shape, jnp.float32)
+            acc_ref[...] = jnp.zeros(acc_ref.shape, jnp.float32)
+            for c in range(pieces):
+                start = c * piece
+
+                def scores_of():
+                    return lax.dot_general(
+                        q, k_ref[start:start + piece, :], (((1,), (1,)), ((), ())),
+                        preferred_element_type=jnp.float32,
+                    ) * HD ** (-0.5)
+
+                def keep(scores):
+                    score_ref[c] = scores
+                    high_ref[...] = jnp.maximum(high_ref[...], jnp.max(scores, axis=-1, keepdims=True))
+
+                @pl.when(start + piece <= live)
+                def _():
+                    keep(scores_of())
+
+                @pl.when(jnp.logical_and(start < live, live < start + piece))
+                def _():
+                    visible = lax.broadcasted_iota(jnp.int32, (1, piece), 1) < live - start
+                    keep(jnp.where(visible, scores_of(), -jnp.inf))
+
+            highest = high_ref[...]
+            for c in range(pieces):
+                start = c * piece
+
+                @pl.when(start < live)
+                def _():
+                    weights = jnp.exp(score_ref[c] - highest)
+                    sum_ref[...] += jnp.sum(weights, axis=-1, keepdims=True)
+                    acc_ref[...] += jnp.dot(
+                        weights.astype(jnp.bfloat16), v_ref[start:start + piece, :],
+                        preferred_element_type=jnp.float32,
+                    )
+
+            totals = sum_ref[...]
+            out_ref[src, :rows, h * HD:(h + 1) * HD] = (acc_ref[...] / totals).astype(out_ref.dtype)
             log_col = jnp.broadcast_to(highest + jnp.log(totals), (rows, HD))
             rest = jnp.transpose(log_col)[0:1, :]
             for _ in range(3):
-                piece = rest.astype(jnp.bfloat16).astype(jnp.float32)
-                log_rows.append(piece)
-                rest = rest - piece
+                part = rest.astype(jnp.bfloat16).astype(jnp.float32)
+                log_rows.append(part)
+                rest = rest - part
         if rows < width:
             log_rows = [jnp.concatenate([r, jnp.zeros((1, width - rows), jnp.float32)], axis=1) for r in log_rows]
         log_rows += [jnp.zeros((1, width), jnp.float32)] * (out_ref.shape[1] - rows - len(log_rows))
         out_ref[src, rows:, :] = jnp.concatenate(log_rows, axis=0).astype(out_ref.dtype)
 
 
+PIECE = 512
 LOG_ROWS = 8
 
 
@@ -114,6 +144,12 @@
             pl.BlockSpec((rows, HD), lambda g, live: (0, g)),
         ],
         out_specs=pl.BlockSpec((per_head, span_rows + LOG_ROWS, width), lambda g, live: (g, 0, 0)),
+        scratch_shapes=[
+            pltpu.VMEM((rows // PIECE, span_rows, PIECE), jnp.float32),
+            pltpu.VMEM((span_rows, 1), jnp.float32),
+            pltpu.VMEM((span_rows, 1), jnp.float32),
+            pltpu.VMEM((span_rows, HD), jnp.float32),
+        ],
     )
     return pl.pallas_call(
         cache_kernel,

time: 214 us -> 270 us (1.26)
  Pallas kernels: 39.7 us -> 95.1 us
    pallas_call x1, Pallas kernels: 31.7 us -> 87.1 us  [cache_attention(): pl.pallas_call(cache_kernel, grid_spec=grid_spec, out_shape=jax.ShapeDtyp...]
  transfers between devices with their start and end apart: 5 -> 5, of which waited for: 5 -> 5; matrix products, arithmetic and copies ran while one was open for 5% -> 4% of each run, Pallas kernels for 0% -> 0%
where the time goes in v5:
time: 270 us; the launch traced here: 269 us
  Pallas kernels  95.1 us (35%)
  waiting for transfers between devices  95 us (35%)
  blocking collectives  30 us (11%)
  starting transfers between devices  21.5 us (8%)
  local copies, waits for them, and re-layouts  11.5 us (4%)
  other arithmetic  8.19 us (3%)
  matrix products  7.09 us (3%)
    pallas_call x1, Pallas kernels, cache_attention(): pl.pallas_call(cache_kernel, grid_spec=grid_spec, out_shape=jax.ShapeDtyp...  87.1 us
    all_to_all x1, blocking collectives, shards(): lax.all_to_all(jnp.broadcast_to(mixed_rows[None], (blocks,) + mixed_rows....  30 us
    all_to_all x1, waiting for transfers between devices, shards(): lax.all_to_all(jnp.broadcast_to(queries[None], (blocks,) + queries.shape)...  28.4 us
    all_to_all x1, waiting for transfers between devices, shards(): lax.all_to_all(head_terms.reshape(blocks, chunk, -1), 'blk', 0, 0, tiled=...  25.8 us
    ppermute x1, waiting for transfers between devices, passed_along(): return lax.ppermute(block, axis, route)  20.7 us
    ppermute x1, waiting for transfers between devices, swapped(): return lax.ppermute(block, axis, route)  18.3 us
    all_to_all x1, starting transfers between devices, shards(): lax.all_to_all(jnp.broadcast_to(queries[None], (blocks,) + queries.shape)...  8.24 us
    pallas_call x1, Pallas kernels, combine(): pl.pallas_call(combine_kernel, out_shape=jax.ShapeDtypeStruct(own_out.sha...  8.04 us
  transfers between devices with their start and end apart: 5, of which 5 were waited for; matrix products, arithmetic and copies ran while one was open for 4% of the time, Pallas kernels for 0%

profile of v5, /device:TPU:2, one launch (start us, length us, event | category | flops | bytes accessed | tf_op | source)
XLA Modules:
  0.0 269.3 jit_solution(16013418362013649389)
XLA Ops:
  0.0 0.0 copy-start
  0.0 2.0 collective-permute-start
  2.7 4.1 %copy.17 = bf16[256,4096]{1,0:T(8,128)(2,1)} copy(bf16[256,4096]{0,1:T(8,128)(2,1)} %bitcast.35) | data formatting | bytes 4194304 | tf_op jit(solution)/shard_map/dot_general | solution.py:226
  6.8 0.3 multiply_cosine_fusion.1
  7.1 20.7 %collective-permute-done = bf16[256,4096]{1,0:T(8,128)(2,1)} collective-permute-done((bf16[256,4096]{1,0:T(8,128)(2,1)}, bf16[256,4096]{1,0:T(8,128)(2,1)}, u32[]{:S(2)}, u32[]{:S(2)}) %collective-permute-start) | collective-permute-done | bytes 2097184 | tf_op jit(solution)/shard_map/ppermute | solution.py:19
  27.8 0.0 copy-start.4
  27.8 3.9 %fusion.31 = (f32[256,4096]{1,0:T(8,128)}, bf16[256,4096]{1,0:T(8,128)(2,1)S(1)}) fusion(bf16[256,4096]{1,0:T(8,128)(2,1)} %param.10, bf16[256,4096]{1,0:T(8,128)(2,1)} %collective-permute-done, pred[]{:T(512)S(6)} %eq.8), kind=kLoop, calls=%fused_computation.57 | loop fusion | flops 2097152 | bytes 10485761 | tf_op jit(solution)/shard_map/convert_element_type | solution.py:220
  31.7 0.0 copy-start.1
  31.7 0.0 copy-start.2
  31.7 0.5 multiply_reduce_fusion
  32.2 0.0 copy-done.4
  32.3 1.8 copy-done.2
  34.1 1.0 fusion.1
  35.1 0.0 copy-done.1
  35.1 0.1 copy.14
  35.2 1.5 broadcast_in_dim.9
  36.8 0.0 copy-start.6
  36.8 8.2 %all-to-all-start = ((bf16[16,256,256]{2,1,0:T(8,128)(2,1)}), bf16[16,256,256]{2,1,0:T(8,128)(2,1)}, u32[]{:S(2)}, u32[]{:S(2)}) async-start(bf16[16,256,256]{2,1,0:T(8,128)(2,1)} %broadcast_in_dim.9), calls=%async_computation | async-start | bytes 4194304 | tf_op jit(solution)/shard_map/all_to_all | solution.py:236
  45.0 0.0 copy-done.6
  45.0 0.7 constant_dynamic-slice_fusion
  45.7 28.4 %all-to-all-done.q_ref = bf16[16,256,256]{2,1,0:T(8,128)(2,1)} async-done(((bf16[16,256,256]{2,1,0:T(8,128)(2,1)}), bf16[16,256,256]{2,1,0:T(8,128)(2,1)}, u32[]{:S(2)}, u32[]{:S(2)}) %all-to-all-start) | async-done | bytes 2097184 | tf_op jit(solution)/shard_map/all_to_all | solution.py:236
  74.1 87.1 %shard_map.100 = bf16[16,264,256]{2,1,0:T(8,128)(2,1)} custom-call(s32[1]{0:T(128)} %bitcast.1.live_ref, bf16[16,256,256]{2,1,0:T(8,128)(2,1)} %all-to-all-done.q_ref, bf16[2048,1024]{1,0:T(8,128)(2,1)} %bitcast.33, bf16[2048,1024]{1,0:T(8,128)(2,1)} %bitcast.34), custom_call_target="tpu_custom_call" | custom-call | tf_op jit(solution)/shard_map/pallas_call | solution.py:154
  161.2 0.0 copy-start.3
  161.2 4.6 %all-to-all-start.1 = ((bf16[16,264,256]{2,1,0:T(8,128)(2,1)}), bf16[16,264,256]{2,1,0:T(8,128)(2,1)}, u32[]{:S(2)}, u32[]{:S(2)}) async-start(bf16[16,264,256]{2,1,0:T(8,128)(2,1)} %shard_map.100), calls=%async_computation.1 | async-start | bytes 4325376 | tf_op jit(solution)/shard_map/all_to_all | solution.py:240
  165.8 0.0 copy-done.3
  165.8 0.0 copy-done.5
  165.8 2.6 fusion.5
  168.4 0.3 fusion.19
  168.7 2.0 collective-permute-start.1
  170.7 0.1 copy.15
  170.9 0.1 copy.16
  171.0 18.3 %collective-permute-done.1 = bf16[256,128]{0,1:T(8,128)(2,1)S(1)} collective-permute-done((bf16[256,128]{0,1:T(8,128)(2,1)S(1)}, bf16[256,128]{0,1:T(8,128)(2,1)S(1)}, u32[]{:S(2)}, u32[]{:S(2)}) %collective-permute-start.1) | collective-permute-done | bytes 65568 | tf_op jit(solution)/shard_map/ppermute | solution.py:29
  189.3 0.3 fusion.32
  189.6 0.1 fusion.7
  189.7 0.8 add.66.own_log_ref
  190.5 0.3 fusion.4
  190.8 0.7 reshape.158.own_out_ref
  191.5 1.9 all-to-all-done.1.parts_ref
  193.4 8.0 %shard_map.101 = bf16[256,256]{1,0:T(8,128)(2,1)} custom-call(bf16[16,264,256]{2,1,0:T(8,128)(2,1)} %all-to-all-done.1.parts_ref, bf16[256,256]{1,0:T(8,128)(2,1)} %reshape.158.own_out_ref, f32[256,2]{1,0:T(8,128)} %add.66.own_log_ref), custom_call_target="tpu_custom_call" | custom-call | tf_op jit(solution)/shard_map/pallas_call | solution.py:193
  201.4 0.0 copy-done
  201.4 2.9 %convolution_convert_fusion = bf16[256,4096]{1,0:T(8,128)(2,1)} fusion(bf16[256,256]{1,0:T(8,128)(2,1)} %shard_map.101, bf16[1,256,4096]{2,1,0:T(8,128)(2,1)S(1)} %copy-done), kind=kOutput, calls=%fused_computation | convolution fusion | flops 537919488 | bytes 4325376 | tf_op jit(solution)/shard_map/dot_general | solution.py:248
  204.4 4.6 %all-to-all-start.2 = ((bf16[16,16,4096]{2,1,0:T(8,128)(2,1)}), bf16[16,16,4096]{2,1,0:T(8,128)(2,1)}, u32[]{:S(2)}, u32[]{:S(2)}) async-start(bf16[16,16,4096]{2,1,0:T(8,128)(2,1)} %bitcast.31), calls=%async_computation.2 | async-start | bytes 4194304 | tf_op jit(solution)/shard_map/all_to_all | solution.py:250
  209.0 25.8 %all-to-all-done.2 = bf16[16,16,4096]{2,1,0:T(8,128)(2,1)} async-done(((bf16[16,16,4096]{2,1,0:T(8,128)(2,1)}), bf16[16,16,4096]{2,1,0:T(8,128)(2,1)}, u32[]{:S(2)}, u32[]{:S(2)}) %all-to-all-start.2) | async-done | bytes 2097184 | tf_op jit(solution)/shard_map/all_to_all | solution.py:250
  234.8 1.9 convert_reduce_fusion
  236.7 1.0 add_convert_fusion
  237.7 0.2 broadcast_in_dim.12
  237.9 30.0 %all_to_all.20 = bf16[16,16,4096]{2,1,0:T(8,128)(2,1)S(1)} all-to-all(bf16[16,16,4096]{2,1,0:T(8,128)(2,1)S(1)} %broadcast_in_dim.12), channel_id=1, replica_groups=mesh['segment'=8,'blk'=16] {'blk'}, dimensions={0} | all-to-all | bytes 4194304 | tf_op jit(solution)/shard_map/all_to_all | solution.py:255
  267.9 1.3 copy.20
  (9 shorter events, 0.1 us)
Async XLA Ops:
  0.0 201.4 %copy-start = (bf16[1,256,4096]{2,1,0:T(8,128)(2,1)S(1)}, bf16[1,256,4096]{2,1,0:T(8,128)(2,1)}, u32[]{:S(2)}) copy-start(bf16[1,256,4096]{2,1,0:T(8,128)(2,1)} %param.17) | copy-start | bytes 6291460
  0.0 27.8 %collective-permute-start = (bf16[256,4096]{1,0:T(8,128)(2,1)}, bf16[256,4096]{1,0:T(8,128)(2,1)}, u32[]{:S(2)}, u32[]{:S(2)}) collective-permute-start(bf16[256,4096]{1,0:T(8,128)(2,1)} %bitcast.41), channel_id=1, source_target_pairs={{0,16},{16,32},{32,48},{48,64},{64,80},{80,96},{96,112},{1,17},{17... | collective-permute-start | bytes 6291464 | tf_op jit(solution)/shard_map/ppermute | solution.py:19
  27.8 4.5 %copy-start.4 = (f32[1,4096]{1,0:T(1,128)S(1)}, f32[1,4096]{1,0:T(1,128)}, u32[]{:S(2)}) copy-start(f32[1,4096]{1,0:T(1,128)} %param.14) | copy-start | bytes 49156
  31.7 3.3 %copy-start.1 = (bf16[256,4096]{1,0:T(8,128)(2,1)}, bf16[256,4096]{1,0:T(8,128)(2,1)S(1)}, u32[]{:S(2)}) copy-start(bf16[256,4096]{1,0:T(8,128)(2,1)S(1)} %get-tuple-element.6) | copy-start | bytes 6291460
  31.7 2.3 copy-start.2
  36.8 8.3 %copy-start.6 = (s32[1,16]{1,0:T(1,128)S(1)}, s32[1,16]{1,0:T(1,128)}, u32[]{:S(2)}) copy-start(s32[1,16]{1,0:T(1,128)} %param.13) | copy-start | bytes 196
  36.8 37.3 %all-to-all-start = ((bf16[16,256,256]{2,1,0:T(8,128)(2,1)}), bf16[16,256,256]{2,1,0:T(8,128)(2,1)}, u32[]{:S(2)}, u32[]{:S(2)}) async-start(bf16[16,256,256]{2,1,0:T(8,128)(2,1)} %broadcast_in_dim.9), calls=%async_computation | async-start | bytes 4194304 | tf_op jit(solution)/shard_map/all_to_all | solution.py:236
  161.2 4.6 %copy-start.3 = (bf16[1,4096,128]{2,1,0:T(8,128)(2,1)S(1)}, bf16[1,4096,128]{2,1,0:T(8,128)(2,1)}, u32[]{:S(2)}) copy-start(bf16[1,4096,128]{2,1,0:T(8,128)(2,1)} %param.16) | copy-start | bytes 3145732
  161.2 4.6 %copy-start.5 = (f32[1,4096]{1,0:T(1,128)S(1)}, f32[1,4096]{1,0:T(1,128)}, u32[]{:S(2)}) copy-start(f32[1,4096]{1,0:T(1,128)} %param.14) | copy-start | bytes 49156
  161.2 32.2 %all-to-all-start.1 = ((bf16[16,264,256]{2,1,0:T(8,128)(2,1)}), bf16[16,264,256]{2,1,0:T(8,128)(2,1)}, u32[]{:S(2)}, u32[]{:S(2)}) async-start(bf16[16,264,256]{2,1,0:T(8,128)(2,1)} %shard_map.100), calls=%async_computation.1 | async-start | bytes 4325376 | tf_op jit(solution)/shard_map/all_to_all | solution.py:240
  168.7 20.6 %collective-permute-start.1 = (bf16[256,128]{0,1:T(8,128)(2,1)S(1)}, bf16[256,128]{0,1:T(8,128)(2,1)S(1)}, u32[]{:S(2)}, u32[]{:S(2)}) collective-permute-start(bf16[256,128]{0,1:T(8,128)(2,1)S(1)} %fusion.22), channel_id=1, source_target_pairs={{0,1},{1,0},{2,3},{3,2},{4,5},{5,4},{6,7},{7,6},{8,9},{9,8},{10,11... | collective-permute-start | bytes 196616 | tf_op jit(solution)/shard_map/ppermute | solution.py:29
  204.4 30.4 %all-to-all-start.2 = ((bf16[16,16,4096]{2,1,0:T(8,128)(2,1)}), bf16[16,16,4096]{2,1,0:T(8,128)(2,1)}, u32[]{:S(2)}, u32[]{:S(2)}) async-start(bf16[16,16,4096]{2,1,0:T(8,128)(2,1)} %bitcast.31), calls=%async_computation.2 | async-start | bytes 4194304 | tf_op jit(solution)/shard_map/all_to_all | solution.py:250

commit v6 on v4

--- a/solution.py
+++ b/solution.py
@@ -72,6 +72,7 @@
     rows = q_ref.shape[1]
     width = out_ref.shape[2]
     visible = lax.broadcasted_iota(jnp.int32, (1, keys.shape[0]), 1) < live
+    ones = jnp.ones((keys.shape[0], HD), jnp.bfloat16)
     for src in range(q_ref.shape[0]):
         log_rows = []
         for h in range(q_ref.shape[2] // HD):
@@ -81,9 +82,9 @@
             ) * HD ** (-0.5)
             scores = jnp.where(visible, scores, -jnp.inf)
             highest = jnp.max(scores, axis=-1, keepdims=True)
-            weights = jnp.exp(scores - highest)
-            totals = jnp.sum(weights, axis=-1, keepdims=True)
-            part = jnp.dot(weights.astype(jnp.bfloat16), values, preferred_element_type=jnp.float32)
+            weights = jnp.exp(scores - highest).astype(jnp.bfloat16)
+            totals = jnp.dot(weights, ones, preferred_element_type=jnp.float32)[:, 0:1]
+            part = jnp.dot(weights, values, preferred_element_type=jnp.float32)
             out_ref[src, :rows, h * HD:(h + 1) * HD] = (part / totals).astype(out_ref.dtype)
             log_col = jnp.broadcast_to(highest + jnp.log(totals), (rows, HD))
             rest = jnp.transpose(log_col)[0:1, :]
@@ -126,30 +127,38 @@
     sources = parts_ref.shape[0]
     rows = out_ref.shape[0]
     heads_here = out_ref.shape[1] // HD
-    log_rows = []
+    logs = [[] for _ in range(heads_here)]
     for b in range(sources):
         packed = parts_ref[b, rows:rows + LOG_ROWS, :].astype(jnp.float32)
         for h in range(heads_here):
-            log_rows.append((packed[3 * h + 2:3 * h + 3] + packed[3 * h + 1:3 * h + 2]) + packed[3 * h:3 * h + 1])
-    table_rows = 128 * pl.cdiv(len(log_rows), 128)
-    which = lax.broadcasted_iota(jnp.int32, (table_rows, rows), 0)
-    table = jnp.zeros((table_rows, rows), jnp.float32)
-    for j, row in enumerate(log_rows):
-        table = jnp.where(which == j, jnp.broadcast_to(row, (table_rows, rows)), table)
+            logs[h].append((packed[3 * h + 2:3 * h + 3] + packed[3 * h + 1:3 * h + 2]) + packed[3 * h:3 * h + 1])
+    own_logs = own_log_ref[...]
+    table_rows = []
+    for h in range(heads_here):
+        own_log = own_logs[h:h + 1]
+        ceiling = own_log
+        for lg in logs[h]:
+            ceiling = jnp.maximum(ceiling, lg)
+        own_factor = jnp.exp(own_log - ceiling)
+        factors = [jnp.exp(lg - ceiling) for lg in logs[h]]
+        total = own_factor
+        for factor in factors:
+            total = total + factor
+        table_rows += [own_factor] + factors + [total]
+    size = 128 * pl.cdiv(len(table_rows), 128)
+    which = lax.broadcasted_iota(jnp.int32, (size, rows), 0)
+    table = jnp.zeros((size, rows), jnp.float32)
+    for j, row in enumerate(table_rows):
+        table = jnp.where(which == j, jnp.broadcast_to(row, (size, rows)), table)
     columns = jnp.transpose(table)
     for h in range(heads_here):
-        own_log = own_log_ref[:, h:h + 1]
-        logs = [columns[:, b * heads_here + h:b * heads_here + h + 1] for b in range(sources)]
-        ceiling = own_log
-        for lg in logs:
-            ceiling = jnp.maximum(ceiling, lg)
-        own_factor = jnp.exp(own_log - ceiling)
-        weighted = own_factor * own_out_ref[:, h * HD:(h + 1) * HD].astype(jnp.float32)
-        total = own_factor
-        for b, lg in enumerate(logs):
-            factor = jnp.exp(lg - ceiling)
-            weighted = weighted + factor * parts_ref[b, :rows, h * HD:(h + 1) * HD].astype(jnp.float32)
-            total = total + factor
+        base = h * (sources + 2)
+        weighted = columns[:, base:base + 1] * own_out_ref[:, h * HD:(h + 1) * HD].astype(jnp.float32)
+        for b in range(sources):
+            weighted = weighted + columns[:, base + 1 + b:base + 2 + b] * parts_ref[
+                b, :rows, h * HD:(h + 1) * HD
+            ].astype(jnp.float32)
+        total = columns[:, base + sources + 1:base + sources + 2]
         out_ref[:, h * HD:(h + 1) * HD] = (weighted / total).astype(out_ref.dtype)
 
 
@@ -207,7 +216,7 @@
     causal = row_tokens[:, None] >= jnp.arange(span_rows, dtype=jnp.int32)[None, :]
     own_out, own_log = attend_rows(query_rows, own_keys, own_values, causal)
     own_out = own_out.reshape(span_rows, heads_here * HD)
-    own_log = own_log.reshape(span_rows, heads_here)
+    own_log = own_log.reshape(span_rows, heads_here).T
     attended = combine(arrived_parts, own_out, own_log)
     head_terms = jnp.dot(attended, w_out[0], preferred_element_type=jnp.float32).astype(jnp.bfloat16)
     chunk = span_rows // blocks

time: 214 us -> 217 us (1.014)
  Pallas kernels: 39.7 us -> 42.6 us
    pallas_call x1, Pallas kernels: 31.7 us -> 38.7 us  [cache_attention(): pl.pallas_call(cache_kernel, grid_spec=grid_spec, out_shape=jax.ShapeDtyp...]
    pallas_call x1, Pallas kernels: 8.04 us -> 3.92 us  [combine(): pl.pallas_call(combine_kernel, out_shape=jax.ShapeDtypeStruct(own_out.sha...]
where the time goes in v6:
time: 217 us
  waiting for transfers between devices  95.6 us (44%)
  Pallas kernels  42.6 us (20%)
  blocking collectives  28.8 us (13%)
  starting transfers between devices  21.9 us (10%)
  local copies, waits for them, and re-layouts  11.5 us (5%)
  other arithmetic  8.19 us (4%)
  matrix products  7.08 us (3%)
    pallas_call x1, Pallas kernels, cache_attention(): pl.pallas_call(cache_kernel, grid_spec=grid_spec, out_shape=jax.ShapeDtyp...  38.7 us
    all_to_all x1, blocking collectives, shards(): lax.all_to_all(jnp.broadcast_to(mixed_rows[None], (blocks,) + mixed_rows....  28.8 us
    all_to_all x1, waiting for transfers between devices, shards(): lax.all_to_all(jnp.broadcast_to(queries[None], (blocks,) + queries.shape)...  28.4 us
    all_to_all x1, waiting for transfers between devices, shards(): lax.all_to_all(head_terms.reshape(blocks, chunk, -1), 'blk', 0, 0, tiled=...  26.3 us
    ppermute x1, waiting for transfers between devices, passed_along(): return lax.ppermute(block, axis, route)  20.7 us
    ppermute x1, waiting for transfers between devices, swapped(): return lax.ppermute(block, axis, route)  16.4 us
    all_to_all x1, starting transfers between devices, shards(): lax.all_to_all(jnp.broadcast_to(queries[None], (blocks,) + queries.shape)...  8.23 us
    all_to_all x1, starting transfers between devices, shards(): lax.all_to_all(head_terms.reshape(blocks, chunk, -1), 'blk', 0, 0, tiled=...  5.11 us
  transfers between devices with their start and end apart: 5, of which 5 were waited for; matrix products, arithmetic and copies ran while one was open for 5% of the time, Pallas kernels for 0%

profile of v6, /device:TPU:2, one launch (start us, length us, event | category | flops | bytes accessed | tf_op | source)
XLA Modules:
  0.0 216.6 jit_solution(7666936964022526846)
XLA Ops:
  0.0 0.0 copy-start
  0.0 2.0 collective-permute-start
  2.7 4.1 %copy.18 = bf16[256,4096]{1,0:T(8,128)(2,1)} copy(bf16[256,4096]{0,1:T(8,128)(2,1)} %bitcast.36) | data formatting | bytes 4194304 | tf_op jit(solution)/shard_map/dot_general | solution.py:199
  6.8 0.3 multiply_cosine_fusion.1
  7.1 20.7 %collective-permute-done = bf16[256,4096]{1,0:T(8,128)(2,1)} collective-permute-done((bf16[256,4096]{1,0:T(8,128)(2,1)}, bf16[256,4096]{1,0:T(8,128)(2,1)}, u32[]{:S(2)}, u32[]{:S(2)}) %collective-permute-start) | collective-permute-done | bytes 2097184 | tf_op jit(solution)/shard_map/ppermute | solution.py:19
  27.8 0.0 copy-start.4
  27.8 3.9 %fusion.31 = (f32[256,4096]{1,0:T(8,128)}, bf16[256,4096]{1,0:T(8,128)(2,1)S(1)}) fusion(bf16[256,4096]{1,0:T(8,128)(2,1)} %param.10, bf16[256,4096]{1,0:T(8,128)(2,1)} %collective-permute-done, pred[]{:T(512)S(6)} %eq.8), kind=kLoop, calls=%fused_computation.57 | loop fusion | flops 2097152 | bytes 10485761 | tf_op jit(solution)/shard_map/convert_element_type | solution.py:193
  31.7 0.0 copy-start.2
  31.7 0.5 multiply_reduce_fusion
  32.2 0.0 copy-done.4
  32.3 1.8 copy-done.2
  34.1 1.0 fusion.1
  35.1 0.0 copy-done.1
  35.1 0.1 copy.14
  35.2 1.5 broadcast_in_dim.9
  36.8 0.0 copy-start.6
  36.8 8.2 %all-to-all-start = ((bf16[16,256,256]{2,1,0:T(8,128)(2,1)}), bf16[16,256,256]{2,1,0:T(8,128)(2,1)}, u32[]{:S(2)}, u32[]{:S(2)}) async-start(bf16[16,256,256]{2,1,0:T(8,128)(2,1)} %broadcast_in_dim.9), calls=%async_computation | async-start | bytes 4194304 | tf_op jit(solution)/shard_map/all_to_all | solution.py:209
  45.0 0.0 copy-done.6
  45.0 0.7 constant_dynamic-slice_fusion
  45.7 28.4 %all-to-all-done.q_ref = bf16[16,256,256]{2,1,0:T(8,128)(2,1)} async-done(((bf16[16,256,256]{2,1,0:T(8,128)(2,1)}), bf16[16,256,256]{2,1,0:T(8,128)(2,1)}, u32[]{:S(2)}, u32[]{:S(2)}) %all-to-all-start) | async-done | bytes 2097184 | tf_op jit(solution)/shard_map/all_to_all | solution.py:209
  74.1 38.7 %shard_map.100 = bf16[16,264,256]{2,1,0:T(8,128)(2,1)} custom-call(s32[1]{0:T(128)} %bitcast.1.live_ref, bf16[16,256,256]{2,1,0:T(8,128)(2,1)} %all-to-all-done.q_ref, bf16[2048,1024]{1,0:T(8,128)(2,1)} %bitcast.34, bf16[2048,1024]{1,0:T(8,128)(2,1)} %bitcast.35), custom_call_target="tpu_custom_call" | custom-call | tf_op jit(solution)/shard_map/pallas_call | solution.py:119
  112.8 0.0 copy-start.3
  112.8 4.6 %all-to-all-start.1 = ((bf16[16,264,256]{2,1,0:T(8,128)(2,1)}), bf16[16,264,256]{2,1,0:T(8,128)(2,1)}, u32[]{:S(2)}, u32[]{:S(2)}) async-start(bf16[16,264,256]{2,1,0:T(8,128)(2,1)} %shard_map.100), calls=%async_computation.1 | async-start | bytes 4325376 | tf_op jit(solution)/shard_map/all_to_all | solution.py:213
  117.4 0.0 copy-done.3
  117.4 0.0 copy-done.5
  117.4 2.6 %fusion.5 = f32[256,128]{0,1:T(8,128)S(1)} fusion(bf16[1,4096,128]{2,1,0:T(8,128)(2,1)S(1)} %copy-done.3, f32[4096]{0:T(1024)S(1)} %bitcast.45, f32[256]{0:T(256)S(1)} %add_rsqrt_fusion, bf16[256,4096]{1,0:T(8,128)(2,1)} %copy-done.1), kind=kOutput, calls=%fused_computation.12 | convolution fusion | flops 272629760 | bytes 3294208 | tf_op jit(solution)/shard_map/dot_general | solution.py:203
  120.0 0.3 fusion.19
  120.3 2.0 collective-permute-start.1
  122.3 0.1 copy.15
  122.5 0.1 copy.16
  122.6 16.4 %collective-permute-done.1 = bf16[256,128]{0,1:T(8,128)(2,1)S(1)} collective-permute-done((bf16[256,128]{0,1:T(8,128)(2,1)S(1)}, bf16[256,128]{0,1:T(8,128)(2,1)S(1)}, u32[]{:S(2)}, u32[]{:S(2)}) %collective-permute-start.1) | collective-permute-done | bytes 65568 | tf_op jit(solution)/shard_map/ppermute | solution.py:29
  139.0 0.3 fusion.32
  139.3 0.1 fusion.7
  139.4 0.1 add.66
  139.6 0.7 copy.17
  140.2 0.3 fusion.4
  140.5 0.7 reshape.158.own_out_ref
  141.2 3.8 %all-to-all-done.1.parts_ref = bf16[16,264,256]{2,1,0:T(8,128)(2,1)} async-done(((bf16[16,264,256]{2,1,0:T(8,128)(2,1)}), bf16[16,264,256]{2,1,0:T(8,128)(2,1)}, u32[]{:S(2)}, u32[]{:S(2)}) %all-to-all-start.1) | async-done | bytes 2162720 | tf_op jit(solution)/shard_map/all_to_all | solution.py:213
  145.0 3.9 %shard_map.101 = bf16[256,256]{1,0:T(8,128)(2,1)} custom-call(bf16[16,264,256]{2,1,0:T(8,128)(2,1)} %all-to-all-done.1.parts_ref, bf16[256,256]{1,0:T(8,128)(2,1)} %reshape.158.own_out_ref, f32[2,256]{1,0:T(2,128)} %bitcast.42), custom_call_target="tpu_custom_call" | custom-call | tf_op jit(solution)/shard_map/pallas_call | solution.py:166
  149.0 0.0 copy-done
  149.0 2.9 %convolution_convert_fusion = bf16[256,4096]{1,0:T(8,128)(2,1)} fusion(bf16[256,256]{1,0:T(8,128)(2,1)} %shard_map.101, bf16[1,256,4096]{2,1,0:T(8,128)(2,1)S(1)} %copy-done), kind=kOutput, calls=%fused_computation | convolution fusion | flops 537919488 | bytes 4325376 | tf_op jit(solution)/shard_map/dot_general | solution.py:221
  151.9 5.1 %all-to-all-start.2 = ((bf16[16,16,4096]{2,1,0:T(8,128)(2,1)}), bf16[16,16,4096]{2,1,0:T(8,128)(2,1)}, u32[]{:S(2)}, u32[]{:S(2)}) async-start(bf16[16,16,4096]{2,1,0:T(8,128)(2,1)} %bitcast.32), calls=%async_computation.2 | async-start | bytes 4194304 | tf_op jit(solution)/shard_map/all_to_all | solution.py:223
  157.0 26.3 %all-to-all-done.2 = bf16[16,16,4096]{2,1,0:T(8,128)(2,1)} async-done(((bf16[16,16,4096]{2,1,0:T(8,128)(2,1)}), bf16[16,16,4096]{2,1,0:T(8,128)(2,1)}, u32[]{:S(2)}, u32[]{:S(2)}) %all-to-all-start.2) | async-done | bytes 2097184 | tf_op jit(solution)/shard_map/all_to_all | solution.py:223
  183.3 1.9 convert_reduce_fusion
  185.2 1.0 add_convert_fusion
  186.2 0.2 broadcast_in_dim.12
  186.5 28.8 %all_to_all.20 = bf16[16,16,4096]{2,1,0:T(8,128)(2,1)S(1)} all-to-all(bf16[16,16,4096]{2,1,0:T(8,128)(2,1)S(1)} %broadcast_in_dim.12), channel_id=1, replica_groups=mesh['segment'=8,'blk'=16] {'blk'}, dimensions={0} | all-to-all | bytes 4194304 | tf_op jit(solution)/shard_map/all_to_all | solution.py:228
  215.3 1.3 copy.21
  (10 shorter events, 0.1 us)
Async XLA Ops:
  0.0 149.0 %copy-start = (bf16[1,256,4096]{2,1,0:T(8,128)(2,1)S(1)}, bf16[1,256,4096]{2,1,0:T(8,128)(2,1)}, u32[]{:S(2)}) copy-start(bf16[1,256,4096]{2,1,0:T(8,128)(2,1)} %param.17) | copy-start | bytes 6291460
  0.0 27.8 %collective-permute-start = (bf16[256,4096]{1,0:T(8,128)(2,1)}, bf16[256,4096]{1,0:T(8,128)(2,1)}, u32[]{:S(2)}, u32[]{:S(2)}) collective-permute-start(bf16[256,4096]{1,0:T(8,128)(2,1)} %bitcast.43), channel_id=1, source_target_pairs={{0,16},{16,32},{32,48},{48,64},{64,80},{80,96},{96,112},{1,17},{17... | collective-permute-start | bytes 6291464 | tf_op jit(solution)/shard_map/ppermute | solution.py:19
  27.8 4.5 %copy-start.4 = (f32[1,4096]{1,0:T(1,128)S(1)}, f32[1,4096]{1,0:T(1,128)}, u32[]{:S(2)}) copy-start(f32[1,4096]{1,0:T(1,128)} %param.14) | copy-start | bytes 49156
  31.7 3.3 %copy-start.1 = (bf16[256,4096]{1,0:T(8,128)(2,1)}, bf16[256,4096]{1,0:T(8,128)(2,1)S(1)}, u32[]{:S(2)}) copy-start(bf16[256,4096]{1,0:T(8,128)(2,1)S(1)} %get-tuple-element.6) | copy-start | bytes 6291460
  31.7 2.3 %copy-start.2 = (bf16[256,4096]{1,0:T(8,128)(2,1)S(1)}, bf16[256,4096]{1,0:T(8,128)(2,1)}, u32[]{:S(2)}) copy-start(bf16[256,4096]{1,0:T(8,128)(2,1)} %copy.18) | copy-start | bytes 6291460
  36.8 8.2 %copy-start.6 = (s32[1,16]{1,0:T(1,128)S(1)}, s32[1,16]{1,0:T(1,128)}, u32[]{:S(2)}) copy-start(s32[1,16]{1,0:T(1,128)} %param.13) | copy-start | bytes 196
  36.8 37.3 %all-to-all-start = ((bf16[16,256,256]{2,1,0:T(8,128)(2,1)}), bf16[16,256,256]{2,1,0:T(8,128)(2,1)}, u32[]{:S(2)}, u32[]{:S(2)}) async-start(bf16[16,256,256]{2,1,0:T(8,128)(2,1)} %broadcast_in_dim.9), calls=%async_computation | async-start | bytes 4194304 | tf_op jit(solution)/shard_map/all_to_all | solution.py:209
  112.8 4.6 %copy-start.3 = (bf16[1,4096,128]{2,1,0:T(8,128)(2,1)S(1)}, bf16[1,4096,128]{2,1,0:T(8,128)(2,1)}, u32[]{:S(2)}) copy-start(bf16[1,4096,128]{2,1,0:T(8,128)(2,1)} %param.16) | copy-start | bytes 3145732
  112.8 4.6 %copy-start.5 = (f32[1,4096]{1,0:T(1,128)S(1)}, f32[1,4096]{1,0:T(1,128)}, u32[]{:S(2)}) copy-start(f32[1,4096]{1,0:T(1,128)} %param.14) | copy-start | bytes 49156
  112.8 32.2 %all-to-all-start.1 = ((bf16[16,264,256]{2,1,0:T(8,128)(2,1)}), bf16[16,264,256]{2,1,0:T(8,128)(2,1)}, u32[]{:S(2)}, u32[]{:S(2)}) async-start(bf16[16,264,256]{2,1,0:T(8,128)(2,1)} %shard_map.100), calls=%async_computation.1 | async-start | bytes 4325376 | tf_op jit(solution)/shard_map/all_to_all | solution.py:213
  120.3 18.6 %collective-permute-start.1 = (bf16[256,128]{0,1:T(8,128)(2,1)S(1)}, bf16[256,128]{0,1:T(8,128)(2,1)S(1)}, u32[]{:S(2)}, u32[]{:S(2)}) collective-permute-start(bf16[256,128]{0,1:T(8,128)(2,1)S(1)} %fusion.22), channel_id=1, source_target_pairs={{0,1},{1,0},{2,3},{3,2},{4,5},{5,4},{6,7},{7,6},{8,9},{9,8},{10,11... | collective-permute-start | bytes 196616 | tf_op jit(solution)/shard_map/ppermute | solution.py:29
  151.9 31.4 %all-to-all-start.2 = ((bf16[16,16,4096]{2,1,0:T(8,128)(2,1)}), bf16[16,16,4096]{2,1,0:T(8,128)(2,1)}, u32[]{:S(2)}, u32[]{:S(2)}) async-start(bf16[16,16,4096]{2,1,0:T(8,128)(2,1)} %bitcast.32), calls=%async_computation.2 | async-start | bytes 4194304 | tf_op jit(solution)/shard_map/all_to_all | solution.py:223

commit v7 on v6

--- a/solution.py
+++ b/solution.py
@@ -72,7 +72,6 @@
     rows = q_ref.shape[1]
     width = out_ref.shape[2]
     visible = lax.broadcasted_iota(jnp.int32, (1, keys.shape[0]), 1) < live
-    ones = jnp.ones((keys.shape[0], HD), jnp.bfloat16)
     for src in range(q_ref.shape[0]):
         log_rows = []
         for h in range(q_ref.shape[2] // HD):
@@ -82,9 +81,9 @@
             ) * HD ** (-0.5)
             scores = jnp.where(visible, scores, -jnp.inf)
             highest = jnp.max(scores, axis=-1, keepdims=True)
-            weights = jnp.exp(scores - highest).astype(jnp.bfloat16)
-            totals = jnp.dot(weights, ones, preferred_element_type=jnp.float32)[:, 0:1]
-            part = jnp.dot(weights, values, preferred_element_type=jnp.float32)
+            weights = jnp.exp(scores - highest)
+            totals = jnp.sum(weights, axis=-1, keepdims=True)
+            part = jnp.dot(weights.astype(jnp.bfloat16), values, preferred_element_type=jnp.float32)
             out_ref[src, :rows, h * HD:(h + 1) * HD] = (part / totals).astype(out_ref.dtype)
             log_col = jnp.broadcast_to(highest + jnp.log(totals), (rows, HD))
             rest = jnp.transpose(log_col)[0:1, :]
@@ -223,7 +222,7 @@
     gathered_terms = lax.all_to_all(
         head_terms.reshape(blocks, chunk, -1), "blk", 0, 0, tiled=True
     )
-    own_rows = lax.dynamic_slice_in_dim(widened, position * chunk, chunk, 0)
+    own_rows = lax.dynamic_slice_in_dim(current, position * chunk, chunk, 0).astype(jnp.float32)
     mixed_rows = (own_rows + jnp.sum(gathered_terms.astype(jnp.float32), axis=0)).astype(jnp.bfloat16)
     mixed = lax.all_to_all(
         jnp.broadcast_to(mixed_rows[None], (blocks,) + mixed_rows.shape), "blk", 0, 0, tiled=True

time: 217 us -> 207 us (0.954)
  Pallas kernels: 42.6 us -> 35.6 us
    pallas_call x1, Pallas kernels: 38.7 us -> 31.7 us  [cache_attention(): pl.pallas_call(cache_kernel, grid_spec=grid_spec, out_shape=jax.ShapeDtyp...]
    convert_element_type x1 -> x0, other arithmetic: 3.95 us -> none  [shards(): widened = current.astype(jnp.float32)]
where the time goes in v7:
time: 207 us; the launch traced here: 206 us
  waiting for transfers between devices  95.8 us (46%)
  Pallas kernels  35.6 us (17%)
  blocking collectives  28.8 us (14%)
  starting transfers between devices  21.8 us (11%)
  local copies, waits for them, and re-layouts  10.1 us (5%)
  matrix products  7 us (3%)
  other arithmetic  6.24 us (3%)
    pallas_call x1, Pallas kernels, cache_attention(): pl.pallas_call(cache_kernel, grid_spec=grid_spec, out_shape=jax.ShapeDtyp...  31.7 us
    all_to_all x1, blocking collectives, shards(): lax.all_to_all(jnp.broadcast_to(mixed_rows[None], (blocks,) + mixed_rows....  28.8 us
    all_to_all x1, waiting for transfers between devices, shards(): lax.all_to_all(jnp.broadcast_to(queries[None], (blocks,) + queries.shape)...  28.4 us
    all_to_all x1, waiting for transfers between devices, shards(): lax.all_to_all(head_terms.reshape(blocks, chunk, -1), 'blk', 0, 0, tiled=...  26.3 us
    ppermute x1, waiting for transfers between devices, passed_along(): return lax.ppermute(block, axis, route)  20.7 us
    ppermute x1, waiting for transfers between devices, swapped(): return lax.ppermute(block, axis, route)  16.5 us
    all_to_all x1, starting transfers between devices, shards(): lax.all_to_all(jnp.broadcast_to(queries[None], (blocks,) + queries.shape)...  8.23 us
    all_to_all x1, starting transfers between devices, shards(): lax.all_to_all(head_terms.reshape(blocks, chunk, -1), 'blk', 0, 0, tiled=...  5.11 us
  transfers between devices with their start and end apart: 5, of which 5 were waited for; matrix products, arithmetic and copies ran while one was open for 5% of the time, Pallas kernels for 0%

profile of v7, /device:TPU:2, one launch (start us, length us, event | category | flops | bytes accessed | tf_op | source)
XLA Modules:
  0.0 206.2 jit_solution(444189619047906099)
XLA Ops:
  0.0 0.0 copy-start
  0.0 2.0 collective-permute-start
  2.7 4.1 %copy.18 = bf16[256,4096]{1,0:T(8,128)(2,1)} copy(bf16[256,4096]{0,1:T(8,128)(2,1)} %bitcast.36) | data formatting | bytes 4194304 | tf_op jit(solution)/shard_map/dot_general | solution.py:198
  6.8 0.3 multiply_cosine_fusion.1
  7.1 0.0 copy-start.2
  7.1 0.0 copy-start.4
  7.1 20.7 %collective-permute-done = bf16[256,4096]{1,0:T(8,128)(2,1)} collective-permute-done((bf16[256,4096]{1,0:T(8,128)(2,1)}, bf16[256,4096]{1,0:T(8,128)(2,1)}, u32[]{:S(2)}, u32[]{:S(2)}) %collective-permute-start) | collective-permute-done | bytes 2097184 | tf_op jit(solution)/shard_map/ppermute | solution.py:19
  27.8 2.5 %fusion = (f32[256]{0:T(256)S(1)}, bf16[256,4096]{1,0:T(8,128)(2,1)S(1)}) fusion(bf16[256,4096]{1,0:T(8,128)(2,1)} %param.10, bf16[256,4096]{1,0:T(8,128)(2,1)} %collective-permute-done, pred[]{:T(512)S(6)} %eq.8), kind=kLoop, calls=%fused_computation.3 | loop fusion | flops 4194048 | bytes 6292481 | tf_op jit(solution)/shard_map/reduce_sum | solution.py:195
  30.3 0.0 copy-start.1
  30.4 0.0 copy-done.2
  30.4 0.0 copy-done.4
  30.4 0.9 fusion.4
  31.3 0.4 copy-done.1
  31.8 0.1 copy.14
  31.9 1.5 broadcast_in_dim.9
  33.4 0.0 copy-start.6
  33.4 8.2 %all-to-all-start = ((bf16[16,256,256]{2,1,0:T(8,128)(2,1)}), bf16[16,256,256]{2,1,0:T(8,128)(2,1)}, u32[]{:S(2)}, u32[]{:S(2)}) async-start(bf16[16,256,256]{2,1,0:T(8,128)(2,1)} %broadcast_in_dim.9), calls=%async_computation | async-start | bytes 4194304 | tf_op jit(solution)/shard_map/all_to_all | solution.py:208
  41.6 0.0 copy-done.6
  41.6 0.7 constant_dynamic-slice_fusion
  42.3 28.4 %all-to-all-done.q_ref = bf16[16,256,256]{2,1,0:T(8,128)(2,1)} async-done(((bf16[16,256,256]{2,1,0:T(8,128)(2,1)}), bf16[16,256,256]{2,1,0:T(8,128)(2,1)}, u32[]{:S(2)}, u32[]{:S(2)}) %all-to-all-start) | async-done | bytes 2097184 | tf_op jit(solution)/shard_map/all_to_all | solution.py:208
  70.7 31.7 %shard_map.100 = bf16[16,264,256]{2,1,0:T(8,128)(2,1)} custom-call(s32[1]{0:T(128)} %bitcast.1.live_ref, bf16[16,256,256]{2,1,0:T(8,128)(2,1)} %all-to-all-done.q_ref, bf16[2048,1024]{1,0:T(8,128)(2,1)} %bitcast.34, bf16[2048,1024]{1,0:T(8,128)(2,1)} %bitcast.35), custom_call_target="tpu_custom_call" | custom-call | tf_op jit(solution)/shard_map/pallas_call | solution.py:118
  102.4 0.0 copy-start.3
  102.4 4.6 %all-to-all-start.1 = ((bf16[16,264,256]{2,1,0:T(8,128)(2,1)}), bf16[16,264,256]{2,1,0:T(8,128)(2,1)}, u32[]{:S(2)}, u32[]{:S(2)}) async-start(bf16[16,264,256]{2,1,0:T(8,128)(2,1)} %shard_map.100), calls=%async_computation.1 | async-start | bytes 4325376 | tf_op jit(solution)/shard_map/all_to_all | solution.py:212
  107.0 0.0 copy-done.3
  107.0 0.0 copy-done.5
  107.0 2.6 %fusion.8 = f32[256,128]{0,1:T(8,128)S(1)} fusion(bf16[1,4096,128]{2,1,0:T(8,128)(2,1)S(1)} %copy-done.3, bf16[256,4096]{1,0:T(8,128)(2,1)} %copy-done.1, f32[4096]{0:T(1024)S(1)} %bitcast.45, f32[256]{0:T(256)S(1)} %add_rsqrt_fusion), kind=kOutput, calls=%fused_computation.15 | convolution fusion | flops 272629760 | bytes 3294208 | tf_op jit(solution)/shard_map/dot_general | solution.py:202
  109.6 0.3 fusion.24
  109.9 1.8 collective-permute-start.1
  111.8 0.1 copy.15
  111.9 0.1 copy.16
  112.0 16.5 %collective-permute-done.1 = bf16[256,128]{0,1:T(8,128)(2,1)S(1)} collective-permute-done((bf16[256,128]{0,1:T(8,128)(2,1)S(1)}, bf16[256,128]{0,1:T(8,128)(2,1)S(1)}, u32[]{:S(2)}, u32[]{:S(2)}) %collective-permute-start.1) | collective-permute-done | bytes 65568 | tf_op jit(solution)/shard_map/ppermute | solution.py:29
  128.5 0.3 fusion.36
  128.8 0.1 fusion.12
  128.9 0.3 fusion.7
  129.2 0.7 reshape.158.own_out_ref
  129.9 0.1 add.66
  130.1 0.7 copy.17
  130.7 3.9 %all-to-all-done.1.parts_ref = bf16[16,264,256]{2,1,0:T(8,128)(2,1)} async-done(((bf16[16,264,256]{2,1,0:T(8,128)(2,1)}), bf16[16,264,256]{2,1,0:T(8,128)(2,1)}, u32[]{:S(2)}, u32[]{:S(2)}) %all-to-all-start.1) | async-done | bytes 2162720 | tf_op jit(solution)/shard_map/all_to_all | solution.py:212
  134.6 3.9 %shard_map.101 = bf16[256,256]{1,0:T(8,128)(2,1)} custom-call(bf16[16,264,256]{2,1,0:T(8,128)(2,1)} %all-to-all-done.1.parts_ref, bf16[256,256]{1,0:T(8,128)(2,1)} %reshape.158.own_out_ref, f32[2,256]{1,0:T(2,128)} %bitcast.42), custom_call_target="tpu_custom_call" | custom-call | tf_op jit(solution)/shard_map/pallas_call | solution.py:165
  138.6 0.0 copy-done
  138.6 2.9 %convolution_convert_fusion = bf16[256,4096]{1,0:T(8,128)(2,1)} fusion(bf16[256,256]{1,0:T(8,128)(2,1)} %shard_map.101, bf16[1,256,4096]{2,1,0:T(8,128)(2,1)S(1)} %copy-done), kind=kOutput, calls=%fused_computation.2 | convolution fusion | flops 537919488 | bytes 4325376 | tf_op jit(solution)/shard_map/dot_general | solution.py:220
  141.5 5.1 %all-to-all-start.2 = ((bf16[16,16,4096]{2,1,0:T(8,128)(2,1)}), bf16[16,16,4096]{2,1,0:T(8,128)(2,1)}, u32[]{:S(2)}, u32[]{:S(2)}) async-start(bf16[16,16,4096]{2,1,0:T(8,128)(2,1)} %bitcast.32), calls=%async_computation.2 | async-start | bytes 4194304 | tf_op jit(solution)/shard_map/all_to_all | solution.py:222
  146.6 26.3 %all-to-all-done.2 = bf16[16,16,4096]{2,1,0:T(8,128)(2,1)} async-done(((bf16[16,16,4096]{2,1,0:T(8,128)(2,1)}), bf16[16,16,4096]{2,1,0:T(8,128)(2,1)}, u32[]{:S(2)}, u32[]{:S(2)}) %all-to-all-start.2) | async-done | bytes 2097184 | tf_op jit(solution)/shard_map/all_to_all | solution.py:222
  173.0 1.9 convert_reduce_fusion
  174.9 0.9 add_convert_fusion
  175.8 0.2 broadcast_in_dim.12
  176.1 28.8 %all_to_all.20 = bf16[16,16,4096]{2,1,0:T(8,128)(2,1)S(1)} all-to-all(bf16[16,16,4096]{2,1,0:T(8,128)(2,1)S(1)} %broadcast_in_dim.12), channel_id=1, replica_groups=mesh['segment'=8,'blk'=16] {'blk'}, dimensions={0} | all-to-all | bytes 4194304 | tf_op jit(solution)/shard_map/all_to_all | solution.py:227
  204.8 1.3 copy.21
  (9 shorter events, 0.1 us)
Async XLA Ops:
  0.0 138.6 %copy-start = (bf16[1,256,4096]{2,1,0:T(8,128)(2,1)S(1)}, bf16[1,256,4096]{2,1,0:T(8,128)(2,1)}, u32[]{:S(2)}) copy-start(bf16[1,256,4096]{2,1,0:T(8,128)(2,1)} %param.17) | copy-start | bytes 6291460
  0.0 27.8 %collective-permute-start = (bf16[256,4096]{1,0:T(8,128)(2,1)}, bf16[256,4096]{1,0:T(8,128)(2,1)}, u32[]{:S(2)}, u32[]{:S(2)}) collective-permute-start(bf16[256,4096]{1,0:T(8,128)(2,1)} %bitcast.43), channel_id=1, source_target_pairs={{0,16},{16,32},{32,48},{48,64},{64,80},{80,96},{96,112},{1,17},{17... | collective-permute-start | bytes 6291464 | tf_op jit(solution)/shard_map/ppermute | solution.py:19
  7.1 23.3 %copy-start.2 = (bf16[256,4096]{1,0:T(8,128)(2,1)S(1)}, bf16[256,4096]{1,0:T(8,128)(2,1)}, u32[]{:S(2)}) copy-start(bf16[256,4096]{1,0:T(8,128)(2,1)} %copy.18) | copy-start | bytes 6291460
  7.1 23.3 %copy-start.4 = (f32[1,4096]{1,0:T(1,128)S(1)}, f32[1,4096]{1,0:T(1,128)}, u32[]{:S(2)}) copy-start(f32[1,4096]{1,0:T(1,128)} %param.14) | copy-start | bytes 49156
  30.3 1.4 copy-start.1
  33.4 8.2 %copy-start.6 = (s32[1,16]{1,0:T(1,128)S(1)}, s32[1,16]{1,0:T(1,128)}, u32[]{:S(2)}) copy-start(s32[1,16]{1,0:T(1,128)} %param.13) | copy-start | bytes 196
  33.4 37.3 %all-to-all-start = ((bf16[16,256,256]{2,1,0:T(8,128)(2,1)}), bf16[16,256,256]{2,1,0:T(8,128)(2,1)}, u32[]{:S(2)}, u32[]{:S(2)}) async-start(bf16[16,256,256]{2,1,0:T(8,128)(2,1)} %broadcast_in_dim.9), calls=%async_computation | async-start | bytes 4194304 | tf_op jit(solution)/shard_map/all_to_all | solution.py:208
  102.4 4.6 %copy-start.3 = (bf16[1,4096,128]{2,1,0:T(8,128)(2,1)S(1)}, bf16[1,4096,128]{2,1,0:T(8,128)(2,1)}, u32[]{:S(2)}) copy-start(bf16[1,4096,128]{2,1,0:T(8,128)(2,1)} %param.16) | copy-start | bytes 3145732
  102.4 4.6 %copy-start.5 = (f32[1,4096]{1,0:T(1,128)S(1)}, f32[1,4096]{1,0:T(1,128)}, u32[]{:S(2)}) copy-start(f32[1,4096]{1,0:T(1,128)} %param.14) | copy-start | bytes 49156
  102.4 32.2 %all-to-all-start.1 = ((bf16[16,264,256]{2,1,0:T(8,128)(2,1)}), bf16[16,264,256]{2,1,0:T(8,128)(2,1)}, u32[]{:S(2)}, u32[]{:S(2)}) async-start(bf16[16,264,256]{2,1,0:T(8,128)(2,1)} %shard_map.100), calls=%async_computation.1 | async-start | bytes 4325376 | tf_op jit(solution)/shard_map/all_to_all | solution.py:212
  109.9 18.5 %collective-permute-start.1 = (bf16[256,128]{0,1:T(8,128)(2,1)S(1)}, bf16[256,128]{0,1:T(8,128)(2,1)S(1)}, u32[]{:S(2)}, u32[]{:S(2)}) collective-permute-start(bf16[256,128]{0,1:T(8,128)(2,1)S(1)} %fusion.27), channel_id=1, source_target_pairs={{0,1},{1,0},{2,3},{3,2},{4,5},{5,4},{6,7},{7,6},{8,9},{9,8},{10,11... | collective-permute-start | bytes 196616 | tf_op jit(solution)/shard_map/ppermute | solution.py:29
  141.5 31.5 %all-to-all-start.2 = ((bf16[16,16,4096]{2,1,0:T(8,128)(2,1)}), bf16[16,16,4096]{2,1,0:T(8,128)(2,1)}, u32[]{:S(2)}, u32[]{:S(2)}) async-start(bf16[16,16,4096]{2,1,0:T(8,128)(2,1)} %bitcast.32), calls=%async_computation.2 | async-start | bytes 4194304 | tf_op jit(solution)/shard_map/all_to_all | solution.py:222

commit v8 on v7

--- a/solution.py
+++ b/solution.py
@@ -71,30 +71,36 @@
     values = v_ref[...]
     rows = q_ref.shape[1]
     width = out_ref.shape[2]
+    heads_here = q_ref.shape[2] // HD
+    sets = [(src, h) for src in range(q_ref.shape[0]) for h in range(heads_here)]
+    stacked = jnp.concatenate([q_ref[src, :, h * HD:(h + 1) * HD] for src, h in sets], axis=0)
     visible = lax.broadcasted_iota(jnp.int32, (1, keys.shape[0]), 1) < live
-    for src in range(q_ref.shape[0]):
-        log_rows = []
-        for h in range(q_ref.shape[2] // HD):
-            q = q_ref[src, :, h * HD:(h + 1) * HD]
-            scores = lax.dot_general(
-                q, keys, (((1,), (1,)), ((), ())), preferred_element_type=jnp.float32
-            ) * HD ** (-0.5)
-            scores = jnp.where(visible, scores, -jnp.inf)
-            highest = jnp.max(scores, axis=-1, keepdims=True)
-            weights = jnp.exp(scores - highest)
-            totals = jnp.sum(weights, axis=-1, keepdims=True)
-            part = jnp.dot(weights.astype(jnp.bfloat16), values, preferred_element_type=jnp.float32)
-            out_ref[src, :rows, h * HD:(h + 1) * HD] = (part / totals).astype(out_ref.dtype)
-            log_col = jnp.broadcast_to(highest + jnp.log(totals), (rows, HD))
-            rest = jnp.transpose(log_col)[0:1, :]
-            for _ in range(3):
-                piece = rest.astype(jnp.bfloat16).astype(jnp.float32)
-                log_rows.append(piece)
-                rest = rest - piece
+    scores = lax.dot_general(
+        stacked, keys, (((1,), (1,)), ((), ())), preferred_element_type=jnp.float32
+    ) * HD ** (-0.5)
+    scores = jnp.where(visible, scores, -jnp.inf)
+    highest = jnp.max(scores, axis=-1, keepdims=True)
+    weights = jnp.exp(scores - highest)
+    totals = jnp.sum(weights, axis=-1, keepdims=True)
+    part = jnp.dot(weights.astype(jnp.bfloat16), values, preferred_element_type=jnp.float32)
+    normalized = (part / totals).astype(out_ref.dtype)
+    log_totals = highest + jnp.log(totals)
+    log_rows = {}
+    for i, (src, h) in enumerate(sets):
+        out_ref[src, :rows, h * HD:(h + 1) * HD] = normalized[i * rows:(i + 1) * rows]
+        log_col = jnp.broadcast_to(log_totals[i * rows:(i + 1) * rows], (rows, HD))
+        rest = jnp.transpose(log_col)[0:1, :]
+        pieces = []
+        for _ in range(3):
+            piece = rest.astype(jnp.bfloat16).astype(jnp.float32)
+            pieces.append(piece)
+            rest = rest - piece
+        log_rows.setdefault(src, []).extend(pieces)
+    for src, rows_here in log_rows.items():
         if rows < width:
-            log_rows = [jnp.concatenate([r, jnp.zeros((1, width - rows), jnp.float32)], axis=1) for r in log_rows]
-        log_rows += [jnp.zeros((1, width), jnp.float32)] * (out_ref.shape[1] - rows - len(log_rows))
-        out_ref[src, rows:, :] = jnp.concatenate(log_rows, axis=0).astype(out_ref.dtype)
+            rows_here = [jnp.concatenate([r, jnp.zeros((1, width - rows), jnp.float32)], axis=1) for r in rows_here]
+        rows_here = rows_here + [jnp.zeros((1, width), jnp.float32)] * (out_ref.shape[1] - rows - len(rows_here))
+        out_ref[src, rows:, :] = jnp.concatenate(rows_here, axis=0).astype(out_ref.dtype)
 
 
 LOG_ROWS = 8

time: 207 us -> 222 us (1.072)
  Pallas kernels: 35.6 us -> 50.7 us
    pallas_call x1, Pallas kernels: 31.7 us -> 46.8 us  [cache_attention(): pl.pallas_call(cache_kernel, grid_spec=grid_spec, out_shape=jax.ShapeDtyp...]
where the time goes in v8:
time: 222 us; the launch traced here: 221 us
  waiting for transfers between devices  95.6 us (43%)
  Pallas kernels  50.7 us (23%)
  blocking collectives  28.8 us (13%)
  starting transfers between devices  21.9 us (10%)
  local copies, waits for them, and re-layouts  10.1 us (5%)
  matrix products  7.01 us (3%)
  other arithmetic  6.24 us (3%)
    pallas_call x1, Pallas kernels, cache_attention(): pl.pallas_call(cache_kernel, grid_spec=grid_spec, out_shape=jax.ShapeDtyp...  46.8 us
    all_to_all x1, blocking collectives, shards(): lax.all_to_all(jnp.broadcast_to(mixed_rows[None], (blocks,) + mixed_rows....  28.8 us
    all_to_all x1, waiting for transfers between devices, shards(): lax.all_to_all(jnp.broadcast_to(queries[None], (blocks,) + queries.shape)...  28.4 us
    all_to_all x1, waiting for transfers between devices, shards(): lax.all_to_all(head_terms.reshape(blocks, chunk, -1), 'blk', 0, 0, tiled=...  26.3 us
    ppermute x1, waiting for transfers between devices, passed_along(): return lax.ppermute(block, axis, route)  20.7 us
    ppermute x1, waiting for transfers between devices, swapped(): return lax.ppermute(block, axis, route)  16.4 us
    all_to_all x1, starting transfers between devices, shards(): lax.all_to_all(jnp.broadcast_to(queries[None], (blocks,) + queries.shape)...  8.23 us
    all_to_all x1, starting transfers between devices, shards(): lax.all_to_all(head_terms.reshape(blocks, chunk, -1), 'blk', 0, 0, tiled=...  5.1 us
  transfers between devices with their start and end apart: 5, of which 5 were waited for; matrix products, arithmetic and copies ran while one was open for 5% of the time, Pallas kernels for 0%

profile of v8, /device:TPU:2, one launch (start us, length us, event | category | flops | bytes accessed | tf_op | source)
XLA Modules:
  0.0 221.2 jit_solution(10865128788238000051)
XLA Ops:
  0.0 0.0 copy-start
  0.0 2.0 collective-permute-start
  2.7 4.1 %copy.18 = bf16[256,4096]{1,0:T(8,128)(2,1)} copy(bf16[256,4096]{0,1:T(8,128)(2,1)} %bitcast.36) | data formatting | bytes 4194304 | tf_op jit(solution)/shard_map/dot_general | solution.py:204
  6.8 0.3 multiply_cosine_fusion.1
  7.1 0.0 copy-start.2
  7.1 0.0 copy-start.4
  7.1 20.7 %collective-permute-done = bf16[256,4096]{1,0:T(8,128)(2,1)} collective-permute-done((bf16[256,4096]{1,0:T(8,128)(2,1)}, bf16[256,4096]{1,0:T(8,128)(2,1)}, u32[]{:S(2)}, u32[]{:S(2)}) %collective-permute-start) | collective-permute-done | bytes 2097184 | tf_op jit(solution)/shard_map/ppermute | solution.py:19
  27.8 2.5 %fusion = (f32[256]{0:T(256)S(1)}, bf16[256,4096]{1,0:T(8,128)(2,1)S(1)}) fusion(bf16[256,4096]{1,0:T(8,128)(2,1)} %param.10, bf16[256,4096]{1,0:T(8,128)(2,1)} %collective-permute-done, pred[]{:T(512)S(6)} %eq.8), kind=kLoop, calls=%fused_computation.3 | loop fusion | flops 4194048 | bytes 6292481 | tf_op jit(solution)/shard_map/reduce_sum | solution.py:201
  30.3 0.0 copy-start.1
  30.4 0.0 copy-done.2
  30.4 0.0 copy-done.4
  30.4 0.9 fusion.4
  31.3 0.4 copy-done.1
  31.8 0.1 copy.14
  31.9 1.5 broadcast_in_dim.9
  33.4 0.0 copy-start.6
  33.4 8.2 %all-to-all-start = ((bf16[16,256,256]{2,1,0:T(8,128)(2,1)}), bf16[16,256,256]{2,1,0:T(8,128)(2,1)}, u32[]{:S(2)}, u32[]{:S(2)}) async-start(bf16[16,256,256]{2,1,0:T(8,128)(2,1)} %broadcast_in_dim.9), calls=%async_computation | async-start | bytes 4194304 | tf_op jit(solution)/shard_map/all_to_all | solution.py:214
  41.6 0.0 copy-done.6
  41.6 0.7 constant_dynamic-slice_fusion
  42.3 28.4 %all-to-all-done.q_ref = bf16[16,256,256]{2,1,0:T(8,128)(2,1)} async-done(((bf16[16,256,256]{2,1,0:T(8,128)(2,1)}), bf16[16,256,256]{2,1,0:T(8,128)(2,1)}, u32[]{:S(2)}, u32[]{:S(2)}) %all-to-all-start) | async-done | bytes 2097184 | tf_op jit(solution)/shard_map/all_to_all | solution.py:214
  70.7 46.8 %shard_map.100 = bf16[16,264,256]{2,1,0:T(8,128)(2,1)} custom-call(s32[1]{0:T(128)} %bitcast.1.live_ref, bf16[16,256,256]{2,1,0:T(8,128)(2,1)} %all-to-all-done.q_ref, bf16[2048,1024]{1,0:T(8,128)(2,1)} %bitcast.34, bf16[2048,1024]{1,0:T(8,128)(2,1)} %bitcast.35), custom_call_target="tpu_custom_call" | custom-call | tf_op jit(solution)/shard_map/pallas_call | solution.py:124
  117.5 0.0 copy-start.3
  117.5 4.6 %all-to-all-start.1 = ((bf16[16,264,256]{2,1,0:T(8,128)(2,1)}), bf16[16,264,256]{2,1,0:T(8,128)(2,1)}, u32[]{:S(2)}, u32[]{:S(2)}) async-start(bf16[16,264,256]{2,1,0:T(8,128)(2,1)} %shard_map.100), calls=%async_computation.1 | async-start | bytes 4325376 | tf_op jit(solution)/shard_map/all_to_all | solution.py:218
  122.1 0.0 copy-done.3
  122.1 0.0 copy-done.5
  122.1 2.6 %fusion.8 = f32[256,128]{0,1:T(8,128)S(1)} fusion(bf16[1,4096,128]{2,1,0:T(8,128)(2,1)S(1)} %copy-done.3, bf16[256,4096]{1,0:T(8,128)(2,1)} %copy-done.1, f32[4096]{0:T(1024)S(1)} %bitcast.45, f32[256]{0:T(256)S(1)} %add_rsqrt_fusion), kind=kOutput, calls=%fused_computation.15 | convolution fusion | flops 272629760 | bytes 3294208 | tf_op jit(solution)/shard_map/dot_general | solution.py:208
  124.7 0.3 fusion.24
  125.0 2.0 collective-permute-start.1
  127.0 0.1 copy.15
  127.1 0.1 copy.16
  127.3 16.4 %collective-permute-done.1 = bf16[256,128]{0,1:T(8,128)(2,1)S(1)} collective-permute-done((bf16[256,128]{0,1:T(8,128)(2,1)S(1)}, bf16[256,128]{0,1:T(8,128)(2,1)S(1)}, u32[]{:S(2)}, u32[]{:S(2)}) %collective-permute-start.1) | collective-permute-done | bytes 65568 | tf_op jit(solution)/shard_map/ppermute | solution.py:29
  143.7 0.3 fusion.36
  144.0 0.1 fusion.12
  144.1 0.3 fusion.7
  144.4 0.7 reshape.158.own_out_ref
  145.1 0.1 add.66
  145.3 0.7 copy.17
  145.9 3.8 %all-to-all-done.1.parts_ref = bf16[16,264,256]{2,1,0:T(8,128)(2,1)} async-done(((bf16[16,264,256]{2,1,0:T(8,128)(2,1)}), bf16[16,264,256]{2,1,0:T(8,128)(2,1)}, u32[]{:S(2)}, u32[]{:S(2)}) %all-to-all-start.1) | async-done | bytes 2162720 | tf_op jit(solution)/shard_map/all_to_all | solution.py:218
  149.7 3.9 %shard_map.101 = bf16[256,256]{1,0:T(8,128)(2,1)} custom-call(bf16[16,264,256]{2,1,0:T(8,128)(2,1)} %all-to-all-done.1.parts_ref, bf16[256,256]{1,0:T(8,128)(2,1)} %reshape.158.own_out_ref, f32[2,256]{1,0:T(2,128)} %bitcast.42), custom_call_target="tpu_custom_call" | custom-call | tf_op jit(solution)/shard_map/pallas_call | solution.py:171
  153.7 0.0 copy-done
  153.7 2.9 %convolution_convert_fusion = bf16[256,4096]{1,0:T(8,128)(2,1)} fusion(bf16[256,256]{1,0:T(8,128)(2,1)} %shard_map.101, bf16[1,256,4096]{2,1,0:T(8,128)(2,1)S(1)} %copy-done), kind=kOutput, calls=%fused_computation.2 | convolution fusion | flops 537919488 | bytes 4325376 | tf_op jit(solution)/shard_map/dot_general | solution.py:226
  156.6 5.1 %all-to-all-start.2 = ((bf16[16,16,4096]{2,1,0:T(8,128)(2,1)}), bf16[16,16,4096]{2,1,0:T(8,128)(2,1)}, u32[]{:S(2)}, u32[]{:S(2)}) async-start(bf16[16,16,4096]{2,1,0:T(8,128)(2,1)} %bitcast.32), calls=%async_computation.2 | async-start | bytes 4194304 | tf_op jit(solution)/shard_map/all_to_all | solution.py:228
  161.7 26.3 %all-to-all-done.2 = bf16[16,16,4096]{2,1,0:T(8,128)(2,1)} async-done(((bf16[16,16,4096]{2,1,0:T(8,128)(2,1)}), bf16[16,16,4096]{2,1,0:T(8,128)(2,1)}, u32[]{:S(2)}, u32[]{:S(2)}) %all-to-all-start.2) | async-done | bytes 2097184 | tf_op jit(solution)/shard_map/all_to_all | solution.py:228
  188.0 1.9 convert_reduce_fusion
  189.9 0.9 add_convert_fusion
  190.9 0.2 broadcast_in_dim.12
  191.1 28.8 %all_to_all.20 = bf16[16,16,4096]{2,1,0:T(8,128)(2,1)S(1)} all-to-all(bf16[16,16,4096]{2,1,0:T(8,128)(2,1)S(1)} %broadcast_in_dim.12), channel_id=1, replica_groups=mesh['segment'=8,'blk'=16] {'blk'}, dimensions={0} | all-to-all | bytes 4194304 | tf_op jit(solution)/shard_map/all_to_all | solution.py:233
  219.9 1.3 copy.21
  (9 shorter events, 0.1 us)
Async XLA Ops:
  0.0 153.7 %copy-start = (bf16[1,256,4096]{2,1,0:T(8,128)(2,1)S(1)}, bf16[1,256,4096]{2,1,0:T(8,128)(2,1)}, u32[]{:S(2)}) copy-start(bf16[1,256,4096]{2,1,0:T(8,128)(2,1)} %param.17) | copy-start | bytes 6291460
  0.0 27.8 %collective-permute-start = (bf16[256,4096]{1,0:T(8,128)(2,1)}, bf16[256,4096]{1,0:T(8,128)(2,1)}, u32[]{:S(2)}, u32[]{:S(2)}) collective-permute-start(bf16[256,4096]{1,0:T(8,128)(2,1)} %bitcast.43), channel_id=1, source_target_pairs={{0,16},{16,32},{32,48},{48,64},{64,80},{80,96},{96,112},{1,17},{17... | collective-permute-start | bytes 6291464 | tf_op jit(solution)/shard_map/ppermute | solution.py:19
  7.1 23.3 %copy-start.2 = (bf16[256,4096]{1,0:T(8,128)(2,1)S(1)}, bf16[256,4096]{1,0:T(8,128)(2,1)}, u32[]{:S(2)}) copy-start(bf16[256,4096]{1,0:T(8,128)(2,1)} %copy.18) | copy-start | bytes 6291460
  7.1 23.3 %copy-start.4 = (f32[1,4096]{1,0:T(1,128)S(1)}, f32[1,4096]{1,0:T(1,128)}, u32[]{:S(2)}) copy-start(f32[1,4096]{1,0:T(1,128)} %param.14) | copy-start | bytes 49156
  30.3 1.4 copy-start.1
  33.4 8.2 %copy-start.6 = (s32[1,16]{1,0:T(1,128)S(1)}, s32[1,16]{1,0:T(1,128)}, u32[]{:S(2)}) copy-start(s32[1,16]{1,0:T(1,128)} %param.13) | copy-start | bytes 196
  33.4 37.3 %all-to-all-start = ((bf16[16,256,256]{2,1,0:T(8,128)(2,1)}), bf16[16,256,256]{2,1,0:T(8,128)(2,1)}, u32[]{:S(2)}, u32[]{:S(2)}) async-start(bf16[16,256,256]{2,1,0:T(8,128)(2,1)} %broadcast_in_dim.9), calls=%async_computation | async-start | bytes 4194304 | tf_op jit(solution)/shard_map/all_to_all | solution.py:214
  117.5 4.6 %copy-start.3 = (bf16[1,4096,128]{2,1,0:T(8,128)(2,1)S(1)}, bf16[1,4096,128]{2,1,0:T(8,128)(2,1)}, u32[]{:S(2)}) copy-start(bf16[1,4096,128]{2,1,0:T(8,128)(2,1)} %param.16) | copy-start | bytes 3145732
  117.5 4.6 %copy-start.5 = (f32[1,4096]{1,0:T(1,128)S(1)}, f32[1,4096]{1,0:T(1,128)}, u32[]{:S(2)}) copy-start(f32[1,4096]{1,0:T(1,128)} %param.14) | copy-start | bytes 49156
  117.5 32.2 %all-to-all-start.1 = ((bf16[16,264,256]{2,1,0:T(8,128)(2,1)}), bf16[16,264,256]{2,1,0:T(8,128)(2,1)}, u32[]{:S(2)}, u32[]{:S(2)}) async-start(bf16[16,264,256]{2,1,0:T(8,128)(2,1)} %shard_map.100), calls=%async_computation.1 | async-start | bytes 4325376 | tf_op jit(solution)/shard_map/all_to_all | solution.py:218
  125.0 18.6 %collective-permute-start.1 = (bf16[256,128]{0,1:T(8,128)(2,1)S(1)}, bf16[256,128]{0,1:T(8,128)(2,1)S(1)}, u32[]{:S(2)}, u32[]{:S(2)}) collective-permute-start(bf16[256,128]{0,1:T(8,128)(2,1)S(1)} %fusion.27), channel_id=1, source_target_pairs={{0,1},{1,0},{2,3},{3,2},{4,5},{5,4},{6,7},{7,6},{8,9},{9,8},{10,11... | collective-permute-start | bytes 196616 | tf_op jit(solution)/shard_map/ppermute | solution.py:29
  156.6 31.4 %all-to-all-start.2 = ((bf16[16,16,4096]{2,1,0:T(8,128)(2,1)}), bf16[16,16,4096]{2,1,0:T(8,128)(2,1)}, u32[]{:S(2)}, u32[]{:S(2)}) async-start(bf16[16,16,4096]{2,1,0:T(8,128)(2,1)} %bitcast.32), calls=%async_computation.2 | async-start | bytes 4194304 | tf_op jit(solution)/shard_map/all_to_all | solution.py:228

commit v9 on v7

--- a/solution.py
+++ b/solution.py
@@ -122,7 +122,17 @@
     )(live, every_query, cached_keys, cached_values)
 
 
-def combine_kernel(parts_ref, own_out_ref, own_log_ref, out_ref):
+def combine_kernel(parts_ref, own_out_ref, own_log_ref, weight_ref, out_ref, attended_ref):
+    @pl.when(pl.program_id(0) == 0)
+    def _():
+        combine_into(parts_ref, own_out_ref, own_log_ref, attended_ref)
+
+    out_ref[...] = jnp.dot(
+        attended_ref[...], weight_ref[...], preferred_element_type=jnp.float32
+    ).astype(out_ref.dtype)
+
+
+def combine_into(parts_ref, own_out_ref, own_log_ref, out_ref):
     sources = parts_ref.shape[0]
     rows = out_ref.shape[0]
     heads_here = out_ref.shape[1] // HD
@@ -161,11 +171,54 @@
         out_ref[:, h * HD:(h + 1) * HD] = (weighted / total).astype(out_ref.dtype)
 
 
-def combine(arrived_parts, own_out, own_log):
+COLUMN_BLOCK = 1024
+
+
+def combine(arrived_parts, own_out, own_log, out_weight):
+    sources, packed_rows, width = arrived_parts.shape
+    rows = own_out.shape[0]
+    columns = out_weight.shape[1]
     return pl.pallas_call(
         combine_kernel,
-        out_shape=jax.ShapeDtypeStruct(own_out.shape, jnp.bfloat16),
-    )(arrived_parts, own_out, own_log)
+        grid=(columns // COLUMN_BLOCK,),
+        in_specs=[
+            pl.BlockSpec((sources, packed_rows, width), lambda j: (0, 0, 0)),
+            pl.BlockSpec(own_out.shape, lambda j: (0, 0)),
+            pl.BlockSpec(own_log.shape, lambda j: (0, 0)),
+            pl.BlockSpec((out_weight.shape[0], COLUMN_BLOCK), lambda j: (0, j)),
+        ],
+        out_specs=pl.BlockSpec((rows, COLUMN_BLOCK), lambda j: (0, j)),
+        out_shape=jax.ShapeDtypeStruct((rows, columns), jnp.bfloat16),
+        scratch_shapes=[pltpu.VMEM(own_out.shape, jnp.bfloat16)],
+        compiler_params=pltpu.CompilerParams(dimension_semantics=("arbitrary",)),
+    )(arrived_parts, own_out, own_log, out_weight)
+
+
+def residual_kernel(position_ref, terms_ref, current_ref, out_ref):
+    total = terms_ref[0].astype(jnp.float32)
+    for n in range(1, terms_ref.shape[0]):
+        total = total + terms_ref[n].astype(jnp.float32)
+    mixed = (current_ref[...].astype(jnp.float32) + total).astype(out_ref.dtype)
+    for n in range(out_ref.shape[0]):
+        out_ref[n] = mixed
+
+
+def residual(position, gathered_terms, current):
+    sources, chunk, width = gathered_terms.shape
+    grid_spec = pltpu.PrefetchScalarGridSpec(
+        num_scalar_prefetch=1,
+        grid=(1,),
+        in_specs=[
+            pl.BlockSpec((sources, chunk, width), lambda i, pos: (0, 0, 0)),
+            pl.BlockSpec((chunk, width), lambda i, pos: (pos[0], 0)),
+        ],
+        out_specs=pl.BlockSpec((sources, chunk, width), lambda i, pos: (0, 0, 0)),
+    )
+    return pl.pallas_call(
+        residual_kernel,
+        grid_spec=grid_spec,
+        out_shape=jax.ShapeDtypeStruct((sources, chunk, width), jnp.bfloat16),
+    )(position, gathered_terms, current)
 
 
 def shards(
@@ -216,17 +269,13 @@
     own_out, own_log = attend_rows(query_rows, own_keys, own_values, causal)
     own_out = own_out.reshape(span_rows, heads_here * HD)
     own_log = own_log.reshape(span_rows, heads_here).T
-    attended = combine(arrived_parts, own_out, own_log)
-    head_terms = jnp.dot(attended, w_out[0], preferred_element_type=jnp.float32).astype(jnp.bfloat16)
+    head_terms = combine(arrived_parts, own_out, own_log, w_out[0])
     chunk = span_rows // blocks
     gathered_terms = lax.all_to_all(
         head_terms.reshape(blocks, chunk, -1), "blk", 0, 0, tiled=True
     )
-    own_rows = lax.dynamic_slice_in_dim(current, position * chunk, chunk, 0).astype(jnp.float32)
-    mixed_rows = (own_rows + jnp.sum(gathered_terms.astype(jnp.float32), axis=0)).astype(jnp.bfloat16)
-    mixed = lax.all_to_all(
-        jnp.broadcast_to(mixed_rows[None], (blocks,) + mixed_rows.shape), "blk", 0, 0, tiled=True
-    ).reshape(span_rows, -1)
+    spread = residual(position.reshape(1), gathered_terms, current)
+    mixed = lax.all_to_all(spread, "blk", 0, 0, tiled=True).reshape(span_rows, -1)
     return mixed[None]
 
 

time: 207 us -> 206 us (level)
  blocking collectives: 28.8 us -> 57.4 us
  waiting for transfers between devices: 95.8 us -> 67.4 us
  Pallas kernels: 35.6 us -> 41.5 us
  starting transfers between devices: 21.8 us -> 16.1 us
  local copies, waits for them, and re-layouts: 10.1 us -> 13.2 us
  other arithmetic: 6.24 us -> 3.38 us
    all_to_all x1 -> x2, blocking collectives: 28.8 us -> 57.4 us  [the longest x1 31 us: shards(): lax.all_to_all(head_terms.reshape(blocks, chunk, -1), 'blk', 0, 0, tiled=...]
    all_to_all x1 -> x0, waiting for transfers between devices: 26.3 us -> none  [shards(): lax.all_to_all(head_terms.reshape(blocks, chunk, -1), 'blk', 0, 0, tiled=...]
    pallas_call x1 -> x2, Pallas kernels: 3.92 us -> 9.92 us  [the longest x1 6.65 us: combine(): pl.pallas_call(combine_kernel, grid=(columns // COLUMN_BLOCK,), in_specs=...]
    all_to_all x1 -> x0, starting transfers between devices: 5.11 us -> none  [shards(): lax.all_to_all(head_terms.reshape(blocks, chunk, -1), 'blk', 0, 0, tiled=...]
    dot_general x1 -> x0, matrix products: 2.94 us -> none  [shards(): jnp.dot(attended, w_out[0], preferred_element_type=jnp.float32)]
    unnamed x15 -> x17, local copies, waits for them, and re-layouts: 1.77 us -> 4.42 us
  transfers between devices with their start and end apart: 5 -> 4, of which waited for: 5 -> 4; matrix products, arithmetic and copies ran while one was open for 5% -> 6% of each run, Pallas kernels for 0% -> 0%
where the time goes in v9:
time: 206 us
  waiting for transfers between devices  67.4 us (33%)
  blocking collectives  57.4 us (28%)
  Pallas kernels  41.5 us (20%)
  starting transfers between devices  16.1 us (8%)
  local copies, waits for them, and re-layouts  13.2 us (6%)
  matrix products  5.79 us (3%)
  other arithmetic  3.38 us (2%)
    pallas_call x1, Pallas kernels, cache_attention(): pl.pallas_call(cache_kernel, grid_spec=grid_spec, out_shape=jax.ShapeDtyp...  31.5 us
    all_to_all x1, blocking collectives, shards(): lax.all_to_all(head_terms.reshape(blocks, chunk, -1), 'blk', 0, 0, tiled=...  31 us
    all_to_all x1, waiting for transfers between devices, shards(): lax.all_to_all(jnp.broadcast_to(queries[None], (blocks,) + queries.shape)...  28.5 us
    all_to_all x1, blocking collectives, shards(): lax.all_to_all(spread, 'blk', 0, 0, tiled=True).reshape(span_rows, -1)  26.4 us
    ppermute x1, waiting for transfers between devices, passed_along(): return lax.ppermute(block, axis, route)  20.5 us
    ppermute x1, waiting for transfers between devices, swapped(): return lax.ppermute(block, axis, route)  16.3 us
    all_to_all x1, starting transfers between devices, shards(): lax.all_to_all(jnp.broadcast_to(queries[None], (blocks,) + queries.shape)...  8.18 us
    pallas_call x1, Pallas kernels, combine(): pl.pallas_call(combine_kernel, grid=(columns // COLUMN_BLOCK,), in_specs=...  6.65 us
  transfers between devices with their start and end apart: 4, of which 4 were waited for; matrix products, arithmetic and copies ran while one was open for 6% of the time, Pallas kernels for 0%

profile of v9, /device:TPU:2, one launch (start us, length us, event | category | flops | bytes accessed | tf_op | source)
XLA Modules:
  0.0 205.7 jit_solution(13596688186986772783)
XLA Ops:
  0.0 0.0 copy-start
  0.0 2.0 collective-permute-start
  2.7 0.0 copy-start.4
  2.7 4.2 %copy.18 = bf16[256,4096]{1,0:T(8,128)(2,1)} copy(bf16[256,4096]{0,1:T(8,128)(2,1)} %bitcast.34) | data formatting | bytes 4194304 | tf_op jit(solution)/shard_map/dot_general | solution.py:251
  7.0 0.3 multiply_cosine_fusion.1
  7.3 0.0 copy-start.5
  7.3 0.0 copy-start.6
  7.3 20.5 %collective-permute-done = bf16[256,4096]{1,0:T(8,128)(2,1)} collective-permute-done((bf16[256,4096]{1,0:T(8,128)(2,1)}, bf16[256,4096]{1,0:T(8,128)(2,1)}, u32[]{:S(2)}, u32[]{:S(2)}) %collective-permute-start) | collective-permute-done | bytes 2097184 | tf_op jit(solution)/shard_map/ppermute | solution.py:19
  27.8 0.0 copy-done.4
  27.8 2.5 %fusion = (f32[256]{0:T(256)S(1)}, bf16[256,4096]{1,0:T(8,128)(2,1)S(1)}) fusion(bf16[256,4096]{1,0:T(8,128)(2,1)S(1)} %copy-done.4, bf16[256,4096]{1,0:T(8,128)(2,1)} %collective-permute-done, pred[]{:T(512)S(6)} %eq.8), kind=kLoop, calls=%fused_computation.2 | loop fusion | flops 4194048 | bytes 6292481 | tf_op jit(solution)/shard_map/reduce_sum | solution.py:248
  30.3 0.0 copy-start.2
  30.4 0.0 copy-done.5
  30.4 0.0 copy-done.6
  30.4 0.9 fusion.3
  31.3 0.4 copy-done.2
  31.7 0.1 copy.14
  31.8 1.5 broadcast_in_dim.7
  33.4 0.0 copy-start.7
  33.4 8.2 %all-to-all-start = ((bf16[16,256,256]{2,1,0:T(8,128)(2,1)}), bf16[16,256,256]{2,1,0:T(8,128)(2,1)S(1)}, u32[]{:S(2)}, u32[]{:S(2)}) async-start(bf16[16,256,256]{2,1,0:T(8,128)(2,1)} %broadcast_in_dim.7), calls=%async_computation | async-start | bytes 4194304 | tf_op jit(solution)/shard_map/all_to_all | solution.py:261
  41.6 0.0 copy-done.7
  41.6 0.6 constant_dynamic-slice_fusion
  42.1 28.5 %all-to-all-done.q_ref = bf16[16,256,256]{2,1,0:T(8,128)(2,1)S(1)} async-done(((bf16[16,256,256]{2,1,0:T(8,128)(2,1)}), bf16[16,256,256]{2,1,0:T(8,128)(2,1)S(1)}, u32[]{:S(2)}, u32[]{:S(2)}) %all-to-all-start) | async-done | bytes 2097184 | tf_op jit(solution)/shard_map/all_to_all | solution.py:261
  70.6 0.0 copy-start.3
  70.6 1.3 copy-done.3
  71.9 31.5 %shard_map.100 = bf16[16,264,256]{2,1,0:T(8,128)(2,1)} custom-call(s32[1]{0:T(128)} %bitcast.1.live_ref, bf16[16,256,256]{2,1,0:T(8,128)(2,1)} %copy-done.3, bf16[2048,1024]{1,0:T(8,128)(2,1)} %bitcast.32, bf16[2048,1024]{1,0:T(8,128)(2,1)} %bitcast.33), custom_call_target="tpu_custom_call" | custom-call | tf_op jit(solution)/shard_map/pallas_call | solution.py:118
  103.4 3.9 %all-to-all-start.1 = ((bf16[16,264,256]{2,1,0:T(8,128)(2,1)}), bf16[16,264,256]{2,1,0:T(8,128)(2,1)S(1)}, u32[]{:S(2)}, u32[]{:S(2)}) async-start(bf16[16,264,256]{2,1,0:T(8,128)(2,1)} %shard_map.100), calls=%async_computation.1 | async-start | bytes 4325376 | tf_op jit(solution)/shard_map/all_to_all | solution.py:265
  107.4 0.0 copy-done
  107.4 2.5 %fusion.7 = f32[256,128]{0,1:T(8,128)S(1)} fusion(bf16[1,4096,128]{2,1,0:T(8,128)(2,1)S(1)} %copy-done, bf16[256,4096]{1,0:T(8,128)(2,1)} %copy-done.2, f32[4096]{0:T(1024)S(1)} %bitcast.44, f32[256]{0:T(256)S(1)} %add_rsqrt_fusion), kind=kOutput, calls=%fused_computation.12 | convolution fusion | flops 272629760 | bytes 3294208 | tf_op jit(solution)/shard_map/dot_general | solution.py:255
  109.9 0.3 fusion.23
  110.3 2.0 collective-permute-start.1
  112.3 0.1 copy.15
  112.4 0.8 copy.16
  113.2 16.3 %collective-permute-done.1 = bf16[256,128]{0,1:T(8,128)(2,1)} collective-permute-done((bf16[256,128]{0,1:T(8,128)(2,1)S(1)}, bf16[256,128]{0,1:T(8,128)(2,1)}, u32[]{:S(2)}, u32[]{:S(2)}) %collective-permute-start.1) | collective-permute-done | bytes 65568 | tf_op jit(solution)/shard_map/ppermute | solution.py:29
  129.4 1.2 fusion.35
  130.7 0.1 fusion.11
  130.8 1.1 fusion.6
  131.9 0.7 reshape.161.own_out_ref
  132.6 0.1 add.59
  132.8 0.7 copy.17
  133.5 2.2 %all-to-all-done.1.parts_ref = bf16[16,264,256]{2,1,0:T(8,128)(2,1)S(1)} async-done(((bf16[16,264,256]{2,1,0:T(8,128)(2,1)}), bf16[16,264,256]{2,1,0:T(8,128)(2,1)S(1)}, u32[]{:S(2)}, u32[]{:S(2)}) %all-to-all-start.1) | async-done | bytes 2162720 | tf_op jit(solution)/shard_map/all_to_all | solution.py:265
  135.7 0.0 copy-start.1
  135.7 1.4 copy-done.1
  137.0 6.6 %shard_map.101 = bf16[256,4096]{1,0:T(8,128)(2,1)} custom-call(bf16[16,264,256]{2,1,0:T(8,128)(2,1)} %copy-done.1, bf16[256,256]{1,0:T(8,128)(2,1)} %reshape.161.own_out_ref, f32[2,256]{1,0:T(2,128)} %bitcast.41, bf16[256,4096]{1,0:T(8,128)(2,1)} %bitcast.35), custom_call_target="tpu_custom_call" | custom-call | tf_op jit(solution)/shard_map/pallas_call | solution.py:181
  143.7 31.0 %all_to_all.20.terms_ref = bf16[16,16,4096]{2,1,0:T(8,128)(2,1)} all-to-all(bf16[16,16,4096]{2,1,0:T(8,128)(2,1)} %bitcast.30), channel_id=1, replica_groups=mesh['segment'=8,'blk'=16] {'blk'}, dimensions={0} | all-to-all | bytes 4194304 | tf_op jit(solution)/shard_map/all_to_all | solution.py:274
  174.7 3.3 %shard_map.102 = bf16[16,16,4096]{2,1,0:T(8,128)(2,1)} custom-call(s32[1]{0:T(128)} %bitcast.position_ref, bf16[16,16,4096]{2,1,0:T(8,128)(2,1)} %all_to_all.20.terms_ref, bf16[256,4096]{1,0:T(8,128)(2,1)} %copy-done.2), custom_call_target="tpu_custom_call" | custom-call | tf_op jit(solution)/shard_map/pallas_call | solution.py:217
  178.0 26.4 %all_to_all.21 = bf16[16,16,4096]{2,1,0:T(8,128)(2,1)S(1)} all-to-all(bf16[16,16,4096]{2,1,0:T(8,128)(2,1)} %shard_map.102), channel_id=1, replica_groups=mesh['segment'=8,'blk'=16] {'blk'}, dimensions={0} | all-to-all | bytes 4194304 | tf_op jit(solution)/shard_map/all_to_all | solution.py:278
  204.3 1.3 copy.21
  (8 shorter events, 0.1 us)
Async XLA Ops:
  0.0 107.4 %copy-start = (bf16[1,4096,128]{2,1,0:T(8,128)(2,1)S(1)}, bf16[1,4096,128]{2,1,0:T(8,128)(2,1)}, u32[]{:S(2)}) copy-start(bf16[1,4096,128]{2,1,0:T(8,128)(2,1)} %param.16) | copy-start | bytes 3145732
  0.0 27.8 %collective-permute-start = (bf16[256,4096]{1,0:T(8,128)(2,1)}, bf16[256,4096]{1,0:T(8,128)(2,1)}, u32[]{:S(2)}, u32[]{:S(2)}) collective-permute-start(bf16[256,4096]{1,0:T(8,128)(2,1)} %bitcast.42), channel_id=1, source_target_pairs={{0,16},{16,32},{32,48},{48,64},{64,80},{80,96},{96,112},{1,17},{17... | collective-permute-start | bytes 6291464 | tf_op jit(solution)/shard_map/ppermute | solution.py:19
  2.7 25.1 %copy-start.4 = (bf16[256,4096]{1,0:T(8,128)(2,1)S(1)}, bf16[256,4096]{1,0:T(8,128)(2,1)}, u32[]{:S(2)}) copy-start(bf16[256,4096]{1,0:T(8,128)(2,1)} %param.10) | copy-start | bytes 6291460
  7.3 23.1 %copy-start.5 = (bf16[256,4096]{1,0:T(8,128)(2,1)S(1)}, bf16[256,4096]{1,0:T(8,128)(2,1)}, u32[]{:S(2)}) copy-start(bf16[256,4096]{1,0:T(8,128)(2,1)} %copy.18) | copy-start | bytes 6291460
  7.3 23.1 %copy-start.6 = (f32[1,4096]{1,0:T(1,128)S(1)}, f32[1,4096]{1,0:T(1,128)}, u32[]{:S(2)}) copy-start(f32[1,4096]{1,0:T(1,128)} %param.14) | copy-start | bytes 49156
  30.3 1.3 copy-start.2
  33.4 8.2 %copy-start.7 = (s32[1,16]{1,0:T(1,128)S(1)}, s32[1,16]{1,0:T(1,128)}, u32[]{:S(2)}) copy-start(s32[1,16]{1,0:T(1,128)} %param.13) | copy-start | bytes 196
  33.4 37.2 %all-to-all-start = ((bf16[16,256,256]{2,1,0:T(8,128)(2,1)}), bf16[16,256,256]{2,1,0:T(8,128)(2,1)S(1)}, u32[]{:S(2)}, u32[]{:S(2)}) async-start(bf16[16,256,256]{2,1,0:T(8,128)(2,1)} %broadcast_in_dim.7), calls=%async_computation | async-start | bytes 4194304 | tf_op jit(solution)/shard_map/all_to_all | solution.py:261
  70.6 1.3 copy-start.3
  103.4 32.2 %all-to-all-start.1 = ((bf16[16,264,256]{2,1,0:T(8,128)(2,1)}), bf16[16,264,256]{2,1,0:T(8,128)(2,1)S(1)}, u32[]{:S(2)}, u32[]{:S(2)}) async-start(bf16[16,264,256]{2,1,0:T(8,128)(2,1)} %shard_map.100), calls=%async_computation.1 | async-start | bytes 4325376 | tf_op jit(solution)/shard_map/all_to_all | solution.py:265
  110.3 19.2 %collective-permute-start.1 = (bf16[256,128]{0,1:T(8,128)(2,1)S(1)}, bf16[256,128]{0,1:T(8,128)(2,1)}, u32[]{:S(2)}, u32[]{:S(2)}) collective-permute-start(bf16[256,128]{0,1:T(8,128)(2,1)S(1)} %fusion.26), channel_id=1, source_target_pairs={{0,1},{1,0},{2,3},{3,2},{4,5},{5,4},{6,7},{7,6},{8,9},{9,8},{10,11... | collective-permute-start | bytes 196616 | tf_op jit(solution)/shard_map/ppermute | solution.py:29
  135.7 1.4 copy-start.1

commit v10 on v9

--- a/solution.py
+++ b/solution.py
@@ -122,10 +122,20 @@
     )(live, every_query, cached_keys, cached_values)
 
 
-def combine_kernel(parts_ref, own_out_ref, own_log_ref, weight_ref, out_ref, attended_ref):
+def combine_kernel(*refs):
+    parts_refs = refs[:-5]
+    own_out_ref, own_log_ref, weight_ref, out_ref, attended_ref = refs[-5:]
+
     @pl.when(pl.program_id(0) == 0)
     def _():
-        combine_into(parts_ref, own_out_ref, own_log_ref, attended_ref)
+        rows = own_out_ref.shape[0] // len(parts_refs)
+        for i, parts_ref in enumerate(parts_refs):
+            combine_into(
+                parts_ref,
+                own_out_ref.at[pl.ds(i * rows, rows), :],
+                own_log_ref.at[:, pl.ds(i * rows, rows)],
+                attended_ref.at[pl.ds(i * rows, rows), :],
+            )
 
     out_ref[...] = jnp.dot(
         attended_ref[...], weight_ref[...], preferred_element_type=jnp.float32
@@ -138,7 +148,7 @@
     heads_here = out_ref.shape[1] // HD
     logs = [[] for _ in range(heads_here)]
     for b in range(sources):
-        packed = parts_ref[b, rows:rows + LOG_ROWS, :].astype(jnp.float32)
+        packed = parts_ref[b, rows:rows + LOG_ROWS, :rows].astype(jnp.float32)
         for h in range(heads_here):
             logs[h].append((packed[3 * h + 2:3 * h + 3] + packed[3 * h + 1:3 * h + 2]) + packed[3 * h:3 * h + 1])
     own_logs = own_log_ref[...]
@@ -174,15 +184,15 @@
 COLUMN_BLOCK = 1024
 
 
-def combine(arrived_parts, own_out, own_log, out_weight):
-    sources, packed_rows, width = arrived_parts.shape
+def combine(arrived_halves, own_out, own_log, out_weight):
+    sources, packed_rows, width = arrived_halves[0].shape
     rows = own_out.shape[0]
     columns = out_weight.shape[1]
     return pl.pallas_call(
         combine_kernel,
         grid=(columns // COLUMN_BLOCK,),
-        in_specs=[
-            pl.BlockSpec((sources, packed_rows, width), lambda j: (0, 0, 0)),
+        in_specs=[pl.BlockSpec((sources, packed_rows, width), lambda j: (0, 0, 0)) for _ in arrived_halves]
+        + [
             pl.BlockSpec(own_out.shape, lambda j: (0, 0)),
             pl.BlockSpec(own_log.shape, lambda j: (0, 0)),
             pl.BlockSpec((out_weight.shape[0], COLUMN_BLOCK), lambda j: (0, j)),
@@ -191,7 +201,7 @@
         out_shape=jax.ShapeDtypeStruct((rows, columns), jnp.bfloat16),
         scratch_shapes=[pltpu.VMEM(own_out.shape, jnp.bfloat16)],
         compiler_params=pltpu.CompilerParams(dimension_semantics=("arbitrary",)),
-    )(arrived_parts, own_out, own_log, out_weight)
+    )(*arrived_halves, own_out, own_log, out_weight)
 
 
 def residual_kernel(position_ref, terms_ref, current_ref, out_ref):
@@ -258,18 +268,24 @@
     partner = swapped(mine, "blk", 0)
     own_keys = jnp.where(odd_member, partner, mine)
     own_values = jnp.where(odd_member, mine, partner)
-    every_query = lax.all_to_all(
-        jnp.broadcast_to(queries[None], (blocks,) + queries.shape), "blk", 0, 0, tiled=True
-    )
-    held = cache_attention(live, every_query, cache_keys[0], cache_values[0])
-    arrived_parts = lax.all_to_all(held, "blk", split_axis=0, concat_axis=0, tiled=True)
+    partner, queries = lax.optimization_barrier((partner, queries))
+    halves = 2
+    half_rows = span_rows // halves
+    arrived_halves = []
+    for i in range(halves):
+        half = queries[i * half_rows:(i + 1) * half_rows]
+        every_query = lax.all_to_all(
+            jnp.broadcast_to(half[None], (blocks,) + half.shape), "blk", 0, 0, tiled=True
+        )
+        held = cache_attention(live, every_query, cache_keys[0], cache_values[0])
+        arrived_halves.append(lax.all_to_all(held, "blk", split_axis=0, concat_axis=0, tiled=True))
     query_rows = queries.reshape(span_rows * heads_here, HD)
     row_tokens = jnp.arange(span_rows * heads_here, dtype=jnp.int32) // heads_here
     causal = row_tokens[:, None] >= jnp.arange(span_rows, dtype=jnp.int32)[None, :]
     own_out, own_log = attend_rows(query_rows, own_keys, own_values, causal)
     own_out = own_out.reshape(span_rows, heads_here * HD)
     own_log = own_log.reshape(span_rows, heads_here).T
-    head_terms = combine(arrived_parts, own_out, own_log, w_out[0])
+    head_terms = combine(arrived_halves, own_out, own_log, w_out[0])
     chunk = span_rows // blocks
     gathered_terms = lax.all_to_all(
         head_terms.reshape(blocks, chunk, -1), "blk", 0, 0, tiled=True

time: 206 us -> 206 us (level)
  the two profiles are of different devices: /device:TPU:2 before, /device:TPU:6 now
where the time goes in v10:
time: 206 us; the launch traced here: 205 us
  blocking collectives  77.7 us (38%)
  Pallas kernels  50.2 us (24%)
  waiting for transfers between devices  35.7 us (17%)
  starting transfers between devices  22.1 us (11%)
  local copies, waits for them, and re-layouts  11 us (5%)
  matrix products  4.12 us (2%)
  other arithmetic  3.38 us (2%)
    pallas_call x2, Pallas kernels, cache_attention(): pl.pallas_call(cache_kernel, grid_spec=grid_spec, out_shape=jax.ShapeDtyp...  40.2 us
    all_to_all x1, blocking collectives, shards(): lax.all_to_all(head_terms.reshape(blocks, chunk, -1), 'blk', 0, 0, tiled=...  34.7 us
    all_to_all x1, blocking collectives, shards(): lax.all_to_all(spread, 'blk', 0, 0, tiled=True).reshape(span_rows, -1)  22.2 us
    all_to_all x1, blocking collectives, shards(): lax.all_to_all(jnp.broadcast_to(half[None], (blocks,) + half.shape), 'blk...  20.9 us
    ppermute x1, waiting for transfers between devices, passed_along(): return lax.ppermute(block, axis, route)  20.5 us
    all_to_all x2, starting transfers between devices, shards(): lax.all_to_all(held, 'blk', split_axis=0, concat_axis=0, tiled=True)  14.4 us
    all_to_all x2, waiting for transfers between devices, shards(): lax.all_to_all(held, 'blk', split_axis=0, concat_axis=0, tiled=True)  13 us
    pallas_call x1, Pallas kernels, combine(): pl.pallas_call(combine_kernel, grid=(columns // COLUMN_BLOCK,), in_specs=...  6.73 us
  transfers between devices with their start and end apart: 5, of which 3 were waited for; matrix products, arithmetic and copies ran while one was open for 4% of the time, Pallas kernels for 20%

profile of v10, /device:TPU:6, one launch (start us, length us, event | category | flops | bytes accessed | tf_op | source)
XLA Modules:
  0.0 205.2 jit_solution(7023165023629050908)
XLA Ops:
  0.0 0.0 copy-start
  0.0 2.0 collective-permute-start
  2.7 0.0 copy-start.5
  2.7 4.2 %copy.19 = bf16[256,4096]{1,0:T(8,128)(2,1)} copy(bf16[256,4096]{0,1:T(8,128)(2,1)} %bitcast.35) | data formatting | bytes 4194304 | tf_op jit(solution)/shard_map/dot_general | solution.py:261
  7.0 0.3 multiply_cosine_fusion
  7.3 0.0 copy-start.6
  7.3 0.0 copy-start.9
  7.3 20.5 %collective-permute-done = bf16[256,4096]{1,0:T(8,128)(2,1)} collective-permute-done((bf16[256,4096]{1,0:T(8,128)(2,1)}, bf16[256,4096]{1,0:T(8,128)(2,1)}, u32[]{:S(2)}, u32[]{:S(2)}) %collective-permute-start) | collective-permute-done | bytes 2097184 | tf_op jit(solution)/shard_map/ppermute | solution.py:19
  27.8 0.0 copy-done.5
  27.8 2.5 %fusion = (f32[256]{0:T(256)S(1)}, bf16[256,4096]{1,0:T(8,128)(2,1)S(1)}) fusion(bf16[256,4096]{1,0:T(8,128)(2,1)S(1)} %copy-done.5, bf16[256,4096]{1,0:T(8,128)(2,1)} %collective-permute-done, pred[]{:T(512)S(6)} %eq.9), kind=kLoop, calls=%fused_computation.2 | loop fusion | flops 4194048 | bytes 6292481 | tf_op jit(solution)/shard_map/reduce_sum | solution.py:258
  30.3 0.0 copy-start.1
  30.4 0.0 copy-done.6
  30.4 0.0 copy-done.9
  30.4 0.9 fusion.3
  31.3 0.4 copy-done.1
  31.7 0.0 copy-done
  31.7 1.0 fusion.7
  32.6 0.3 fusion.20
  33.0 0.0 copy-start.7
  33.0 2.0 collective-permute-start.1
  35.1 2.3 %collective-permute-done.1 = bf16[256,128]{0,1:T(8,128)(2,1)S(1)} collective-permute-done((bf16[256,128]{0,1:T(8,128)(2,1)S(1)}, bf16[256,128]{0,1:T(8,128)(2,1)S(1)}, u32[]{:S(2)}, u32[]{:S(2)}) %collective-permute-start.1) | collective-permute-done | bytes 65568 | tf_op jit(solution)/shard_map/ppermute | solution.py:29
  37.4 0.0 copy-done.7
  37.4 0.6 copy-done.8
  38.0 0.1 copy.15
  38.1 0.1 broadcast_in_dim.11
  38.2 20.9 %all_to_all.30.q_ref = bf16[16,128,256]{2,1,0:T(8,128)(2,1)} all-to-all(bf16[16,128,256]{2,1,0:T(8,128)(2,1)S(1)} %broadcast_in_dim.11), channel_id=1, replica_groups=mesh['segment'=8,'blk'=16] {'blk'}, dimensions={0} | all-to-all | bytes 2097152 | tf_op jit(solution)/shard_map/all_to_all | solution.py:277
  59.1 1.1 broadcast_in_dim.10
  60.1 3.7 %all-to-all-start = ((bf16[16,128,256]{2,1,0:T(8,128)(2,1)}), bf16[16,128,256]{2,1,0:T(8,128)(2,1)S(1)}, u32[]{:S(2)}, u32[]{:S(2)}) async-start(bf16[16,128,256]{2,1,0:T(8,128)(2,1)} %broadcast_in_dim.10), calls=%async_computation | async-start | bytes 2097152 | tf_op jit(solution)/shard_map/all_to_all | solution.py:277
  63.8 0.6 constant_dynamic-slice_fusion
  64.4 20.1 %shard_map.101 = bf16[16,136,256]{2,1,0:T(8,128)(2,1)} custom-call(s32[1]{0:T(128)} %bitcast.1.live_ref, bf16[16,128,256]{2,1,0:T(8,128)(2,1)} %all_to_all.30.q_ref, bf16[2048,1024]{1,0:T(8,128)(2,1)} %bitcast.29, bf16[2048,1024]{1,0:T(8,128)(2,1)} %bitcast.31), custom_call_target="tpu_custom_call" | custom-call | tf_op jit(solution)/shard_map/pallas_call | solution.py:118
  84.6 0.0 all-to-all-done.q_ref
  84.6 7.2 %all-to-all-start.3 = ((bf16[16,136,256]{2,1,0:T(8,128)(2,1)}), bf16[16,136,256]{2,1,0:T(8,128)(2,1)S(1)}, u32[]{:S(2)}, u32[]{:S(2)}) async-start(bf16[16,136,256]{2,1,0:T(8,128)(2,1)} %shard_map.101), calls=%async_computation.3 | async-start | bytes 2228224 | tf_op jit(solution)/shard_map/all_to_all | solution.py:281
  91.7 20.1 %shard_map.100 = bf16[16,136,256]{2,1,0:T(8,128)(2,1)} custom-call(s32[1]{0:T(128)} %bitcast.1.live_ref, bf16[16,128,256]{2,1,0:T(8,128)(2,1)} %copy-done.4, bf16[2048,1024]{1,0:T(8,128)(2,1)} %bitcast.30, bf16[2048,1024]{1,0:T(8,128)(2,1)} %bitcast.32), custom_call_target="tpu_custom_call" | custom-call | tf_op jit(solution)/shard_map/pallas_call | solution.py:118
  111.9 0.0 all-to-all-done.3.refs_1_
  111.9 7.2 %all-to-all-start.1 = ((bf16[16,136,256]{2,1,0:T(8,128)(2,1)}), bf16[16,136,256]{2,1,0:T(8,128)(2,1)S(1)}, u32[]{:S(2)}, u32[]{:S(2)}) async-start(bf16[16,136,256]{2,1,0:T(8,128)(2,1)} %shard_map.100), calls=%async_computation.1 | async-start | bytes 2228224 | tf_op jit(solution)/shard_map/all_to_all | solution.py:281
  119.2 1.1 fusion.32
  120.3 0.1 fusion.11
  120.4 1.1 fusion.6
  121.6 0.7 reshape.160.refs_2_
  122.3 0.1 add.59
  122.4 0.7 copy.18
  123.1 13.0 %all-to-all-done.1.refs_0_ = bf16[16,136,256]{2,1,0:T(8,128)(2,1)S(1)} async-done(((bf16[16,136,256]{2,1,0:T(8,128)(2,1)}), bf16[16,136,256]{2,1,0:T(8,128)(2,1)S(1)}, u32[]{:S(2)}, u32[]{:S(2)}) %all-to-all-start.1) | async-done | bytes 1114144 | tf_op jit(solution)/shard_map/all_to_all | solution.py:281
  136.0 1.0 copy-done.3
  137.1 6.7 %shard_map.102 = bf16[256,4096]{1,0:T(8,128)(2,1)} custom-call(bf16[16,136,256]{2,1,0:T(8,128)(2,1)} %copy-done.3, bf16[16,136,256]{2,1,0:T(8,128)(2,1)} %copy-done.2, bf16[256,256]{1,0:T(8,128)(2,1)} %reshape.160.refs_2_, f32[2,256]{1,0:T(2,128)} %bitcast.40, bf16[256,4096]{1,0:T(8,128)(2,1)} %bitcast.36), custom_call_target="tpu_custom_call" | custom-call | tf_op jit(solution)/shard_map/pallas_call | solution.py:191
  143.8 34.7 %all_to_all.31.terms_ref = bf16[16,16,4096]{2,1,0:T(8,128)(2,1)} all-to-all(bf16[16,16,4096]{2,1,0:T(8,128)(2,1)} %bitcast.33), channel_id=1, replica_groups=mesh['segment'=8,'blk'=16] {'blk'}, dimensions={0} | all-to-all | bytes 4194304 | tf_op jit(solution)/shard_map/all_to_all | solution.py:290
  178.5 3.3 %shard_map.103 = bf16[16,16,4096]{2,1,0:T(8,128)(2,1)} custom-call(s32[1]{0:T(128)} %bitcast.position_ref, bf16[16,16,4096]{2,1,0:T(8,128)(2,1)} %all_to_all.31.terms_ref, bf16[256,4096]{1,0:T(8,128)(2,1)} %copy-done.1), custom_call_target="tpu_custom_call" | custom-call | tf_op jit(solution)/shard_map/pallas_call | solution.py:227
  181.7 22.2 %all_to_all.32 = bf16[16,16,4096]{2,1,0:T(8,128)(2,1)S(1)} all-to-all(bf16[16,16,4096]{2,1,0:T(8,128)(2,1)} %shard_map.103), channel_id=1, replica_groups=mesh['segment'=8,'blk'=16] {'blk'}, dimensions={0} | all-to-all | bytes 4194304 | tf_op jit(solution)/shard_map/all_to_all | solution.py:294
  203.9 1.3 copy.22
  (18 shorter events, 0.2 us)
Async XLA Ops:
  0.0 31.7 %copy-start = (bf16[1,4096,128]{2,1,0:T(8,128)(2,1)S(1)}, bf16[1,4096,128]{2,1,0:T(8,128)(2,1)}, u32[]{:S(2)}) copy-start(bf16[1,4096,128]{2,1,0:T(8,128)(2,1)} %param.16) | copy-start | bytes 3145732
  0.0 27.8 %collective-permute-start = (bf16[256,4096]{1,0:T(8,128)(2,1)}, bf16[256,4096]{1,0:T(8,128)(2,1)}, u32[]{:S(2)}, u32[]{:S(2)}) collective-permute-start(bf16[256,4096]{1,0:T(8,128)(2,1)} %bitcast.41), channel_id=1, source_target_pairs={{0,16},{16,32},{32,48},{48,64},{64,80},{80,96},{96,112},{1,17},{17... | collective-permute-start | bytes 6291464 | tf_op jit(solution)/shard_map/ppermute | solution.py:19
  2.7 25.1 %copy-start.5 = (bf16[256,4096]{1,0:T(8,128)(2,1)S(1)}, bf16[256,4096]{1,0:T(8,128)(2,1)}, u32[]{:S(2)}) copy-start(bf16[256,4096]{1,0:T(8,128)(2,1)} %param.10) | copy-start | bytes 6291460
  7.3 23.1 %copy-start.6 = (bf16[256,4096]{1,0:T(8,128)(2,1)S(1)}, bf16[256,4096]{1,0:T(8,128)(2,1)}, u32[]{:S(2)}) copy-start(bf16[256,4096]{1,0:T(8,128)(2,1)} %copy.19) | copy-start | bytes 6291460
  7.3 23.1 %copy-start.9 = (f32[1,4096]{1,0:T(1,128)S(1)}, f32[1,4096]{1,0:T(1,128)}, u32[]{:S(2)}) copy-start(f32[1,4096]{1,0:T(1,128)} %param.14) | copy-start | bytes 49156
  30.3 1.3 copy-start.1
  33.0 4.4 %copy-start.7 = (bf16[256,128]{0,1:T(8,128)(2,1)}, bf16[256,128]{0,1:T(8,128)(2,1)S(1)}, u32[]{:S(2)}) copy-start(bf16[256,128]{0,1:T(8,128)(2,1)S(1)} %fusion.23) | copy-start | bytes 196612
  33.0 4.3 %collective-permute-start.1 = (bf16[256,128]{0,1:T(8,128)(2,1)S(1)}, bf16[256,128]{0,1:T(8,128)(2,1)S(1)}, u32[]{:S(2)}, u32[]{:S(2)}) collective-permute-start(bf16[256,128]{0,1:T(8,128)(2,1)S(1)} %fusion.23), channel_id=1, source_target_pairs={{0,1},{1,0},{2,3},{3,2},{4,5},{5,4},{6,7},{7,6},{8,9},{9,8},{10,11... | collective-permute-start | bytes 196616 | tf_op jit(solution)/shard_map/ppermute | solution.py:29
  37.4 0.6 copy-start.8
  59.1 4.7 %copy-start.10 = (s32[1,16]{1,0:T(1,128)S(1)}, s32[1,16]{1,0:T(1,128)}, u32[]{:S(2)}) copy-start(s32[1,16]{1,0:T(1,128)} %param.13) | copy-start | bytes 196
  60.1 24.4 %all-to-all-start = ((bf16[16,128,256]{2,1,0:T(8,128)(2,1)}), bf16[16,128,256]{2,1,0:T(8,128)(2,1)S(1)}, u32[]{:S(2)}, u32[]{:S(2)}) async-start(bf16[16,128,256]{2,1,0:T(8,128)(2,1)} %broadcast_in_dim.10), calls=%async_computation | async-start | bytes 2097152 | tf_op jit(solution)/shard_map/all_to_all | solution.py:277
  84.6 7.2 %copy-start.4 = (bf16[16,128,256]{2,1,0:T(8,128)(2,1)}, bf16[16,128,256]{2,1,0:T(8,128)(2,1)S(1)}, u32[]{:S(2)}) copy-start(bf16[16,128,256]{2,1,0:T(8,128)(2,1)S(1)} %all-to-all-done.q_ref) | copy-start | bytes 3145732
  84.6 27.3 %all-to-all-start.3 = ((bf16[16,136,256]{2,1,0:T(8,128)(2,1)}), bf16[16,136,256]{2,1,0:T(8,128)(2,1)S(1)}, u32[]{:S(2)}, u32[]{:S(2)}) async-start(bf16[16,136,256]{2,1,0:T(8,128)(2,1)} %shard_map.101), calls=%async_computation.3 | async-start | bytes 2228224 | tf_op jit(solution)/shard_map/all_to_all | solution.py:281
  111.9 9.7 %copy-start.2 = (bf16[16,136,256]{2,1,0:T(8,128)(2,1)}, bf16[16,136,256]{2,1,0:T(8,128)(2,1)S(1)}, u32[]{:S(2)}) copy-start(bf16[16,136,256]{2,1,0:T(8,128)(2,1)S(1)} %all-to-all-done.3.refs_1_) | copy-start | bytes 3342340
  111.9 24.2 %all-to-all-start.1 = ((bf16[16,136,256]{2,1,0:T(8,128)(2,1)}), bf16[16,136,256]{2,1,0:T(8,128)(2,1)S(1)}, u32[]{:S(2)}, u32[]{:S(2)}) async-start(bf16[16,136,256]{2,1,0:T(8,128)(2,1)} %shard_map.100), calls=%async_computation.1 | async-start | bytes 2228224 | tf_op jit(solution)/shard_map/all_to_all | solution.py:281
  136.0 1.0 copy-start.3

commit v11 on v10

--- a/solution.py
+++ b/solution.py
@@ -69,13 +69,15 @@
     live = live_ref[0]
     keys = k_ref[...]
     values = v_ref[...]
-    rows = q_ref.shape[1]
+    sources, rows = q_ref.shape[0], q_ref.shape[1]
     width = out_ref.shape[2]
+    group = max(1, min(sources, 256 // rows))
     visible = lax.broadcasted_iota(jnp.int32, (1, keys.shape[0]), 1) < live
-    for src in range(q_ref.shape[0]):
-        log_rows = []
+    log_rows = {src: [] for src in range(sources)}
+    for first in range(0, sources, group):
+        members = list(range(first, min(first + group, sources)))
         for h in range(q_ref.shape[2] // HD):
-            q = q_ref[src, :, h * HD:(h + 1) * HD]
+            q = jnp.concatenate([q_ref[src, :, h * HD:(h + 1) * HD] for src in members], axis=0)
             scores = lax.dot_general(
                 q, keys, (((1,), (1,)), ((), ())), preferred_element_type=jnp.float32
             ) * HD ** (-0.5)
@@ -84,17 +86,22 @@
             weights = jnp.exp(scores - highest)
             totals = jnp.sum(weights, axis=-1, keepdims=True)
             part = jnp.dot(weights.astype(jnp.bfloat16), values, preferred_element_type=jnp.float32)
-            out_ref[src, :rows, h * HD:(h + 1) * HD] = (part / totals).astype(out_ref.dtype)
-            log_col = jnp.broadcast_to(highest + jnp.log(totals), (rows, HD))
-            rest = jnp.transpose(log_col)[0:1, :]
-            for _ in range(3):
-                piece = rest.astype(jnp.bfloat16).astype(jnp.float32)
-                log_rows.append(piece)
-                rest = rest - piece
+            normalized = (part / totals).astype(out_ref.dtype)
+            log_totals = highest + jnp.log(totals)
+            for i, src in enumerate(members):
+                out_ref[src, :rows, h * HD:(h + 1) * HD] = normalized[i * rows:(i + 1) * rows]
+                log_col = jnp.broadcast_to(log_totals[i * rows:(i + 1) * rows], (rows, HD))
+                rest = jnp.transpose(log_col)[0:1, :]
+                for _ in range(3):
+                    piece = rest.astype(jnp.bfloat16).astype(jnp.float32)
+                    log_rows[src].append(piece)
+                    rest = rest - piece
+    for src in range(sources):
+        rows_here = log_rows[src]
         if rows < width:
-            log_rows = [jnp.concatenate([r, jnp.zeros((1, width - rows), jnp.float32)], axis=1) for r in log_rows]
-        log_rows += [jnp.zeros((1, width), jnp.float32)] * (out_ref.shape[1] - rows - len(log_rows))
-        out_ref[src, rows:, :] = jnp.concatenate(log_rows, axis=0).astype(out_ref.dtype)
+            rows_here = [jnp.concatenate([r, jnp.zeros((1, width - rows), jnp.float32)], axis=1) for r in rows_here]
+        rows_here = rows_here + [jnp.zeros((1, width), jnp.float32)] * (out_ref.shape[1] - rows - len(rows_here))
+        out_ref[src, rows:, :] = jnp.concatenate(rows_here, axis=0).astype(out_ref.dtype)
 
 
 LOG_ROWS = 8

time: 206 us -> 196 us (0.951)
  the two profiles are of different devices: /device:TPU:6 before, /device:TPU:2 now
where the time goes in v11:
time: 196 us; the launch traced here: 195 us
  blocking collectives  75.6 us (39%)
  Pallas kernels  46 us (23%)
  waiting for transfers between devices  32.4 us (17%)
  starting transfers between devices  22.1 us (11%)
  local copies, waits for them, and re-layouts  11.1 us (6%)
  matrix products  4.11 us (2%)
  other arithmetic  3.38 us (2%)
    pallas_call x2, Pallas kernels, cache_attention(): pl.pallas_call(cache_kernel, grid_spec=grid_spec, out_shape=jax.ShapeDtyp...  36 us
    all_to_all x1, blocking collectives, shards(): lax.all_to_all(head_terms.reshape(blocks, chunk, -1), 'blk', 0, 0, tiled=...  26.9 us
    all_to_all x1, blocking collectives, shards(): lax.all_to_all(spread, 'blk', 0, 0, tiled=True).reshape(span_rows, -1)  25.5 us
    all_to_all x1, blocking collectives, shards(): lax.all_to_all(jnp.broadcast_to(half[None], (blocks,) + half.shape), 'blk...  23.2 us
    ppermute x1, waiting for transfers between devices, passed_along(): return lax.ppermute(block, axis, route)  20.5 us
    all_to_all x2, starting transfers between devices, shards(): lax.all_to_all(held, 'blk', split_axis=0, concat_axis=0, tiled=True)  14.4 us
    all_to_all x2, waiting for transfers between devices, shards(): lax.all_to_all(held, 'blk', split_axis=0, concat_axis=0, tiled=True)  9.63 us
    pallas_call x1, Pallas kernels, combine(): pl.pallas_call(combine_kernel, grid=(columns // COLUMN_BLOCK,), in_specs=...  6.73 us
  transfers between devices with their start and end apart: 5, of which 3 were waited for; matrix products, arithmetic and copies ran while one was open for 5% of the time, Pallas kernels for 18%

profile of v11, /device:TPU:2, one launch (start us, length us, event | category | flops | bytes accessed | tf_op | source)
XLA Modules:
  0.0 195.5 jit_solution(10767256616460779269)
XLA Ops:
  0.0 0.0 copy-start
  0.0 2.0 %collective-permute-start = (bf16[256,4096]{1,0:T(8,128)(2,1)}, bf16[256,4096]{1,0:T(8,128)(2,1)}, u32[]{:S(2)}, u32[]{:S(2)}) collective-permute-start(bf16[256,4096]{1,0:T(8,128)(2,1)} %bitcast.41), channel_id=1, source_target_pairs={{0,16},{16,32},{32,48},{48,64},{64,80},{80,96},{96,112},{1,17},{17... | collective-permute-start | bytes 6291464 | tf_op jit(solution)/shard_map/ppermute | solution.py:19
  2.7 0.0 copy-start.5
  2.7 4.2 %copy.19 = bf16[256,4096]{1,0:T(8,128)(2,1)} copy(bf16[256,4096]{0,1:T(8,128)(2,1)} %bitcast.35) | data formatting | bytes 4194304 | tf_op jit(solution)/shard_map/dot_general | solution.py:268
  7.0 0.3 multiply_cosine_fusion
  7.3 0.0 copy-start.6
  7.3 0.0 copy-start.9
  7.3 20.5 %collective-permute-done = bf16[256,4096]{1,0:T(8,128)(2,1)} collective-permute-done((bf16[256,4096]{1,0:T(8,128)(2,1)}, bf16[256,4096]{1,0:T(8,128)(2,1)}, u32[]{:S(2)}, u32[]{:S(2)}) %collective-permute-start) | collective-permute-done | bytes 2097184 | tf_op jit(solution)/shard_map/ppermute | solution.py:19
  27.8 0.0 copy-done.5
  27.8 2.5 %fusion = (f32[256]{0:T(256)S(1)}, bf16[256,4096]{1,0:T(8,128)(2,1)S(1)}) fusion(bf16[256,4096]{1,0:T(8,128)(2,1)S(1)} %copy-done.5, bf16[256,4096]{1,0:T(8,128)(2,1)} %collective-permute-done, pred[]{:T(512)S(6)} %eq.9), kind=kLoop, calls=%fused_computation.2 | loop fusion | flops 4194048 | bytes 6292481 | tf_op jit(solution)/shard_map/reduce_sum | solution.py:265
  30.3 0.0 copy-start.1
  30.4 0.0 copy-done.6
  30.4 0.0 copy-done.9
  30.4 0.9 fusion.3
  31.3 0.4 copy-done.1
  31.7 0.0 copy-done
  31.7 1.0 fusion.7
  32.6 0.3 fusion.20
  33.0 0.0 copy-start.7
  33.0 2.0 %collective-permute-start.1 = (bf16[256,128]{0,1:T(8,128)(2,1)S(1)}, bf16[256,128]{0,1:T(8,128)(2,1)S(1)}, u32[]{:S(2)}, u32[]{:S(2)}) collective-permute-start(bf16[256,128]{0,1:T(8,128)(2,1)S(1)} %fusion.23), channel_id=1, source_target_pairs={{0,1},{1,0},{2,3},{3,2},{4,5},{5,4},{6,7},{7,6},{8,9},{9,8},{10,11... | collective-permute-start | bytes 196616 | tf_op jit(solution)/shard_map/ppermute | solution.py:29
  35.1 2.3 %collective-permute-done.1 = bf16[256,128]{0,1:T(8,128)(2,1)S(1)} collective-permute-done((bf16[256,128]{0,1:T(8,128)(2,1)S(1)}, bf16[256,128]{0,1:T(8,128)(2,1)S(1)}, u32[]{:S(2)}, u32[]{:S(2)}) %collective-permute-start.1) | collective-permute-done | bytes 65568 | tf_op jit(solution)/shard_map/ppermute | solution.py:29
  37.4 0.6 copy-done.8
  38.0 0.1 copy.15
  38.1 0.1 broadcast_in_dim.11
  38.2 23.2 %all_to_all.30.q_ref = bf16[16,128,256]{2,1,0:T(8,128)(2,1)} all-to-all(bf16[16,128,256]{2,1,0:T(8,128)(2,1)S(1)} %broadcast_in_dim.11), channel_id=1, replica_groups=mesh['segment'=8,'blk'=16] {'blk'}, dimensions={0} | all-to-all | bytes 2097152 | tf_op jit(solution)/shard_map/all_to_all | solution.py:284
  61.4 1.1 broadcast_in_dim.10
  62.5 3.7 %all-to-all-start = ((bf16[16,128,256]{2,1,0:T(8,128)(2,1)}), bf16[16,128,256]{2,1,0:T(8,128)(2,1)S(1)}, u32[]{:S(2)}, u32[]{:S(2)}) async-start(bf16[16,128,256]{2,1,0:T(8,128)(2,1)} %broadcast_in_dim.10), calls=%async_computation | async-start | bytes 2097152 | tf_op jit(solution)/shard_map/all_to_all | solution.py:284
  66.2 0.6 constant_dynamic-slice_fusion
  66.8 18.0 %shard_map.101 = bf16[16,136,256]{2,1,0:T(8,128)(2,1)} custom-call(s32[1]{0:T(128)} %bitcast.1.live_ref, bf16[16,128,256]{2,1,0:T(8,128)(2,1)} %all_to_all.30.q_ref, bf16[2048,1024]{1,0:T(8,128)(2,1)} %bitcast.29, bf16[2048,1024]{1,0:T(8,128)(2,1)} %bitcast.31), custom_call_target="tpu_custom_call" | custom-call | tf_op jit(solution)/shard_map/pallas_call | solution.py:125
  84.7 0.0 all-to-all-done.q_ref
  84.8 7.2 %all-to-all-start.3 = ((bf16[16,136,256]{2,1,0:T(8,128)(2,1)}), bf16[16,136,256]{2,1,0:T(8,128)(2,1)S(1)}, u32[]{:S(2)}, u32[]{:S(2)}) async-start(bf16[16,136,256]{2,1,0:T(8,128)(2,1)} %shard_map.101), calls=%async_computation.3 | async-start | bytes 2228224 | tf_op jit(solution)/shard_map/all_to_all | solution.py:288
  91.9 18.0 %shard_map.100 = bf16[16,136,256]{2,1,0:T(8,128)(2,1)} custom-call(s32[1]{0:T(128)} %bitcast.1.live_ref, bf16[16,128,256]{2,1,0:T(8,128)(2,1)} %copy-done.4, bf16[2048,1024]{1,0:T(8,128)(2,1)} %bitcast.30, bf16[2048,1024]{1,0:T(8,128)(2,1)} %bitcast.32), custom_call_target="tpu_custom_call" | custom-call | tf_op jit(solution)/shard_map/pallas_call | solution.py:125
  109.9 0.0 all-to-all-done.3.refs_1_
  109.9 7.2 %all-to-all-start.1 = ((bf16[16,136,256]{2,1,0:T(8,128)(2,1)}), bf16[16,136,256]{2,1,0:T(8,128)(2,1)S(1)}, u32[]{:S(2)}, u32[]{:S(2)}) async-start(bf16[16,136,256]{2,1,0:T(8,128)(2,1)} %shard_map.100), calls=%async_computation.1 | async-start | bytes 2228224 | tf_op jit(solution)/shard_map/all_to_all | solution.py:288
  117.2 1.1 fusion.32
  118.3 0.1 fusion.11
  118.5 1.1 fusion.6
  119.6 0.0 copy-done.2
  119.6 0.7 reshape.160.refs_2_
  120.3 0.1 add.59
  120.5 0.7 copy.18
  121.1 9.6 %all-to-all-done.1.refs_0_ = bf16[16,136,256]{2,1,0:T(8,128)(2,1)S(1)} async-done(((bf16[16,136,256]{2,1,0:T(8,128)(2,1)}), bf16[16,136,256]{2,1,0:T(8,128)(2,1)S(1)}, u32[]{:S(2)}, u32[]{:S(2)}) %all-to-all-start.1) | async-done | bytes 1114144 | tf_op jit(solution)/shard_map/all_to_all | solution.py:288
  130.7 1.0 copy-done.3
  131.7 6.7 %shard_map.102 = bf16[256,4096]{1,0:T(8,128)(2,1)} custom-call(bf16[16,136,256]{2,1,0:T(8,128)(2,1)} %copy-done.3, bf16[16,136,256]{2,1,0:T(8,128)(2,1)} %copy-done.2, bf16[256,256]{1,0:T(8,128)(2,1)} %reshape.160.refs_2_, f32[2,256]{1,0:T(2,128)} %bitcast.40, bf16[256,4096]{1,0:T(8,128)(2,1)} %bitcast.36), custom_call_target="tpu_custom_call" | custom-call | tf_op jit(solution)/shard_map/pallas_call | solution.py:198
  138.5 26.9 %all_to_all.31.terms_ref = bf16[16,16,4096]{2,1,0:T(8,128)(2,1)} all-to-all(bf16[16,16,4096]{2,1,0:T(8,128)(2,1)} %bitcast.33), channel_id=1, replica_groups=mesh['segment'=8,'blk'=16] {'blk'}, dimensions={0} | all-to-all | bytes 4194304 | tf_op jit(solution)/shard_map/all_to_all | solution.py:297
  165.4 3.3 %shard_map.103 = bf16[16,16,4096]{2,1,0:T(8,128)(2,1)} custom-call(s32[1]{0:T(128)} %bitcast.position_ref, bf16[16,16,4096]{2,1,0:T(8,128)(2,1)} %all_to_all.31.terms_ref, bf16[256,4096]{1,0:T(8,128)(2,1)} %copy-done.1), custom_call_target="tpu_custom_call" | custom-call | tf_op jit(solution)/shard_map/pallas_call | solution.py:234
  168.6 25.5 %all_to_all.32 = bf16[16,16,4096]{2,1,0:T(8,128)(2,1)S(1)} all-to-all(bf16[16,16,4096]{2,1,0:T(8,128)(2,1)} %shard_map.103), channel_id=1, replica_groups=mesh['segment'=8,'blk'=16] {'blk'}, dimensions={0} | all-to-all | bytes 4194304 | tf_op jit(solution)/shard_map/all_to_all | solution.py:301
  194.2 1.3 copy.22
  (18 shorter events, 0.2 us)
Async XLA Ops:
  0.0 31.7 %copy-start = (bf16[1,4096,128]{2,1,0:T(8,128)(2,1)S(1)}, bf16[1,4096,128]{2,1,0:T(8,128)(2,1)}, u32[]{:S(2)}) copy-start(bf16[1,4096,128]{2,1,0:T(8,128)(2,1)} %param.16) | copy-start | bytes 3145732
  0.0 27.8 %collective-permute-start = (bf16[256,4096]{1,0:T(8,128)(2,1)}, bf16[256,4096]{1,0:T(8,128)(2,1)}, u32[]{:S(2)}, u32[]{:S(2)}) collective-permute-start(bf16[256,4096]{1,0:T(8,128)(2,1)} %bitcast.41), channel_id=1, source_target_pairs={{0,16},{16,32},{32,48},{48,64},{64,80},{80,96},{96,112},{1,17},{17... | collective-permute-start | bytes 6291464 | tf_op jit(solution)/shard_map/ppermute | solution.py:19
  2.7 25.1 %copy-start.5 = (bf16[256,4096]{1,0:T(8,128)(2,1)S(1)}, bf16[256,4096]{1,0:T(8,128)(2,1)}, u32[]{:S(2)}) copy-start(bf16[256,4096]{1,0:T(8,128)(2,1)} %param.10) | copy-start | bytes 6291460
  7.3 23.1 %copy-start.6 = (bf16[256,4096]{1,0:T(8,128)(2,1)S(1)}, bf16[256,4096]{1,0:T(8,128)(2,1)}, u32[]{:S(2)}) copy-start(bf16[256,4096]{1,0:T(8,128)(2,1)} %copy.19) | copy-start | bytes 6291460
  7.3 23.1 %copy-start.9 = (f32[1,4096]{1,0:T(1,128)S(1)}, f32[1,4096]{1,0:T(1,128)}, u32[]{:S(2)}) copy-start(f32[1,4096]{1,0:T(1,128)} %param.14) | copy-start | bytes 49156
  30.3 1.3 copy-start.1
  33.0 4.4 %copy-start.7 = (bf16[256,128]{0,1:T(8,128)(2,1)}, bf16[256,128]{0,1:T(8,128)(2,1)S(1)}, u32[]{:S(2)}) copy-start(bf16[256,128]{0,1:T(8,128)(2,1)S(1)} %fusion.23) | copy-start | bytes 196612
  33.0 4.3 %collective-permute-start.1 = (bf16[256,128]{0,1:T(8,128)(2,1)S(1)}, bf16[256,128]{0,1:T(8,128)(2,1)S(1)}, u32[]{:S(2)}, u32[]{:S(2)}) collective-permute-start(bf16[256,128]{0,1:T(8,128)(2,1)S(1)} %fusion.23), channel_id=1, source_target_pairs={{0,1},{1,0},{2,3},{3,2},{4,5},{5,4},{6,7},{7,6},{8,9},{9,8},{10,11... | collective-permute-start | bytes 196616 | tf_op jit(solution)/shard_map/ppermute | solution.py:29
  37.4 0.6 copy-start.8
  61.4 4.7 %copy-start.10 = (s32[1,16]{1,0:T(1,128)S(1)}, s32[1,16]{1,0:T(1,128)}, u32[]{:S(2)}) copy-start(s32[1,16]{1,0:T(1,128)} %param.13) | copy-start | bytes 196
  62.5 22.3 %all-to-all-start = ((bf16[16,128,256]{2,1,0:T(8,128)(2,1)}), bf16[16,128,256]{2,1,0:T(8,128)(2,1)S(1)}, u32[]{:S(2)}, u32[]{:S(2)}) async-start(bf16[16,128,256]{2,1,0:T(8,128)(2,1)} %broadcast_in_dim.10), calls=%async_computation | async-start | bytes 2097152 | tf_op jit(solution)/shard_map/all_to_all | solution.py:284
  84.7 7.2 %copy-start.4 = (bf16[16,128,256]{2,1,0:T(8,128)(2,1)}, bf16[16,128,256]{2,1,0:T(8,128)(2,1)S(1)}, u32[]{:S(2)}) copy-start(bf16[16,128,256]{2,1,0:T(8,128)(2,1)S(1)} %all-to-all-done.q_ref) | copy-start | bytes 3145732
  84.8 25.2 %all-to-all-start.3 = ((bf16[16,136,256]{2,1,0:T(8,128)(2,1)}), bf16[16,136,256]{2,1,0:T(8,128)(2,1)S(1)}, u32[]{:S(2)}, u32[]{:S(2)}) async-start(bf16[16,136,256]{2,1,0:T(8,128)(2,1)} %shard_map.101), calls=%async_computation.3 | async-start | bytes 2228224 | tf_op jit(solution)/shard_map/all_to_all | solution.py:288
  109.9 9.7 %copy-start.2 = (bf16[16,136,256]{2,1,0:T(8,128)(2,1)}, bf16[16,136,256]{2,1,0:T(8,128)(2,1)S(1)}, u32[]{:S(2)}) copy-start(bf16[16,136,256]{2,1,0:T(8,128)(2,1)S(1)} %all-to-all-done.3.refs_1_) | copy-start | bytes 3342340
  109.9 20.8 %all-to-all-start.1 = ((bf16[16,136,256]{2,1,0:T(8,128)(2,1)}), bf16[16,136,256]{2,1,0:T(8,128)(2,1)S(1)}, u32[]{:S(2)}, u32[]{:S(2)}) async-start(bf16[16,136,256]{2,1,0:T(8,128)(2,1)} %shard_map.100), calls=%async_computation.1 | async-start | bytes 2228224 | tf_op jit(solution)/shard_map/all_to_all | solution.py:288
  130.7 1.0 copy-start.3

commit v12 on v11

--- a/solution.py
+++ b/solution.py
@@ -257,35 +257,51 @@
     heads_here = w_query.shape[2] // HD
     odd_member = position % 2 == 1
     live = cache_counts[0, position].reshape(1)
-    arrived = passed_along(previous[0], "segment", 1)
-    current = jnp.where(lax.axis_index("segment") == 0, fresh, arrived)
-    widened = current.astype(jnp.float32)
-    normed = (
-        widened
-        * lax.rsqrt(jnp.mean(widened * widened, axis=-1, keepdims=True) + EPSILON)
-        * norm_gain[0]
-    ).astype(jnp.bfloat16)
-    queries = jnp.dot(normed, w_query[0], preferred_element_type=jnp.float32).reshape(
-        span_rows, heads_here, HD
-    )
-    queries = rotate(queries, first_span).astype(jnp.bfloat16).reshape(span_rows, heads_here * HD)
-    projected = jnp.dot(normed, w_keyval[0], preferred_element_type=jnp.float32)
-    as_key = rotate(projected[:, None, :], first_span)[:, 0, :].astype(jnp.bfloat16)
-    mine = jnp.where(odd_member, projected.astype(jnp.bfloat16), as_key)
-    partner = swapped(mine, "blk", 0)
-    own_keys = jnp.where(odd_member, partner, mine)
-    own_values = jnp.where(odd_member, mine, partner)
-    partner, queries = lax.optimization_barrier((partner, queries))
+    first_segment = lax.axis_index("segment") == 0
     halves = 2
     half_rows = span_rows // halves
-    arrived_halves = []
+    currents, query_parts, key_parts, value_parts, arrived_halves = [], [], [], [], []
+    outgoing = previous[0, :half_rows]
     for i in range(halves):
-        half = queries[i * half_rows:(i + 1) * half_rows]
+        rows_of = slice(i * half_rows, (i + 1) * half_rows)
+        received = passed_along(outgoing, "segment", 1)
+        if i + 1 < halves:
+            outgoing, received = lax.optimization_barrier(
+                (previous[0, (i + 1) * half_rows:(i + 2) * half_rows], received)
+            )
+        if i > 0:
+            received, every_query = lax.optimization_barrier((received, every_query))
+            held = cache_attention(live, every_query, cache_keys[0], cache_values[0])
+            arrived_halves.append(lax.all_to_all(held, "blk", split_axis=0, concat_axis=0, tiled=True))
+        current = jnp.where(first_segment, fresh[rows_of], received)
+        currents.append(current)
+        widened = current.astype(jnp.float32)
+        normed = (
+            widened
+            * lax.rsqrt(jnp.mean(widened * widened, axis=-1, keepdims=True) + EPSILON)
+            * norm_gain[0]
+        ).astype(jnp.bfloat16)
+        part_span = first_span * halves + i
+        queries = jnp.dot(normed, w_query[0], preferred_element_type=jnp.float32).reshape(
+            half_rows, heads_here, HD
+        )
+        queries = rotate(queries, part_span).astype(jnp.bfloat16).reshape(half_rows, heads_here * HD)
+        projected = jnp.dot(normed, w_keyval[0], preferred_element_type=jnp.float32)
+        as_key = rotate(projected[:, None, :], part_span)[:, 0, :].astype(jnp.bfloat16)
+        mine = jnp.where(odd_member, projected.astype(jnp.bfloat16), as_key)
+        partner = swapped(mine, "blk", 0)
+        key_parts.append(jnp.where(odd_member, partner, mine))
+        value_parts.append(jnp.where(odd_member, mine, partner))
+        query_parts.append(queries)
         every_query = lax.all_to_all(
-            jnp.broadcast_to(half[None], (blocks,) + half.shape), "blk", 0, 0, tiled=True
+            jnp.broadcast_to(queries[None], (blocks,) + queries.shape), "blk", 0, 0, tiled=True
         )
-        held = cache_attention(live, every_query, cache_keys[0], cache_values[0])
-        arrived_halves.append(lax.all_to_all(held, "blk", split_axis=0, concat_axis=0, tiled=True))
+    held = cache_attention(live, every_query, cache_keys[0], cache_values[0])
+    arrived_halves.append(lax.all_to_all(held, "blk", split_axis=0, concat_axis=0, tiled=True))
+    current = jnp.concatenate(currents, axis=0)
+    queries = jnp.concatenate(query_parts, axis=0)
+    own_keys = jnp.concatenate(key_parts, axis=0)
+    own_values = jnp.concatenate(value_parts, axis=0)
     query_rows = queries.reshape(span_rows * heads_here, HD)
     row_tokens = jnp.arange(span_rows * heads_here, dtype=jnp.int32) // heads_here
     causal = row_tokens[:, None] >= jnp.arange(span_rows, dtype=jnp.int32)[None, :]

time: 196 us -> 217 us (1.11)
  waiting for transfers between devices: 32.4 us -> 57.9 us
  blocking collectives: 75.6 us -> 56.2 us
  starting transfers between devices: 22.1 us -> 28 us
  other arithmetic: 3.38 us -> 8.4 us
  local copies, waits for them, and re-layouts: 11.1 us -> 14.2 us
    all_to_all x1 -> x2, waiting for transfers between devices: 0.01 us -> 24.8 us  [the longest x1 24.8 us: shards(): lax.all_to_all(head_terms.reshape(blocks, chunk, -1), 'blk', 0, 0, tiled=...]
    all_to_all x2 -> x1, blocking collectives: 50.1 us -> 26 us  [shards(): lax.all_to_all(jnp.broadcast_to(queries[None], (blocks,) + queries.shape)...]
    ppermute x1 -> x2, waiting for transfers between devices: 20.5 us -> 10.5 us  [passed_along(): return lax.ppermute(block, axis, route)]
    ppermute x1 -> x2, waiting for transfers between devices: 2.29 us -> 11.6 us  [swapped(): return lax.ppermute(block, axis, route)]
    all_to_all x1, blocking collectives: 25.5 us -> 30.3 us  [shards(): lax.all_to_all(spread, 'blk', 0, 0, tiled=True).reshape(span_rows, -1)]
    all_to_all x1 -> x2, starting transfers between devices: 3.66 us -> 8.06 us  [the longest x1 4.34 us: shards(): lax.all_to_all(jnp.broadcast_to(queries[None], (blocks,) + queries.shape)...]
    squeeze x0 -> x1, local copies, waits for them, and re-layouts: none -> 3.24 us  [shards(): outgoing = previous[0, :half_rows]]
    concatenate x0 -> x2, other arithmetic: none -> 3.07 us  [the longest x1 3.06 us: shards(): current = jnp.concatenate(currents, axis=0)]
  transfers between devices with their start and end apart: 5 -> 8, of which waited for: 3 -> 4; matrix products, arithmetic and copies ran while one was open for 5% -> 6% of each run, Pallas kernels for 18% -> 17%
where the time goes in v12:
time: 217 us; the launch traced here: 216 us
  waiting for transfers between devices  57.9 us (27%)
  blocking collectives  56.2 us (26%)
  Pallas kernels  45.9 us (21%)
  starting transfers between devices  28 us (13%)
  local copies, waits for them, and re-layouts  14.2 us (7%)
  other arithmetic  8.4 us (4%)
  matrix products  4.42 us (2%)
    pallas_call x2, Pallas kernels, cache_attention(): pl.pallas_call(cache_kernel, grid_spec=grid_spec, out_shape=jax.ShapeDtyp...  35.9 us
    all_to_all x1, blocking collectives, shards(): lax.all_to_all(spread, 'blk', 0, 0, tiled=True).reshape(span_rows, -1)  30.3 us
    all_to_all x1, blocking collectives, shards(): lax.all_to_all(jnp.broadcast_to(queries[None], (blocks,) + queries.shape)...  26 us
    all_to_all x1, waiting for transfers between devices, shards(): lax.all_to_all(head_terms.reshape(blocks, chunk, -1), 'blk', 0, 0, tiled=...  24.8 us
    all_to_all x2, starting transfers between devices, shards(): lax.all_to_all(held, 'blk', split_axis=0, concat_axis=0, tiled=True)  13.9 us
    ppermute x2, waiting for transfers between devices, swapped(): return lax.ppermute(block, axis, route)  11.6 us
    all_to_all x2, waiting for transfers between devices, shards(): lax.all_to_all(held, 'blk', split_axis=0, concat_axis=0, tiled=True)  11.1 us
    ppermute x2, waiting for transfers between devices, passed_along(): return lax.ppermute(block, axis, route)  10.5 us
  transfers between devices with their start and end apart: 8, of which 4 were waited for; matrix products, arithmetic and copies ran while one was open for 6% of the time, Pallas kernels for 17%

profile of v12, /device:TPU:2, one launch (start us, length us, event | category | flops | bytes accessed | tf_op | source)
XLA Modules:
  0.0 216.2 jit_solution(14445635330228512710)
XLA Ops:
  0.0 3.2 %slice_bitcast_fusion = (bf16[128,4096]{1,0:T(8,128)(2,1)}, bf16[128,4096]{1,0:T(8,128)(2,1)}) fusion(bf16[1,256,4096]{2,1,0:T(8,128)(2,1)} %param.11), kind=kLoop, calls=%fused_computation.25 | loop fusion | bytes 4194304 | tf_op jit(solution)/shard_map/squeeze | solution.py:264
  3.2 1.9 collective-permute-start
  5.2 2.9 %copy.22 = bf16[256,4096]{1,0:T(8,128)(2,1)} copy(bf16[256,4096]{0,1:T(8,128)(2,1)S(1)} %bitcast.51) | data formatting | bytes 4194304 | tf_op jit(solution)/shard_map/dot_general | solution.py:285
  8.8 0.0 copy-start.8
  8.8 0.3 multiply_cosine_fusion.2
  9.2 10.5 %collective-permute-done = bf16[128,4096]{1,0:T(8,128)(2,1)} collective-permute-done((bf16[128,4096]{1,0:T(8,128)(2,1)}, bf16[128,4096]{1,0:T(8,128)(2,1)}, u32[]{:S(2)}, u32[]{:S(2)}) %collective-permute-start) | collective-permute-done | bytes 1048608 | tf_op jit(solution)/shard_map/ppermute | solution.py:19
  19.7 2.0 fusion
  21.7 1.9 collective-permute-start.1
  23.7 0.8 fusion.14
  24.5 0.1 copy.16
  24.6 0.0 copy-start.7
  24.6 0.1 broadcast_in_dim.11
  24.7 26.0 %all_to_all.30.q_ref = bf16[16,128,256]{2,1,0:T(8,128)(2,1)} all-to-all(bf16[16,128,256]{2,1,0:T(8,128)(2,1)S(1)} %broadcast_in_dim.11), channel_id=1, replica_groups=mesh['segment'=8,'blk'=16] {'blk'}, dimensions={0} | all-to-all | bytes 2097152 | tf_op jit(solution)/shard_map/all_to_all | solution.py:296
  50.7 1.8 fusion.3
  52.6 0.0 copy-done.9
  52.6 0.8 fusion.12
  53.5 0.1 copy.18
  53.6 1.1 broadcast_in_dim.12
  54.7 4.3 %all-to-all-start.2 = ((bf16[16,128,256]{2,1,0:T(8,128)(2,1)}), bf16[16,128,256]{2,1,0:T(8,128)(2,1)}, u32[]{:S(2)}, u32[]{:S(2)}) async-start(bf16[16,128,256]{2,1,0:T(8,128)(2,1)} %broadcast_in_dim.12), calls=%async_computation.2 | async-start | bytes 2097152 | tf_op jit(solution)/shard_map/all_to_all | solution.py:296
  59.1 0.6 constant_dynamic-slice_fusion
  59.7 0.6 fusion.10
  60.3 18.0 %shard_map.100 = bf16[16,136,256]{2,1,0:T(8,128)(2,1)} custom-call(s32[1]{0:T(128)} %bitcast.1.live_ref, bf16[16,128,256]{2,1,0:T(8,128)(2,1)} %all_to_all.30.q_ref, bf16[2048,1024]{1,0:T(8,128)(2,1)} %bitcast.45, bf16[2048,1024]{1,0:T(8,128)(2,1)} %bitcast.47), custom_call_target="tpu_custom_call" | custom-call | tf_op jit(solution)/shard_map/pallas_call | solution.py:125
  78.3 7.1 %all-to-all-start.1 = ((bf16[16,136,256]{2,1,0:T(8,128)(2,1)}), bf16[16,136,256]{2,1,0:T(8,128)(2,1)S(1)}, u32[]{:S(2)}, u32[]{:S(2)}) async-start(bf16[16,136,256]{2,1,0:T(8,128)(2,1)} %shard_map.100), calls=%async_computation.1 | async-start | bytes 2228224 | tf_op jit(solution)/shard_map/all_to_all | solution.py:275
  85.4 0.6 fusion.8
  86.0 0.3 fusion.43
  86.3 2.0 collective-permute-start.2
  88.4 0.2 collective-permute-start.3
  88.6 11.6 %collective-permute-done.2 = bf16[128,128]{0,1:T(8,128)(2,1)S(1)} collective-permute-done((bf16[128,128]{0,1:T(8,128)(2,1)S(1)}, bf16[128,128]{0,1:T(8,128)(2,1)S(1)}, u32[]{:S(2)}, u32[]{:S(2)}) %collective-permute-start.2) | collective-permute-done | bytes 32800 | tf_op jit(solution)/shard_map/ppermute | solution.py:29
  100.2 17.9 %shard_map.101 = bf16[16,136,256]{2,1,0:T(8,128)(2,1)} custom-call(s32[1]{0:T(128)} %bitcast.1.live_ref, bf16[16,128,256]{2,1,0:T(8,128)(2,1)} %all-to-all-done.2.q_ref, bf16[2048,1024]{1,0:T(8,128)(2,1)} %bitcast.46, bf16[2048,1024]{1,0:T(8,128)(2,1)} %bitcast.48), custom_call_target="tpu_custom_call" | custom-call | tf_op jit(solution)/shard_map/pallas_call | solution.py:125
  118.2 6.8 %all-to-all-start.3 = ((bf16[16,136,256]{2,1,0:T(8,128)(2,1)}), bf16[16,136,256]{2,1,0:T(8,128)(2,1)S(1)}, u32[]{:S(2)}, u32[]{:S(2)}) async-start(bf16[16,136,256]{2,1,0:T(8,128)(2,1)} %shard_map.101), calls=%async_computation.3 | async-start | bytes 2228224 | tf_op jit(solution)/shard_map/all_to_all | solution.py:300
  125.0 0.6 broadcast_select_fusion
  125.6 0.3 fusion.53
  125.9 0.8 copy-done.11
  126.7 0.1 fusion.16
  126.8 0.1 add.91
  127.0 0.7 copy.21
  127.6 1.3 fusion.7
  129.0 0.7 reshape.286.refs_2_
  129.7 11.1 %all-to-all-done.3.refs_1_ = bf16[16,136,256]{2,1,0:T(8,128)(2,1)S(1)} async-done(((bf16[16,136,256]{2,1,0:T(8,128)(2,1)}), bf16[16,136,256]{2,1,0:T(8,128)(2,1)S(1)}, u32[]{:S(2)}, u32[]{:S(2)}) %all-to-all-start.3) | async-done | bytes 1114144 | tf_op jit(solution)/shard_map/all_to_all | solution.py:300
  140.7 1.0 copy-done.3
  141.7 6.7 %shard_map.102 = bf16[256,4096]{1,0:T(8,128)(2,1)} custom-call(bf16[16,136,256]{2,1,0:T(8,128)(2,1)} %copy-done.2, bf16[16,136,256]{2,1,0:T(8,128)(2,1)} %copy-done.3, bf16[256,256]{1,0:T(8,128)(2,1)} %reshape.286.refs_2_, f32[2,256]{1,0:T(2,128)} %bitcast.59, bf16[256,4096]{1,0:T(8,128)(2,1)} %bitcast.52), custom_call_target="tpu_custom_call" | custom-call | tf_op jit(solution)/shard_map/pallas_call | solution.py:198
  148.5 3.7 %all-to-all-start.4 = ((bf16[16,16,4096]{2,1,0:T(8,128)(2,1)}), bf16[16,16,4096]{2,1,0:T(8,128)(2,1)S(1)}, u32[]{:S(2)}, u32[]{:S(2)}) async-start(bf16[16,16,4096]{2,1,0:T(8,128)(2,1)} %bitcast.49), calls=%async_computation.4 | async-start | bytes 4194304 | tf_op jit(solution)/shard_map/all_to_all | solution.py:313
  152.2 3.1 %pad_maximum_fusion.current_ref = bf16[256,4096]{1,0:T(8,128)(2,1)} fusion(bf16[128,4096]{1,0:T(8,128)(2,1)} %copy-done.5, bf16[128,4096]{1,0:T(8,128)(2,1)} %copy-done.4), kind=kLoop, calls=%fused_computation.10 | loop fusion | flops 4194304 | bytes 4194304 | tf_op jit(solution)/shard_map/concatenate | solution.py:301
  155.3 24.8 %all-to-all-done.4.terms_ref = bf16[16,16,4096]{2,1,0:T(8,128)(2,1)S(1)} async-done(((bf16[16,16,4096]{2,1,0:T(8,128)(2,1)}), bf16[16,16,4096]{2,1,0:T(8,128)(2,1)S(1)}, u32[]{:S(2)}, u32[]{:S(2)}) %all-to-all-start.4) | async-done | bytes 2097184 | tf_op jit(solution)/shard_map/all_to_all | solution.py:313
  180.0 1.3 copy-done.1
  181.3 3.3 %shard_map.103 = bf16[16,16,4096]{2,1,0:T(8,128)(2,1)} custom-call(s32[1]{0:T(128)} %bitcast.position_ref, bf16[16,16,4096]{2,1,0:T(8,128)(2,1)} %copy-done.1, bf16[256,4096]{1,0:T(8,128)(2,1)} %pad_maximum_fusion.current_ref), custom_call_target="tpu_custom_call" | custom-call | tf_op jit(solution)/shard_map/pallas_call | solution.py:234
  184.6 30.3 %all_to_all.31 = bf16[16,16,4096]{2,1,0:T(8,128)(2,1)S(1)} all-to-all(bf16[16,16,4096]{2,1,0:T(8,128)(2,1)} %shard_map.103), channel_id=1, replica_groups=mesh['segment'=8,'blk'=16] {'blk'}, dimensions={0} | all-to-all | bytes 4194304 | tf_op jit(solution)/shard_map/all_to_all | solution.py:317
  214.9 1.3 copy.25
  (41 shorter events, 0.3 us)
Async XLA Ops:
  0.0 59.7 %copy-start = (bf16[1,4096,128]{2,1,0:T(8,128)(2,1)S(1)}, bf16[1,4096,128]{2,1,0:T(8,128)(2,1)}, u32[]{:S(2)}) copy-start(bf16[1,4096,128]{2,1,0:T(8,128)(2,1)} %param.16) | copy-start | bytes 3145732
  0.0 5.2 %copy-start.6 = (bf16[1,4096,256]{2,1,0:T(8,128)(2,1)S(1)}, bf16[1,4096,256]{2,1,0:T(8,128)(2,1)}, u32[]{:S(2)}) copy-start(bf16[1,4096,256]{2,1,0:T(8,128)(2,1)} %param.15) | copy-start | bytes 6291460
  3.2 16.4 %collective-permute-start = (bf16[128,4096]{1,0:T(8,128)(2,1)}, bf16[128,4096]{1,0:T(8,128)(2,1)}, u32[]{:S(2)}, u32[]{:S(2)}) collective-permute-start(bf16[128,4096]{1,0:T(8,128)(2,1)} %get-tuple-element.17), channel_id=1, source_target_pairs={{0,16},{16,32},{32,48},{48,64},{64,80},{80,96},{96,112},{1,17},{17... | collective-permute-start | bytes 3145736 | tf_op jit(solution)/shard_map/ppermute | solution.py:19
  8.0 13.7 %copy-start.10 = (bf16[128,4096]{1,0:T(8,128)(2,1)S(1)}, bf16[128,4096]{1,0:T(8,128)(2,1)}, u32[]{:S(2)}) copy-start(bf16[128,4096]{1,0:T(8,128)(2,1)} %get-tuple-element.9) | copy-start | bytes 3145732
  8.0 15.6 %copy-start.12 = (f32[1,4096]{1,0:T(1,128)S(1)}, f32[1,4096]{1,0:T(1,128)}, u32[]{:S(2)}) copy-start(f32[1,4096]{1,0:T(1,128)} %param.14) | copy-start | bytes 49156
  8.8 14.9 %copy-start.8 = (bf16[256,4096]{1,0:T(8,128)(2,1)S(1)}, bf16[256,4096]{1,0:T(8,128)(2,1)}, u32[]{:S(2)}) copy-start(bf16[256,4096]{1,0:T(8,128)(2,1)} %copy.22) | copy-start | bytes 6291460
  21.7 38.0 %copy-start.4 = (bf16[128,4096]{1,0:T(8,128)(2,1)}, bf16[128,4096]{1,0:T(8,128)(2,1)S(1)}, u32[]{:S(2)}) copy-start(bf16[128,4096]{1,0:T(8,128)(2,1)S(1)} %get-tuple-element.16) | copy-start | bytes 3145732
  21.7 29.0 %collective-permute-start.1 = (bf16[128,4096]{1,0:T(8,128)(2,1)S(1)}, bf16[128,4096]{1,0:T(8,128)(2,1)}, u32[]{:S(2)}, u32[]{:S(2)}) collective-permute-start(bf16[128,4096]{1,0:T(8,128)(2,1)S(1)} %copy-done.10), channel_id=1, source_target_pairs={{0,16},{16,32},{32,48},{48,64},{64,80},{80,96},{96,112},{1,17},{17... | collective-permute-start | bytes 3145736 | tf_op jit(solution)/shard_map/ppermute | solution.py:19
  24.6 26.1 %copy-start.7 = (bf16[256,4096]{1,0:T(8,128)(2,1)S(1)}, bf16[256,4096]{1,0:T(8,128)(2,1)}, u32[]{:S(2)}) copy-start(bf16[256,4096]{1,0:T(8,128)(2,1)} %param.10) | copy-start | bytes 6291460
  50.7 1.9 copy-start.9
  52.6 32.8 %copy-start.5 = (bf16[128,4096]{1,0:T(8,128)(2,1)}, bf16[128,4096]{1,0:T(8,128)(2,1)S(1)}, u32[]{:S(2)}) copy-start(bf16[128,4096]{1,0:T(8,128)(2,1)S(1)} %get-tuple-element.14) | copy-start | bytes 3145732
  53.4 5.6 %copy-start.13 = (s32[1,16]{1,0:T(1,128)S(1)}, s32[1,16]{1,0:T(1,128)}, u32[]{:S(2)}) copy-start(s32[1,16]{1,0:T(1,128)} %param.13) | copy-start | bytes 196
  54.7 23.6 %all-to-all-start.2 = ((bf16[16,128,256]{2,1,0:T(8,128)(2,1)}), bf16[16,128,256]{2,1,0:T(8,128)(2,1)}, u32[]{:S(2)}, u32[]{:S(2)}) async-start(bf16[16,128,256]{2,1,0:T(8,128)(2,1)} %broadcast_in_dim.12), calls=%async_computation.2 | async-start | bytes 2097152 | tf_op jit(solution)/shard_map/all_to_all | solution.py:296
  78.3 39.9 %all-to-all-start.1 = ((bf16[16,136,256]{2,1,0:T(8,128)(2,1)}), bf16[16,136,256]{2,1,0:T(8,128)(2,1)S(1)}, u32[]{:S(2)}, u32[]{:S(2)}) async-start(bf16[16,136,256]{2,1,0:T(8,128)(2,1)} %shard_map.100), calls=%async_computation.1 | async-start | bytes 2228224 | tf_op jit(solution)/shard_map/all_to_all | solution.py:275
  86.3 13.8 %collective-permute-start.2 = (bf16[128,128]{0,1:T(8,128)(2,1)S(1)}, bf16[128,128]{0,1:T(8,128)(2,1)S(1)}, u32[]{:S(2)}, u32[]{:S(2)}) collective-permute-start(bf16[128,128]{0,1:T(8,128)(2,1)S(1)} %fusion.46), channel_id=1, source_target_pairs={{0,1},{1,0},{2,3},{3,2},{4,5},{5,4},{6,7},{7,6},{8,9},{9,8},{10,11... | collective-permute-start | bytes 98312 | tf_op jit(solution)/shard_map/ppermute | solution.py:29
  88.4 36.6 %collective-permute-start.3 = (bf16[128,128]{0,1:T(8,128)(2,1)S(1)}, bf16[128,128]{0,1:T(8,128)(2,1)S(1)}, u32[]{:S(2)}, u32[]{:S(2)}) collective-permute-start(bf16[128,128]{0,1:T(8,128)(2,1)S(1)} %fusion.47), channel_id=1, source_target_pairs={{0,1},{1,0},{2,3},{3,2},{4,5},{5,4},{6,7},{7,6},{8,9},{9,8},{10,11... | collective-permute-start | bytes 98312 | tf_op jit(solution)/shard_map/ppermute | solution.py:29
  118.2 10.8 %copy-start.2 = (bf16[16,136,256]{2,1,0:T(8,128)(2,1)}, bf16[16,136,256]{2,1,0:T(8,128)(2,1)S(1)}, u32[]{:S(2)}) copy-start(bf16[16,136,256]{2,1,0:T(8,128)(2,1)S(1)} %all-to-all-done.1.refs_0_) | copy-start | bytes 3342340
  118.2 22.6 %all-to-all-start.3 = ((bf16[16,136,256]{2,1,0:T(8,128)(2,1)}), bf16[16,136,256]{2,1,0:T(8,128)(2,1)S(1)}, u32[]{:S(2)}, u32[]{:S(2)}) async-start(bf16[16,136,256]{2,1,0:T(8,128)(2,1)} %shard_map.101), calls=%async_computation.3 | async-start | bytes 2228224 | tf_op jit(solution)/shard_map/all_to_all | solution.py:300
  125.9 0.8 copy-start.11
  140.7 1.0 copy-start.3
  148.5 31.6 %all-to-all-start.4 = ((bf16[16,16,4096]{2,1,0:T(8,128)(2,1)}), bf16[16,16,4096]{2,1,0:T(8,128)(2,1)S(1)}, u32[]{:S(2)}, u32[]{:S(2)}) async-start(bf16[16,16,4096]{2,1,0:T(8,128)(2,1)} %bitcast.49), calls=%async_computation.4 | async-start | bytes 4194304 | tf_op jit(solution)/shard_map/all_to_all | solution.py:313
  180.0 1.3 copy-start.1

commit v13 on v11

--- a/solution.py
+++ b/solution.py
@@ -292,7 +292,18 @@
     own_out, own_log = attend_rows(query_rows, own_keys, own_values, causal)
     own_out = own_out.reshape(span_rows, heads_here * HD)
     own_log = own_log.reshape(span_rows, heads_here).T
-    head_terms = combine(arrived_halves, own_out, own_log, w_out[0])
+    head_terms = jnp.concatenate(
+        [
+            combine(
+                [part],
+                own_out[i * half_rows:(i + 1) * half_rows],
+                own_log[:, i * half_rows:(i + 1) * half_rows],
+                w_out[0],
+            )
+            for i, part in enumerate(arrived_halves)
+        ],
+        axis=0,
+    )
     chunk = span_rows // blocks
     gathered_terms = lax.all_to_all(
         head_terms.reshape(blocks, chunk, -1), "blk", 0, 0, tiled=True

time: 196 us -> 202 us (1.031)
  the two profiles are of different devices: /device:TPU:2 before, /device:TPU:6 now
where the time goes in v13:
time: 202 us; the launch traced here: 200 us
  blocking collectives  75.9 us (38%)
  Pallas kernels  50.2 us (25%)
  waiting for transfers between devices  29.3 us (15%)
  starting transfers between devices  22.8 us (11%)
  local copies, waits for them, and re-layouts  11.3 us (6%)
  other arithmetic  5.82 us (3%)
  matrix products  4.35 us (2%)
    pallas_call x2, Pallas kernels, cache_attention(): pl.pallas_call(cache_kernel, grid_spec=grid_spec, out_shape=jax.ShapeDtyp...  36.1 us
    all_to_all x1, blocking collectives, shards(): lax.all_to_all(head_terms.reshape(blocks, chunk, -1), 'blk', 0, 0, tiled=...  32.4 us
    all_to_all x1, blocking collectives, shards(): lax.all_to_all(spread, 'blk', 0, 0, tiled=True).reshape(span_rows, -1)  22.6 us
    all_to_all x1, blocking collectives, shards(): lax.all_to_all(jnp.broadcast_to(half[None], (blocks,) + half.shape), 'blk...  20.9 us
    ppermute x1, waiting for transfers between devices, passed_along(): return lax.ppermute(block, axis, route)  20.5 us
    all_to_all x2, starting transfers between devices, shards(): lax.all_to_all(held, 'blk', split_axis=0, concat_axis=0, tiled=True)  15.1 us
    pallas_call x2, Pallas kernels, combine(): pl.pallas_call(combine_kernel, grid=(columns // COLUMN_BLOCK,), in_specs=...  10.8 us
    all_to_all x2, waiting for transfers between devices, shards(): lax.all_to_all(held, 'blk', split_axis=0, concat_axis=0, tiled=True)  7.44 us
  transfers between devices with their start and end apart: 5, of which 3 were waited for; matrix products, arithmetic and copies ran while one was open for 6% of the time, Pallas kernels for 21%

profile of v13, /device:TPU:6, one launch (start us, length us, event | category | flops | bytes accessed | tf_op | source)
XLA Modules:
  0.0 200.5 jit_solution(5555936861137213367)
XLA Ops:
  0.0 2.0 %collective-permute-start = (bf16[256,4096]{1,0:T(8,128)(2,1)}, bf16[256,4096]{1,0:T(8,128)(2,1)}, u32[]{:S(2)}, u32[]{:S(2)}) collective-permute-start(bf16[256,4096]{1,0:T(8,128)(2,1)} %bitcast.42), channel_id=1, source_target_pairs={{0,16},{16,32},{32,48},{48,64},{64,80},{80,96},{96,112},{1,17},{17... | collective-permute-start | bytes 6291464 | tf_op jit(solution)/shard_map/ppermute | solution.py:19
  2.7 4.2 %copy.19 = bf16[256,4096]{1,0:T(8,128)(2,1)} copy(bf16[256,4096]{0,1:T(8,128)(2,1)} %bitcast.37) | data formatting | bytes 4194304 | tf_op jit(solution)/shard_map/dot_general | solution.py:268
  7.0 0.3 multiply_cosine_fusion
  7.3 0.0 copy-start.11
  7.3 20.5 %collective-permute-done = bf16[256,4096]{1,0:T(8,128)(2,1)} collective-permute-done((bf16[256,4096]{1,0:T(8,128)(2,1)}, bf16[256,4096]{1,0:T(8,128)(2,1)}, u32[]{:S(2)}, u32[]{:S(2)}) %collective-permute-start) | collective-permute-done | bytes 2097184 | tf_op jit(solution)/shard_map/ppermute | solution.py:19
  27.8 2.5 %fusion = (f32[256]{0:T(256)S(1)}, bf16[256,4096]{1,0:T(8,128)(2,1)S(1)}) fusion(bf16[256,4096]{1,0:T(8,128)(2,1)S(1)} %copy-done.6, bf16[256,4096]{1,0:T(8,128)(2,1)} %collective-permute-done, pred[]{:T(512)S(6)} %eq.9), kind=kLoop, calls=%fused_computation.2 | loop fusion | flops 4194048 | bytes 6292481 | tf_op jit(solution)/shard_map/reduce_sum | solution.py:265
  30.3 0.0 copy-start.1
  30.4 0.0 copy-start.7
  30.4 1.0 fusion.7
  31.4 0.3 fusion.20
  31.7 2.0 collective-permute-start.1
  33.7 0.0 copy-done.1
  33.7 1.0 fusion.3
  34.8 1.3 collective-permute-done.1
  36.1 0.6 copy-done.10
  36.7 0.1 copy.15
  36.8 0.1 broadcast_in_dim.10
  36.9 20.9 %all_to_all.30.q_ref = bf16[16,128,256]{2,1,0:T(8,128)(2,1)} all-to-all(bf16[16,128,256]{2,1,0:T(8,128)(2,1)S(1)} %broadcast_in_dim.10), channel_id=1, replica_groups=mesh['segment'=8,'blk'=16] {'blk'}, dimensions={0} | all-to-all | bytes 2097152 | tf_op jit(solution)/shard_map/all_to_all | solution.py:284
  57.8 1.1 broadcast_in_dim.12
  58.9 3.7 %all-to-all-start.2 = ((bf16[16,128,256]{2,1,0:T(8,128)(2,1)}), bf16[16,128,256]{2,1,0:T(8,128)(2,1)S(1)}, u32[]{:S(2)}, u32[]{:S(2)}) async-start(bf16[16,128,256]{2,1,0:T(8,128)(2,1)} %broadcast_in_dim.12), calls=%async_computation.2 | async-start | bytes 2097152 | tf_op jit(solution)/shard_map/all_to_all | solution.py:284
  62.5 0.0 copy-done.12
  62.5 0.7 constant_dynamic-slice_fusion
  63.2 18.1 %shard_map.100 = bf16[16,136,256]{2,1,0:T(8,128)(2,1)} custom-call(s32[1]{0:T(128)} %bitcast.1.live_ref, bf16[16,128,256]{2,1,0:T(8,128)(2,1)} %all_to_all.30.q_ref, bf16[2048,1024]{1,0:T(8,128)(2,1)} %bitcast.29, bf16[2048,1024]{1,0:T(8,128)(2,1)} %bitcast.31), custom_call_target="tpu_custom_call" | custom-call | tf_op jit(solution)/shard_map/pallas_call | solution.py:125
  81.3 0.0 all-to-all-done.2.q_ref
  81.3 7.2 %all-to-all-start.1 = ((bf16[16,136,256]{2,1,0:T(8,128)(2,1)}), bf16[16,136,256]{2,1,0:T(8,128)(2,1)S(1)}, u32[]{:S(2)}, u32[]{:S(2)}) async-start(bf16[16,136,256]{2,1,0:T(8,128)(2,1)} %shard_map.100), calls=%async_computation.1 | async-start | bytes 2228224 | tf_op jit(solution)/shard_map/all_to_all | solution.py:288
  88.5 1.1 fusion.34
  89.6 0.0 copy-done.5
  89.6 18.0 %shard_map.102 = bf16[16,136,256]{2,1,0:T(8,128)(2,1)} custom-call(s32[1]{0:T(128)} %bitcast.1.live_ref, bf16[16,128,256]{2,1,0:T(8,128)(2,1)} %copy-done.5, bf16[2048,1024]{1,0:T(8,128)(2,1)} %bitcast.30, bf16[2048,1024]{1,0:T(8,128)(2,1)} %bitcast.32), custom_call_target="tpu_custom_call" | custom-call | tf_op jit(solution)/shard_map/pallas_call | solution.py:125
  107.6 0.0 all-to-all-done.1.refs_0_
  107.6 7.9 %all-to-all-start.3 = ((bf16[16,136,256]{2,1,0:T(8,128)(2,1)}), bf16[16,136,256]{2,1,0:T(8,128)(2,1)S(1)}, u32[]{:S(2)}, u32[]{:S(2)}) async-start(bf16[16,136,256]{2,1,0:T(8,128)(2,1)} %shard_map.102), calls=%async_computation.3 | async-start | bytes 2228224 | tf_op jit(solution)/shard_map/all_to_all | solution.py:288
  115.6 1.1 fusion.11
  116.7 0.1 add.59
  116.9 0.1 copy.17
  116.9 0.0 copy-done.9
  116.9 1.3 fusion.6
  118.3 0.0 copy-done.2
  118.3 0.7 slice.42.refs_1_
  119.0 0.6 slice.46.refs_1_
  119.6 0.6 fusion.33
  120.2 5.4 %shard_map.101 = bf16[128,4096]{1,0:T(8,128)(2,1)} custom-call(bf16[16,136,256]{2,1,0:T(8,128)(2,1)} %copy-done.2, bf16[128,256]{1,0:T(8,128)(2,1)} %slice.42.refs_1_, f32[2,128]{1,0:T(2,128)} %get-tuple-element.17.refs_2_, bf16[256,4096]{1,0:T(8,128)(2,1)} %bitcast.33), custom_call_target="tpu_custom_call" | custom-call | tf_op jit(solution)/shard_map/pallas_call | solution.py:198
  125.6 7.4 %all-to-all-done.3.refs_0_ = bf16[16,136,256]{2,1,0:T(8,128)(2,1)S(1)} async-done(((bf16[16,136,256]{2,1,0:T(8,128)(2,1)}), bf16[16,136,256]{2,1,0:T(8,128)(2,1)S(1)}, u32[]{:S(2)}, u32[]{:S(2)}) %all-to-all-start.3) | async-done | bytes 1114144 | tf_op jit(solution)/shard_map/all_to_all | solution.py:288
  133.0 1.0 copy-done.3
  134.0 5.5 %shard_map.103 = bf16[128,4096]{1,0:T(8,128)(2,1)} custom-call(bf16[16,136,256]{2,1,0:T(8,128)(2,1)} %copy-done.3, bf16[128,256]{1,0:T(8,128)(2,1)} %slice.46.refs_1_, f32[2,128]{1,0:T(2,128)} %get-tuple-element.18.refs_2_, bf16[256,4096]{1,0:T(8,128)(2,1)} %bitcast.34), custom_call_target="tpu_custom_call" | custom-call | tf_op jit(solution)/shard_map/pallas_call | solution.py:198
  139.5 1.4 pad_maximum_fusion
  140.9 32.4 %all_to_all.31.terms_ref = bf16[16,16,4096]{2,1,0:T(8,128)(2,1)} all-to-all(bf16[16,16,4096]{2,1,0:T(8,128)(2,1)S(1)} %bitcast.35), channel_id=1, replica_groups=mesh['segment'=8,'blk'=16] {'blk'}, dimensions={0} | all-to-all | bytes 4194304 | tf_op jit(solution)/shard_map/all_to_all | solution.py:308
  173.3 3.3 %shard_map.104 = bf16[16,16,4096]{2,1,0:T(8,128)(2,1)} custom-call(s32[1]{0:T(128)} %bitcast.position_ref, bf16[16,16,4096]{2,1,0:T(8,128)(2,1)} %all_to_all.31.terms_ref, bf16[256,4096]{1,0:T(8,128)(2,1)} %copy-done.1), custom_call_target="tpu_custom_call" | custom-call | tf_op jit(solution)/shard_map/pallas_call | solution.py:234
  176.6 22.6 %all_to_all.32 = bf16[16,16,4096]{2,1,0:T(8,128)(2,1)S(1)} all-to-all(bf16[16,16,4096]{2,1,0:T(8,128)(2,1)} %shard_map.104), channel_id=1, replica_groups=mesh['segment'=8,'blk'=16] {'blk'}, dimensions={0} | all-to-all | bytes 4194304 | tf_op jit(solution)/shard_map/all_to_all | solution.py:312
  199.2 1.3 copy.22
  (27 shorter events, 0.2 us)
Async XLA Ops:
  0.0 30.4 %copy-start = (bf16[1,4096,128]{2,1,0:T(8,128)(2,1)S(1)}, bf16[1,4096,128]{2,1,0:T(8,128)(2,1)}, u32[]{:S(2)}) copy-start(bf16[1,4096,128]{2,1,0:T(8,128)(2,1)} %param.16) | copy-start | bytes 3145732
  0.0 27.8 %collective-permute-start = (bf16[256,4096]{1,0:T(8,128)(2,1)}, bf16[256,4096]{1,0:T(8,128)(2,1)}, u32[]{:S(2)}, u32[]{:S(2)}) collective-permute-start(bf16[256,4096]{1,0:T(8,128)(2,1)} %bitcast.42), channel_id=1, source_target_pairs={{0,16},{16,32},{32,48},{48,64},{64,80},{80,96},{96,112},{1,17},{17... | collective-permute-start | bytes 6291464 | tf_op jit(solution)/shard_map/ppermute | solution.py:19
  2.7 25.1 %copy-start.6 = (bf16[256,4096]{1,0:T(8,128)(2,1)S(1)}, bf16[256,4096]{1,0:T(8,128)(2,1)}, u32[]{:S(2)}) copy-start(bf16[256,4096]{1,0:T(8,128)(2,1)} %param.10) | copy-start | bytes 6291460
  7.3 23.1 %copy-start.11 = (f32[1,4096]{1,0:T(1,128)S(1)}, f32[1,4096]{1,0:T(1,128)}, u32[]{:S(2)}) copy-start(f32[1,4096]{1,0:T(1,128)} %param.14) | copy-start | bytes 49156
  30.3 3.4 %copy-start.1 = (bf16[256,4096]{1,0:T(8,128)(2,1)}, bf16[256,4096]{1,0:T(8,128)(2,1)S(1)}, u32[]{:S(2)}) copy-start(bf16[256,4096]{1,0:T(8,128)(2,1)S(1)} %get-tuple-element.8.current_ref) | copy-start | bytes 6291460
  30.4 3.3 %copy-start.7 = (bf16[256,4096]{1,0:T(8,128)(2,1)S(1)}, bf16[256,4096]{1,0:T(8,128)(2,1)}, u32[]{:S(2)}) copy-start(bf16[256,4096]{1,0:T(8,128)(2,1)} %copy.19) | copy-start | bytes 6291460
  31.7 56.8 %copy-start.8 = (bf16[256,128]{0,1:T(8,128)(2,1)}, bf16[256,128]{0,1:T(8,128)(2,1)S(1)}, u32[]{:S(2)}) copy-start(bf16[256,128]{0,1:T(8,128)(2,1)S(1)} %fusion.23) | copy-start | bytes 196612
  31.7 4.3 %collective-permute-start.1 = (bf16[256,128]{0,1:T(8,128)(2,1)S(1)}, bf16[256,128]{0,1:T(8,128)(2,1)S(1)}, u32[]{:S(2)}, u32[]{:S(2)}) collective-permute-start(bf16[256,128]{0,1:T(8,128)(2,1)S(1)} %fusion.23), channel_id=1, source_target_pairs={{0,1},{1,0},{2,3},{3,2},{4,5},{5,4},{6,7},{7,6},{8,9},{9,8},{10,11... | collective-permute-start | bytes 196616 | tf_op jit(solution)/shard_map/ppermute | solution.py:29
  36.1 0.6 copy-start.10
  57.8 4.7 %copy-start.12 = (s32[1,16]{1,0:T(1,128)S(1)}, s32[1,16]{1,0:T(1,128)}, u32[]{:S(2)}) copy-start(s32[1,16]{1,0:T(1,128)} %param.13) | copy-start | bytes 196
  58.9 22.4 %all-to-all-start.2 = ((bf16[16,128,256]{2,1,0:T(8,128)(2,1)}), bf16[16,128,256]{2,1,0:T(8,128)(2,1)S(1)}, u32[]{:S(2)}, u32[]{:S(2)}) async-start(bf16[16,128,256]{2,1,0:T(8,128)(2,1)} %broadcast_in_dim.12), calls=%async_computation.2 | async-start | bytes 2097152 | tf_op jit(solution)/shard_map/all_to_all | solution.py:284
  81.3 8.3 %copy-start.5 = (bf16[16,128,256]{2,1,0:T(8,128)(2,1)}, bf16[16,128,256]{2,1,0:T(8,128)(2,1)S(1)}, u32[]{:S(2)}) copy-start(bf16[16,128,256]{2,1,0:T(8,128)(2,1)S(1)} %all-to-all-done.2.q_ref) | copy-start | bytes 3145732
  81.3 26.4 %all-to-all-start.1 = ((bf16[16,136,256]{2,1,0:T(8,128)(2,1)}), bf16[16,136,256]{2,1,0:T(8,128)(2,1)S(1)}, u32[]{:S(2)}, u32[]{:S(2)}) async-start(bf16[16,136,256]{2,1,0:T(8,128)(2,1)} %shard_map.100), calls=%async_computation.1 | async-start | bytes 2228224 | tf_op jit(solution)/shard_map/all_to_all | solution.py:288
  107.6 9.3 %copy-start.9 = (bf16[256,128]{0,1:T(8,128)(2,1)S(1)}, bf16[256,128]{0,1:T(8,128)(2,1)}, u32[]{:S(2)}) copy-start(bf16[256,128]{0,1:T(8,128)(2,1)} %copy-done.8) | copy-start | bytes 196612
  107.6 10.7 %copy-start.2 = (bf16[16,136,256]{2,1,0:T(8,128)(2,1)}, bf16[16,136,256]{2,1,0:T(8,128)(2,1)S(1)}, u32[]{:S(2)}) copy-start(bf16[16,136,256]{2,1,0:T(8,128)(2,1)S(1)} %all-to-all-done.1.refs_0_) | copy-start | bytes 3342340
  107.6 25.4 %all-to-all-start.3 = ((bf16[16,136,256]{2,1,0:T(8,128)(2,1)}), bf16[16,136,256]{2,1,0:T(8,128)(2,1)S(1)}, u32[]{:S(2)}, u32[]{:S(2)}) async-start(bf16[16,136,256]{2,1,0:T(8,128)(2,1)} %shard_map.102), calls=%async_computation.3 | async-start | bytes 2228224 | tf_op jit(solution)/shard_map/all_to_all | solution.py:288
  133.0 1.0 copy-start.3
  134.0 5.5 %copy-start.4 = (bf16[128,4096]{1,0:T(8,128)(2,1)S(1)}, bf16[128,4096]{1,0:T(8,128)(2,1)}, u32[]{:S(2)}) copy-start(bf16[128,4096]{1,0:T(8,128)(2,1)} %shard_map.101) | copy-start | bytes 3145732

commit v14 on v11

--- a/solution.py
+++ b/solution.py
@@ -275,7 +275,6 @@
     partner = swapped(mine, "blk", 0)
     own_keys = jnp.where(odd_member, partner, mine)
     own_values = jnp.where(odd_member, mine, partner)
-    partner, queries = lax.optimization_barrier((partner, queries))
     halves = 2
     half_rows = span_rows // halves
     arrived_halves = []

time: 196 us -> 203 us (1.036)
  blocking collectives: 75.6 us -> 59.4 us
  waiting for transfers between devices: 32.4 us -> 48.1 us
  starting transfers between devices: 22.1 us -> 30.7 us
    all_to_all x1 -> x0, blocking collectives: 23.2 us -> none  [shards(): lax.all_to_all(jnp.broadcast_to(half[None], (blocks,) + half.shape), 'blk...]
    all_to_all x1 -> x2, waiting for transfers between devices: 0.01 us -> 16.5 us  [shards(): lax.all_to_all(jnp.broadcast_to(half[None], (blocks,) + half.shape), 'blk...]
    all_to_all x2, waiting for transfers between devices: 9.63 us -> 0.01 us  [shards(): lax.all_to_all(held, 'blk', split_axis=0, concat_axis=0, tiled=True)]
    all_to_all x1 -> x2, starting transfers between devices: 3.66 us -> 12.4 us  [shards(): lax.all_to_all(jnp.broadcast_to(half[None], (blocks,) + half.shape), 'blk...]
    ppermute x1, waiting for transfers between devices: 2.29 us -> 11 us  [swapped(): return lax.ppermute(block, axis, route)]
    all_to_all x1, blocking collectives: 26.9 us -> 31.1 us  [shards(): lax.all_to_all(head_terms.reshape(blocks, chunk, -1), 'blk', 0, 0, tiled=...]
    all_to_all x1, blocking collectives: 25.5 us -> 28.3 us  [shards(): lax.all_to_all(spread, 'blk', 0, 0, tiled=True).reshape(span_rows, -1)]
  transfers between devices with their start and end apart: 5 -> 6, of which waited for: 3 -> 3; matrix products, arithmetic and copies ran while one was open for 5% -> 4% of each run, Pallas kernels for 18% -> 18%
where the time goes in v14:
time: 203 us; the launch traced here: 202 us
  blocking collectives  59.4 us (29%)
  waiting for transfers between devices  48.1 us (24%)
  Pallas kernels  45.9 us (23%)
  starting transfers between devices  30.7 us (15%)
  local copies, waits for them, and re-layouts  11.2 us (6%)
  other arithmetic  3.39 us (2%)
  matrix products  2.46 us (1%)
    pallas_call x2, Pallas kernels, cache_attention(): pl.pallas_call(cache_kernel, grid_spec=grid_spec, out_shape=jax.ShapeDtyp...  35.9 us
    all_to_all x1, blocking collectives, shards(): lax.all_to_all(head_terms.reshape(blocks, chunk, -1), 'blk', 0, 0, tiled=...  31.1 us
    all_to_all x1, blocking collectives, shards(): lax.all_to_all(spread, 'blk', 0, 0, tiled=True).reshape(span_rows, -1)  28.3 us
    ppermute x1, waiting for transfers between devices, passed_along(): return lax.ppermute(block, axis, route)  20.7 us
    all_to_all x2, waiting for transfers between devices, shards(): lax.all_to_all(jnp.broadcast_to(half[None], (blocks,) + half.shape), 'blk...  16.5 us
    all_to_all x2, starting transfers between devices, shards(): lax.all_to_all(held, 'blk', split_axis=0, concat_axis=0, tiled=True)  14.3 us
    all_to_all x2, starting transfers between devices, shards(): lax.all_to_all(jnp.broadcast_to(half[None], (blocks,) + half.shape), 'blk...  12.4 us
    ppermute x1, waiting for transfers between devices, swapped(): return lax.ppermute(block, axis, route)  11 us
  transfers between devices with their start and end apart: 6, of which 3 were waited for; matrix products, arithmetic and copies ran while one was open for 4% of the time, Pallas kernels for 18%

profile of v14, /device:TPU:2, one launch (start us, length us, event | category | flops | bytes accessed | tf_op | source)
XLA Modules:
  0.0 202.1 jit_solution(9896408784741897521)
XLA Ops:
  0.0 0.0 copy-start
  0.0 2.0 %collective-permute-start = (bf16[256,4096]{1,0:T(8,128)(2,1)}, bf16[256,4096]{1,0:T(8,128)(2,1)}, u32[]{:S(2)}, u32[]{:S(2)}) collective-permute-start(bf16[256,4096]{1,0:T(8,128)(2,1)} %bitcast.46), channel_id=1, source_target_pairs={{0,16},{16,32},{32,48},{48,64},{64,80},{80,96},{96,112},{1,17},{17... | collective-permute-start | bytes 6291464 | tf_op jit(solution)/shard_map/ppermute | solution.py:19
  2.7 4.1 %copy.20 = bf16[256,4096]{1,0:T(8,128)(2,1)} copy(bf16[256,4096]{0,1:T(8,128)(2,1)} %bitcast.37) | data formatting | bytes 4194304 | tf_op jit(solution)/shard_map/dot_general | solution.py:268
  6.8 0.3 multiply_cosine_fusion.1
  7.1 0.0 copy-start.3
  7.1 0.0 copy-start.4
  7.1 20.7 %collective-permute-done = bf16[256,4096]{1,0:T(8,128)(2,1)} collective-permute-done((bf16[256,4096]{1,0:T(8,128)(2,1)}, bf16[256,4096]{1,0:T(8,128)(2,1)}, u32[]{:S(2)}, u32[]{:S(2)}) %collective-permute-start) | collective-permute-done | bytes 2097184 | tf_op jit(solution)/shard_map/ppermute | solution.py:19
  27.8 2.5 %fusion = (f32[256]{0:T(256)S(1)}, bf16[256,4096]{1,0:T(8,128)(2,1)S(1)}) fusion(bf16[256,4096]{1,0:T(8,128)(2,1)} %param.10, bf16[256,4096]{1,0:T(8,128)(2,1)} %collective-permute-done, pred[]{:T(512)S(6)} %eq.8), kind=kLoop, calls=%fused_computation.2 | loop fusion | flops 4194048 | bytes 6292481 | tf_op jit(solution)/shard_map/reduce_sum | solution.py:265
  30.3 0.0 copy-start.1
  30.4 0.0 copy-done.3
  30.4 0.9 fusion.3
  31.4 0.1 copy.15
  31.5 1.1 broadcast_in_dim.14
  32.5 8.1 %all-to-all-start = ((bf16[16,128,256]{2,1,0:T(8,128)(2,1)}), bf16[16,128,256]{2,1,0:T(8,128)(2,1)}, u32[]{:S(2)}, u32[]{:S(2)}) async-start(bf16[16,128,256]{2,1,0:T(8,128)(2,1)} %broadcast_in_dim.14), calls=%async_computation | async-start | bytes 2097152 | tf_op jit(solution)/shard_map/all_to_all | solution.py:283
  40.6 0.0 copy-start.5
  40.7 0.1 copy.16
  40.8 16.5 %all-to-all-done.q_ref = bf16[16,128,256]{2,1,0:T(8,128)(2,1)} async-done(((bf16[16,128,256]{2,1,0:T(8,128)(2,1)}), bf16[16,128,256]{2,1,0:T(8,128)(2,1)}, u32[]{:S(2)}, u32[]{:S(2)}) %all-to-all-start) | async-done | bytes 1048608 | tf_op jit(solution)/shard_map/all_to_all | solution.py:283
  57.3 1.1 broadcast_in_dim.16
  58.4 4.3 %all-to-all-start.2 = ((bf16[16,128,256]{2,1,0:T(8,128)(2,1)}), bf16[16,128,256]{2,1,0:T(8,128)(2,1)}, u32[]{:S(2)}, u32[]{:S(2)}) async-start(bf16[16,128,256]{2,1,0:T(8,128)(2,1)} %broadcast_in_dim.16), calls=%async_computation.2 | async-start | bytes 2097152 | tf_op jit(solution)/shard_map/all_to_all | solution.py:283
  62.7 0.0 copy-done.5
  62.8 0.6 constant_dynamic-slice_fusion
  63.3 18.0 %shard_map.100 = bf16[16,136,256]{2,1,0:T(8,128)(2,1)} custom-call(s32[1]{0:T(128)} %bitcast.1.live_ref, bf16[16,128,256]{2,1,0:T(8,128)(2,1)} %all-to-all-done.q_ref, bf16[2048,1024]{1,0:T(8,128)(2,1)} %bitcast.31, bf16[2048,1024]{1,0:T(8,128)(2,1)} %bitcast.33), custom_call_target="tpu_custom_call" | custom-call | tf_op jit(solution)/shard_map/pallas_call | solution.py:125
  81.3 0.0 all-to-all-done.2.q_ref
  81.3 7.1 %all-to-all-start.1 = ((bf16[16,136,256]{2,1,0:T(8,128)(2,1)}), bf16[16,136,256]{2,1,0:T(8,128)(2,1)}, u32[]{:S(2)}, u32[]{:S(2)}) async-start(bf16[16,136,256]{2,1,0:T(8,128)(2,1)} %shard_map.100), calls=%async_computation.1 | async-start | bytes 2228224 | tf_op jit(solution)/shard_map/all_to_all | solution.py:287
  88.5 0.0 copy-done.1
  88.5 0.0 copy-done
  88.5 1.0 fusion.7
  89.4 0.3 fusion.23
  89.8 18.0 %shard_map.101 = bf16[16,136,256]{2,1,0:T(8,128)(2,1)} custom-call(s32[1]{0:T(128)} %bitcast.1.live_ref, bf16[16,128,256]{2,1,0:T(8,128)(2,1)} %all-to-all-done.2.q_ref, bf16[2048,1024]{1,0:T(8,128)(2,1)} %bitcast.32, bf16[2048,1024]{1,0:T(8,128)(2,1)} %bitcast.34), custom_call_target="tpu_custom_call" | custom-call | tf_op jit(solution)/shard_map/pallas_call | solution.py:125
  107.7 0.0 all-to-all-done.1.refs_0_
  107.7 7.2 %all-to-all-start.3 = ((bf16[16,136,256]{2,1,0:T(8,128)(2,1)}), bf16[16,136,256]{2,1,0:T(8,128)(2,1)S(1)}, u32[]{:S(2)}, u32[]{:S(2)}) async-start(bf16[16,136,256]{2,1,0:T(8,128)(2,1)} %shard_map.101), calls=%async_computation.3 | async-start | bytes 2228224 | tf_op jit(solution)/shard_map/all_to_all | solution.py:287
  114.9 2.0 collective-permute-start.1
  116.9 0.1 copy.18
  117.0 0.1 copy.17
  117.2 11.0 %collective-permute-done.1 = bf16[256,128]{0,1:T(8,128)(2,1)S(1)} collective-permute-done((bf16[256,128]{0,1:T(8,128)(2,1)S(1)}, bf16[256,128]{0,1:T(8,128)(2,1)S(1)}, u32[]{:S(2)}, u32[]{:S(2)}) %collective-permute-start.1) | collective-permute-done | bytes 65568 | tf_op jit(solution)/shard_map/ppermute | solution.py:29
  128.1 0.3 fusion.36
  128.5 0.1 fusion.11
  128.6 0.3 fusion.6
  128.9 0.7 reshape.162.refs_2_
  129.6 0.1 add.59
  129.7 0.7 copy.19
  130.4 0.0 all-to-all-done.3.refs_1_
  130.4 1.0 copy-done.2
  131.4 6.7 %shard_map.102 = bf16[256,4096]{1,0:T(8,128)(2,1)} custom-call(bf16[16,136,256]{2,1,0:T(8,128)(2,1)} %all-to-all-done.1.refs_0_, bf16[16,136,256]{2,1,0:T(8,128)(2,1)} %copy-done.2, bf16[256,256]{1,0:T(8,128)(2,1)} %reshape.162.refs_2_, f32[2,256]{1,0:T(2,128)} %bitcast.45, bf16[256,4096]{1,0:T(8,128)(2,1)} %bitcast.38), custom_call_target="tpu_custom_call" | custom-call | tf_op jit(solution)/shard_map/pallas_call | solution.py:198
  138.1 31.1 %all_to_all.30.terms_ref = bf16[16,16,4096]{2,1,0:T(8,128)(2,1)} all-to-all(bf16[16,16,4096]{2,1,0:T(8,128)(2,1)} %bitcast.35), channel_id=1, replica_groups=mesh['segment'=8,'blk'=16] {'blk'}, dimensions={0} | all-to-all | bytes 4194304 | tf_op jit(solution)/shard_map/all_to_all | solution.py:296
  169.2 3.3 %shard_map.103 = bf16[16,16,4096]{2,1,0:T(8,128)(2,1)} custom-call(s32[1]{0:T(128)} %bitcast.position_ref, bf16[16,16,4096]{2,1,0:T(8,128)(2,1)} %all_to_all.30.terms_ref, bf16[256,4096]{1,0:T(8,128)(2,1)} %copy-done.1), custom_call_target="tpu_custom_call" | custom-call | tf_op jit(solution)/shard_map/pallas_call | solution.py:234
  172.5 28.3 %all_to_all.31 = bf16[16,16,4096]{2,1,0:T(8,128)(2,1)S(1)} all-to-all(bf16[16,16,4096]{2,1,0:T(8,128)(2,1)} %shard_map.103), channel_id=1, replica_groups=mesh['segment'=8,'blk'=16] {'blk'}, dimensions={0} | all-to-all | bytes 4194304 | tf_op jit(solution)/shard_map/all_to_all | solution.py:300
  200.8 1.3 copy.23
  (10 shorter events, 0.1 us)
Async XLA Ops:
  0.0 88.5 %copy-start = (bf16[1,4096,128]{2,1,0:T(8,128)(2,1)S(1)}, bf16[1,4096,128]{2,1,0:T(8,128)(2,1)}, u32[]{:S(2)}) copy-start(bf16[1,4096,128]{2,1,0:T(8,128)(2,1)} %param.16) | copy-start | bytes 3145732
  0.0 27.8 %collective-permute-start = (bf16[256,4096]{1,0:T(8,128)(2,1)}, bf16[256,4096]{1,0:T(8,128)(2,1)}, u32[]{:S(2)}, u32[]{:S(2)}) collective-permute-start(bf16[256,4096]{1,0:T(8,128)(2,1)} %bitcast.46), channel_id=1, source_target_pairs={{0,16},{16,32},{32,48},{48,64},{64,80},{80,96},{96,112},{1,17},{17... | collective-permute-start | bytes 6291464 | tf_op jit(solution)/shard_map/ppermute | solution.py:19
  7.1 23.3 %copy-start.3 = (bf16[256,4096]{1,0:T(8,128)(2,1)S(1)}, bf16[256,4096]{1,0:T(8,128)(2,1)}, u32[]{:S(2)}) copy-start(bf16[256,4096]{1,0:T(8,128)(2,1)} %copy.20) | copy-start | bytes 6291460
  7.1 23.3 %copy-start.4 = (f32[1,4096]{1,0:T(1,128)S(1)}, f32[1,4096]{1,0:T(1,128)}, u32[]{:S(2)}) copy-start(f32[1,4096]{1,0:T(1,128)} %param.14) | copy-start | bytes 49156
  30.3 58.1 %copy-start.1 = (bf16[256,4096]{1,0:T(8,128)(2,1)}, bf16[256,4096]{1,0:T(8,128)(2,1)S(1)}, u32[]{:S(2)}) copy-start(bf16[256,4096]{1,0:T(8,128)(2,1)S(1)} %get-tuple-element.6.current_ref) | copy-start | bytes 6291460
  32.5 24.8 %all-to-all-start = ((bf16[16,128,256]{2,1,0:T(8,128)(2,1)}), bf16[16,128,256]{2,1,0:T(8,128)(2,1)}, u32[]{:S(2)}, u32[]{:S(2)}) async-start(bf16[16,128,256]{2,1,0:T(8,128)(2,1)} %broadcast_in_dim.14), calls=%async_computation | async-start | bytes 2097152 | tf_op jit(solution)/shard_map/all_to_all | solution.py:283
  40.6 22.1 %copy-start.5 = (s32[1,16]{1,0:T(1,128)S(1)}, s32[1,16]{1,0:T(1,128)}, u32[]{:S(2)}) copy-start(s32[1,16]{1,0:T(1,128)} %param.13) | copy-start | bytes 196
  58.4 22.9 %all-to-all-start.2 = ((bf16[16,128,256]{2,1,0:T(8,128)(2,1)}), bf16[16,128,256]{2,1,0:T(8,128)(2,1)}, u32[]{:S(2)}, u32[]{:S(2)}) async-start(bf16[16,128,256]{2,1,0:T(8,128)(2,1)} %broadcast_in_dim.16), calls=%async_computation.2 | async-start | bytes 2097152 | tf_op jit(solution)/shard_map/all_to_all | solution.py:283
  81.3 26.4 %all-to-all-start.1 = ((bf16[16,136,256]{2,1,0:T(8,128)(2,1)}), bf16[16,136,256]{2,1,0:T(8,128)(2,1)}, u32[]{:S(2)}, u32[]{:S(2)}) async-start(bf16[16,136,256]{2,1,0:T(8,128)(2,1)} %shard_map.100), calls=%async_computation.1 | async-start | bytes 2228224 | tf_op jit(solution)/shard_map/all_to_all | solution.py:287
  107.7 22.7 %all-to-all-start.3 = ((bf16[16,136,256]{2,1,0:T(8,128)(2,1)}), bf16[16,136,256]{2,1,0:T(8,128)(2,1)S(1)}, u32[]{:S(2)}, u32[]{:S(2)}) async-start(bf16[16,136,256]{2,1,0:T(8,128)(2,1)} %shard_map.101), calls=%async_computation.3 | async-start | bytes 2228224 | tf_op jit(solution)/shard_map/all_to_all | solution.py:287
  114.9 13.2 %collective-permute-start.1 = (bf16[256,128]{0,1:T(8,128)(2,1)S(1)}, bf16[256,128]{0,1:T(8,128)(2,1)S(1)}, u32[]{:S(2)}, u32[]{:S(2)}) collective-permute-start(bf16[256,128]{0,1:T(8,128)(2,1)S(1)} %fusion.27), channel_id=1, source_target_pairs={{0,1},{1,0},{2,3},{3,2},{4,5},{5,4},{6,7},{7,6},{8,9},{9,8},{10,11... | collective-permute-start | bytes 196616 | tf_op jit(solution)/shard_map/ppermute | solution.py:29
  130.4 1.0 copy-start.2

commit v15 on v14

--- a/solution.py
+++ b/solution.py
@@ -258,6 +258,9 @@
     odd_member = position % 2 == 1
     live = cache_counts[0, position].reshape(1)
     arrived = passed_along(previous[0], "segment", 1)
+    partner_weight = swapped(w_keyval[0], "blk", 0)
+    key_weight = jnp.where(odd_member, partner_weight, w_keyval[0])
+    value_weight = jnp.where(odd_member, w_keyval[0], partner_weight)
     current = jnp.where(lax.axis_index("segment") == 0, fresh, arrived)
     widened = current.astype(jnp.float32)
     normed = (
@@ -265,16 +268,14 @@
         * lax.rsqrt(jnp.mean(widened * widened, axis=-1, keepdims=True) + EPSILON)
         * norm_gain[0]
     ).astype(jnp.bfloat16)
+    key_weight, value_weight, normed = lax.optimization_barrier((key_weight, value_weight, normed))
     queries = jnp.dot(normed, w_query[0], preferred_element_type=jnp.float32).reshape(
         span_rows, heads_here, HD
     )
     queries = rotate(queries, first_span).astype(jnp.bfloat16).reshape(span_rows, heads_here * HD)
-    projected = jnp.dot(normed, w_keyval[0], preferred_element_type=jnp.float32)
-    as_key = rotate(projected[:, None, :], first_span)[:, 0, :].astype(jnp.bfloat16)
-    mine = jnp.where(odd_member, projected.astype(jnp.bfloat16), as_key)
-    partner = swapped(mine, "blk", 0)
-    own_keys = jnp.where(odd_member, partner, mine)
-    own_values = jnp.where(odd_member, mine, partner)
+    key_projected = jnp.dot(normed, key_weight, preferred_element_type=jnp.float32)
+    own_keys = rotate(key_projected[:, None, :], first_span)[:, 0, :].astype(jnp.bfloat16)
+    own_values = jnp.dot(normed, value_weight, preferred_element_type=jnp.float32).astype(jnp.bfloat16)
     halves = 2
     half_rows = span_rows // halves
     arrived_halves = []

time: 203 us -> 211 us (1.039)
  matrix products: 2.46 us -> 6.69 us
  local copies, waits for them, and re-layouts: 11.2 us -> 14.7 us
    ppermute x1, waiting for transfers between devices: 20.7 us -> 0.01 us  [passed_along(): return lax.ppermute(block, axis, route)]
    all_to_all x2, waiting for transfers between devices: 0.01 us -> 9.34 us  [shards(): lax.all_to_all(held, 'blk', split_axis=0, concat_axis=0, tiled=True)]
    ppermute x1, waiting for transfers between devices: 11 us -> 18.5 us  [swapped(): return lax.ppermute(block, axis, route)]
    select_n x1, other arithmetic: 0.02 us -> 2.77 us  [shards(): value_weight = jnp.where(odd_member, w_keyval[0], partner_weight)]
    unnamed x13 -> x21, local copies, waits for them, and re-layouts: 2.36 us -> 4.99 us
    dot_general x1, matrix products: 0.29 us -> 2.43 us  [attend_rows(): jnp.dot(weights.astype(jnp.bfloat16), value_rows, preferred_element_type=...]
  transfers between devices with their start and end apart: 6 -> 6, of which waited for: 3 -> 3; matrix products, arithmetic and copies ran while one was open for 4% -> 8% of each run, Pallas kernels for 18% -> 17%
where the time goes in v15:
time: 211 us; the launch traced here: 210 us
  blocking collectives  59.6 us (28%)
  Pallas kernels  46.1 us (22%)
  waiting for transfers between devices  46 us (22%)
  starting transfers between devices  30.4 us (14%)
  local copies, waits for them, and re-layouts  14.7 us (7%)
  matrix products  6.69 us (3%)
  other arithmetic  5.21 us (2%)
    pallas_call x2, Pallas kernels, cache_attention(): pl.pallas_call(cache_kernel, grid_spec=grid_spec, out_shape=jax.ShapeDtyp...  36.1 us
    all_to_all x1, blocking collectives, shards(): lax.all_to_all(head_terms.reshape(blocks, chunk, -1), 'blk', 0, 0, tiled=...  30.9 us
    all_to_all x1, blocking collectives, shards(): lax.all_to_all(spread, 'blk', 0, 0, tiled=True).reshape(span_rows, -1)  28.7 us
    ppermute x1, waiting for transfers between devices, swapped(): return lax.ppermute(block, axis, route)  18.5 us
    all_to_all x2, waiting for transfers between devices, shards(): lax.all_to_all(jnp.broadcast_to(half[None], (blocks,) + half.shape), 'blk...  18.2 us
    all_to_all x2, starting transfers between devices, shards(): lax.all_to_all(held, 'blk', split_axis=0, concat_axis=0, tiled=True)  14.4 us
    all_to_all x2, starting transfers between devices, shards(): lax.all_to_all(jnp.broadcast_to(half[None], (blocks,) + half.shape), 'blk...  11.9 us
    all_to_all x2, waiting for transfers between devices, shards(): lax.all_to_all(held, 'blk', split_axis=0, concat_axis=0, tiled=True)  9.34 us
  transfers between devices with their start and end apart: 6, of which 3 were waited for; matrix products, arithmetic and copies ran while one was open for 8% of the time, Pallas kernels for 17%

profile of v15, /device:TPU:2, one launch (start us, length us, event | category | flops | bytes accessed | tf_op | source)
XLA Modules:
  0.0 209.6 jit_solution(13470475251808796895)
XLA Ops:
  0.0 2.0 collective-permute-start.1
  2.1 2.0 collective-permute-start
  4.7 4.2 %copy.20 = bf16[256,4096]{1,0:T(8,128)(2,1)} copy(bf16[256,4096]{0,1:T(8,128)(2,1)} %bitcast.43) | data formatting | bytes 4194304 | tf_op jit(solution)/shard_map/dot_general | solution.py:272
  8.9 0.3 multiply_cosine_fusion.1
  9.2 0.0 copy-start.5
  9.2 18.5 %collective-permute-done = bf16[4096,128]{1,0:T(8,128)(2,1)} collective-permute-done((bf16[4096,128]{1,0:T(8,128)(2,1)}, bf16[4096,128]{1,0:T(8,128)(2,1)}, u32[]{:S(2)}, u32[]{:S(2)}) %collective-permute-start) | collective-permute-done | bytes 1048608 | tf_op jit(solution)/shard_map/ppermute | solution.py:29
  27.7 2.8 %broadcast_select_fusion.1 = (bf16[4096,128]{1,0:T(8,128)(2,1)}, bf16[4096,128]{1,0:T(8,128)(2,1)}) fusion(bf16[4096,128]{1,0:T(8,128)(2,1)} %collective-permute-done, pred[]{:T(512)S(6)} %eq.8, bf16[1,4096,128]{2,1,0:T(8,128)(2,1)S(1)} %copy-done.7), kind=kLoop, calls=%fused_computation.14 | loop fusion | flops 1048576 | bytes 4194305 | tf_op jit(solution)/shard_map/jit(_where)/select_n | solution.py:263
  30.5 0.0 collective-permute-done.1
  30.5 1.0 fusion
  31.5 0.0 copy-start.1
  31.5 0.0 copy-start.6
  31.5 0.6 fusion.2
  32.1 0.7 copy-done.1
  32.8 1.0 copy-done.6
  33.8 1.0 fusion.3
  34.9 0.1 copy.16
  35.0 1.1 broadcast_in_dim.16
  36.1 8.3 %all-to-all-start.2 = ((bf16[16,128,256]{2,1,0:T(8,128)(2,1)}), bf16[16,128,256]{2,1,0:T(8,128)(2,1)S(1)}, u32[]{:S(2)}, u32[]{:S(2)}) async-start(bf16[16,128,256]{2,1,0:T(8,128)(2,1)} %broadcast_in_dim.16), calls=%async_computation.2 | async-start | bytes 2097152 | tf_op jit(solution)/shard_map/all_to_all | solution.py:284
  44.4 0.1 copy.15
  44.5 18.2 %all-to-all-done.2.q_ref = bf16[16,128,256]{2,1,0:T(8,128)(2,1)S(1)} async-done(((bf16[16,128,256]{2,1,0:T(8,128)(2,1)}), bf16[16,128,256]{2,1,0:T(8,128)(2,1)S(1)}, u32[]{:S(2)}, u32[]{:S(2)}) %all-to-all-start.2) | async-done | bytes 1048608 | tf_op jit(solution)/shard_map/all_to_all | solution.py:284
  62.7 1.2 broadcast_in_dim.14
  63.8 0.2 copy-done.4
  64.0 3.7 %all-to-all-start = ((bf16[16,128,256]{2,1,0:T(8,128)(2,1)}), bf16[16,128,256]{2,1,0:T(8,128)(2,1)S(1)}, u32[]{:S(2)}, u32[]{:S(2)}) async-start(bf16[16,128,256]{2,1,0:T(8,128)(2,1)} %broadcast_in_dim.14), calls=%async_computation | async-start | bytes 2097152 | tf_op jit(solution)/shard_map/all_to_all | solution.py:284
  67.7 0.7 constant_dynamic-slice_fusion
  68.4 18.0 %shard_map.101 = bf16[16,136,256]{2,1,0:T(8,128)(2,1)} custom-call(s32[1]{0:T(128)} %bitcast.1.live_ref, bf16[16,128,256]{2,1,0:T(8,128)(2,1)} %copy-done.4, bf16[2048,1024]{1,0:T(8,128)(2,1)} %bitcast.37, bf16[2048,1024]{1,0:T(8,128)(2,1)} %bitcast.39), custom_call_target="tpu_custom_call" | custom-call | tf_op jit(solution)/shard_map/pallas_call | solution.py:125
  86.4 0.0 all-to-all-done.q_ref
  86.4 1.0 copy-done.3
  87.4 7.2 %all-to-all-start.3 = ((bf16[16,136,256]{2,1,0:T(8,128)(2,1)}), bf16[16,136,256]{2,1,0:T(8,128)(2,1)S(1)}, u32[]{:S(2)}, u32[]{:S(2)}) async-start(bf16[16,136,256]{2,1,0:T(8,128)(2,1)} %shard_map.101), calls=%async_computation.3 | async-start | bytes 2228224 | tf_op jit(solution)/shard_map/all_to_all | solution.py:288
  94.6 0.1 copy.17
  94.7 0.8 copy.18
  95.5 2.1 convolution_bitcast_fusion
  97.5 18.0 %shard_map.100 = bf16[16,136,256]{2,1,0:T(8,128)(2,1)} custom-call(s32[1]{0:T(128)} %bitcast.1.live_ref, bf16[16,128,256]{2,1,0:T(8,128)(2,1)} %copy-done.3, bf16[2048,1024]{1,0:T(8,128)(2,1)} %bitcast.38, bf16[2048,1024]{1,0:T(8,128)(2,1)} %bitcast.40), custom_call_target="tpu_custom_call" | custom-call | tf_op jit(solution)/shard_map/pallas_call | solution.py:125
  115.6 0.0 all-to-all-done.3.refs_1_
  115.6 7.3 %all-to-all-start.1 = ((bf16[16,136,256]{2,1,0:T(8,128)(2,1)}), bf16[16,136,256]{2,1,0:T(8,128)(2,1)}, u32[]{:S(2)}, u32[]{:S(2)}) async-start(bf16[16,136,256]{2,1,0:T(8,128)(2,1)} %shard_map.100), calls=%async_computation.1 | async-start | bytes 2228224 | tf_op jit(solution)/shard_map/all_to_all | solution.py:288
  122.9 0.3 fusion.19
  123.2 1.2 fusion.29
  124.5 0.8 copy-done.8
  125.2 0.1 fusion.7
  125.4 0.1 add.59
  125.5 0.7 copy.19
  126.2 2.4 %fusion.6 = bf16[512,128]{1,0:T(8,128)(2,1)S(1)} fusion(bf16[256,4096]{1,0:T(8,128)(2,1)S(1)} %fusion.2, bf16[4096,128]{1,0:T(8,128)(2,1)} %get-tuple-element.10, f32[512,256]{0,1:T(8,128)} %copy-done.8, f32[512]{0:T(512)S(1)} %get-tuple-element.23, f32[512]{0:T(512)S(1)} %fusion.7), kind=kOutput, calls=%fused_computation.11 | convolution fusion | flops 302415872 | bytes 3805184 | tf_op jit(solution)/shard_map/dot_general | solution.py:62
  128.6 0.7 reshape.162.refs_2_
  129.3 9.3 %all-to-all-done.1.refs_0_ = bf16[16,136,256]{2,1,0:T(8,128)(2,1)} async-done(((bf16[16,136,256]{2,1,0:T(8,128)(2,1)}), bf16[16,136,256]{2,1,0:T(8,128)(2,1)}, u32[]{:S(2)}, u32[]{:S(2)}) %all-to-all-start.1) | async-done | bytes 1114144 | tf_op jit(solution)/shard_map/all_to_all | solution.py:288
  138.7 6.7 %shard_map.102 = bf16[256,4096]{1,0:T(8,128)(2,1)} custom-call(bf16[16,136,256]{2,1,0:T(8,128)(2,1)} %all-to-all-done.1.refs_0_, bf16[16,136,256]{2,1,0:T(8,128)(2,1)} %copy-done.2, bf16[256,256]{1,0:T(8,128)(2,1)} %reshape.162.refs_2_, f32[2,256]{1,0:T(2,128)} %bitcast.52, bf16[256,4096]{1,0:T(8,128)(2,1)} %bitcast.44), custom_call_target="tpu_custom_call" | custom-call | tf_op jit(solution)/shard_map/pallas_call | solution.py:198
  145.4 30.9 %all_to_all.30.terms_ref = bf16[16,16,4096]{2,1,0:T(8,128)(2,1)} all-to-all(bf16[16,16,4096]{2,1,0:T(8,128)(2,1)} %bitcast.41), channel_id=1, replica_groups=mesh['segment'=8,'blk'=16] {'blk'}, dimensions={0} | all-to-all | bytes 4194304 | tf_op jit(solution)/shard_map/all_to_all | solution.py:297
  176.3 3.3 %shard_map.103 = bf16[16,16,4096]{2,1,0:T(8,128)(2,1)} custom-call(s32[1]{0:T(128)} %bitcast.position_ref, bf16[16,16,4096]{2,1,0:T(8,128)(2,1)} %all_to_all.30.terms_ref, bf16[256,4096]{1,0:T(8,128)(2,1)} %copy-done.1), custom_call_target="tpu_custom_call" | custom-call | tf_op jit(solution)/shard_map/pallas_call | solution.py:234
  179.6 28.7 %all_to_all.31 = bf16[16,16,4096]{2,1,0:T(8,128)(2,1)S(1)} all-to-all(bf16[16,16,4096]{2,1,0:T(8,128)(2,1)} %shard_map.103), channel_id=1, replica_groups=mesh['segment'=8,'blk'=16] {'blk'}, dimensions={0} | all-to-all | bytes 4194304 | tf_op jit(solution)/shard_map/all_to_all | solution.py:301
  208.3 1.3 copy.23
  (19 shorter events, 0.1 us)
Async XLA Ops:
  0.0 67.7 %copy-start = (s32[1,16]{1,0:T(1,128)S(1)}, s32[1,16]{1,0:T(1,128)}, u32[]{:S(2)}) copy-start(s32[1,16]{1,0:T(1,128)} %param.13) | copy-start | bytes 196
  0.0 30.5 %collective-permute-start.1 = (bf16[256,4096]{1,0:T(8,128)(2,1)}, bf16[256,4096]{1,0:T(8,128)(2,1)S(1)}, u32[]{:S(2)}, u32[]{:S(2)}) collective-permute-start(bf16[256,4096]{1,0:T(8,128)(2,1)} %bitcast.53), channel_id=1, source_target_pairs={{0,16},{16,32},{32,48},{48,64},{64,80},{80,96},{96,112},{1,17},{17... | collective-permute-start | bytes 6291464 | tf_op jit(solution)/shard_map/ppermute | solution.py:19
  2.1 25.7 %collective-permute-start = (bf16[4096,128]{1,0:T(8,128)(2,1)}, bf16[4096,128]{1,0:T(8,128)(2,1)}, u32[]{:S(2)}, u32[]{:S(2)}) collective-permute-start(bf16[4096,128]{1,0:T(8,128)(2,1)} %bitcast.46), channel_id=1, source_target_pairs={{0,1},{1,0},{2,3},{3,2},{4,5},{5,4},{6,7},{7,6},{8,9},{9,8},{10,11... | collective-permute-start | bytes 3145736 | tf_op jit(solution)/shard_map/ppermute | solution.py:29
  4.7 23.0 %copy-start.7 = (bf16[1,4096,128]{2,1,0:T(8,128)(2,1)S(1)}, bf16[1,4096,128]{2,1,0:T(8,128)(2,1)}, u32[]{:S(2)}) copy-start(bf16[1,4096,128]{2,1,0:T(8,128)(2,1)} %param.16) | copy-start | bytes 3145732
  9.2 21.3 %copy-start.5 = (bf16[256,4096]{1,0:T(8,128)(2,1)S(1)}, bf16[256,4096]{1,0:T(8,128)(2,1)}, u32[]{:S(2)}) copy-start(bf16[256,4096]{1,0:T(8,128)(2,1)} %param.10) | copy-start | bytes 6291460
  30.5 1.0 copy-start.9
  31.5 1.3 copy-start.1
  31.5 2.3 %copy-start.6 = (bf16[256,4096]{1,0:T(8,128)(2,1)S(1)}, bf16[256,4096]{1,0:T(8,128)(2,1)}, u32[]{:S(2)}) copy-start(bf16[256,4096]{1,0:T(8,128)(2,1)} %copy.20) | copy-start | bytes 6291460
  36.1 26.6 %all-to-all-start.2 = ((bf16[16,128,256]{2,1,0:T(8,128)(2,1)}), bf16[16,128,256]{2,1,0:T(8,128)(2,1)S(1)}, u32[]{:S(2)}, u32[]{:S(2)}) async-start(bf16[16,128,256]{2,1,0:T(8,128)(2,1)} %broadcast_in_dim.16), calls=%async_computation.2 | async-start | bytes 2097152 | tf_op jit(solution)/shard_map/all_to_all | solution.py:284
  62.7 1.3 copy-start.4
  64.0 22.4 %all-to-all-start = ((bf16[16,128,256]{2,1,0:T(8,128)(2,1)}), bf16[16,128,256]{2,1,0:T(8,128)(2,1)S(1)}, u32[]{:S(2)}, u32[]{:S(2)}) async-start(bf16[16,128,256]{2,1,0:T(8,128)(2,1)} %broadcast_in_dim.14), calls=%async_computation | async-start | bytes 2097152 | tf_op jit(solution)/shard_map/all_to_all | solution.py:284
  86.4 1.0 copy-start.3
  87.4 28.2 %all-to-all-start.3 = ((bf16[16,136,256]{2,1,0:T(8,128)(2,1)}), bf16[16,136,256]{2,1,0:T(8,128)(2,1)S(1)}, u32[]{:S(2)}, u32[]{:S(2)}) async-start(bf16[16,136,256]{2,1,0:T(8,128)(2,1)} %shard_map.101), calls=%async_computation.3 | async-start | bytes 2228224 | tf_op jit(solution)/shard_map/all_to_all | solution.py:288
  115.6 13.0 %copy-start.2 = (bf16[16,136,256]{2,1,0:T(8,128)(2,1)}, bf16[16,136,256]{2,1,0:T(8,128)(2,1)S(1)}, u32[]{:S(2)}) copy-start(bf16[16,136,256]{2,1,0:T(8,128)(2,1)S(1)} %all-to-all-done.3.refs_1_) | copy-start | bytes 3342340
  115.6 23.1 %all-to-all-start.1 = ((bf16[16,136,256]{2,1,0:T(8,128)(2,1)}), bf16[16,136,256]{2,1,0:T(8,128)(2,1)}, u32[]{:S(2)}, u32[]{:S(2)}) async-start(bf16[16,136,256]{2,1,0:T(8,128)(2,1)} %shard_map.100), calls=%async_computation.1 | async-start | bytes 2228224 | tf_op jit(solution)/shard_map/all_to_all | solution.py:288
  124.4 0.8 copy-start.8

commit v16 on v11

--- a/solution.py
+++ b/solution.py
@@ -211,32 +211,35 @@
     )(*arrived_halves, own_out, own_log, out_weight)
 
 
-def residual_kernel(position_ref, terms_ref, current_ref, out_ref):
-    total = terms_ref[0].astype(jnp.float32)
-    for n in range(1, terms_ref.shape[0]):
-        total = total + terms_ref[n].astype(jnp.float32)
-    mixed = (current_ref[...].astype(jnp.float32) + total).astype(out_ref.dtype)
-    for n in range(out_ref.shape[0]):
-        out_ref[n] = mixed
+def residual_kernel(position_ref, terms_ref, current_ref, out_ref, mixed_ref):
+    @pl.when(pl.program_id(0) == 0)
+    def _():
+        total = terms_ref[0].astype(jnp.float32)
+        for n in range(1, terms_ref.shape[0]):
+            total = total + terms_ref[n].astype(jnp.float32)
+        mixed_ref[...] = (current_ref[...].astype(jnp.float32) + total).astype(mixed_ref.dtype)
+
+    out_ref[0] = mixed_ref[...]
 
 
 def residual(position, gathered_terms, current):
     sources, chunk, width = gathered_terms.shape
     grid_spec = pltpu.PrefetchScalarGridSpec(
         num_scalar_prefetch=1,
-        grid=(1,),
+        grid=(sources,),
         in_specs=[
             pl.BlockSpec((sources, chunk, width), lambda i, pos: (0, 0, 0)),
             pl.BlockSpec((chunk, width), lambda i, pos: (pos[0], 0)),
         ],
-        out_specs=pl.BlockSpec((sources, chunk, width), lambda i, pos: (0, 0, 0)),
+        out_specs=pl.BlockSpec((1, chunk, width), lambda i, pos: (i, 0, 0)),
+        scratch_shapes=[pltpu.VMEM((chunk, width), jnp.bfloat16)],
     )
     return pl.pallas_call(
         residual_kernel,
         grid_spec=grid_spec,
         out_shape=jax.ShapeDtypeStruct((sources, chunk, width), jnp.bfloat16),
+        compiler_params=pltpu.CompilerParams(dimension_semantics=("arbitrary",)),
     )(position, gathered_terms, current)
-
 
 def shards(
     fresh,

time: 196 us -> 200 us (1.020)
  Pallas kernels: 46 us -> 49.9 us
    pallas_call x1, Pallas kernels: 3.27 us -> 7.23 us  [residual(): pl.pallas_call(residual_kernel, grid_spec=grid_spec, out_shape=jax.ShapeD...]
where the time goes in v16:
time: 200 us; the launch traced here: 199 us
  blocking collectives  75.6 us (38%)
  Pallas kernels  49.9 us (25%)
  waiting for transfers between devices  32.4 us (16%)
  starting transfers between devices  22.1 us (11%)
  local copies, waits for them, and re-layouts  11.1 us (6%)
  matrix products  4.11 us (2%)
  other arithmetic  3.38 us (2%)
    pallas_call x2, Pallas kernels, cache_attention(): pl.pallas_call(cache_kernel, grid_spec=grid_spec, out_shape=jax.ShapeDtyp...  36 us
    all_to_all x1, blocking collectives, shards(): lax.all_to_all(head_terms.reshape(blocks, chunk, -1), 'blk', 0, 0, tiled=...  26.9 us
    all_to_all x1, blocking collectives, shards(): lax.all_to_all(spread, 'blk', 0, 0, tiled=True).reshape(span_rows, -1)  25.5 us
    all_to_all x1, blocking collectives, shards(): lax.all_to_all(jnp.broadcast_to(half[None], (blocks,) + half.shape), 'blk...  23.2 us
    ppermute x1, waiting for transfers between devices, passed_along(): return lax.ppermute(block, axis, route)  20.5 us
    all_to_all x2, starting transfers between devices, shards(): lax.all_to_all(held, 'blk', split_axis=0, concat_axis=0, tiled=True)  14.4 us
    all_to_all x2, waiting for transfers between devices, shards(): lax.all_to_all(held, 'blk', split_axis=0, concat_axis=0, tiled=True)  9.63 us
    pallas_call x1, Pallas kernels, residual(): pl.pallas_call(residual_kernel, grid_spec=grid_spec, out_shape=jax.ShapeD...  7.23 us
  transfers between devices with their start and end apart: 5, of which 3 were waited for; matrix products, arithmetic and copies ran while one was open for 5% of the time, Pallas kernels for 18%

profile of v16, /device:TPU:2, one launch (start us, length us, event | category | flops | bytes accessed | tf_op | source)
XLA Modules:
  0.0 199.4 jit_solution(7106144562886813)
XLA Ops:
  0.0 0.0 copy-start
  0.0 2.0 %collective-permute-start = (bf16[256,4096]{1,0:T(8,128)(2,1)}, bf16[256,4096]{1,0:T(8,128)(2,1)}, u32[]{:S(2)}, u32[]{:S(2)}) collective-permute-start(bf16[256,4096]{1,0:T(8,128)(2,1)} %bitcast.41), channel_id=1, source_target_pairs={{0,16},{16,32},{32,48},{48,64},{64,80},{80,96},{96,112},{1,17},{17... | collective-permute-start | bytes 6291464 | tf_op jit(solution)/shard_map/ppermute | solution.py:19
  2.7 0.0 copy-start.5
  2.7 4.2 %copy.19 = bf16[256,4096]{1,0:T(8,128)(2,1)} copy(bf16[256,4096]{0,1:T(8,128)(2,1)} %bitcast.35) | data formatting | bytes 4194304 | tf_op jit(solution)/shard_map/dot_general | solution.py:271
  7.0 0.3 multiply_cosine_fusion
  7.3 0.0 copy-start.6
  7.3 0.0 copy-start.9
  7.3 20.5 %collective-permute-done = bf16[256,4096]{1,0:T(8,128)(2,1)} collective-permute-done((bf16[256,4096]{1,0:T(8,128)(2,1)}, bf16[256,4096]{1,0:T(8,128)(2,1)}, u32[]{:S(2)}, u32[]{:S(2)}) %collective-permute-start) | collective-permute-done | bytes 2097184 | tf_op jit(solution)/shard_map/ppermute | solution.py:19
  27.8 0.0 copy-done.5
  27.8 2.5 %fusion = (f32[256]{0:T(256)S(1)}, bf16[256,4096]{1,0:T(8,128)(2,1)S(1)}) fusion(bf16[256,4096]{1,0:T(8,128)(2,1)S(1)} %copy-done.5, bf16[256,4096]{1,0:T(8,128)(2,1)} %collective-permute-done, pred[]{:T(512)S(6)} %eq.9), kind=kLoop, calls=%fused_computation.2 | loop fusion | flops 4194048 | bytes 6292481 | tf_op jit(solution)/shard_map/reduce_sum | solution.py:268
  30.3 0.0 copy-start.1
  30.4 0.0 copy-done.6
  30.4 0.0 copy-done.9
  30.4 0.9 fusion.3
  31.3 0.4 copy-done.1
  31.7 0.0 copy-done
  31.7 1.0 fusion.7
  32.6 0.3 fusion.20
  33.0 0.0 copy-start.7
  33.0 2.0 %collective-permute-start.1 = (bf16[256,128]{0,1:T(8,128)(2,1)S(1)}, bf16[256,128]{0,1:T(8,128)(2,1)S(1)}, u32[]{:S(2)}, u32[]{:S(2)}) collective-permute-start(bf16[256,128]{0,1:T(8,128)(2,1)S(1)} %fusion.23), channel_id=1, source_target_pairs={{0,1},{1,0},{2,3},{3,2},{4,5},{5,4},{6,7},{7,6},{8,9},{9,8},{10,11... | collective-permute-start | bytes 196616 | tf_op jit(solution)/shard_map/ppermute | solution.py:29
  35.1 2.3 %collective-permute-done.1 = bf16[256,128]{0,1:T(8,128)(2,1)S(1)} collective-permute-done((bf16[256,128]{0,1:T(8,128)(2,1)S(1)}, bf16[256,128]{0,1:T(8,128)(2,1)S(1)}, u32[]{:S(2)}, u32[]{:S(2)}) %collective-permute-start.1) | collective-permute-done | bytes 65568 | tf_op jit(solution)/shard_map/ppermute | solution.py:29
  37.4 0.6 copy-done.8
  38.0 0.1 copy.15
  38.1 0.1 broadcast_in_dim.11
  38.2 23.2 %all_to_all.30.q_ref = bf16[16,128,256]{2,1,0:T(8,128)(2,1)} all-to-all(bf16[16,128,256]{2,1,0:T(8,128)(2,1)S(1)} %broadcast_in_dim.11), channel_id=1, replica_groups=mesh['segment'=8,'blk'=16] {'blk'}, dimensions={0} | all-to-all | bytes 2097152 | tf_op jit(solution)/shard_map/all_to_all | solution.py:287
  61.4 1.1 broadcast_in_dim.10
  62.5 3.7 %all-to-all-start = ((bf16[16,128,256]{2,1,0:T(8,128)(2,1)}), bf16[16,128,256]{2,1,0:T(8,128)(2,1)S(1)}, u32[]{:S(2)}, u32[]{:S(2)}) async-start(bf16[16,128,256]{2,1,0:T(8,128)(2,1)} %broadcast_in_dim.10), calls=%async_computation | async-start | bytes 2097152 | tf_op jit(solution)/shard_map/all_to_all | solution.py:287
  66.2 0.6 constant_dynamic-slice_fusion
  66.8 18.0 %shard_map.101 = bf16[16,136,256]{2,1,0:T(8,128)(2,1)} custom-call(s32[1]{0:T(128)} %bitcast.1.live_ref, bf16[16,128,256]{2,1,0:T(8,128)(2,1)} %all_to_all.30.q_ref, bf16[2048,1024]{1,0:T(8,128)(2,1)} %bitcast.29, bf16[2048,1024]{1,0:T(8,128)(2,1)} %bitcast.31), custom_call_target="tpu_custom_call" | custom-call | tf_op jit(solution)/shard_map/pallas_call | solution.py:125
  84.7 0.0 all-to-all-done.q_ref
  84.8 7.2 %all-to-all-start.3 = ((bf16[16,136,256]{2,1,0:T(8,128)(2,1)}), bf16[16,136,256]{2,1,0:T(8,128)(2,1)S(1)}, u32[]{:S(2)}, u32[]{:S(2)}) async-start(bf16[16,136,256]{2,1,0:T(8,128)(2,1)} %shard_map.101), calls=%async_computation.3 | async-start | bytes 2228224 | tf_op jit(solution)/shard_map/all_to_all | solution.py:291
  91.9 18.0 %shard_map.100 = bf16[16,136,256]{2,1,0:T(8,128)(2,1)} custom-call(s32[1]{0:T(128)} %bitcast.1.live_ref, bf16[16,128,256]{2,1,0:T(8,128)(2,1)} %copy-done.4, bf16[2048,1024]{1,0:T(8,128)(2,1)} %bitcast.30, bf16[2048,1024]{1,0:T(8,128)(2,1)} %bitcast.32), custom_call_target="tpu_custom_call" | custom-call | tf_op jit(solution)/shard_map/pallas_call | solution.py:125
  109.9 0.0 all-to-all-done.3.refs_1_
  109.9 7.2 %all-to-all-start.1 = ((bf16[16,136,256]{2,1,0:T(8,128)(2,1)}), bf16[16,136,256]{2,1,0:T(8,128)(2,1)S(1)}, u32[]{:S(2)}, u32[]{:S(2)}) async-start(bf16[16,136,256]{2,1,0:T(8,128)(2,1)} %shard_map.100), calls=%async_computation.1 | async-start | bytes 2228224 | tf_op jit(solution)/shard_map/all_to_all | solution.py:291
  117.2 1.1 fusion.32
  118.3 0.1 fusion.11
  118.5 1.1 fusion.6
  119.6 0.0 copy-done.2
  119.6 0.7 reshape.160.refs_2_
  120.3 0.1 add.59
  120.5 0.7 copy.18
  121.1 9.6 %all-to-all-done.1.refs_0_ = bf16[16,136,256]{2,1,0:T(8,128)(2,1)S(1)} async-done(((bf16[16,136,256]{2,1,0:T(8,128)(2,1)}), bf16[16,136,256]{2,1,0:T(8,128)(2,1)S(1)}, u32[]{:S(2)}, u32[]{:S(2)}) %all-to-all-start.1) | async-done | bytes 1114144 | tf_op jit(solution)/shard_map/all_to_all | solution.py:291
  130.7 1.0 copy-done.3
  131.7 6.7 %shard_map.102 = bf16[256,4096]{1,0:T(8,128)(2,1)} custom-call(bf16[16,136,256]{2,1,0:T(8,128)(2,1)} %copy-done.3, bf16[16,136,256]{2,1,0:T(8,128)(2,1)} %copy-done.2, bf16[256,256]{1,0:T(8,128)(2,1)} %reshape.160.refs_2_, f32[2,256]{1,0:T(2,128)} %bitcast.40, bf16[256,4096]{1,0:T(8,128)(2,1)} %bitcast.36), custom_call_target="tpu_custom_call" | custom-call | tf_op jit(solution)/shard_map/pallas_call | solution.py:198
  138.5 26.9 %all_to_all.31.terms_ref = bf16[16,16,4096]{2,1,0:T(8,128)(2,1)} all-to-all(bf16[16,16,4096]{2,1,0:T(8,128)(2,1)} %bitcast.33), channel_id=1, replica_groups=mesh['segment'=8,'blk'=16] {'blk'}, dimensions={0} | all-to-all | bytes 4194304 | tf_op jit(solution)/shard_map/all_to_all | solution.py:300
  165.4 7.2 %shard_map.103 = bf16[16,16,4096]{2,1,0:T(8,128)(2,1)} custom-call(s32[1]{0:T(128)} %bitcast.position_ref, bf16[16,16,4096]{2,1,0:T(8,128)(2,1)} %all_to_all.31.terms_ref, bf16[256,4096]{1,0:T(8,128)(2,1)} %copy-done.1), custom_call_target="tpu_custom_call" | custom-call | tf_op jit(solution)/shard_map/pallas_call | solution.py:237
  172.6 25.5 %all_to_all.32 = bf16[16,16,4096]{2,1,0:T(8,128)(2,1)S(1)} all-to-all(bf16[16,16,4096]{2,1,0:T(8,128)(2,1)} %shard_map.103), channel_id=1, replica_groups=mesh['segment'=8,'blk'=16] {'blk'}, dimensions={0} | all-to-all | bytes 4194304 | tf_op jit(solution)/shard_map/all_to_all | solution.py:304
  198.1 1.3 copy.22
  (18 shorter events, 0.2 us)
Async XLA Ops:
  0.0 31.7 %copy-start = (bf16[1,4096,128]{2,1,0:T(8,128)(2,1)S(1)}, bf16[1,4096,128]{2,1,0:T(8,128)(2,1)}, u32[]{:S(2)}) copy-start(bf16[1,4096,128]{2,1,0:T(8,128)(2,1)} %param.16) | copy-start | bytes 3145732
  0.0 27.8 %collective-permute-start = (bf16[256,4096]{1,0:T(8,128)(2,1)}, bf16[256,4096]{1,0:T(8,128)(2,1)}, u32[]{:S(2)}, u32[]{:S(2)}) collective-permute-start(bf16[256,4096]{1,0:T(8,128)(2,1)} %bitcast.41), channel_id=1, source_target_pairs={{0,16},{16,32},{32,48},{48,64},{64,80},{80,96},{96,112},{1,17},{17... | collective-permute-start | bytes 6291464 | tf_op jit(solution)/shard_map/ppermute | solution.py:19
  2.7 25.1 %copy-start.5 = (bf16[256,4096]{1,0:T(8,128)(2,1)S(1)}, bf16[256,4096]{1,0:T(8,128)(2,1)}, u32[]{:S(2)}) copy-start(bf16[256,4096]{1,0:T(8,128)(2,1)} %param.10) | copy-start | bytes 6291460
  7.3 23.1 %copy-start.6 = (bf16[256,4096]{1,0:T(8,128)(2,1)S(1)}, bf16[256,4096]{1,0:T(8,128)(2,1)}, u32[]{:S(2)}) copy-start(bf16[256,4096]{1,0:T(8,128)(2,1)} %copy.19) | copy-start | bytes 6291460
  7.3 23.1 %copy-start.9 = (f32[1,4096]{1,0:T(1,128)S(1)}, f32[1,4096]{1,0:T(1,128)}, u32[]{:S(2)}) copy-start(f32[1,4096]{1,0:T(1,128)} %param.14) | copy-start | bytes 49156
  30.3 1.3 copy-start.1
  33.0 4.4 %copy-start.7 = (bf16[256,128]{0,1:T(8,128)(2,1)}, bf16[256,128]{0,1:T(8,128)(2,1)S(1)}, u32[]{:S(2)}) copy-start(bf16[256,128]{0,1:T(8,128)(2,1)S(1)} %fusion.23) | copy-start | bytes 196612
  33.0 4.3 %collective-permute-start.1 = (bf16[256,128]{0,1:T(8,128)(2,1)S(1)}, bf16[256,128]{0,1:T(8,128)(2,1)S(1)}, u32[]{:S(2)}, u32[]{:S(2)}) collective-permute-start(bf16[256,128]{0,1:T(8,128)(2,1)S(1)} %fusion.23), channel_id=1, source_target_pairs={{0,1},{1,0},{2,3},{3,2},{4,5},{5,4},{6,7},{7,6},{8,9},{9,8},{10,11... | collective-permute-start | bytes 196616 | tf_op jit(solution)/shard_map/ppermute | solution.py:29
  37.4 0.6 copy-start.8
  61.4 4.7 %copy-start.10 = (s32[1,16]{1,0:T(1,128)S(1)}, s32[1,16]{1,0:T(1,128)}, u32[]{:S(2)}) copy-start(s32[1,16]{1,0:T(1,128)} %param.13) | copy-start | bytes 196
  62.5 22.3 %all-to-all-start = ((bf16[16,128,256]{2,1,0:T(8,128)(2,1)}), bf16[16,128,256]{2,1,0:T(8,128)(2,1)S(1)}, u32[]{:S(2)}, u32[]{:S(2)}) async-start(bf16[16,128,256]{2,1,0:T(8,128)(2,1)} %broadcast_in_dim.10), calls=%async_computation | async-start | bytes 2097152 | tf_op jit(solution)/shard_map/all_to_all | solution.py:287
  84.7 7.2 %copy-start.4 = (bf16[16,128,256]{2,1,0:T(8,128)(2,1)}, bf16[16,128,256]{2,1,0:T(8,128)(2,1)S(1)}, u32[]{:S(2)}) copy-start(bf16[16,128,256]{2,1,0:T(8,128)(2,1)S(1)} %all-to-all-done.q_ref) | copy-start | bytes 3145732
  84.8 25.2 %all-to-all-start.3 = ((bf16[16,136,256]{2,1,0:T(8,128)(2,1)}), bf16[16,136,256]{2,1,0:T(8,128)(2,1)S(1)}, u32[]{:S(2)}, u32[]{:S(2)}) async-start(bf16[16,136,256]{2,1,0:T(8,128)(2,1)} %shard_map.101), calls=%async_computation.3 | async-start | bytes 2228224 | tf_op jit(solution)/shard_map/all_to_all | solution.py:291
  109.9 9.7 %copy-start.2 = (bf16[16,136,256]{2,1,0:T(8,128)(2,1)}, bf16[16,136,256]{2,1,0:T(8,128)(2,1)S(1)}, u32[]{:S(2)}) copy-start(bf16[16,136,256]{2,1,0:T(8,128)(2,1)S(1)} %all-to-all-done.3.refs_1_) | copy-start | bytes 3342340
  109.9 20.8 %all-to-all-start.1 = ((bf16[16,136,256]{2,1,0:T(8,128)(2,1)}), bf16[16,136,256]{2,1,0:T(8,128)(2,1)S(1)}, u32[]{:S(2)}, u32[]{:S(2)}) async-start(bf16[16,136,256]{2,1,0:T(8,128)(2,1)} %shard_map.100), calls=%async_computation.1 | async-start | bytes 2228224 | tf_op jit(solution)/shard_map/all_to_all | solution.py:291
  130.7 1.0 copy-start.3

commit v17 on v11

--- a/solution.py
+++ b/solution.py
@@ -73,6 +73,7 @@
     width = out_ref.shape[2]
     group = max(1, min(sources, 256 // rows))
     visible = lax.broadcasted_iota(jnp.int32, (1, keys.shape[0]), 1) < live
+    bias = jnp.where(visible, 0.0, -jnp.inf).astype(jnp.float32)
     log_rows = {src: [] for src in range(sources)}
     for first in range(0, sources, group):
         members = list(range(first, min(first + group, sources)))
@@ -80,8 +81,7 @@
             q = jnp.concatenate([q_ref[src, :, h * HD:(h + 1) * HD] for src in members], axis=0)
             scores = lax.dot_general(
                 q, keys, (((1,), (1,)), ((), ())), preferred_element_type=jnp.float32
-            ) * HD ** (-0.5)
-            scores = jnp.where(visible, scores, -jnp.inf)
+            ) * HD ** (-0.5) + bias
             highest = jnp.max(scores, axis=-1, keepdims=True)
             weights = jnp.exp(scores - highest)
             totals = jnp.sum(weights, axis=-1, keepdims=True)

time: 196 us -> 196 us (level)
  no operation moved by 1% of the time
where the time goes in v17:
time: 196 us; the launch traced here: 195 us
  blocking collectives  75.6 us (39%)
  Pallas kernels  45.3 us (23%)
  waiting for transfers between devices  32.4 us (17%)
  starting transfers between devices  22.1 us (11%)
  local copies, waits for them, and re-layouts  11.1 us (6%)
  matrix products  4.11 us (2%)
  other arithmetic  3.38 us (2%)
    pallas_call x2, Pallas kernels, cache_attention(): pl.pallas_call(cache_kernel, grid_spec=grid_spec, out_shape=jax.ShapeDtyp...  35.3 us
    all_to_all x1, blocking collectives, shards(): lax.all_to_all(head_terms.reshape(blocks, chunk, -1), 'blk', 0, 0, tiled=...  26.9 us
    all_to_all x1, blocking collectives, shards(): lax.all_to_all(spread, 'blk', 0, 0, tiled=True).reshape(span_rows, -1)  25.5 us
    all_to_all x1, blocking collectives, shards(): lax.all_to_all(jnp.broadcast_to(half[None], (blocks,) + half.shape), 'blk...  23.2 us
    ppermute x1, waiting for transfers between devices, passed_along(): return lax.ppermute(block, axis, route)  20.5 us
    all_to_all x2, starting transfers between devices, shards(): lax.all_to_all(held, 'blk', split_axis=0, concat_axis=0, tiled=True)  14.4 us
    all_to_all x2, waiting for transfers between devices, shards(): lax.all_to_all(held, 'blk', split_axis=0, concat_axis=0, tiled=True)  9.61 us
    pallas_call x1, Pallas kernels, combine(): pl.pallas_call(combine_kernel, grid=(columns // COLUMN_BLOCK,), in_specs=...  6.73 us
  transfers between devices with their start and end apart: 5, of which 3 were waited for; matrix products, arithmetic and copies ran while one was open for 5% of the time, Pallas kernels for 18%

profile of v17, /device:TPU:2, one launch (start us, length us, event | category | flops | bytes accessed | tf_op | source)
XLA Modules:
  0.0 194.8 jit_solution(6245782230331232515)
XLA Ops:
  0.0 0.0 copy-start
  0.0 2.0 %collective-permute-start = (bf16[256,4096]{1,0:T(8,128)(2,1)}, bf16[256,4096]{1,0:T(8,128)(2,1)}, u32[]{:S(2)}, u32[]{:S(2)}) collective-permute-start(bf16[256,4096]{1,0:T(8,128)(2,1)} %bitcast.41), channel_id=1, source_target_pairs={{0,16},{16,32},{32,48},{48,64},{64,80},{80,96},{96,112},{1,17},{17... | collective-permute-start | bytes 6291464 | tf_op jit(solution)/shard_map/ppermute | solution.py:19
  2.7 0.0 copy-start.5
  2.7 4.2 %copy.19 = bf16[256,4096]{1,0:T(8,128)(2,1)} copy(bf16[256,4096]{0,1:T(8,128)(2,1)} %bitcast.35) | data formatting | bytes 4194304 | tf_op jit(solution)/shard_map/dot_general | solution.py:268
  7.0 0.3 multiply_cosine_fusion
  7.3 0.0 copy-start.6
  7.3 0.0 copy-start.9
  7.3 20.5 %collective-permute-done = bf16[256,4096]{1,0:T(8,128)(2,1)} collective-permute-done((bf16[256,4096]{1,0:T(8,128)(2,1)}, bf16[256,4096]{1,0:T(8,128)(2,1)}, u32[]{:S(2)}, u32[]{:S(2)}) %collective-permute-start) | collective-permute-done | bytes 2097184 | tf_op jit(solution)/shard_map/ppermute | solution.py:19
  27.8 0.0 copy-done.5
  27.8 2.5 %fusion = (f32[256]{0:T(256)S(1)}, bf16[256,4096]{1,0:T(8,128)(2,1)S(1)}) fusion(bf16[256,4096]{1,0:T(8,128)(2,1)S(1)} %copy-done.5, bf16[256,4096]{1,0:T(8,128)(2,1)} %collective-permute-done, pred[]{:T(512)S(6)} %eq.9), kind=kLoop, calls=%fused_computation.2 | loop fusion | flops 4194048 | bytes 6292481 | tf_op jit(solution)/shard_map/reduce_sum | solution.py:265
  30.3 0.0 copy-start.1
  30.4 0.0 copy-done.6
  30.4 0.0 copy-done.9
  30.4 0.9 fusion.3
  31.3 0.4 copy-done.1
  31.7 0.0 copy-done
  31.7 1.0 fusion.7
  32.6 0.3 fusion.20
  33.0 0.0 copy-start.7
  33.0 2.0 %collective-permute-start.1 = (bf16[256,128]{0,1:T(8,128)(2,1)S(1)}, bf16[256,128]{0,1:T(8,128)(2,1)S(1)}, u32[]{:S(2)}, u32[]{:S(2)}) collective-permute-start(bf16[256,128]{0,1:T(8,128)(2,1)S(1)} %fusion.23), channel_id=1, source_target_pairs={{0,1},{1,0},{2,3},{3,2},{4,5},{5,4},{6,7},{7,6},{8,9},{9,8},{10,11... | collective-permute-start | bytes 196616 | tf_op jit(solution)/shard_map/ppermute | solution.py:29
  35.1 2.3 %collective-permute-done.1 = bf16[256,128]{0,1:T(8,128)(2,1)S(1)} collective-permute-done((bf16[256,128]{0,1:T(8,128)(2,1)S(1)}, bf16[256,128]{0,1:T(8,128)(2,1)S(1)}, u32[]{:S(2)}, u32[]{:S(2)}) %collective-permute-start.1) | collective-permute-done | bytes 65568 | tf_op jit(solution)/shard_map/ppermute | solution.py:29
  37.3 0.0 copy-done.7
  37.4 0.6 copy-done.8
  38.0 0.1 copy.15
  38.1 0.1 broadcast_in_dim.11
  38.2 23.2 %all_to_all.30.q_ref = bf16[16,128,256]{2,1,0:T(8,128)(2,1)} all-to-all(bf16[16,128,256]{2,1,0:T(8,128)(2,1)S(1)} %broadcast_in_dim.11), channel_id=1, replica_groups=mesh['segment'=8,'blk'=16] {'blk'}, dimensions={0} | all-to-all | bytes 2097152 | tf_op jit(solution)/shard_map/all_to_all | solution.py:284
  61.4 1.1 broadcast_in_dim.10
  62.5 3.7 %all-to-all-start = ((bf16[16,128,256]{2,1,0:T(8,128)(2,1)}), bf16[16,128,256]{2,1,0:T(8,128)(2,1)S(1)}, u32[]{:S(2)}, u32[]{:S(2)}) async-start(bf16[16,128,256]{2,1,0:T(8,128)(2,1)} %broadcast_in_dim.10), calls=%async_computation | async-start | bytes 2097152 | tf_op jit(solution)/shard_map/all_to_all | solution.py:284
  66.2 0.6 constant_dynamic-slice_fusion
  66.8 17.7 %shard_map.101 = bf16[16,136,256]{2,1,0:T(8,128)(2,1)} custom-call(s32[1]{0:T(128)} %bitcast.1.live_ref, bf16[16,128,256]{2,1,0:T(8,128)(2,1)} %all_to_all.30.q_ref, bf16[2048,1024]{1,0:T(8,128)(2,1)} %bitcast.29, bf16[2048,1024]{1,0:T(8,128)(2,1)} %bitcast.31), custom_call_target="tpu_custom_call" | custom-call | tf_op jit(solution)/shard_map/pallas_call | solution.py:125
  84.4 0.0 all-to-all-done.q_ref
  84.4 7.2 %all-to-all-start.3 = ((bf16[16,136,256]{2,1,0:T(8,128)(2,1)}), bf16[16,136,256]{2,1,0:T(8,128)(2,1)S(1)}, u32[]{:S(2)}, u32[]{:S(2)}) async-start(bf16[16,136,256]{2,1,0:T(8,128)(2,1)} %shard_map.101), calls=%async_computation.3 | async-start | bytes 2228224 | tf_op jit(solution)/shard_map/all_to_all | solution.py:288
  91.6 17.7 %shard_map.100 = bf16[16,136,256]{2,1,0:T(8,128)(2,1)} custom-call(s32[1]{0:T(128)} %bitcast.1.live_ref, bf16[16,128,256]{2,1,0:T(8,128)(2,1)} %copy-done.4, bf16[2048,1024]{1,0:T(8,128)(2,1)} %bitcast.30, bf16[2048,1024]{1,0:T(8,128)(2,1)} %bitcast.32), custom_call_target="tpu_custom_call" | custom-call | tf_op jit(solution)/shard_map/pallas_call | solution.py:125
  109.3 0.0 all-to-all-done.3.refs_1_
  109.3 7.2 %all-to-all-start.1 = ((bf16[16,136,256]{2,1,0:T(8,128)(2,1)}), bf16[16,136,256]{2,1,0:T(8,128)(2,1)S(1)}, u32[]{:S(2)}, u32[]{:S(2)}) async-start(bf16[16,136,256]{2,1,0:T(8,128)(2,1)} %shard_map.100), calls=%async_computation.1 | async-start | bytes 2228224 | tf_op jit(solution)/shard_map/all_to_all | solution.py:288
  116.6 1.1 fusion.32
  117.7 0.1 fusion.11
  117.8 1.1 fusion.6
  119.0 0.7 reshape.160.refs_2_
  119.7 0.1 add.59
  119.8 0.7 copy.18
  120.5 9.6 %all-to-all-done.1.refs_0_ = bf16[16,136,256]{2,1,0:T(8,128)(2,1)S(1)} async-done(((bf16[16,136,256]{2,1,0:T(8,128)(2,1)}), bf16[16,136,256]{2,1,0:T(8,128)(2,1)S(1)}, u32[]{:S(2)}, u32[]{:S(2)}) %all-to-all-start.1) | async-done | bytes 1114144 | tf_op jit(solution)/shard_map/all_to_all | solution.py:288
  130.1 1.0 copy-done.3
  131.1 6.7 %shard_map.102 = bf16[256,4096]{1,0:T(8,128)(2,1)} custom-call(bf16[16,136,256]{2,1,0:T(8,128)(2,1)} %copy-done.3, bf16[16,136,256]{2,1,0:T(8,128)(2,1)} %copy-done.2, bf16[256,256]{1,0:T(8,128)(2,1)} %reshape.160.refs_2_, f32[2,256]{1,0:T(2,128)} %bitcast.40, bf16[256,4096]{1,0:T(8,128)(2,1)} %bitcast.36), custom_call_target="tpu_custom_call" | custom-call | tf_op jit(solution)/shard_map/pallas_call | solution.py:198
  137.8 26.9 %all_to_all.31.terms_ref = bf16[16,16,4096]{2,1,0:T(8,128)(2,1)} all-to-all(bf16[16,16,4096]{2,1,0:T(8,128)(2,1)} %bitcast.33), channel_id=1, replica_groups=mesh['segment'=8,'blk'=16] {'blk'}, dimensions={0} | all-to-all | bytes 4194304 | tf_op jit(solution)/shard_map/all_to_all | solution.py:297
  164.7 3.3 %shard_map.103 = bf16[16,16,4096]{2,1,0:T(8,128)(2,1)} custom-call(s32[1]{0:T(128)} %bitcast.position_ref, bf16[16,16,4096]{2,1,0:T(8,128)(2,1)} %all_to_all.31.terms_ref, bf16[256,4096]{1,0:T(8,128)(2,1)} %copy-done.1), custom_call_target="tpu_custom_call" | custom-call | tf_op jit(solution)/shard_map/pallas_call | solution.py:234
  168.0 25.5 %all_to_all.32 = bf16[16,16,4096]{2,1,0:T(8,128)(2,1)S(1)} all-to-all(bf16[16,16,4096]{2,1,0:T(8,128)(2,1)} %shard_map.103), channel_id=1, replica_groups=mesh['segment'=8,'blk'=16] {'blk'}, dimensions={0} | all-to-all | bytes 4194304 | tf_op jit(solution)/shard_map/all_to_all | solution.py:301
  193.5 1.3 copy.22
  (18 shorter events, 0.2 us)
Async XLA Ops:
  0.0 31.7 %copy-start = (bf16[1,4096,128]{2,1,0:T(8,128)(2,1)S(1)}, bf16[1,4096,128]{2,1,0:T(8,128)(2,1)}, u32[]{:S(2)}) copy-start(bf16[1,4096,128]{2,1,0:T(8,128)(2,1)} %param.16) | copy-start | bytes 3145732
  0.0 27.8 %collective-permute-start = (bf16[256,4096]{1,0:T(8,128)(2,1)}, bf16[256,4096]{1,0:T(8,128)(2,1)}, u32[]{:S(2)}, u32[]{:S(2)}) collective-permute-start(bf16[256,4096]{1,0:T(8,128)(2,1)} %bitcast.41), channel_id=1, source_target_pairs={{0,16},{16,32},{32,48},{48,64},{64,80},{80,96},{96,112},{1,17},{17... | collective-permute-start | bytes 6291464 | tf_op jit(solution)/shard_map/ppermute | solution.py:19
  2.7 25.1 %copy-start.5 = (bf16[256,4096]{1,0:T(8,128)(2,1)S(1)}, bf16[256,4096]{1,0:T(8,128)(2,1)}, u32[]{:S(2)}) copy-start(bf16[256,4096]{1,0:T(8,128)(2,1)} %param.10) | copy-start | bytes 6291460
  7.3 23.1 %copy-start.6 = (bf16[256,4096]{1,0:T(8,128)(2,1)S(1)}, bf16[256,4096]{1,0:T(8,128)(2,1)}, u32[]{:S(2)}) copy-start(bf16[256,4096]{1,0:T(8,128)(2,1)} %copy.19) | copy-start | bytes 6291460
  7.3 23.1 %copy-start.9 = (f32[1,4096]{1,0:T(1,128)S(1)}, f32[1,4096]{1,0:T(1,128)}, u32[]{:S(2)}) copy-start(f32[1,4096]{1,0:T(1,128)} %param.14) | copy-start | bytes 49156
  30.3 1.3 copy-start.1
  33.0 4.4 %copy-start.7 = (bf16[256,128]{0,1:T(8,128)(2,1)}, bf16[256,128]{0,1:T(8,128)(2,1)S(1)}, u32[]{:S(2)}) copy-start(bf16[256,128]{0,1:T(8,128)(2,1)S(1)} %fusion.23) | copy-start | bytes 196612
  33.0 4.3 %collective-permute-start.1 = (bf16[256,128]{0,1:T(8,128)(2,1)S(1)}, bf16[256,128]{0,1:T(8,128)(2,1)S(1)}, u32[]{:S(2)}, u32[]{:S(2)}) collective-permute-start(bf16[256,128]{0,1:T(8,128)(2,1)S(1)} %fusion.23), channel_id=1, source_target_pairs={{0,1},{1,0},{2,3},{3,2},{4,5},{5,4},{6,7},{7,6},{8,9},{9,8},{10,11... | collective-permute-start | bytes 196616 | tf_op jit(solution)/shard_map/ppermute | solution.py:29
  37.4 0.6 copy-start.8
  61.4 4.7 %copy-start.10 = (s32[1,16]{1,0:T(1,128)S(1)}, s32[1,16]{1,0:T(1,128)}, u32[]{:S(2)}) copy-start(s32[1,16]{1,0:T(1,128)} %param.13) | copy-start | bytes 196
  62.5 21.9 %all-to-all-start = ((bf16[16,128,256]{2,1,0:T(8,128)(2,1)}), bf16[16,128,256]{2,1,0:T(8,128)(2,1)S(1)}, u32[]{:S(2)}, u32[]{:S(2)}) async-start(bf16[16,128,256]{2,1,0:T(8,128)(2,1)} %broadcast_in_dim.10), calls=%async_computation | async-start | bytes 2097152 | tf_op jit(solution)/shard_map/all_to_all | solution.py:284
  84.4 7.2 %copy-start.4 = (bf16[16,128,256]{2,1,0:T(8,128)(2,1)}, bf16[16,128,256]{2,1,0:T(8,128)(2,1)S(1)}, u32[]{:S(2)}) copy-start(bf16[16,128,256]{2,1,0:T(8,128)(2,1)S(1)} %all-to-all-done.q_ref) | copy-start | bytes 3145732
  84.4 24.8 %all-to-all-start.3 = ((bf16[16,136,256]{2,1,0:T(8,128)(2,1)}), bf16[16,136,256]{2,1,0:T(8,128)(2,1)S(1)}, u32[]{:S(2)}, u32[]{:S(2)}) async-start(bf16[16,136,256]{2,1,0:T(8,128)(2,1)} %shard_map.101), calls=%async_computation.3 | async-start | bytes 2228224 | tf_op jit(solution)/shard_map/all_to_all | solution.py:288
  109.3 9.7 %copy-start.2 = (bf16[16,136,256]{2,1,0:T(8,128)(2,1)}, bf16[16,136,256]{2,1,0:T(8,128)(2,1)S(1)}, u32[]{:S(2)}) copy-start(bf16[16,136,256]{2,1,0:T(8,128)(2,1)S(1)} %all-to-all-done.3.refs_1_) | copy-start | bytes 3342340
  109.3 20.8 %all-to-all-start.1 = ((bf16[16,136,256]{2,1,0:T(8,128)(2,1)}), bf16[16,136,256]{2,1,0:T(8,128)(2,1)S(1)}, u32[]{:S(2)}, u32[]{:S(2)}) async-start(bf16[16,136,256]{2,1,0:T(8,128)(2,1)} %shard_map.100), calls=%async_computation.1 | async-start | bytes 2228224 | tf_op jit(solution)/shard_map/all_to_all | solution.py:288
  130.1 1.0 copy-start.3

commit v18 on v17

--- a/solution.py
+++ b/solution.py
@@ -188,7 +188,7 @@
         out_ref[:, h * HD:(h + 1) * HD] = (weighted / total).astype(out_ref.dtype)
 
 
-COLUMN_BLOCK = 1024
+COLUMN_BLOCK = 2048
 
 
 def combine(arrived_halves, own_out, own_log, out_weight):

time: 196 us -> 194 us (0.990)
  no operation moved by 1% of the time
where the time goes in v18:
time: 194 us
  blocking collectives  75.6 us (39%)
  Pallas kernels  44 us (23%)
  waiting for transfers between devices  32.4 us (17%)
  starting transfers between devices  22.1 us (11%)
  local copies, waits for them, and re-layouts  11.1 us (6%)
  matrix products  4.11 us (2%)
  other arithmetic  3.38 us (2%)
    pallas_call x2, Pallas kernels, cache_attention(): pl.pallas_call(cache_kernel, grid_spec=grid_spec, out_shape=jax.ShapeDtyp...  35.3 us
    all_to_all x1, blocking collectives, shards(): lax.all_to_all(head_terms.reshape(blocks, chunk, -1), 'blk', 0, 0, tiled=...  26.9 us
    all_to_all x1, blocking collectives, shards(): lax.all_to_all(spread, 'blk', 0, 0, tiled=True).reshape(span_rows, -1)  25.5 us
    all_to_all x1, blocking collectives, shards(): lax.all_to_all(jnp.broadcast_to(half[None], (blocks,) + half.shape), 'blk...  23.2 us
    ppermute x1, waiting for transfers between devices, passed_along(): return lax.ppermute(block, axis, route)  20.5 us
    all_to_all x2, starting transfers between devices, shards(): lax.all_to_all(held, 'blk', split_axis=0, concat_axis=0, tiled=True)  14.4 us
    all_to_all x2, waiting for transfers between devices, shards(): lax.all_to_all(held, 'blk', split_axis=0, concat_axis=0, tiled=True)  9.61 us
    pallas_call x1, Pallas kernels, combine(): pl.pallas_call(combine_kernel, grid=(columns // COLUMN_BLOCK,), in_specs=...  5.45 us
  transfers between devices with their start and end apart: 5, of which 3 were waited for; matrix products, arithmetic and copies ran while one was open for 5% of the time, Pallas kernels for 18%

profile of v18, /device:TPU:2, one launch (start us, length us, event | category | flops | bytes accessed | tf_op | source)
XLA Modules:
  0.0 193.5 jit_solution(18239598109603350407)
XLA Ops:
  0.0 0.0 copy-start
  0.0 2.0 %collective-permute-start = (bf16[256,4096]{1,0:T(8,128)(2,1)}, bf16[256,4096]{1,0:T(8,128)(2,1)}, u32[]{:S(2)}, u32[]{:S(2)}) collective-permute-start(bf16[256,4096]{1,0:T(8,128)(2,1)} %bitcast.41), channel_id=1, source_target_pairs={{0,16},{16,32},{32,48},{48,64},{64,80},{80,96},{96,112},{1,17},{17... | collective-permute-start | bytes 6291464 | tf_op jit(solution)/shard_map/ppermute | solution.py:19
  2.7 0.0 copy-start.5
  2.7 4.2 %copy.19 = bf16[256,4096]{1,0:T(8,128)(2,1)} copy(bf16[256,4096]{0,1:T(8,128)(2,1)} %bitcast.35) | data formatting | bytes 4194304 | tf_op jit(solution)/shard_map/dot_general | solution.py:268
  7.0 0.3 multiply_cosine_fusion
  7.3 0.0 copy-start.6
  7.3 0.0 copy-start.9
  7.3 20.5 %collective-permute-done = bf16[256,4096]{1,0:T(8,128)(2,1)} collective-permute-done((bf16[256,4096]{1,0:T(8,128)(2,1)}, bf16[256,4096]{1,0:T(8,128)(2,1)}, u32[]{:S(2)}, u32[]{:S(2)}) %collective-permute-start) | collective-permute-done | bytes 2097184 | tf_op jit(solution)/shard_map/ppermute | solution.py:19
  27.8 0.0 copy-done.5
  27.8 2.5 %fusion = (f32[256]{0:T(256)S(1)}, bf16[256,4096]{1,0:T(8,128)(2,1)S(1)}) fusion(bf16[256,4096]{1,0:T(8,128)(2,1)S(1)} %copy-done.5, bf16[256,4096]{1,0:T(8,128)(2,1)} %collective-permute-done, pred[]{:T(512)S(6)} %eq.9), kind=kLoop, calls=%fused_computation.2 | loop fusion | flops 4194048 | bytes 6292481 | tf_op jit(solution)/shard_map/reduce_sum | solution.py:265
  30.3 0.0 copy-start.1
  30.4 0.0 copy-done.6
  30.4 0.0 copy-done.9
  30.4 0.9 fusion.3
  31.3 0.4 copy-done.1
  31.7 0.0 copy-done
  31.7 1.0 fusion.7
  32.6 0.3 fusion.20
  33.0 2.0 %collective-permute-start.1 = (bf16[256,128]{0,1:T(8,128)(2,1)S(1)}, bf16[256,128]{0,1:T(8,128)(2,1)S(1)}, u32[]{:S(2)}, u32[]{:S(2)}) collective-permute-start(bf16[256,128]{0,1:T(8,128)(2,1)S(1)} %fusion.23), channel_id=1, source_target_pairs={{0,1},{1,0},{2,3},{3,2},{4,5},{5,4},{6,7},{7,6},{8,9},{9,8},{10,11... | collective-permute-start | bytes 196616 | tf_op jit(solution)/shard_map/ppermute | solution.py:29
  35.1 2.3 %collective-permute-done.1 = bf16[256,128]{0,1:T(8,128)(2,1)S(1)} collective-permute-done((bf16[256,128]{0,1:T(8,128)(2,1)S(1)}, bf16[256,128]{0,1:T(8,128)(2,1)S(1)}, u32[]{:S(2)}, u32[]{:S(2)}) %collective-permute-start.1) | collective-permute-done | bytes 65568 | tf_op jit(solution)/shard_map/ppermute | solution.py:29
  37.3 0.0 copy-done.7
  37.4 0.6 copy-done.8
  38.0 0.1 copy.15
  38.1 0.1 broadcast_in_dim.11
  38.2 23.2 %all_to_all.30.q_ref = bf16[16,128,256]{2,1,0:T(8,128)(2,1)} all-to-all(bf16[16,128,256]{2,1,0:T(8,128)(2,1)S(1)} %broadcast_in_dim.11), channel_id=1, replica_groups=mesh['segment'=8,'blk'=16] {'blk'}, dimensions={0} | all-to-all | bytes 2097152 | tf_op jit(solution)/shard_map/all_to_all | solution.py:284
  61.4 1.1 broadcast_in_dim.10
  62.5 3.7 %all-to-all-start = ((bf16[16,128,256]{2,1,0:T(8,128)(2,1)}), bf16[16,128,256]{2,1,0:T(8,128)(2,1)S(1)}, u32[]{:S(2)}, u32[]{:S(2)}) async-start(bf16[16,128,256]{2,1,0:T(8,128)(2,1)} %broadcast_in_dim.10), calls=%async_computation | async-start | bytes 2097152 | tf_op jit(solution)/shard_map/all_to_all | solution.py:284
  66.2 0.6 constant_dynamic-slice_fusion
  66.8 17.7 %shard_map.101 = bf16[16,136,256]{2,1,0:T(8,128)(2,1)} custom-call(s32[1]{0:T(128)} %bitcast.1.live_ref, bf16[16,128,256]{2,1,0:T(8,128)(2,1)} %all_to_all.30.q_ref, bf16[2048,1024]{1,0:T(8,128)(2,1)} %bitcast.29, bf16[2048,1024]{1,0:T(8,128)(2,1)} %bitcast.31), custom_call_target="tpu_custom_call" | custom-call | tf_op jit(solution)/shard_map/pallas_call | solution.py:125
  84.4 0.0 all-to-all-done.q_ref
  84.4 7.2 %all-to-all-start.3 = ((bf16[16,136,256]{2,1,0:T(8,128)(2,1)}), bf16[16,136,256]{2,1,0:T(8,128)(2,1)S(1)}, u32[]{:S(2)}, u32[]{:S(2)}) async-start(bf16[16,136,256]{2,1,0:T(8,128)(2,1)} %shard_map.101), calls=%async_computation.3 | async-start | bytes 2228224 | tf_op jit(solution)/shard_map/all_to_all | solution.py:288
  91.6 0.0 copy-done.4
  91.6 17.7 %shard_map.100 = bf16[16,136,256]{2,1,0:T(8,128)(2,1)} custom-call(s32[1]{0:T(128)} %bitcast.1.live_ref, bf16[16,128,256]{2,1,0:T(8,128)(2,1)} %copy-done.4, bf16[2048,1024]{1,0:T(8,128)(2,1)} %bitcast.30, bf16[2048,1024]{1,0:T(8,128)(2,1)} %bitcast.32), custom_call_target="tpu_custom_call" | custom-call | tf_op jit(solution)/shard_map/pallas_call | solution.py:125
  109.3 0.0 all-to-all-done.3.refs_1_
  109.3 7.2 %all-to-all-start.1 = ((bf16[16,136,256]{2,1,0:T(8,128)(2,1)}), bf16[16,136,256]{2,1,0:T(8,128)(2,1)S(1)}, u32[]{:S(2)}, u32[]{:S(2)}) async-start(bf16[16,136,256]{2,1,0:T(8,128)(2,1)} %shard_map.100), calls=%async_computation.1 | async-start | bytes 2228224 | tf_op jit(solution)/shard_map/all_to_all | solution.py:288
  116.6 1.1 fusion.32
  117.7 0.1 fusion.11
  117.8 1.1 fusion.6
  119.0 0.7 reshape.160.refs_2_
  119.7 0.1 add.59
  119.8 0.7 copy.18
  120.5 9.6 %all-to-all-done.1.refs_0_ = bf16[16,136,256]{2,1,0:T(8,128)(2,1)S(1)} async-done(((bf16[16,136,256]{2,1,0:T(8,128)(2,1)}), bf16[16,136,256]{2,1,0:T(8,128)(2,1)S(1)}, u32[]{:S(2)}, u32[]{:S(2)}) %all-to-all-start.1) | async-done | bytes 1114144 | tf_op jit(solution)/shard_map/all_to_all | solution.py:288
  130.1 1.0 copy-done.3
  131.1 5.5 %shard_map.102 = bf16[256,4096]{1,0:T(8,128)(2,1)} custom-call(bf16[16,136,256]{2,1,0:T(8,128)(2,1)} %copy-done.3, bf16[16,136,256]{2,1,0:T(8,128)(2,1)} %copy-done.2, bf16[256,256]{1,0:T(8,128)(2,1)} %reshape.160.refs_2_, f32[2,256]{1,0:T(2,128)} %bitcast.40, bf16[256,4096]{1,0:T(8,128)(2,1)} %bitcast.36), custom_call_target="tpu_custom_call" | custom-call | tf_op jit(solution)/shard_map/pallas_call | solution.py:198
  136.6 26.9 %all_to_all.31.terms_ref = bf16[16,16,4096]{2,1,0:T(8,128)(2,1)} all-to-all(bf16[16,16,4096]{2,1,0:T(8,128)(2,1)} %bitcast.33), channel_id=1, replica_groups=mesh['segment'=8,'blk'=16] {'blk'}, dimensions={0} | all-to-all | bytes 4194304 | tf_op jit(solution)/shard_map/all_to_all | solution.py:297
  163.5 3.3 %shard_map.103 = bf16[16,16,4096]{2,1,0:T(8,128)(2,1)} custom-call(s32[1]{0:T(128)} %bitcast.position_ref, bf16[16,16,4096]{2,1,0:T(8,128)(2,1)} %all_to_all.31.terms_ref, bf16[256,4096]{1,0:T(8,128)(2,1)} %copy-done.1), custom_call_target="tpu_custom_call" | custom-call | tf_op jit(solution)/shard_map/pallas_call | solution.py:234
  166.7 25.5 %all_to_all.32 = bf16[16,16,4096]{2,1,0:T(8,128)(2,1)S(1)} all-to-all(bf16[16,16,4096]{2,1,0:T(8,128)(2,1)} %shard_map.103), channel_id=1, replica_groups=mesh['segment'=8,'blk'=16] {'blk'}, dimensions={0} | all-to-all | bytes 4194304 | tf_op jit(solution)/shard_map/all_to_all | solution.py:301
  192.2 1.3 copy.22
  (18 shorter events, 0.2 us)
Async XLA Ops:
  0.0 31.7 %copy-start = (bf16[1,4096,128]{2,1,0:T(8,128)(2,1)S(1)}, bf16[1,4096,128]{2,1,0:T(8,128)(2,1)}, u32[]{:S(2)}) copy-start(bf16[1,4096,128]{2,1,0:T(8,128)(2,1)} %param.16) | copy-start | bytes 3145732
  0.0 27.8 %collective-permute-start = (bf16[256,4096]{1,0:T(8,128)(2,1)}, bf16[256,4096]{1,0:T(8,128)(2,1)}, u32[]{:S(2)}, u32[]{:S(2)}) collective-permute-start(bf16[256,4096]{1,0:T(8,128)(2,1)} %bitcast.41), channel_id=1, source_target_pairs={{0,16},{16,32},{32,48},{48,64},{64,80},{80,96},{96,112},{1,17},{17... | collective-permute-start | bytes 6291464 | tf_op jit(solution)/shard_map/ppermute | solution.py:19
  2.7 25.1 %copy-start.5 = (bf16[256,4096]{1,0:T(8,128)(2,1)S(1)}, bf16[256,4096]{1,0:T(8,128)(2,1)}, u32[]{:S(2)}) copy-start(bf16[256,4096]{1,0:T(8,128)(2,1)} %param.10) | copy-start | bytes 6291460
  7.3 23.1 %copy-start.6 = (bf16[256,4096]{1,0:T(8,128)(2,1)S(1)}, bf16[256,4096]{1,0:T(8,128)(2,1)}, u32[]{:S(2)}) copy-start(bf16[256,4096]{1,0:T(8,128)(2,1)} %copy.19) | copy-start | bytes 6291460
  7.3 23.1 %copy-start.9 = (f32[1,4096]{1,0:T(1,128)S(1)}, f32[1,4096]{1,0:T(1,128)}, u32[]{:S(2)}) copy-start(f32[1,4096]{1,0:T(1,128)} %param.14) | copy-start | bytes 49156
  30.3 1.3 copy-start.1
  33.0 4.4 %copy-start.7 = (bf16[256,128]{0,1:T(8,128)(2,1)}, bf16[256,128]{0,1:T(8,128)(2,1)S(1)}, u32[]{:S(2)}) copy-start(bf16[256,128]{0,1:T(8,128)(2,1)S(1)} %fusion.23) | copy-start | bytes 196612
  33.0 4.3 %collective-permute-start.1 = (bf16[256,128]{0,1:T(8,128)(2,1)S(1)}, bf16[256,128]{0,1:T(8,128)(2,1)S(1)}, u32[]{:S(2)}, u32[]{:S(2)}) collective-permute-start(bf16[256,128]{0,1:T(8,128)(2,1)S(1)} %fusion.23), channel_id=1, source_target_pairs={{0,1},{1,0},{2,3},{3,2},{4,5},{5,4},{6,7},{7,6},{8,9},{9,8},{10,11... | collective-permute-start | bytes 196616 | tf_op jit(solution)/shard_map/ppermute | solution.py:29
  37.4 0.6 copy-start.8
  61.4 4.7 %copy-start.10 = (s32[1,16]{1,0:T(1,128)S(1)}, s32[1,16]{1,0:T(1,128)}, u32[]{:S(2)}) copy-start(s32[1,16]{1,0:T(1,128)} %param.13) | copy-start | bytes 196
  62.5 21.9 %all-to-all-start = ((bf16[16,128,256]{2,1,0:T(8,128)(2,1)}), bf16[16,128,256]{2,1,0:T(8,128)(2,1)S(1)}, u32[]{:S(2)}, u32[]{:S(2)}) async-start(bf16[16,128,256]{2,1,0:T(8,128)(2,1)} %broadcast_in_dim.10), calls=%async_computation | async-start | bytes 2097152 | tf_op jit(solution)/shard_map/all_to_all | solution.py:284
  84.4 7.2 %copy-start.4 = (bf16[16,128,256]{2,1,0:T(8,128)(2,1)}, bf16[16,128,256]{2,1,0:T(8,128)(2,1)S(1)}, u32[]{:S(2)}) copy-start(bf16[16,128,256]{2,1,0:T(8,128)(2,1)S(1)} %all-to-all-done.q_ref) | copy-start | bytes 3145732
  84.4 24.8 %all-to-all-start.3 = ((bf16[16,136,256]{2,1,0:T(8,128)(2,1)}), bf16[16,136,256]{2,1,0:T(8,128)(2,1)S(1)}, u32[]{:S(2)}, u32[]{:S(2)}) async-start(bf16[16,136,256]{2,1,0:T(8,128)(2,1)} %shard_map.101), calls=%async_computation.3 | async-start | bytes 2228224 | tf_op jit(solution)/shard_map/all_to_all | solution.py:288
  109.3 9.7 %copy-start.2 = (bf16[16,136,256]{2,1,0:T(8,128)(2,1)}, bf16[16,136,256]{2,1,0:T(8,128)(2,1)S(1)}, u32[]{:S(2)}) copy-start(bf16[16,136,256]{2,1,0:T(8,128)(2,1)S(1)} %all-to-all-done.3.refs_1_) | copy-start | bytes 3342340
  109.3 20.8 %all-to-all-start.1 = ((bf16[16,136,256]{2,1,0:T(8,128)(2,1)}), bf16[16,136,256]{2,1,0:T(8,128)(2,1)S(1)}, u32[]{:S(2)}, u32[]{:S(2)}) async-start(bf16[16,136,256]{2,1,0:T(8,128)(2,1)} %shard_map.100), calls=%async_computation.1 | async-start | bytes 2228224 | tf_op jit(solution)/shard_map/all_to_all | solution.py:288
  130.1 1.0 copy-start.3

commit v19 on v18

--- a/solution.py
+++ b/solution.py
@@ -188,7 +188,7 @@
         out_ref[:, h * HD:(h + 1) * HD] = (weighted / total).astype(out_ref.dtype)
 
 
-COLUMN_BLOCK = 2048
+COLUMN_BLOCK = 4096
 
 
 def combine(arrived_halves, own_out, own_log, out_weight):

time: 194 us -> 198 us (1.021); the launches traced: 194 us -> 194 us
  no operation moved by 1% of the time
where the time goes in v19:
time: 198 us; the launch traced here: 194 us
  blocking collectives  75.6 us (38%)
  Pallas kernels  44.7 us (23%)
  waiting for transfers between devices  32.4 us (16%)
  starting transfers between devices  22.1 us (11%)
  local copies, waits for them, and re-layouts  11.1 us (6%)
  matrix products  4.11 us (2%)
  other arithmetic  3.38 us (2%)
    pallas_call x2, Pallas kernels, cache_attention(): pl.pallas_call(cache_kernel, grid_spec=grid_spec, out_shape=jax.ShapeDtyp...  35.3 us
    all_to_all x1, blocking collectives, shards(): lax.all_to_all(head_terms.reshape(blocks, chunk, -1), 'blk', 0, 0, tiled=...  26.9 us
    all_to_all x1, blocking collectives, shards(): lax.all_to_all(spread, 'blk', 0, 0, tiled=True).reshape(span_rows, -1)  25.5 us
    all_to_all x1, blocking collectives, shards(): lax.all_to_all(jnp.broadcast_to(half[None], (blocks,) + half.shape), 'blk...  23.2 us
    ppermute x1, waiting for transfers between devices, passed_along(): return lax.ppermute(block, axis, route)  20.5 us
    all_to_all x2, starting transfers between devices, shards(): lax.all_to_all(held, 'blk', split_axis=0, concat_axis=0, tiled=True)  14.4 us
    all_to_all x2, waiting for transfers between devices, shards(): lax.all_to_all(held, 'blk', split_axis=0, concat_axis=0, tiled=True)  9.61 us
    pallas_call x1, Pallas kernels, combine(): pl.pallas_call(combine_kernel, grid=(columns // COLUMN_BLOCK,), in_specs=...  6.08 us
  transfers between devices with their start and end apart: 5, of which 3 were waited for; matrix products, arithmetic and copies ran while one was open for 5% of the time, Pallas kernels for 18%

profile of v19, /device:TPU:2, one launch (start us, length us, event | category | flops | bytes accessed | tf_op | source)
XLA Modules:
  0.0 194.2 jit_solution(6306626333502040776)
XLA Ops:
  0.0 0.0 copy-start
  0.0 2.0 %collective-permute-start = (bf16[256,4096]{1,0:T(8,128)(2,1)}, bf16[256,4096]{1,0:T(8,128)(2,1)}, u32[]{:S(2)}, u32[]{:S(2)}) collective-permute-start(bf16[256,4096]{1,0:T(8,128)(2,1)} %bitcast.41), channel_id=1, source_target_pairs={{0,16},{16,32},{32,48},{48,64},{64,80},{80,96},{96,112},{1,17},{17... | collective-permute-start | bytes 6291464 | tf_op jit(solution)/shard_map/ppermute | solution.py:19
  2.7 0.0 copy-start.5
  2.7 4.2 %copy.19 = bf16[256,4096]{1,0:T(8,128)(2,1)} copy(bf16[256,4096]{0,1:T(8,128)(2,1)} %bitcast.35) | data formatting | bytes 4194304 | tf_op jit(solution)/shard_map/dot_general | solution.py:268
  7.0 0.3 multiply_cosine_fusion
  7.3 0.0 copy-start.6
  7.3 0.0 copy-start.9
  7.3 20.5 %collective-permute-done = bf16[256,4096]{1,0:T(8,128)(2,1)} collective-permute-done((bf16[256,4096]{1,0:T(8,128)(2,1)}, bf16[256,4096]{1,0:T(8,128)(2,1)}, u32[]{:S(2)}, u32[]{:S(2)}) %collective-permute-start) | collective-permute-done | bytes 2097184 | tf_op jit(solution)/shard_map/ppermute | solution.py:19
  27.8 0.0 copy-done.5
  27.8 2.5 %fusion = (f32[256]{0:T(256)S(1)}, bf16[256,4096]{1,0:T(8,128)(2,1)S(1)}) fusion(bf16[256,4096]{1,0:T(8,128)(2,1)S(1)} %copy-done.5, bf16[256,4096]{1,0:T(8,128)(2,1)} %collective-permute-done, pred[]{:T(512)S(6)} %eq.9), kind=kLoop, calls=%fused_computation.2 | loop fusion | flops 4194048 | bytes 6292481 | tf_op jit(solution)/shard_map/reduce_sum | solution.py:265
  30.3 0.0 copy-start.1
  30.4 0.0 copy-done.6
  30.4 0.0 copy-done.9
  30.4 0.9 fusion.3
  31.3 0.4 copy-done.1
  31.7 0.0 copy-done
  31.7 1.0 fusion.7
  32.6 0.3 fusion.20
  33.0 0.0 copy-start.7
  33.0 2.0 %collective-permute-start.1 = (bf16[256,128]{0,1:T(8,128)(2,1)S(1)}, bf16[256,128]{0,1:T(8,128)(2,1)S(1)}, u32[]{:S(2)}, u32[]{:S(2)}) collective-permute-start(bf16[256,128]{0,1:T(8,128)(2,1)S(1)} %fusion.23), channel_id=1, source_target_pairs={{0,1},{1,0},{2,3},{3,2},{4,5},{5,4},{6,7},{7,6},{8,9},{9,8},{10,11... | collective-permute-start | bytes 196616 | tf_op jit(solution)/shard_map/ppermute | solution.py:29
  35.1 2.3 %collective-permute-done.1 = bf16[256,128]{0,1:T(8,128)(2,1)S(1)} collective-permute-done((bf16[256,128]{0,1:T(8,128)(2,1)S(1)}, bf16[256,128]{0,1:T(8,128)(2,1)S(1)}, u32[]{:S(2)}, u32[]{:S(2)}) %collective-permute-start.1) | collective-permute-done | bytes 65568 | tf_op jit(solution)/shard_map/ppermute | solution.py:29
  37.4 0.6 copy-done.8
  38.0 0.1 copy.15
  38.1 0.1 broadcast_in_dim.11
  38.2 23.2 %all_to_all.30.q_ref = bf16[16,128,256]{2,1,0:T(8,128)(2,1)} all-to-all(bf16[16,128,256]{2,1,0:T(8,128)(2,1)S(1)} %broadcast_in_dim.11), channel_id=1, replica_groups=mesh['segment'=8,'blk'=16] {'blk'}, dimensions={0} | all-to-all | bytes 2097152 | tf_op jit(solution)/shard_map/all_to_all | solution.py:284
  61.4 1.1 broadcast_in_dim.10
  62.5 3.7 %all-to-all-start = ((bf16[16,128,256]{2,1,0:T(8,128)(2,1)}), bf16[16,128,256]{2,1,0:T(8,128)(2,1)S(1)}, u32[]{:S(2)}, u32[]{:S(2)}) async-start(bf16[16,128,256]{2,1,0:T(8,128)(2,1)} %broadcast_in_dim.10), calls=%async_computation | async-start | bytes 2097152 | tf_op jit(solution)/shard_map/all_to_all | solution.py:284
  66.2 0.0 copy-done.10
  66.2 0.6 constant_dynamic-slice_fusion
  66.8 17.7 %shard_map.101 = bf16[16,136,256]{2,1,0:T(8,128)(2,1)} custom-call(s32[1]{0:T(128)} %bitcast.1.live_ref, bf16[16,128,256]{2,1,0:T(8,128)(2,1)} %all_to_all.30.q_ref, bf16[2048,1024]{1,0:T(8,128)(2,1)} %bitcast.29, bf16[2048,1024]{1,0:T(8,128)(2,1)} %bitcast.31), custom_call_target="tpu_custom_call" | custom-call | tf_op jit(solution)/shard_map/pallas_call | solution.py:125
  84.4 0.0 all-to-all-done.q_ref
  84.4 7.2 %all-to-all-start.3 = ((bf16[16,136,256]{2,1,0:T(8,128)(2,1)}), bf16[16,136,256]{2,1,0:T(8,128)(2,1)S(1)}, u32[]{:S(2)}, u32[]{:S(2)}) async-start(bf16[16,136,256]{2,1,0:T(8,128)(2,1)} %shard_map.101), calls=%async_computation.3 | async-start | bytes 2228224 | tf_op jit(solution)/shard_map/all_to_all | solution.py:288
  91.6 17.7 %shard_map.100 = bf16[16,136,256]{2,1,0:T(8,128)(2,1)} custom-call(s32[1]{0:T(128)} %bitcast.1.live_ref, bf16[16,128,256]{2,1,0:T(8,128)(2,1)} %copy-done.4, bf16[2048,1024]{1,0:T(8,128)(2,1)} %bitcast.30, bf16[2048,1024]{1,0:T(8,128)(2,1)} %bitcast.32), custom_call_target="tpu_custom_call" | custom-call | tf_op jit(solution)/shard_map/pallas_call | solution.py:125
  109.3 0.0 all-to-all-done.3.refs_1_
  109.3 7.2 %all-to-all-start.1 = ((bf16[16,136,256]{2,1,0:T(8,128)(2,1)}), bf16[16,136,256]{2,1,0:T(8,128)(2,1)S(1)}, u32[]{:S(2)}, u32[]{:S(2)}) async-start(bf16[16,136,256]{2,1,0:T(8,128)(2,1)} %shard_map.100), calls=%async_computation.1 | async-start | bytes 2228224 | tf_op jit(solution)/shard_map/all_to_all | solution.py:288
  116.6 1.1 fusion.32
  117.7 0.1 fusion.11
  117.8 1.1 fusion.6
  119.0 0.7 reshape.160.refs_2_
  119.7 0.1 add.59
  119.8 0.7 copy.18
  120.5 9.6 %all-to-all-done.1.refs_0_ = bf16[16,136,256]{2,1,0:T(8,128)(2,1)S(1)} async-done(((bf16[16,136,256]{2,1,0:T(8,128)(2,1)}), bf16[16,136,256]{2,1,0:T(8,128)(2,1)S(1)}, u32[]{:S(2)}, u32[]{:S(2)}) %all-to-all-start.1) | async-done | bytes 1114144 | tf_op jit(solution)/shard_map/all_to_all | solution.py:288
  130.1 1.0 copy-done.3
  131.1 6.1 %shard_map.102 = bf16[256,4096]{1,0:T(8,128)(2,1)} custom-call(bf16[16,136,256]{2,1,0:T(8,128)(2,1)} %copy-done.3, bf16[16,136,256]{2,1,0:T(8,128)(2,1)} %copy-done.2, bf16[256,256]{1,0:T(8,128)(2,1)} %reshape.160.refs_2_, f32[2,256]{1,0:T(2,128)} %bitcast.40, bf16[256,4096]{1,0:T(8,128)(2,1)} %bitcast.36), custom_call_target="tpu_custom_call" | custom-call | tf_op jit(solution)/shard_map/pallas_call | solution.py:198
  137.2 26.9 %all_to_all.31.terms_ref = bf16[16,16,4096]{2,1,0:T(8,128)(2,1)} all-to-all(bf16[16,16,4096]{2,1,0:T(8,128)(2,1)} %bitcast.33), channel_id=1, replica_groups=mesh['segment'=8,'blk'=16] {'blk'}, dimensions={0} | all-to-all | bytes 4194304 | tf_op jit(solution)/shard_map/all_to_all | solution.py:297
  164.1 3.3 %shard_map.103 = bf16[16,16,4096]{2,1,0:T(8,128)(2,1)} custom-call(s32[1]{0:T(128)} %bitcast.position_ref, bf16[16,16,4096]{2,1,0:T(8,128)(2,1)} %all_to_all.31.terms_ref, bf16[256,4096]{1,0:T(8,128)(2,1)} %copy-done.1), custom_call_target="tpu_custom_call" | custom-call | tf_op jit(solution)/shard_map/pallas_call | solution.py:234
  167.4 25.5 %all_to_all.32 = bf16[16,16,4096]{2,1,0:T(8,128)(2,1)S(1)} all-to-all(bf16[16,16,4096]{2,1,0:T(8,128)(2,1)} %shard_map.103), channel_id=1, replica_groups=mesh['segment'=8,'blk'=16] {'blk'}, dimensions={0} | all-to-all | bytes 4194304 | tf_op jit(solution)/shard_map/all_to_all | solution.py:301
  192.8 1.3 copy.22
  (18 shorter events, 0.2 us)
Async XLA Ops:
  0.0 31.7 %copy-start = (bf16[1,4096,128]{2,1,0:T(8,128)(2,1)S(1)}, bf16[1,4096,128]{2,1,0:T(8,128)(2,1)}, u32[]{:S(2)}) copy-start(bf16[1,4096,128]{2,1,0:T(8,128)(2,1)} %param.16) | copy-start | bytes 3145732
  0.0 27.8 %collective-permute-start = (bf16[256,4096]{1,0:T(8,128)(2,1)}, bf16[256,4096]{1,0:T(8,128)(2,1)}, u32[]{:S(2)}, u32[]{:S(2)}) collective-permute-start(bf16[256,4096]{1,0:T(8,128)(2,1)} %bitcast.41), channel_id=1, source_target_pairs={{0,16},{16,32},{32,48},{48,64},{64,80},{80,96},{96,112},{1,17},{17... | collective-permute-start | bytes 6291464 | tf_op jit(solution)/shard_map/ppermute | solution.py:19
  2.7 25.1 %copy-start.5 = (bf16[256,4096]{1,0:T(8,128)(2,1)S(1)}, bf16[256,4096]{1,0:T(8,128)(2,1)}, u32[]{:S(2)}) copy-start(bf16[256,4096]{1,0:T(8,128)(2,1)} %param.10) | copy-start | bytes 6291460
  7.3 23.1 %copy-start.6 = (bf16[256,4096]{1,0:T(8,128)(2,1)S(1)}, bf16[256,4096]{1,0:T(8,128)(2,1)}, u32[]{:S(2)}) copy-start(bf16[256,4096]{1,0:T(8,128)(2,1)} %copy.19) | copy-start | bytes 6291460
  7.3 23.1 %copy-start.9 = (f32[1,4096]{1,0:T(1,128)S(1)}, f32[1,4096]{1,0:T(1,128)}, u32[]{:S(2)}) copy-start(f32[1,4096]{1,0:T(1,128)} %param.14) | copy-start | bytes 49156
  30.3 1.3 copy-start.1
  33.0 4.4 %copy-start.7 = (bf16[256,128]{0,1:T(8,128)(2,1)}, bf16[256,128]{0,1:T(8,128)(2,1)S(1)}, u32[]{:S(2)}) copy-start(bf16[256,128]{0,1:T(8,128)(2,1)S(1)} %fusion.23) | copy-start | bytes 196612
  33.0 4.3 %collective-permute-start.1 = (bf16[256,128]{0,1:T(8,128)(2,1)S(1)}, bf16[256,128]{0,1:T(8,128)(2,1)S(1)}, u32[]{:S(2)}, u32[]{:S(2)}) collective-permute-start(bf16[256,128]{0,1:T(8,128)(2,1)S(1)} %fusion.23), channel_id=1, source_target_pairs={{0,1},{1,0},{2,3},{3,2},{4,5},{5,4},{6,7},{7,6},{8,9},{9,8},{10,11... | collective-permute-start | bytes 196616 | tf_op jit(solution)/shard_map/ppermute | solution.py:29
  37.4 0.6 copy-start.8
  61.4 4.7 %copy-start.10 = (s32[1,16]{1,0:T(1,128)S(1)}, s32[1,16]{1,0:T(1,128)}, u32[]{:S(2)}) copy-start(s32[1,16]{1,0:T(1,128)} %param.13) | copy-start | bytes 196
  62.5 21.9 %all-to-all-start = ((bf16[16,128,256]{2,1,0:T(8,128)(2,1)}), bf16[16,128,256]{2,1,0:T(8,128)(2,1)S(1)}, u32[]{:S(2)}, u32[]{:S(2)}) async-start(bf16[16,128,256]{2,1,0:T(8,128)(2,1)} %broadcast_in_dim.10), calls=%async_computation | async-start | bytes 2097152 | tf_op jit(solution)/shard_map/all_to_all | solution.py:284
  84.4 7.2 %copy-start.4 = (bf16[16,128,256]{2,1,0:T(8,128)(2,1)}, bf16[16,128,256]{2,1,0:T(8,128)(2,1)S(1)}, u32[]{:S(2)}) copy-start(bf16[16,128,256]{2,1,0:T(8,128)(2,1)S(1)} %all-to-all-done.q_ref) | copy-start | bytes 3145732
  84.4 24.8 %all-to-all-start.3 = ((bf16[16,136,256]{2,1,0:T(8,128)(2,1)}), bf16[16,136,256]{2,1,0:T(8,128)(2,1)S(1)}, u32[]{:S(2)}, u32[]{:S(2)}) async-start(bf16[16,136,256]{2,1,0:T(8,128)(2,1)} %shard_map.101), calls=%async_computation.3 | async-start | bytes 2228224 | tf_op jit(solution)/shard_map/all_to_all | solution.py:288
  109.3 9.7 %copy-start.2 = (bf16[16,136,256]{2,1,0:T(8,128)(2,1)}, bf16[16,136,256]{2,1,0:T(8,128)(2,1)S(1)}, u32[]{:S(2)}) copy-start(bf16[16,136,256]{2,1,0:T(8,128)(2,1)S(1)} %all-to-all-done.3.refs_1_) | copy-start | bytes 3342340
  109.3 20.8 %all-to-all-start.1 = ((bf16[16,136,256]{2,1,0:T(8,128)(2,1)}), bf16[16,136,256]{2,1,0:T(8,128)(2,1)S(1)}, u32[]{:S(2)}, u32[]{:S(2)}) async-start(bf16[16,136,256]{2,1,0:T(8,128)(2,1)} %shard_map.100), calls=%async_computation.1 | async-start | bytes 2228224 | tf_op jit(solution)/shard_map/all_to_all | solution.py:288
  130.1 1.0 copy-start.3
